TPU v7x, 256 devices: a whole 4x4x8 slice. The times are simulated.
256 devices in a mesh: samp: 64 (over x, z, core), chan: 4 (over y).
Axes of the slice: x: 4, y: 4, z: 8, core: 2. Of those that a mesh axis runs over, the one named last changes fastest.
Arguments:
- loads: float32 [256, 196608], P('chan', 'samp')
- coords: float32 [6, 196608], P(None, 'samp'), may hold values from -6 to 6
- coreg_factor: float32 [256, 256], P('chan'), may hold values from -0.375 to 0.375
- noise: float32 [256], P('chan'), may hold values from 0.1 to 1
- run_perm: int32 [196608], P('samp'), may hold values from 0 to 196607, as said below
- block_nbrs: int32 [1536, 12], P('samp'), may hold values from 0 to 1535, as said below
- nbr_count: int32 [1536], P('samp'), may hold values from 1 to 12, as said below
Outputs:
- solution: float32 [256, 196608], P('chan', 'samp')
- residual: float32 [256, 196608], P('chan', 'samp')
Inputs may be any that keep to these rules, and one draw needn't show every extreme that they name: `block_nbrs`: the blocks are cut into clusters of consecutive blocks, each of 1 to 12 blocks. Row b lists the blocks of b's cluster in increasing order in its first nbr_count[b] entries; its other entries hold b itself. `nbr_count`: the size of block b's cluster; some block's cluster has 12 blocks. `run_perm`: within each aligned range of 3072 positions (the runs of one samp device), a permutation of that range.
All inputs are finite; a program needn't handle non-finite values.
Results may differ from a plain program's by a relative error of at most 0.0035.
Values may be sent and summed in bfloat16 or wider, within the bound.
No kernel may reach another device: no remote copies, remote signals or barrier semaphores. Data moves between devices by JAX's collectives and lax.ppermute only.
A program may use at most 64 MiB of HBM per device.

v0:
```python
import jax
import jax.numpy as jnp
from jax import lax
from jax.sharding import PartitionSpec as P

ITERS = 2


SUPPORT = 5.0
AMPLITUDE = 0.05


def extended(block, sides, width):
    for axis, dim in sides:
        count = lax.axis_size(axis)
        forward = [(i, i + 1) for i in range(count - 1)]
        backward = [(target, source) for source, target in forward]
        low = lax.ppermute(
            lax.slice_in_dim(block, block.shape[dim] - width, None, axis=dim), axis, forward
        )
        high = lax.ppermute(lax.slice_in_dim(block, 0, width, axis=dim), axis, backward)
        block = jnp.concatenate([low, block, high], axis=dim)
    return block


def wendland(squared):
    radius_frac = jnp.sqrt(squared) / SUPPORT
    remain = jnp.maximum(1.0 - radius_frac, 0.0)
    cubed = remain * remain * remain
    return cubed * cubed * (6.0 * radius_frac + 1.0)


def squared_norm(remainder):
    return lax.psum(jnp.sum(remainder * remainder), ("samp", "chan"))


def per_device(loads, coords, coreg_factor, noise, run_perm, block_nbrs, nbr_count):
    chan_local, runs_local = loads.shape
    blocks_local = nbr_count.shape[0]
    block_runs = runs_local // blocks_local
    dims = coords.shape[0]
    slot_limit = block_nbrs.shape[1]
    device_pos = lax.axis_index("samp")
    local_perm = run_perm - device_pos * runs_local
    sorted_coords = jnp.take(coords, local_perm, axis=1)
    sorted_loads = jnp.take(loads, local_perm, axis=1)
    full_factor = lax.all_gather(coreg_factor, "chan", axis=0, tiled=True)
    reach_runs = blocks_local * block_runs
    window_blocks = blocks_local + 2 * blocks_local
    widened_coords = extended(sorted_coords, (("samp", 1),), reach_runs)
    coord_blocks = widened_coords.reshape(dims, window_blocks, block_runs)
    own_coords = sorted_coords.reshape(dims, blocks_local, block_runs)
    nbr_local = block_nbrs - (device_pos * blocks_local - blocks_local)
    slot_total = jnp.max(nbr_count)

    def build_tile(slot_index):
        partner_ids = lax.dynamic_index_in_dim(nbr_local, slot_index, 1, keepdims=False)
        live_mask = (slot_index < nbr_count).astype(jnp.float32)
        partner = jnp.take(coord_blocks, partner_ids, axis=1)
        squared = jnp.zeros((blocks_local, block_runs, block_runs), jnp.float32)
        for component in range(dims):
            difference = own_coords[component][:, :, None] - partner[component][:, None, :]
            squared = squared + difference * difference
        return (wendland(squared) * live_mask[:, None, None]).astype(jnp.bfloat16)

    all_tiles = lax.map(build_tile, jnp.arange(slot_limit, dtype=jnp.int32))
    iterate = jnp.zeros_like(sorted_loads)
    remainder = sorted_loads
    direction = sorted_loads
    norm_now = squared_norm(remainder)
    for iteration in range(ITERS):
        rounded = direction.astype(jnp.bfloat16)
        coreg_cols = jnp.dot(full_factor, coreg_factor.T, precision=lax.Precision.HIGHEST)
        rounded_wide = rounded.astype(jnp.float32)
        mixed = lax.psum_scatter(
            jnp.dot(coreg_cols, rounded_wide, precision=lax.Precision.HIGHEST),
            "chan",
            scatter_dimension=0,
            tiled=True,
        )
        mixed_b = mixed.astype(jnp.bfloat16)
        widened = extended(mixed_b, (("samp", 1),), reach_runs)
        value_blocks = widened.reshape(chan_local, window_blocks, block_runs)

        def slot_step(slot_index, summed):
            partner_ids = lax.dynamic_index_in_dim(nbr_local, slot_index, 1, keepdims=False)
            kernel_tile = lax.dynamic_index_in_dim(all_tiles, slot_index, 0, keepdims=False)
            partner_vals = jnp.take(value_blocks, partner_ids, axis=1)
            return summed + jnp.einsum(
                "bim,cbm->cbi", kernel_tile, partner_vals, preferred_element_type=jnp.float32
            )

        summed = lax.fori_loop(
            0, slot_total, slot_step, jnp.zeros((chan_local, blocks_local, block_runs), jnp.float32)
        )
        mapped = AMPLITUDE * summed.reshape(chan_local, runs_local) + noise[:, None] * direction
        step_size = norm_now / lax.psum(jnp.sum(direction * mapped), ("samp", "chan"))
        iterate = iterate + step_size * direction
        remainder = remainder - step_size * mapped
        if iteration + 1 < ITERS:
            norm_next = squared_norm(remainder)
            direction = remainder + norm_next / norm_now * direction
            norm_now = norm_next
    solution = jnp.zeros_like(iterate).at[:, local_perm].set(iterate)
    residual = jnp.zeros_like(remainder).at[:, local_perm].set(remainder)
    return (solution, residual)


def solution(mesh):
    return jax.shard_map(
        per_device,
        mesh=mesh,
        in_specs=(
            P("chan", "samp"),
            P(None, "samp"),
            P("chan", None),
            P("chan"),
            P("samp"),
            P("samp", None),
            P("samp"),
        ),
        out_specs=(P("chan", "samp"), P("chan", "samp")),
        check_vma=False,
    )
```

profile of v0, /device:TPU:2, one launch (start us, length us, event | category | flops | bytes accessed | tf_op | source)
XLA Modules:
  0.0 663.8 jit_solution(14506131887120780203)
XLA Ops:
  9.6 12.8 %all_gather.3 = f32[256,256]{1,0:T(8,128)S(1)} all-gather(f32[64,256]{1,0:T(8,128)S(1)} %copy-done.6), channel_id=1, replica_groups=mesh['samp'=64,'chan'=4] {'chan'}, dimensions={0}, use_global_device_ids=true | all-gather | bytes 327680 | tf_op jit(solution)/shard_map/all_gather | solution.py:47
  22.7 8.1 %gather_fusion.3 = f32[3072,64]{1,0:T(8,128)S(1)} fusion(f32[64,3072]{0,1:T(8,128)S(1)} %copy.31, s32[3072]{0:T(1024)S(1)} %broadcast_clamp_fusion), kind=kCustom, calls=%fused_computation.3 | custom fusion | bytes 1585152 | tf_op jit(solution)/shard_map/jit(_take)/gather | solution.py:46
  30.9 4.1 fusion.35
  37.5 9.5 %gather_fusion.4 = f32[3072,6]{1,0:T(8,128)S(1)} fusion(f32[6,3072]{0,1:T(8,128)} %copy.33, s32[3072]{0:T(1024)S(1)} %broadcast_clamp_fusion), kind=kCustom, calls=%fused_computation.4 | custom fusion | bytes 159744 | tf_op jit(solution)/shard_map/jit(_take)/gather | solution.py:45
  47.1 2.5 bitcast_select_fusion
  49.6 1.9 copy.35
  51.5 1.9 collective-permute-start.2
  53.4 5.8 collective-permute-start.3
  60.2 2.2 multiply_reduce_fusion
  63.9 14.3 %reduce-scatter.3.cloned.1.call-done = f32[64,3072]{1,0:T(8,128)} async-done(((f32[256,3072]{1,0:T(8,128)}), f32[64,3072]{1,0:T(8,128)}) %reduce-scatter.3.cloned.1.call-update) | async-done | bytes 786448 | tf_op jit(solution)/shard_map/reduce_scatter | solution.py:75
  79.4 1.9 collective-permute-start
  81.4 5.8 collective-permute-start.1
  87.1 111.9 %while.32 = (s32[]{:T(128)}, bf16[12,24,128,128]{3,2,1,0:T(8,128)(2,1)}, f32[6,24,128]{2,1,0:T(8,128)S(1)}, s32[12]{0:T(128)S(1)}, s32[24,12]{0,1:T(8,128)}, /*i...) while((s32[]{:T(128)}, bf16[12,24,128,128]{3,2,1,0:T(8,128)(2,1)}, ...), condition=%wide.region_4.5_spmd, body=%wide.region_3.4_spmd.sunk | while | flops 11029701 | bytes 1529195 | solution.py:66
  91.8 4.7 fusion.63
  101.1 4.7 fusion.63
  110.4 4.7 fusion.63
  119.8 4.7 fusion.63
  129.1 4.7 fusion.63
  138.4 4.7 fusion.63
  147.7 4.7 fusion.63
  157.0 4.7 fusion.63
  166.4 4.7 fusion.63
  175.7 4.7 fusion.63
  185.0 4.7 fusion.63
  194.4 4.7 fusion.63
  199.1 2.4 copy_bitcast_fusion.1
  201.6 61.9 %while.33 = (s32[]{:T(128)}, f32[64,24,128]{2,0,1:T(8,128)S(1)}, s32[]{:T(128)}, s32[24,12]{0,1:T(8,128)}, bf16[64,72,128]{2,0,1:T(8,128)(2,1)}, /*index=5*/bf16...) while((s32[]{:T(128)}, f32[64,24,128]{2,0,1:T(8,128)S(1)}, s32[]{:T(128)}, s32[24,12]{0,1:T(8,128)}, ...), condition=%wide.region_7.9_spmd, body=%wide.region_6.8_spmd.sunk | while | flops 50726036 | bytes 3543607 | solution.py:93
  202.9 1.9 gather_fusion.1
  264.5 74.1 %all-reduce = (f32[]{:T(128)}, f32[]{:T(128)}) all-reduce(f32[]{:T(128)} %multiply_reduce_fusion, f32[]{:T(128)} %multiply_reduce_fusion.3), channel_id=1, replica_groups=mesh['samp'=64,'chan'=4] {'samp','chan'}, use_global_device_ids=true, to_apply=%region_1.2 | all-reduce | flops 2 | bytes 16 | tf_op jit(solution)/shard_map/psum | solution.py:34
  341.8 73.6 %psum.30 = f32[]{:T(128)} all-reduce(f32[]{:T(128)} %get-tuple-element.274), channel_id=1, replica_groups=mesh['samp'=64,'chan'=4] {'samp','chan'}, use_global_device_ids=true, to_apply=%region_11.13 | all-reduce | flops 1 | bytes 8 | tf_op jit(solution)/shard_map/psum | solution.py:34
  416.7 2.8 copy.40
  419.5 2.7 multiply_add_fusion
  423.4 3.1 fusion.38
  426.6 38.3 %reduce-scatter.5.cloned.1.call-done = f32[64,3072]{1,0:T(8,128)} async-done(((f32[256,3072]{1,0:T(8,128)}), f32[64,3072]{1,0:T(8,128)}) %reduce-scatter.5.cloned.1.call-update) | async-done | bytes 786448 | tf_op jit(solution)/shard_map/reduce_scatter | solution.py:75
  466.1 1.9 collective-permute-start.4
  468.0 5.8 collective-permute-start.5
  473.8 3.5 collective-permute-done.4
  480.4 61.9 %while.34 = (s32[]{:T(128)}, f32[64,24,128]{2,0,1:T(8,128)S(1)}, s32[]{:T(128)}, s32[24,12]{0,1:T(8,128)}, bf16[64,72,128]{2,0,1:T(8,128)(2,1)}, /*index=5*/bf16...) while((s32[]{:T(128)}, f32[64,24,128]{2,0,1:T(8,128)S(1)}, s32[]{:T(128)}, ...), condition=%wide.region_14.16_spmd, body=%wide.region_13.15_spmd.sunk | while | flops 50726036 | bytes 3543607 | solution.py:93
  481.8 1.9 gather_fusion.2
  532.9 1.9 gather_fusion.2
  542.4 3.1 broadcast_multiply_fusion
  545.4 2.9 copy.42
  548.3 77.1 %psum.31 = f32[]{:T(128)} all-reduce(f32[]{:T(128)} %get-tuple-element.273), channel_id=1, replica_groups=mesh['samp'=64,'chan'=4] {'samp','chan'}, use_global_device_ids=true, to_apply=%region_16.18 | all-reduce | flops 1 | bytes 8 | tf_op jit(solution)/shard_map/psum | solution.py:97
  626.7 3.6 fusion.26
  630.4 9.8 %scatter_custom_fusion.1 = f32[64,3072]{0,1:T(8,128)} fusion(s32[3072]{0:T(1024)} %copy-done.8, f32[64,3072]{0,1:T(8,128)} %fusion.26, f32[]{:T(128)} %constant.140.clone.1), kind=kCustom, calls=%fused_computation.50 | custom fusion | bytes 2359808 | tf_op jit(solution)/shard_map/scatter | solution.py:105
  640.1 2.9 copy.44
  643.0 11.2 %scatter_custom_fusion = f32[64,3072]{0,1:T(8,128)} fusion(s32[3072]{0:T(1024)} %copy-done.8, f32[64,3072]{0,1:T(8,128)S(1)} %copy-done.2, f32[3072,64]{1,0:T(8,128)S(1)} %gather_fusion.3, f32[]{:T(128)S(6)} %div.14, f32[]{:T(128)S(6)} %div.12, f32[]{:T(128)} %constant.146.clone.1, f32[]{:T(128)} %constant.140.clone.1, ...), kind=kCustom, calls=%fused_computation.55 | custom fusion | flops 786432 | bytes 2363400 | tf_op jit(solution)/shard_map/scatter | solution.py:104
  654.2 2.7 copy.43
  (242 shorter events, 151.0 us)
Async XLA Ops:
  7.2 2.4 copy-start.6
  7.2 71.1 %reduce-scatter.3.cloned.1.call-start = ((), (), s32[]{:S(2)}) async-start(), calls=%async_computation.2 | async-start | bytes 3932160 | tf_op jit(solution)/shard_map/reduce_scatter | solution.py:75
  7.9 22.9 %copy-start.8 = (s32[3072]{0:T(1024)}, s32[3072]{0:T(1024)S(1)}, u32[]{:S(2)}) copy-start(s32[3072]{0:T(1024)S(1)} %get-tuple-element.259) | copy-start | bytes 36868
  22.7 8.1 %copy-start.4 = (f32[256,64]{0,1:T(8,128)}, f32[256,64]{0,1:T(8,128)S(1)}, u32[]{:S(2)}) copy-start(f32[256,64]{0,1:T(8,128)S(1)} %fusion.49) | copy-start | bytes 196612
  35.0 0.9 copy-start.7
  35.0 429.9 %reduce-scatter.5.cloned.1.call-start = ((), (), s32[]{:S(2)}) async-start(), calls=%async_computation.3 | async-start | bytes 3932160 | tf_op jit(solution)/shard_map/reduce_scatter | solution.py:75
  49.6 10.1 %copy-start.10 = (s32[24,12]{0,1:T(8,128)S(1)}, s32[24,12]{0,1:T(8,128)}, u32[]{:S(2)}) copy-start(s32[24,12]{0,1:T(8,128)} %param.20) | copy-start | bytes 3460
  51.5 12.4 %collective-permute-start.2 = (f32[6,3072]{1,0:T(8,128)S(1)}, f32[6,3072]{1,0:T(8,128)S(1)}, u32[]{:S(2)}, u32[]{:S(2)}) collective-permute-start(f32[6,3072]{1,0:T(8,128)S(1)} %copy.35), channel_id=1, source_target_pairs={{0,4},{4,8},{8,12},{12,16},{16,20},{20,24},{24,28},{28,32},{32,36}... | collective-permute-start | bytes 221192 | tf_op jit(solution)/shard_map/ppermute | solution.py:18
  53.4 10.5 %collective-permute-start.3 = (f32[6,3072]{1,0:T(8,128)S(1)}, f32[6,3072]{1,0:T(8,128)S(1)}, u32[]{:S(2)}, u32[]{:S(2)}) collective-permute-start(f32[6,3072]{1,0:T(8,128)S(1)} %copy.35), channel_id=1, source_target_pairs={{4,0},{8,4},{12,8},{16,12},{20,16},{24,20},{28,24},{32,28},{36,32}... | collective-permute-start | bytes 221192 | tf_op jit(solution)/shard_map/ppermute | solution.py:21
  62.4 0.7 copy-start.11
  63.1 276.9 %copy-start.3 = (f32[64,24,128]{2,0,1:T(8,128)}, f32[64,24,128]{2,0,1:T(8,128)S(1)}, u32[]{:S(2)}) copy-start(f32[64,24,128]{2,0,1:T(8,128)S(1)} %copy.32) | copy-start | bytes 2359300
  79.4 119.6 %collective-permute-start = (bf16[64,3072]{1,0:T(8,128)(2,1)S(1)}, bf16[64,3072]{1,0:T(8,128)(2,1)}, u32[]{:S(2)}, u32[]{:S(2)}) collective-permute-start(bf16[64,3072]{1,0:T(8,128)(2,1)S(1)} %convert_element_type.38), channel_id=1, source_target_pairs={{0,4},{4,8},{8,12},{12,16},{16,20},{20,24},{24,28},{28,32},{32,36}... | collective-permute-start | bytes 1179656 | tf_op jit(solution)/shard_map/ppermute | solution.py:18
  81.4 117.7 %collective-permute-start.1 = (bf16[64,3072]{1,0:T(8,128)(2,1)S(1)}, bf16[64,3072]{1,0:T(8,128)(2,1)}, u32[]{:S(2)}, u32[]{:S(2)}) collective-permute-start(bf16[64,3072]{1,0:T(8,128)(2,1)S(1)} %convert_element_type.38), channel_id=1, source_target_pairs={{4,0},{8,4},{12,8},{16,12},{20,16},{24,20},{28,24},{32,28},{36,32}... | collective-permute-start | bytes 1179656 | tf_op jit(solution)/shard_map/ppermute | solution.py:21
  201.6 61.9 %copy-start.9 = (f32[64]{0:T(128)S(1)}, f32[64]{0:T(128)}, u32[]{:S(2)}) copy-start(f32[64]{0:T(128)} %param.18) | copy-start | bytes 772
  419.5 4.0 copy-start.5
  422.2 1.2 copy-start.1
  466.1 11.2 %collective-permute-start.4 = (bf16[64,3072]{1,0:T(8,128)(2,1)S(1)}, bf16[64,3072]{1,0:T(8,128)(2,1)S(1)}, u32[]{:S(2)}, u32[]{:S(2)}) collective-permute-start(bf16[64,3072]{1,0:T(8,128)(2,1)S(1)} %convert_element_type.40), channel_id=1, source_target_pairs={{0,4},{4,8},{8,12},{12,16},{16,20},{20,24},{24,28},{28,32},{32,36}... | collective-permute-start | bytes 1179656 | tf_op jit(solution)/shard_map/ppermute | solution.py:18
  468.0 11.0 %collective-permute-start.5 = (bf16[64,3072]{1,0:T(8,128)(2,1)S(1)}, bf16[64,3072]{1,0:T(8,128)(2,1)S(1)}, u32[]{:S(2)}, u32[]{:S(2)}) collective-permute-start(bf16[64,3072]{1,0:T(8,128)(2,1)S(1)} %convert_element_type.40), channel_id=1, source_target_pairs={{4,0},{8,4},{12,8},{16,12},{20,16},{24,20},{28,24},{32,28},{36,32}... | collective-permute-start | bytes 1179656 | tf_op jit(solution)/shard_map/ppermute | solution.py:21
  545.4 81.3 %copy-start = (f32[64,24,128]{0,2,1:T(8,128)S(1)}, f32[64,24,128]{0,2,1:T(8,128)}, u32[]{:S(2)}) copy-start(f32[64,24,128]{0,2,1:T(8,128)} %copy.40) | copy-start | bytes 2359300
  640.1 2.9 copy-start.2
Sparse Core Ops, SparseCore 0:
  35.1 43.1 reduce-scatter.2
  426.7 38.1 reduce-scatter.4
where the time goes:
time: 670 us; the launch traced here: 664 us
  blocking collectives  238 us (36%)
  other arithmetic  127 us (19%)
  local copies, waits for them, and re-layouts  108 us (16%)
  waiting for transfers between devices  58 us (9%)
  matrix products  52.5 us (8%)
  loops' own time  40.1 us (6%)
  starting transfers between devices  23.1 us (3%)
  between operations  18.4 us (3%)
    psum x2, blocking collectives, squared_norm(): return lax.psum(jnp.sum(remainder * remainder), ('samp', 'chan'))  148 us
    psum x1, blocking collectives, per_device(): lax.psum(jnp.sum(direction * mapped), ('samp', 'chan'))  77.1 us
    dynamic_update_slice x12, other arithmetic, per_device(): all_tiles = lax.map(build_tile, jnp.arange(slot_limit, dtype=jnp.int32))  56.4 us
    reduce_scatter x2, waiting for transfers between devices, per_device(): lax.psum_scatter(jnp.dot(coreg_cols, rounded_wide, precision=lax.Precisio...  52.6 us
    gather x24, local copies, waits for them, and re-layouts, slot_step(): partner_vals = jnp.take(value_blocks, partner_ids, axis=1)  45.4 us
    dot_general x24, matrix products, slot_step(): jnp.einsum('bim,cbm->cbi', kernel_tile, partner_vals, preferred_element_t...  44.9 us
    another operation x1, loops' own time, per_device(): all_tiles = lax.map(build_tile, jnp.arange(slot_limit, dtype=jnp.int32))  23.4 us
    ppermute x3, starting transfers between devices, extended(): lax.ppermute(lax.slice_in_dim(block, 0, width, axis=dim), axis, backward)  17.3 us
  transfers between devices with their start and end apart: 8, of which 4 were waited for; matrix products, arithmetic and copies ran while one was open for 16% of the time, Pallas kernels for 0%

commit v1 on v0

--- a/solution.py
+++ b/solution.py
@@ -10,17 +10,15 @@
 AMPLITUDE = 0.05
 
 
-def extended(block, sides, width):
-    for axis, dim in sides:
-        count = lax.axis_size(axis)
-        forward = [(i, i + 1) for i in range(count - 1)]
-        backward = [(target, source) for source, target in forward]
-        low = lax.ppermute(
-            lax.slice_in_dim(block, block.shape[dim] - width, None, axis=dim), axis, forward
-        )
-        high = lax.ppermute(lax.slice_in_dim(block, 0, width, axis=dim), axis, backward)
-        block = jnp.concatenate([low, block, high], axis=dim)
-    return block
+def extended(block, axis, dim, width):
+    count = lax.axis_size(axis)
+    forward = [(i, i + 1) for i in range(count - 1)]
+    backward = [(target, source) for source, target in forward]
+    low = lax.ppermute(
+        lax.slice_in_dim(block, block.shape[dim] - width, None, axis=dim), axis, forward
+    )
+    high = lax.ppermute(lax.slice_in_dim(block, 0, width, axis=dim), axis, backward)
+    return jnp.concatenate([low, block, high], axis=dim)
 
 
 def wendland(squared):
@@ -30,8 +28,15 @@
     return cubed * cubed * (6.0 * radius_frac + 1.0)
 
 
-def squared_norm(remainder):
-    return lax.psum(jnp.sum(remainder * remainder), ("samp", "chan"))
+def global_sum(value):
+    for axis in ("chan", "samp"):
+        count = lax.axis_size(axis)
+        step = 1
+        while step < count:
+            pairs = [(i, i ^ step) for i in range(count)]
+            value = value + lax.ppermute(value, axis, pairs)
+            step *= 2
+    return value
 
 
 def per_device(loads, coords, coreg_factor, noise, run_perm, block_nbrs, nbr_count):
@@ -40,17 +45,20 @@
     block_runs = runs_local // blocks_local
     dims = coords.shape[0]
     slot_limit = block_nbrs.shape[1]
+    halo = slot_limit - 1
     device_pos = lax.axis_index("samp")
     local_perm = run_perm - device_pos * runs_local
     sorted_coords = jnp.take(coords, local_perm, axis=1)
     sorted_loads = jnp.take(loads, local_perm, axis=1)
+    norm_now = global_sum(jnp.sum(sorted_loads * sorted_loads))
     full_factor = lax.all_gather(coreg_factor, "chan", axis=0, tiled=True)
-    reach_runs = blocks_local * block_runs
-    window_blocks = blocks_local + 2 * blocks_local
-    widened_coords = extended(sorted_coords, (("samp", 1),), reach_runs)
+    coreg_rows = jnp.dot(coreg_factor, full_factor.T, precision=lax.Precision.HIGHEST)
+    reach_runs = halo * block_runs
+    window_blocks = blocks_local + 2 * halo
+    widened_coords = extended(sorted_coords, "samp", 1, reach_runs)
     coord_blocks = widened_coords.reshape(dims, window_blocks, block_runs)
     own_coords = sorted_coords.reshape(dims, blocks_local, block_runs)
-    nbr_local = block_nbrs - (device_pos * blocks_local - blocks_local)
+    nbr_local = block_nbrs - (device_pos * blocks_local - halo)
     slot_total = jnp.max(nbr_count)
 
     def build_tile(slot_index):
@@ -67,19 +75,14 @@
     iterate = jnp.zeros_like(sorted_loads)
     remainder = sorted_loads
     direction = sorted_loads
-    norm_now = squared_norm(remainder)
     for iteration in range(ITERS):
         rounded = direction.astype(jnp.bfloat16)
-        coreg_cols = jnp.dot(full_factor, coreg_factor.T, precision=lax.Precision.HIGHEST)
-        rounded_wide = rounded.astype(jnp.float32)
-        mixed = lax.psum_scatter(
-            jnp.dot(coreg_cols, rounded_wide, precision=lax.Precision.HIGHEST),
-            "chan",
-            scatter_dimension=0,
-            tiled=True,
+        gathered = lax.all_gather(rounded, "chan", axis=0, tiled=True)
+        mixed = jnp.dot(
+            coreg_rows, gathered.astype(jnp.float32), precision=lax.Precision.HIGHEST
         )
         mixed_b = mixed.astype(jnp.bfloat16)
-        widened = extended(mixed_b, (("samp", 1),), reach_runs)
+        widened = extended(mixed_b, "samp", 1, reach_runs)
         value_blocks = widened.reshape(chan_local, window_blocks, block_runs)
 
         def slot_step(slot_index, summed):
@@ -94,11 +97,11 @@
             0, slot_total, slot_step, jnp.zeros((chan_local, blocks_local, block_runs), jnp.float32)
         )
         mapped = AMPLITUDE * summed.reshape(chan_local, runs_local) + noise[:, None] * direction
-        step_size = norm_now / lax.psum(jnp.sum(direction * mapped), ("samp", "chan"))
+        step_size = norm_now / global_sum(jnp.sum(direction * mapped))
         iterate = iterate + step_size * direction
         remainder = remainder - step_size * mapped
         if iteration + 1 < ITERS:
-            norm_next = squared_norm(remainder)
+            norm_next = global_sum(jnp.sum(remainder * remainder))
             direction = remainder + norm_next / norm_now * direction
             norm_now = norm_next
     solution = jnp.zeros_like(iterate).at[:, local_perm].set(iterate)

time: 670 us -> 499 us (0.74)
  blocking collectives: 238 us -> 12.4 us
  starting transfers between devices: 23.1 us -> 90.8 us
  other arithmetic: 127 us -> 79.2 us
  waiting for transfers between devices: 58 us -> 104 us
  local copies, waits for them, and re-layouts: 108 us -> 81.5 us
  between operations: 18.4 us -> 37 us
    psum x3 -> x0, blocking collectives: 225 us -> none  [the longest x2 148 us: squared_norm(): return lax.psum(jnp.sum(remainder * remainder), ('samp', 'chan'))]
    ppermute x0 -> x32, waiting for transfers between devices: none -> 73.2 us  [global_sum(): value = value + lax.ppermute(value, axis, pairs)]
    ppermute x0 -> x32, starting transfers between devices: none -> 66.2 us  [global_sum(): value = value + lax.ppermute(value, axis, pairs)]
    reduce_scatter x2 -> x0, waiting for transfers between devices: 52.6 us -> none  [per_device(): lax.psum_scatter(jnp.dot(coreg_cols, rounded_wide, precision=lax.Precisio...]
    gather x24, local copies, waits for them, and re-layouts: 45.4 us -> 14.9 us  [slot_step(): partner_vals = jnp.take(value_blocks, partner_ids, axis=1)]
    all_gather x0 -> x2, waiting for transfers between devices: none -> 27.8 us  [per_device(): gathered = lax.all_gather(rounded, 'chan', axis=0, tiled=True)]
    and x24, other arithmetic: 16.7 us -> 0.37 us  [slot_step(): partner_vals = jnp.take(value_blocks, partner_ids, axis=1)]
    scatter x1 -> x0, other arithmetic: 11.2 us -> none  [per_device(): solution = jnp.zeros_like(iterate).at[:, local_perm].set(iterate)]
  transfers between devices with their start and end apart: 8 -> 40, of which waited for: 4 -> 34; matrix products, arithmetic and copies ran while one was open for 16% -> 20% of each run, Pallas kernels for 0% -> 0%
where the time goes in v1:
time: 499 us; the launch traced here: 497 us
  waiting for transfers between devices  104 us (21%)
  starting transfers between devices  90.8 us (18%)
  local copies, waits for them, and re-layouts  81.5 us (16%)
  other arithmetic  79.2 us (16%)
  matrix products  50 us (10%)
  loops' own time  41.6 us (8%)
  between operations  37 us (7%)
  blocking collectives  12.4 us (2%)
    ppermute x32, waiting for transfers between devices, global_sum(): value = value + lax.ppermute(value, axis, pairs)  73.2 us
    ppermute x32, starting transfers between devices, global_sum(): value = value + lax.ppermute(value, axis, pairs)  66.2 us
    dynamic_update_slice x12, other arithmetic, per_device(): all_tiles = lax.map(build_tile, jnp.arange(slot_limit, dtype=jnp.int32))  56.4 us
    dot_general x24, matrix products, slot_step(): jnp.einsum('bim,cbm->cbi', kernel_tile, partner_vals, preferred_element_t...  44.9 us
    all_gather x2, waiting for transfers between devices, per_device(): gathered = lax.all_gather(rounded, 'chan', axis=0, tiled=True)  27.8 us
    another operation x1, loops' own time, per_device(): all_tiles = lax.map(build_tile, jnp.arange(slot_limit, dtype=jnp.int32))  24 us
    ppermute x3, starting transfers between devices, extended(): lax.ppermute(lax.slice_in_dim(block, 0, width, axis=dim), axis, backward)  18.7 us
    another operation x2, loops' own time, per_device(): lax.fori_loop(0, slot_total, slot_step, jnp.zeros((chan_local, blocks_loc...  17.6 us
  transfers between devices with their start and end apart: 40, of which 34 were waited for; matrix products, arithmetic and copies ran while one was open for 20% of the time, Pallas kernels for 0%

profile of v1, /device:TPU:2, one launch (start us, length us, event | category | flops | bytes accessed | tf_op | source)
XLA Modules:
  0.0 496.5 jit_solution(6958527566573883469)
XLA Ops:
  9.5 10.9 %gather_fusion.3 = f32[3072,64]{1,0:T(8,128)} fusion(f32[64,3072]{0,1:T(8,128)S(1)} %copy.47, s32[3072]{0:T(1024)S(1)} %broadcast_clamp_fusion), kind=kCustom, calls=%fused_computation.3 | custom fusion | bytes 1585152 | tf_op jit(solution)/shard_map/jit(_take)/gather | solution.py:52
  24.9 9.5 %gather_fusion.4 = f32[3072,6]{1,0:T(8,128)S(1)} fusion(f32[6,3072]{0,1:T(8,128)} %copy.50, s32[3072]{0:T(1024)S(1)} %broadcast_clamp_fusion), kind=kCustom, calls=%fused_computation.4 | custom fusion | bytes 159744 | tf_op jit(solution)/shard_map/jit(_take)/gather | solution.py:51
  34.4 2.5 bitcast_select_fusion
  41.0 7.2 %collective-permute-start.11 = (f32[6,1408]{1,0:T(8,128)S(1)}, f32[6,1408]{1,0:T(8,128)S(1)}, u32[]{:S(2)}, u32[]{:S(2)}) collective-permute-start(f32[6,1408]{1,0:T(8,128)S(1)} %get-tuple-element.302), channel_id=1, source_target_pairs={{4,0},{8,4},{12,8},{16,12},{20,16},{24,20},{28,24},{32,28},{36,32}... | collective-permute-start | bytes 101384 | tf_op jit(solution)/shard_map/ppermute | solution.py:20
  51.0 12.4 %all_gather.9 = f32[256,256]{1,0:T(8,128)S(1)} all-gather(f32[64,256]{1,0:T(8,128)S(1)} %copy-done.3), channel_id=1, replica_groups=mesh['samp'=64,'chan'=4] {'chan'}, dimensions={0}, use_global_device_ids=true | all-gather | bytes 327680 | tf_op jit(solution)/shard_map/all_gather | solution.py:54
  65.7 2.8 collective-permute-start.1
  79.8 2.6 collective-permute-done.4
  83.0 6.5 %collective-permute-start.5 = (f32[]{:T(128)}, f32[]{:T(128)}, u32[]{:S(2)}, u32[]{:S(2)}) collective-permute-start(f32[]{:T(128)} %add.263), channel_id=1, source_target_pairs={{0,32},{4,36},{8,40},{12,44},{16,48},{20,52},{24,56},{28,60},{32,0... | collective-permute-start | bytes 20 | tf_op jit(solution)/shard_map/ppermute | solution.py:37
  95.5 3.8 collective-permute-start.7
  105.7 5.8 %collective-permute-start.9 = (bf16[64,1408]{1,0:T(8,128)(2,1)S(1)}, bf16[64,1408]{1,0:T(8,128)(2,1)S(1)}, u32[]{:S(2)}, u32[]{:S(2)}) collective-permute-start(bf16[64,1408]{1,0:T(8,128)(2,1)S(1)} %get-tuple-element.300), channel_id=1, source_target_pairs={{4,0},{8,4},{12,8},{16,12},{20,16},{24,20},{28,24},{32,28},{36,32}... | collective-permute-start | bytes 540680 | tf_op jit(solution)/shard_map/ppermute | solution.py:20
  111.5 104.2 %while.32 = (s32[]{:T(128)}, bf16[12,24,128,128]{3,2,1,0:T(8,128)(2,1)}, f32[6,24,128]{2,1,0:T(8,128)S(1)}, s32[12]{0:T(128)S(1)}, s32[24,12]{0,1:T(8,128)S(1)},...) while((s32[]{:T(128)}, bf16[12,24,128,128]{3,2,1,0:T(8,128)(2,1)}, ...), condition=%wide.region_3.4_spmd, body=%wide.region_2.3_spmd.sunk | while | flops 11029701 | bytes 1529195 | solution.py:74
  115.5 4.7 fusion.57
  124.1 4.7 fusion.57
  132.8 4.7 fusion.57
  141.5 4.7 fusion.57
  150.2 4.7 fusion.57
  158.8 4.7 fusion.57
  167.5 4.7 fusion.57
  176.2 4.7 fusion.57
  184.9 4.7 fusion.57
  193.6 4.7 fusion.57
  202.3 4.7 fusion.57
  211.0 4.7 fusion.57
  216.0 39.0 %while.33 = (s32[]{:T(128)}, f32[64,24,128]{2,0,1:T(8,128)S(1)}, s32[]{:T(128)}, s32[24,12]{0,1:T(8,128)S(1)}, bf16[64,46,128]{2,0,1:T(8,128)(2,1)S(1)}, /*index...) while((s32[]{:T(128)}, f32[64,24,128]{2,0,1:T(8,128)S(1)}, s32[]{:T(128)}, ...), condition=%wide.region_5.7_spmd, body=%wide.region_4.6_spmd.sunk | while | flops 50726036 | bytes 3543607 | solution.py:96
  256.7 3.0 collective-permute-done.12
  261.0 2.8 collective-permute-start.13
  274.8 3.2 collective-permute-done.16
  278.7 2.4 collective-permute-start.17
  281.1 5.2 %collective-permute-done.17 = f32[]{:T(128)} collective-permute-done((f32[]{:T(128)}, f32[]{:T(128)}, u32[]{:S(2)}, u32[]{:S(2)}) %collective-permute-start.17) | collective-permute-done | bytes 36 | tf_op jit(solution)/shard_map/ppermute | solution.py:37
  293.6 2.9 collective-permute-done.19
  299.0 3.0 collective-permute-done.20
  303.3 2.8 collective-permute-start.21
  316.9 3.2 collective-permute-done.24
  320.8 4.2 collective-permute-start.25
  325.0 3.4 collective-permute-done.25
  335.7 2.9 collective-permute-done.27
  340.4 27.8 %all-gather.5.cloned.1.call-done = bf16[256,3072]{1,0:T(8,128)(2,1)} async-done(((bf16[64,3072]{1,0:T(8,128)(2,1)}), bf16[256,3072]{1,0:T(8,128)(2,1)}) %all-gather.5.cloned.1.call-update) | async-done | bytes 1572880 | tf_op jit(solution)/shard_map/all_gather | solution.py:80
  372.4 5.8 %collective-permute-start.29 = (bf16[64,1408]{1,0:T(8,128)(2,1)S(1)}, bf16[64,1408]{1,0:T(8,128)(2,1)S(1)}, u32[]{:S(2)}, u32[]{:S(2)}) collective-permute-start(bf16[64,1408]{1,0:T(8,128)(2,1)S(1)} %get-tuple-element.298), channel_id=1, source_target_pairs={{4,0},{8,4},{12,8},{16,12},{20,16},{24,20},{28,24},{32,28},{36,32}... | collective-permute-start | bytes 540680 | tf_op jit(solution)/shard_map/ppermute | solution.py:20
  381.5 39.0 %while.34 = (s32[]{:T(128)}, f32[64,24,128]{2,0,1:T(8,128)S(1)}, s32[]{:T(128)}, s32[24,12]{0,1:T(8,128)S(1)}, bf16[64,46,128]{2,0,1:T(8,128)(2,1)S(1)}, /*index...) while((s32[]{:T(128)}, f32[64,24,128]{2,0,1:T(8,128)S(1)}, s32[]{:T(128)}, ...), condition=%wide.region_9.11_spmd, body=%wide.region_8.10_spmd.sunk | while | flops 50726036 | bytes 3543607 | solution.py:96
  422.8 3.3 collective-permute-done.30
  427.3 3.2 collective-permute-start.31
  439.8 2.8 collective-permute-start.34
  445.0 3.6 collective-permute-start.35
  448.7 4.0 collective-permute-done.35
  460.1 2.9 collective-permute-done.37
  463.6 2.4 fusion.25
  467.7 8.8 %scatter_custom_fusion.1 = f32[64,3072]{0,1:T(8,128)S(1)} fusion(s32[3072]{0:T(1024)S(1)} %get-tuple-element.278, f32[3072,64]{1,0:T(8,128)} %copy.61, f32[]{:T(128)} %constant.141.clone.1), kind=kCustom, calls=%fused_computation.70 | custom fusion | bytes 786944 | tf_op jit(solution)/shard_map/scatter | solution.py:108
  479.5 8.8 %scatter_custom_fusion = f32[64,3072]{0,1:T(8,128)S(1)} fusion(s32[3072]{0:T(1024)S(1)} %get-tuple-element.278, f32[3072,64]{1,0:T(8,128)} %copy.59, f32[]{:T(128)} %constant.141.clone.1), kind=kCustom, calls=%fused_computation.72 | custom fusion | bytes 786944 | tf_op jit(solution)/shard_map/scatter | solution.py:107
  (297 shorter events, 184.7 us)
Async XLA Ops:
  7.2 94.2 %all-gather.3.cloned.1.call-start = ((), (), s32[]{:S(2)}) async-start(), calls=%async_computation | async-start | bytes 1966080 | tf_op jit(solution)/shard_map/all_gather | solution.py:80
  20.4 2.8 copy-start.4
  23.2 344.9 %all-gather.5.cloned.1.call-start = ((), (), s32[]{:S(2)}) async-start(), calls=%async_computation.1 | async-start | bytes 1966080 | tf_op jit(solution)/shard_map/all_gather | solution.py:80
  38.9 12.1 %copy-start.3 = (f32[64,256]{1,0:T(8,128)S(1)}, f32[64,256]{1,0:T(8,128)}, u32[]{:S(2)}) copy-start(f32[64,256]{1,0:T(8,128)} %param.17) | copy-start | bytes 196612
  38.9 62.4 %collective-permute-start.10 = (f32[6,1408]{1,0:T(8,128)S(1)}, f32[6,1408]{1,0:T(8,128)S(1)}, u32[]{:S(2)}, u32[]{:S(2)}) collective-permute-start(f32[6,1408]{1,0:T(8,128)S(1)} %get-tuple-element.301), channel_id=1, source_target_pairs={{0,4},{4,8},{8,12},{12,16},{16,20},{20,24},{24,28},{28,32},{32,36}... | collective-permute-start | bytes 101384 | tf_op jit(solution)/shard_map/ppermute | solution.py:17
  41.0 22.9 %copy-start.6 = (s32[24,12]{0,1:T(8,128)S(1)}, s32[24,12]{0,1:T(8,128)}, u32[]{:S(2)}) copy-start(s32[24,12]{0,1:T(8,128)} %param.20) | copy-start | bytes 3460
  41.0 22.9 %copy-start.7 = (s32[24]{0:T(128)S(1)}, s32[24]{0:T(128)}, u32[]{:S(2)}) copy-start(s32[24]{0:T(128)} %param.21) | copy-start | bytes 292
  41.0 60.3 %collective-permute-start.11 = (f32[6,1408]{1,0:T(8,128)S(1)}, f32[6,1408]{1,0:T(8,128)S(1)}, u32[]{:S(2)}, u32[]{:S(2)}) collective-permute-start(f32[6,1408]{1,0:T(8,128)S(1)} %get-tuple-element.302), channel_id=1, source_target_pairs={{4,0},{8,4},{12,8},{16,12},{20,16},{24,20},{28,24},{32,28},{36,32}... | collective-permute-start | bytes 101384 | tf_op jit(solution)/shard_map/ppermute | solution.py:20
  49.0 15.6 %collective-permute-start = (f32[]{:T(128)}, f32[]{:T(128)}, u32[]{:S(2)}, u32[]{:S(2)}) collective-permute-start(f32[]{:T(128)} %multiply_reduce_fusion.3), channel_id=1, source_target_pairs={{0,1},{1,0},{2,3},{3,2},{4,5},{5,4},{6,7},{7,6},{8,9},{9,8},{10,11... | collective-permute-start | bytes 20 | tf_op jit(solution)/shard_map/ppermute | solution.py:37
  65.7 5.2 %collective-permute-start.1 = (f32[]{:T(128)}, f32[]{:T(128)}, u32[]{:S(2)}, u32[]{:S(2)}) collective-permute-start(f32[]{:T(128)} %add.259), channel_id=1, source_target_pairs={{0,2},{1,3},{2,0},{3,1},{4,6},{5,7},{6,4},{7,5},{8,10},{9,11},{10,... | collective-permute-start | bytes 20 | tf_op jit(solution)/shard_map/ppermute | solution.py:37
  71.5 1.3 collective-permute-start.2
  73.5 3.7 collective-permute-start.3
  77.8 4.6 collective-permute-start.4
  83.0 7.6 %collective-permute-start.5 = (f32[]{:T(128)}, f32[]{:T(128)}, u32[]{:S(2)}, u32[]{:S(2)}) collective-permute-start(f32[]{:T(128)} %add.263), channel_id=1, source_target_pairs={{0,32},{4,36},{8,40},{12,44},{16,48},{20,52},{24,56},{28,60},{32,0... | collective-permute-start | bytes 20 | tf_op jit(solution)/shard_map/ppermute | solution.py:37
  91.2 3.7 collective-permute-start.6
  95.5 5.2 %collective-permute-start.7 = (f32[]{:T(128)}, f32[]{:T(128)}, u32[]{:S(2)}, u32[]{:S(2)}) collective-permute-start(f32[]{:T(128)} %add.265), channel_id=1, source_target_pairs={{0,128},{4,132},{8,136},{12,140},{16,144},{20,148},{24,152},{28,15... | collective-permute-start | bytes 20 | tf_op jit(solution)/shard_map/ppermute | solution.py:37
  103.8 111.9 %collective-permute-start.8 = (bf16[64,1408]{1,0:T(8,128)(2,1)S(1)}, bf16[64,1408]{1,0:T(8,128)(2,1)S(1)}, u32[]{:S(2)}, u32[]{:S(2)}) collective-permute-start(bf16[64,1408]{1,0:T(8,128)(2,1)S(1)} %get-tuple-element.299), channel_id=1, source_target_pairs={{0,4},{4,8},{8,12},{12,16},{16,20},{20,24},{24,28},{28,32},{32,36}... | collective-permute-start | bytes 540680 | tf_op jit(solution)/shard_map/ppermute | solution.py:17
  105.7 110.0 %collective-permute-start.9 = (bf16[64,1408]{1,0:T(8,128)(2,1)S(1)}, bf16[64,1408]{1,0:T(8,128)(2,1)S(1)}, u32[]{:S(2)}, u32[]{:S(2)}) collective-permute-start(bf16[64,1408]{1,0:T(8,128)(2,1)S(1)} %get-tuple-element.300), channel_id=1, source_target_pairs={{4,0},{8,4},{12,8},{16,12},{20,16},{24,20},{28,24},{32,28},{36,32}... | collective-permute-start | bytes 540680 | tf_op jit(solution)/shard_map/ppermute | solution.py:20
  216.0 39.0 %copy-start.5 = (f32[64]{0:T(128)S(1)}, f32[64]{0:T(128)}, u32[]{:S(2)}) copy-start(f32[64]{0:T(128)} %param.18) | copy-start | bytes 772
  255.9 3.8 collective-permute-start.12
  261.0 5.2 %collective-permute-start.13 = (f32[]{:T(128)}, f32[]{:T(128)}, u32[]{:S(2)}, u32[]{:S(2)}) collective-permute-start(f32[]{:T(128)} %add.268), channel_id=1, source_target_pairs={{0,2},{1,3},{2,0},{3,1},{4,6},{5,7},{6,4},{7,5},{8,10},{9,11},{10,... | collective-permute-start | bytes 20 | tf_op jit(solution)/shard_map/ppermute | solution.py:37
  266.9 1.5 collective-permute-start.14
  269.0 3.7 collective-permute-start.15
  273.4 4.6 collective-permute-start.16
  278.7 7.6 %collective-permute-start.17 = (f32[]{:T(128)}, f32[]{:T(128)}, u32[]{:S(2)}, u32[]{:S(2)}) collective-permute-start(f32[]{:T(128)} %add.272), channel_id=1, source_target_pairs={{0,32},{4,36},{8,40},{12,44},{16,48},{20,52},{24,56},{28,60},{32,0... | collective-permute-start | bytes 20 | tf_op jit(solution)/shard_map/ppermute | solution.py:37
  286.9 3.7 collective-permute-start.18
  291.3 5.2 %collective-permute-start.19 = (f32[]{:T(128)}, f32[]{:T(128)}, u32[]{:S(2)}, u32[]{:S(2)}) collective-permute-start(f32[]{:T(128)} %add.274), channel_id=1, source_target_pairs={{0,128},{4,132},{8,136},{12,140},{16,144},{20,148},{24,152},{28,15... | collective-permute-start | bytes 20 | tf_op jit(solution)/shard_map/ppermute | solution.py:37
  298.2 72.2 %copy-start = (f32[24,8,8,128]{3,2,1,0:T(8,128)}, f32[24,8,8,128]{3,2,1,0:T(8,128)S(1)}, u32[]{:S(2)}) copy-start(f32[24,8,8,128]{3,2,1,0:T(8,128)S(1)} %get-tuple-element.296) | copy-start | bytes 2359300
  298.2 3.8 collective-permute-start.20
  303.3 5.2 %collective-permute-start.21 = (f32[]{:T(128)}, f32[]{:T(128)}, u32[]{:S(2)}, u32[]{:S(2)}) collective-permute-start(f32[]{:T(128)} %add.276), channel_id=1, source_target_pairs={{0,2},{1,3},{2,0},{3,1},{4,6},{5,7},{6,4},{7,5},{8,10},{9,11},{10,... | collective-permute-start | bytes 20 | tf_op jit(solution)/shard_map/ppermute | solution.py:37
  309.1 1.3 collective-permute-start.22
  311.1 3.7 collective-permute-start.23
  315.5 4.6 collective-permute-start.24
  320.8 7.6 %collective-permute-start.25 = (f32[]{:T(128)}, f32[]{:T(128)}, u32[]{:S(2)}, u32[]{:S(2)}) collective-permute-start(f32[]{:T(128)} %add.280), channel_id=1, source_target_pairs={{0,32},{4,36},{8,40},{12,44},{16,48},{20,52},{24,56},{28,60},{32,0... | collective-permute-start | bytes 20 | tf_op jit(solution)/shard_map/ppermute | solution.py:37
  329.1 3.7 collective-permute-start.26
  333.4 5.2 %collective-permute-start.27 = (f32[]{:T(128)}, f32[]{:T(128)}, u32[]{:S(2)}, u32[]{:S(2)}) collective-permute-start(f32[]{:T(128)} %add.282), channel_id=1, source_target_pairs={{0,128},{4,132},{8,136},{12,140},{16,144},{20,148},{24,152},{28,15... | collective-permute-start | bytes 20 | tf_op jit(solution)/shard_map/ppermute | solution.py:37
  370.5 8.9 %collective-permute-start.28 = (bf16[64,1408]{1,0:T(8,128)(2,1)S(1)}, bf16[64,1408]{1,0:T(8,128)(2,1)S(1)}, u32[]{:S(2)}, u32[]{:S(2)}) collective-permute-start(bf16[64,1408]{1,0:T(8,128)(2,1)S(1)} %get-tuple-element.297), channel_id=1, source_target_pairs={{0,4},{4,8},{8,12},{12,16},{16,20},{20,24},{24,28},{28,32},{32,36}... | collective-permute-start | bytes 540680 | tf_op jit(solution)/shard_map/ppermute | solution.py:17
  372.4 8.8 %collective-permute-start.29 = (bf16[64,1408]{1,0:T(8,128)(2,1)S(1)}, bf16[64,1408]{1,0:T(8,128)(2,1)S(1)}, u32[]{:S(2)}, u32[]{:S(2)}) collective-permute-start(bf16[64,1408]{1,0:T(8,128)(2,1)S(1)} %get-tuple-element.298), channel_id=1, source_target_pairs={{4,0},{8,4},{12,8},{16,12},{20,16},{24,20},{28,24},{32,28},{36,32}... | collective-permute-start | bytes 540680 | tf_op jit(solution)/shard_map/ppermute | solution.py:20
  420.4 43.2 %copy-start.1 = (f32[24,8,8,128]{3,2,1,0:T(8,128)S(1)}, f32[24,8,8,128]{3,2,1,0:T(8,128)}, u32[]{:S(2)}) copy-start(f32[24,8,8,128]{3,2,1,0:T(8,128)} %copy-done) | copy-start | bytes 2359300
  422.3 3.7 collective-permute-start.30
  427.3 5.2 %collective-permute-start.31 = (f32[]{:T(128)}, f32[]{:T(128)}, u32[]{:S(2)}, u32[]{:S(2)}) collective-permute-start(f32[]{:T(128)} %add.288), channel_id=1, source_target_pairs={{0,2},{1,3},{2,0},{3,1},{4,6},{5,7},{6,4},{7,5},{8,10},{9,11},{10,... | collective-permute-start | bytes 20 | tf_op jit(solution)/shard_map/ppermute | solution.py:37
  433.2 1.3 collective-permute-start.32
  435.2 4.0 collective-permute-start.33
  439.8 4.6 collective-permute-start.34
  445.0 7.6 %collective-permute-start.35 = (f32[]{:T(128)}, f32[]{:T(128)}, u32[]{:S(2)}, u32[]{:S(2)}) collective-permute-start(f32[]{:T(128)} %add.292), channel_id=1, source_target_pairs={{0,32},{4,36},{8,40},{12,44},{16,48},{20,52},{24,56},{28,60},{32,0... | collective-permute-start | bytes 20 | tf_op jit(solution)/shard_map/ppermute | solution.py:37
  453.3 3.7 collective-permute-start.36
  457.7 5.2 %collective-permute-start.37 = (f32[]{:T(128)}, f32[]{:T(128)}, u32[]{:S(2)}, u32[]{:S(2)}) collective-permute-start(f32[]{:T(128)} %add.294), channel_id=1, source_target_pairs={{0,128},{4,132},{8,136},{12,140},{16,144},{20,148},{24,152},{28,15... | collective-permute-start | bytes 20 | tf_op jit(solution)/shard_map/ppermute | solution.py:37
  476.5 1.3 copy-start.2
Sparse Core Ops, SparseCore 0:
  23.3 32.3 all-gather.2
  340.5 27.5 all-gather.4

commit v2 on v1

v2 whole, which is shorter than its diff:
```python
import functools

import jax
import jax.numpy as jnp
from jax import lax
from jax.experimental import pallas as pl
from jax.experimental.pallas import tpu as pltpu
from jax.sharding import PartitionSpec as P

ITERS = 2
SUPPORT = 5.0
AMPLITUDE = 0.05


def tile_kernel(begin_ref, count_ref, own_ref, win_ref, out_ref, *, slots, dims, runs):
    b = pl.program_id(0)
    start = begin_ref[b]
    count = count_ref[b]
    own = own_ref[0]
    for s in range(slots):
        @pl.when(s < count)
        def _():
            part = win_ref[start + s]
            squared = jnp.zeros((runs, runs), jnp.float32)
            for d in range(dims):
                diff = own[:, d:d + 1] - part[d:d + 1, :]
                squared = squared + diff * diff
            radius_frac = jnp.sqrt(squared) / SUPPORT
            remain = jnp.maximum(1.0 - radius_frac, 0.0)
            cubed = remain * remain * remain
            val = cubed * cubed * (6.0 * radius_frac + 1.0)
            out_ref[0, :, s * runs:(s + 1) * runs] = val.astype(out_ref.dtype)

        @pl.when(s >= count)
        def _():
            out_ref[0, :, s * runs:(s + 1) * runs] = jnp.zeros((runs, runs), out_ref.dtype)


def build_tiles(begin, count, own_t, win_c, slots):
    blocks, runs, dpad = own_t.shape
    kern = functools.partial(tile_kernel, slots=slots, dims=dpad, runs=runs)
    return pl.pallas_call(
        kern,
        grid_spec=pltpu.PrefetchScalarGridSpec(
            num_scalar_prefetch=2,
            grid=(blocks,),
            in_specs=[
                pl.BlockSpec((1, runs, dpad), lambda b, *_: (b, 0, 0)),
                pl.BlockSpec(win_c.shape, lambda b, *_: (0, 0, 0)),
            ],
            out_specs=pl.BlockSpec((1, runs, slots * runs), lambda b, *_: (b, 0, 0)),
        ),
        out_shape=jax.ShapeDtypeStruct((blocks, runs, slots * runs), jnp.bfloat16),
    )(begin, count, own_t, win_c)


def apply_kernel(begin_ref, win_ref, tile_ref, p_ref, noise_ref, out_ref, *, per_step, slots, runs):
    g = pl.program_id(0)
    noise = noise_ref[...]
    for k in range(per_step):
        start = begin_ref[g * per_step + k]
        vals = win_ref[pl.ds(start, slots)]
        cat = jnp.concatenate([vals[s] for s in range(slots)], axis=1)
        acc = lax.dot_general(
            cat, tile_ref[k], (((1,), (1,)), ((), ())), preferred_element_type=jnp.float32
        )
        cols = slice(k * runs, (k + 1) * runs)
        out_ref[:, cols] = AMPLITUDE * acc + noise * p_ref[:, cols]


def apply_operator(begin, win_v, tiles, direction, noise_col, per_step):
    blocks, runs, width = tiles.shape
    slots = width // runs
    chans, total = direction.shape
    kern = functools.partial(apply_kernel, per_step=per_step, slots=slots, runs=runs)
    return pl.pallas_call(
        kern,
        grid_spec=pltpu.PrefetchScalarGridSpec(
            num_scalar_prefetch=1,
            grid=(blocks // per_step,),
            in_specs=[
                pl.BlockSpec(win_v.shape, lambda g, *_: (0, 0, 0)),
                pl.BlockSpec((per_step, runs, width), lambda g, *_: (g, 0, 0)),
                pl.BlockSpec((chans, per_step * runs), lambda g, *_: (0, g)),
                pl.BlockSpec((chans, 1), lambda g, *_: (0, 0)),
            ],
            out_specs=pl.BlockSpec((chans, per_step * runs), lambda g, *_: (0, g)),
        ),
        out_shape=jax.ShapeDtypeStruct((chans, total), jnp.float32),
    )(begin, win_v, tiles, direction, noise_col)


def extended(block, axis, dim, width):
    count = lax.axis_size(axis)
    forward = [(i, i + 1) for i in range(count - 1)]
    backward = [(target, source) for source, target in forward]
    low = lax.ppermute(
        lax.slice_in_dim(block, block.shape[dim] - width, None, axis=dim), axis, forward
    )
    high = lax.ppermute(lax.slice_in_dim(block, 0, width, axis=dim), axis, backward)
    return jnp.concatenate([low, block, high], axis=dim)


def global_sum(value):
    for axis in ("chan", "samp"):
        count = lax.axis_size(axis)
        step = 1
        while step < count:
            pairs = [(i, i ^ step) for i in range(count)]
            value = value + lax.ppermute(value, axis, pairs)
            step *= 2
    return value


def gather_chan(rounded):
    count = lax.axis_size("chan")
    parts = [rounded]
    for shift in range(1, count):
        pairs = [((i + shift) % count, i) for i in range(count)]
        parts.append(lax.ppermute(rounded, "chan", pairs))
    return jnp.concatenate(parts, axis=0)


def per_device(loads, coords, coreg_factor, noise, run_perm, block_nbrs, nbr_count):
    chan_local, runs_local = loads.shape
    blocks_local = nbr_count.shape[0]
    block_runs = runs_local // blocks_local
    dims = coords.shape[0]
    dpad = 8
    slot_limit = block_nbrs.shape[1]
    halo = slot_limit - 1
    device_pos = lax.axis_index("samp")
    chan_pos = lax.axis_index("chan")
    local_perm = run_perm - device_pos * runs_local
    sorted_coords = jnp.take(coords, local_perm, axis=1)
    sorted_loads = jnp.take(loads, local_perm, axis=1)
    norm_now = global_sum(jnp.sum(sorted_loads * sorted_loads))
    full_factor = lax.all_gather(coreg_factor, "chan", axis=0, tiled=True)
    coreg_rows = jnp.dot(coreg_factor, full_factor.T, precision=lax.Precision.HIGHEST)
    coreg_perm = jnp.roll(coreg_rows, -chan_pos * chan_local, axis=1)
    reach_runs = halo * block_runs
    window_blocks = blocks_local + 2 * halo
    widened_coords = extended(sorted_coords, "samp", 1, reach_runs)
    win_c = jnp.pad(
        widened_coords.reshape(dims, window_blocks, block_runs), ((0, dpad - dims), (0, 0), (0, 0))
    ).transpose(1, 0, 2)
    own_t = jnp.pad(
        sorted_coords.reshape(dims, blocks_local, block_runs), ((0, dpad - dims), (0, 0), (0, 0))
    ).transpose(1, 2, 0)
    begin = jnp.clip(
        block_nbrs[:, 0] - (device_pos * blocks_local - halo), 0, window_blocks - slot_limit
    ).astype(jnp.int32)
    tiles = build_tiles(begin, nbr_count.astype(jnp.int32), own_t, win_c, slot_limit)
    noise_col = noise[:, None]
    iterate = jnp.zeros_like(sorted_loads)
    remainder = sorted_loads
    direction = sorted_loads
    for iteration in range(ITERS):
        rounded = direction.astype(jnp.bfloat16)
        gathered = gather_chan(rounded)
        mixed = jnp.dot(
            coreg_perm, gathered.astype(jnp.float32), precision=lax.Precision.HIGHEST
        )
        mixed_b = mixed.astype(jnp.bfloat16)
        widened = extended(mixed_b, "samp", 1, reach_runs)
        win_v = widened.reshape(chan_local, window_blocks, block_runs).transpose(1, 0, 2)
        mapped = apply_operator(begin, win_v, tiles, direction, noise_col, 4)
        step_size = norm_now / global_sum(jnp.sum(direction * mapped))
        iterate = iterate + step_size * direction
        remainder = remainder - step_size * mapped
        if iteration + 1 < ITERS:
            norm_next = global_sum(jnp.sum(remainder * remainder))
            direction = remainder + norm_next / norm_now * direction
            norm_now = norm_next
    solution = jnp.zeros_like(iterate).at[:, local_perm].set(iterate)
    residual = jnp.zeros_like(remainder).at[:, local_perm].set(remainder)
    return (solution, residual)


def solution(mesh):
    return jax.shard_map(
        per_device,
        mesh=mesh,
        in_specs=(
            P("chan", "samp"),
            P(None, "samp"),
            P("chan", None),
            P("chan"),
            P("samp"),
            P("samp", None),
            P("samp"),
        ),
        out_specs=(P("chan", "samp"), P("chan", "samp")),
        check_vma=False,
    )
```

time: 499 us -> 350 us (0.70)
  Pallas kernels: 0 us -> 79.8 us
  other arithmetic: 79.2 us -> 14.8 us
  waiting for transfers between devices: 104 us -> 55.3 us
  matrix products: 50 us -> 3.71 us
  loops' own time: 41.6 us -> 0 us
  local copies, waits for them, and re-layouts: 81.5 us -> 44 us
  starting transfers between devices: 90.8 us -> 116 us
  between operations: 37 us -> 25 us
    pallas_call x0 -> x3, Pallas kernels: none -> 79.8 us  [the longest x1 62 us: build_tiles(): pl.pallas_call(kern, grid_spec=pltpu.PrefetchScalarGridSpec(num_scalar_pr...]
    dynamic_update_slice x12 -> x0, other arithmetic: 56.4 us -> none  [per_device(): all_tiles = lax.map(build_tile, jnp.arange(slot_limit, dtype=jnp.int32))]
    dot_general x26 -> x2, matrix products: 49.6 us -> 3.34 us  [per_device(): jnp.dot(coreg_perm, gathered.astype(jnp.float32), precision=lax.Precision...]
    another operation x3 -> x0, loops' own time: 41.6 us -> none  [the longest x1 24 us: per_device(): all_tiles = lax.map(build_tile, jnp.arange(slot_limit, dtype=jnp.int32))]
    ppermute x32, waiting for transfers between devices: 73.2 us -> 39.2 us  [global_sum(): value = value + lax.ppermute(value, axis, pairs)]
    all_gather x2 -> x0, waiting for transfers between devices: 27.8 us -> none  [per_device(): gathered = lax.all_gather(rounded, 'chan', axis=0, tiled=True)]
    gather x36 -> x0, local copies, waits for them, and re-layouts: 21.9 us -> none  [the longest x24 14.9 us: slot_step(): partner_vals = jnp.take(value_blocks, partner_ids, axis=1)]
    ppermute x32, starting transfers between devices: 66.2 us -> 82.7 us  [global_sum(): value = value + lax.ppermute(value, axis, pairs)]
  transfers between devices with their start and end apart: 40 -> 44, of which waited for: 34 -> 22; matrix products, arithmetic and copies ran while one was open for 20% -> 5% of each run, Pallas kernels for 0% -> 18%
where the time goes in v2:
time: 350 us; the launch traced here: 351 us
  starting transfers between devices  116 us (33%)
  Pallas kernels  79.8 us (23%)
  waiting for transfers between devices  55.3 us (16%)
  local copies, waits for them, and re-layouts  44 us (13%)
  between operations  25 us (7%)
  other arithmetic  14.8 us (4%)
  blocking collectives  12.2 us (3%)
  matrix products  3.71 us (1%)
    ppermute x32, starting transfers between devices, global_sum(): value = value + lax.ppermute(value, axis, pairs)  82.7 us
    pallas_call x1, Pallas kernels, build_tiles(): pl.pallas_call(kern, grid_spec=pltpu.PrefetchScalarGridSpec(num_scalar_pr...  62 us
    ppermute x32, waiting for transfers between devices, global_sum(): value = value + lax.ppermute(value, axis, pairs)  39.2 us
    pallas_call x2, Pallas kernels, apply_operator(): pl.pallas_call(kern, grid_spec=pltpu.PrefetchScalarGridSpec(num_scalar_pr...  17.9 us
    ppermute x3, starting transfers between devices, extended(): lax.ppermute(lax.slice_in_dim(block, 0, width, axis=dim), axis, backward)  17.8 us
    ppermute x6, waiting for transfers between devices, gather_chan(): parts.append(lax.ppermute(rounded, 'chan', pairs))  13 us
    all_gather x1, blocking collectives, per_device(): full_factor = lax.all_gather(coreg_factor, 'chan', axis=0, tiled=True)  12.2 us
    ppermute x6, starting transfers between devices, gather_chan(): parts.append(lax.ppermute(rounded, 'chan', pairs))  9.92 us
  transfers between devices with their start and end apart: 44, of which 22 were waited for; matrix products, arithmetic and copies ran while one was open for 5% of the time, Pallas kernels for 18%

profile of v2, /device:TPU:2, one launch (start us, length us, event | category | flops | bytes accessed | tf_op | source)
XLA Modules:
  0.0 351.1 jit_solution(17422255147226602205)
XLA Ops:
  3.0 8.1 %gather_fusion = f32[3072,64]{1,0:T(8,128)S(1)} fusion(f32[64,3072]{0,1:T(8,128)S(1)} %copy.31, s32[3072]{0:T(1024)S(1)} %broadcast_clamp_fusion), kind=kCustom, calls=%fused_computation | custom fusion | bytes 1585152 | tf_op jit(solution)/shard_map/jit(_take)/gather | solution.py:136
  14.2 2.9 collective-permute-start.9
  19.0 8.1 %gather_fusion.1 = f32[3072,6]{1,0:T(8,128)S(1)} fusion(f32[6,3072]{0,1:T(8,128)S(1)} %copy.34, s32[3072]{0:T(1024)S(1)} %broadcast_clamp_fusion), kind=kCustom, calls=%fused_computation.1 | custom fusion | bytes 159744 | tf_op jit(solution)/shard_map/jit(_take)/gather | solution.py:135
  29.2 1.9 collective-permute-start.13
  31.1 6.3 %collective-permute-start.14 = (f32[6,1408]{1,0:T(8,128)S(1)}, f32[6,1408]{1,0:T(8,128)S(1)}, u32[]{:S(2)}, u32[]{:S(2)}) collective-permute-start(f32[6,1408]{1,0:T(8,128)S(1)} %get-tuple-element.23), channel_id=1, source_target_pairs={{4,0},{8,4},{12,8},{16,12},{20,16},{24,20},{28,24},{32,28},{36,32}... | collective-permute-start | bytes 101384 | tf_op jit(solution)/shard_map/ppermute | solution.py:100
  39.6 12.2 %all_gather.3 = f32[256,256]{1,0:T(8,128)S(1)} all-gather(f32[64,256]{1,0:T(8,128)S(1)} %copy-done.5), channel_id=1, replica_groups=mesh['samp'=64,'chan'=4] {'chan'}, dimensions={0}, use_global_device_ids=true | all-gather | bytes 327680 | tf_op jit(solution)/shard_map/all_gather | solution.py:138
  54.3 2.3 convolution_convert_fusion.1
  56.6 1.9 collective-permute-start.11
  58.6 5.8 %collective-permute-start.12 = (bf16[64,1408]{1,0:T(8,128)(2,1)S(1)}, bf16[64,1408]{1,0:T(8,128)(2,1)S(1)}, u32[]{:S(2)}, u32[]{:S(2)}) collective-permute-start(bf16[64,1408]{1,0:T(8,128)(2,1)S(1)} %get-tuple-element.21), channel_id=1, source_target_pairs={{4,0},{8,4},{12,8},{16,12},{20,16},{24,20},{28,24},{32,28},{36,32}... | collective-permute-start | bytes 540680 | tf_op jit(solution)/shard_map/ppermute | solution.py:100
  65.1 62.0 %shard_map.86.tile_ref = bf16[24,128,1536]{2,1,0:T(8,128)(2,1)} custom-call(s32[24]{0:T(128)} %clamp_bitcast_fusion.begin_ref, s32[24]{0:T(128)} %count_ref.1, f32[24,128,8]{2,1,0:T(8,128)} %pad_bitcast_fusion.own_ref, f32[46,8,128]{2,1,0:T(8,128)} %pad_bitcast_fusion.1.win_ref), custom_call_target="tpu_custom_call" | custom-call | tf_op jit(solution)/shard_map/pallas_call | solution.py:42
  128.1 8.9 %shard_map.87 = f32[64,3072]{1,0:T(8,128)} custom-call(s32[24]{0:T(128)} %clamp_bitcast_fusion.begin_ref, bf16[46,64,128]{2,1,0:T(8,128)(2,1)} %bitcast_bitcast_fusion.1.win_ref, bf16[24,128,1536]{2,1,0:T(8,128)(2,1)} %shard_map.86.tile_ref, f32[64,3072]{1,0:T(8,128)} %get-tuple-element.13.p_ref, f32[64,1]{1,0:T(8,128)} %copy.39.noise_ref), custom_call_target="tpu_custom_call" | custom-call | tf_op jit(solution)/shard_map/pallas_call | solution.py:76
  137.1 2.1 multiply_reduce_fusion.2
  139.2 2.0 collective-permute-start
  144.1 2.9 collective-permute-start.16
  148.3 3.4 collective-permute-start.1
  158.4 3.4 collective-permute-start.3
  164.6 4.3 %collective-permute-start.4 = (f32[]{:T(128)}, f32[]{:T(128)}, u32[]{:S(2)}, u32[]{:S(2)}) collective-permute-start(f32[]{:T(128)} %add.133), channel_id=1, source_target_pairs={{0,16},{4,20},{8,24},{12,28},{16,0},{20,4},{24,8},{28,12},{32,48},... | collective-permute-start | bytes 20 | tf_op jit(solution)/shard_map/ppermute | solution.py:110
  171.6 7.3 %collective-permute-start.5 = (f32[]{:T(128)}, f32[]{:T(128)}, u32[]{:S(2)}, u32[]{:S(2)}) collective-permute-start(f32[]{:T(128)} %add.134), channel_id=1, source_target_pairs={{0,32},{4,36},{8,40},{12,44},{16,48},{20,52},{24,56},{28,60},{32,0... | collective-permute-start | bytes 20 | tf_op jit(solution)/shard_map/ppermute | solution.py:110
  179.6 2.5 collective-permute-start.21
  182.8 4.5 %collective-permute-start.6 = (f32[]{:T(128)}, f32[]{:T(128)}, u32[]{:S(2)}, u32[]{:S(2)}) collective-permute-start(f32[]{:T(128)} %add.135), channel_id=1, source_target_pairs={{0,64},{4,68},{8,72},{12,76},{16,80},{20,84},{24,88},{28,92},{32,9... | collective-permute-start | bytes 20 | tf_op jit(solution)/shard_map/ppermute | solution.py:110
  188.0 8.9 %collective-permute-start.22 = (f32[]{:T(128)}, f32[]{:T(128)}, u32[]{:S(2)}, u32[]{:S(2)}) collective-permute-start(f32[]{:T(128)} %add.146), channel_id=1, source_target_pairs={{0,128},{4,132},{8,136},{12,140},{16,144},{20,148},{24,152},{28,15... | collective-permute-start | bytes 20 | tf_op jit(solution)/shard_map/ppermute | solution.py:110
  199.8 2.9 collective-permute-done.7
  204.2 3.6 %collective-permute-done.23 = f32[]{:T(128)} collective-permute-done((f32[]{:T(128)}, f32[]{:T(128)}, u32[]{:S(2)}, u32[]{:S(2)}) %collective-permute-start.23) | collective-permute-done | bytes 36 | tf_op jit(solution)/shard_map/ppermute | solution.py:110
  209.2 2.8 collective-permute-start.24
  212.0 2.2 collective-permute-done.24
  218.3 2.1 collective-permute-done.26
  221.0 4.3 %collective-permute-start.27 = (f32[]{:T(128)}, f32[]{:T(128)}, u32[]{:S(2)}, u32[]{:S(2)}) collective-permute-start(f32[]{:T(128)} %add.151), channel_id=1, source_target_pairs={{0,16},{4,20},{8,24},{12,28},{16,0},{20,4},{24,8},{28,12},{32,48},... | collective-permute-start | bytes 20 | tf_op jit(solution)/shard_map/ppermute | solution.py:110
  226.2 5.3 %collective-permute-start.28 = (f32[]{:T(128)}, f32[]{:T(128)}, u32[]{:S(2)}, u32[]{:S(2)}) collective-permute-start(f32[]{:T(128)} %add.152), channel_id=1, source_target_pairs={{0,32},{4,36},{8,40},{12,44},{16,48},{20,52},{24,56},{28,60},{32,0... | collective-permute-start | bytes 20 | tf_op jit(solution)/shard_map/ppermute | solution.py:110
  231.5 2.2 collective-permute-done.28
  234.4 4.0 %collective-permute-start.29 = (f32[]{:T(128)}, f32[]{:T(128)}, u32[]{:S(2)}, u32[]{:S(2)}) collective-permute-start(f32[]{:T(128)} %add.153), channel_id=1, source_target_pairs={{0,64},{4,68},{8,72},{12,76},{16,80},{20,84},{24,88},{28,92},{32,9... | collective-permute-start | bytes 20 | tf_op jit(solution)/shard_map/ppermute | solution.py:110
  240.6 3.7 %collective-permute-done.30 = f32[]{:T(128)} collective-permute-done((f32[]{:T(128)}, f32[]{:T(128)}, u32[]{:S(2)}, u32[]{:S(2)}) %collective-permute-start.30) | collective-permute-done | bytes 36 | tf_op jit(solution)/shard_map/ppermute | solution.py:110
  246.0 2.0 collective-permute-start.32
  248.1 2.1 collective-permute-start.31
  250.1 12.4 %collective-permute-done.33 = bf16[64,3072]{1,0:T(8,128)(2,1)S(1)} collective-permute-done((bf16[64,3072]{1,0:T(8,128)(2,1)S(1)}, bf16[64,3072]{1,0:T(8,128)(2,1)S(1)}, u32[]{:S(2)}, u32[]{:S(2)}) %collective-permute-start.33) | collective-permute-done | bytes 393248 | tf_op jit(solution)/shard_map/ppermute | solution.py:120
  264.2 1.9 collective-permute-start.34
  266.1 5.8 %collective-permute-start.35 = (bf16[64,1408]{1,0:T(8,128)(2,1)S(1)}, bf16[64,1408]{1,0:T(8,128)(2,1)S(1)}, u32[]{:S(2)}, u32[]{:S(2)}) collective-permute-start(bf16[64,1408]{1,0:T(8,128)(2,1)S(1)} %get-tuple-element.19), channel_id=1, source_target_pairs={{4,0},{8,4},{12,8},{16,12},{20,16},{24,20},{28,24},{32,28},{36,32}... | collective-permute-start | bytes 540680 | tf_op jit(solution)/shard_map/ppermute | solution.py:100
  276.0 8.9 %shard_map.88 = f32[64,3072]{1,0:T(8,128)} custom-call(s32[24]{0:T(128)} %clamp_bitcast_fusion.begin_ref, bf16[46,64,128]{2,1,0:T(8,128)(2,1)} %bitcast_bitcast_fusion.win_ref, bf16[24,128,1536]{2,1,0:T(8,128)(2,1)} %shard_map.86.tile_ref, f32[64,3072]{1,0:T(8,128)} %get-tuple-element.11.p_ref, f32[64,1]{1,0:T(8,128)} %copy.39.noise_ref), custom_call_target="tpu_custom_call" | custom-call | tf_op jit(solution)/shard_map/pallas_call | solution.py:76
  284.9 2.0 multiply_reduce_fusion
  287.7 3.0 collective-permute-done.36
  292.0 3.4 collective-permute-start.37
  301.2 2.3 collective-permute-done.39
  306.1 2.7 collective-permute-done.40
  309.4 3.5 %collective-permute-start.41 = (f32[]{:T(128)}, f32[]{:T(128)}, u32[]{:S(2)}, u32[]{:S(2)}) collective-permute-start(f32[]{:T(128)} %add.161), channel_id=1, source_target_pairs={{0,32},{4,36},{8,40},{12,44},{16,48},{20,52},{24,56},{28,60},{32,0... | collective-permute-start | bytes 20 | tf_op jit(solution)/shard_map/ppermute | solution.py:110
  313.0 4.1 %collective-permute-done.41 = f32[]{:T(128)} collective-permute-done((f32[]{:T(128)}, f32[]{:T(128)}, u32[]{:S(2)}, u32[]{:S(2)}) %collective-permute-start.41) | collective-permute-done | bytes 36 | tf_op jit(solution)/shard_map/ppermute | solution.py:110
  319.1 2.3 collective-permute-done.42
  323.7 3.6 %collective-permute-done.43 = f32[]{:T(128)} collective-permute-done((f32[]{:T(128)}, f32[]{:T(128)}, u32[]{:S(2)}, u32[]{:S(2)}) %collective-permute-start.43) | collective-permute-done | bytes 36 | tf_op jit(solution)/shard_map/ppermute | solution.py:110
  330.9 8.5 %scatter_custom_fusion.1 = f32[64,3072]{0,1:T(8,128)S(1)} fusion(s32[3072]{0:T(1024)S(1)} %get-tuple-element.15, f32[3072,64]{1,0:T(8,128)S(1)} %copy.43, f32[]{:T(128)} %constant.60.clone.1), kind=kCustom, calls=%fused_computation.32 | custom fusion | bytes 786436 | tf_op jit(solution)/shard_map/scatter | solution.py:176
  341.2 8.5 %scatter_custom_fusion = f32[64,3072]{0,1:T(8,128)S(1)} fusion(s32[3072]{0:T(1024)S(1)} %get-tuple-element.15, f32[3072,64]{1,0:T(8,128)S(1)} %copy.42, f32[]{:T(128)} %constant.60.clone.1), kind=kCustom, calls=%fused_computation.34 | custom fusion | bytes 786436 | tf_op jit(solution)/shard_map/scatter | solution.py:175
  (95 shorter events, 53.9 us)
Async XLA Ops:
  12.7 41.6 %collective-permute-start.10 = (bf16[64,3072]{1,0:T(8,128)(2,1)}, bf16[64,3072]{1,0:T(8,128)(2,1)}, u32[]{:S(2)}, u32[]{:S(2)}) collective-permute-start(bf16[64,3072]{1,0:T(8,128)(2,1)} %get-tuple-element.12), channel_id=1, source_target_pairs={{3,0},{0,1},{1,2},{2,3},{7,4},{4,5},{5,6},{6,7},{11,8},{8,9},{9,10... | collective-permute-start | bytes 1179656 | tf_op jit(solution)/shard_map/ppermute | solution.py:120
  14.2 40.0 %collective-permute-start.9 = (bf16[64,3072]{1,0:T(8,128)(2,1)}, bf16[64,3072]{1,0:T(8,128)(2,1)}, u32[]{:S(2)}, u32[]{:S(2)}) collective-permute-start(bf16[64,3072]{1,0:T(8,128)(2,1)} %get-tuple-element.12), channel_id=1, source_target_pairs={{2,0},{3,1},{0,2},{1,3},{6,4},{7,5},{4,6},{5,7},{10,8},{11,9},{8,1... | collective-permute-start | bytes 1179656 | tf_op jit(solution)/shard_map/ppermute | solution.py:120
  17.1 37.1 %collective-permute-start.8 = (bf16[64,3072]{1,0:T(8,128)(2,1)}, bf16[64,3072]{1,0:T(8,128)(2,1)}, u32[]{:S(2)}, u32[]{:S(2)}) collective-permute-start(bf16[64,3072]{1,0:T(8,128)(2,1)} %get-tuple-element.12), channel_id=1, source_target_pairs={{1,0},{2,1},{3,2},{0,3},{5,4},{6,5},{7,6},{4,7},{9,8},{10,9},{11,1... | collective-permute-start | bytes 1179656 | tf_op jit(solution)/shard_map/ppermute | solution.py:120
  29.2 35.1 %collective-permute-start.13 = (f32[6,1408]{1,0:T(8,128)S(1)}, f32[6,1408]{1,0:T(8,128)S(1)}, u32[]{:S(2)}, u32[]{:S(2)}) collective-permute-start(f32[6,1408]{1,0:T(8,128)S(1)} %get-tuple-element.22), channel_id=1, source_target_pairs={{0,4},{4,8},{8,12},{12,16},{16,20},{20,24},{24,28},{28,32},{32,36}... | collective-permute-start | bytes 101384 | tf_op jit(solution)/shard_map/ppermute | solution.py:97
  31.1 33.2 %collective-permute-start.14 = (f32[6,1408]{1,0:T(8,128)S(1)}, f32[6,1408]{1,0:T(8,128)S(1)}, u32[]{:S(2)}, u32[]{:S(2)}) collective-permute-start(f32[6,1408]{1,0:T(8,128)S(1)} %get-tuple-element.23), channel_id=1, source_target_pairs={{4,0},{8,4},{12,8},{16,12},{20,16},{24,20},{28,24},{32,28},{36,32}... | collective-permute-start | bytes 101384 | tf_op jit(solution)/shard_map/ppermute | solution.py:100
  38.8 13.1 %copy-start.7 = (f32[64]{0:T(128)S(1)}, f32[64]{0:T(128)}, u32[]{:S(2)}) copy-start(f32[64]{0:T(128)} %param.10) | copy-start | bytes 772
  56.6 70.4 %collective-permute-start.11 = (bf16[64,1408]{1,0:T(8,128)(2,1)S(1)}, bf16[64,1408]{1,0:T(8,128)(2,1)S(1)}, u32[]{:S(2)}, u32[]{:S(2)}) collective-permute-start(bf16[64,1408]{1,0:T(8,128)(2,1)S(1)} %get-tuple-element.20), channel_id=1, source_target_pairs={{0,4},{4,8},{8,12},{12,16},{16,20},{20,24},{24,28},{28,32},{32,36}... | collective-permute-start | bytes 540680 | tf_op jit(solution)/shard_map/ppermute | solution.py:97
  58.6 68.5 %collective-permute-start.12 = (bf16[64,1408]{1,0:T(8,128)(2,1)S(1)}, bf16[64,1408]{1,0:T(8,128)(2,1)S(1)}, u32[]{:S(2)}, u32[]{:S(2)}) collective-permute-start(bf16[64,1408]{1,0:T(8,128)(2,1)S(1)} %get-tuple-element.21), channel_id=1, source_target_pairs={{4,0},{8,4},{12,8},{16,12},{20,16},{24,20},{28,24},{32,28},{36,32}... | collective-permute-start | bytes 540680 | tf_op jit(solution)/shard_map/ppermute | solution.py:100
  128.1 8.9 %copy-start = (f32[64,3072]{1,0:T(8,128)S(1)}, f32[64,3072]{1,0:T(8,128)}, u32[]{:S(2)}) copy-start(f32[64,3072]{1,0:T(8,128)} %get-tuple-element.13.p_ref) | copy-start | bytes 2359300
  137.1 66.3 %copy-start.1 = (f32[64,3072]{1,0:T(8,128)S(1)}, f32[64,3072]{1,0:T(8,128)}, u32[]{:S(2)}) copy-start(f32[64,3072]{1,0:T(8,128)} %shard_map.87) | copy-start | bytes 2359300
  139.2 3.6 %collective-permute-start.15 = (f32[]{:T(128)}, f32[]{:T(128)}, u32[]{:S(2)}, u32[]{:S(2)}) collective-permute-start(f32[]{:T(128)} %get-tuple-element.8), channel_id=1, source_target_pairs={{0,1},{1,0},{2,3},{3,2},{4,5},{5,4},{6,7},{7,6},{8,9},{9,8},{10,11... | collective-permute-start | bytes 20 | tf_op jit(solution)/shard_map/ppermute | solution.py:110
  139.2 7.8 %collective-permute-start = (f32[]{:T(128)}, f32[]{:T(128)}, u32[]{:S(2)}, u32[]{:S(2)}) collective-permute-start(f32[]{:T(128)} %get-tuple-element.9), channel_id=1, source_target_pairs={{0,1},{1,0},{2,3},{3,2},{4,5},{5,4},{6,7},{7,6},{8,9},{9,8},{10,11... | collective-permute-start | bytes 20 | tf_op jit(solution)/shard_map/ppermute | solution.py:110
  144.1 7.6 %collective-permute-start.16 = (f32[]{:T(128)}, f32[]{:T(128)}, u32[]{:S(2)}, u32[]{:S(2)}) collective-permute-start(f32[]{:T(128)} %add.140), channel_id=1, source_target_pairs={{0,2},{1,3},{2,0},{3,1},{4,6},{5,7},{6,4},{7,5},{8,10},{9,11},{10,... | collective-permute-start | bytes 20 | tf_op jit(solution)/shard_map/ppermute | solution.py:110
  148.3 5.2 %collective-permute-start.1 = (f32[]{:T(128)}, f32[]{:T(128)}, u32[]{:S(2)}, u32[]{:S(2)}) collective-permute-start(f32[]{:T(128)} %add.130), channel_id=1, source_target_pairs={{0,2},{1,3},{2,0},{3,1},{4,6},{5,7},{6,4},{7,5},{8,10},{9,11},{10,... | collective-permute-start | bytes 20 | tf_op jit(solution)/shard_map/ppermute | solution.py:110
  152.4 3.2 collective-permute-start.17
  154.2 3.5 collective-permute-start.2
  156.3 5.5 %collective-permute-start.18 = (f32[]{:T(128)}, f32[]{:T(128)}, u32[]{:S(2)}, u32[]{:S(2)}) collective-permute-start(f32[]{:T(128)} %add.142), channel_id=1, source_target_pairs={{0,8},{4,12},{8,0},{12,4},{16,24},{20,28},{24,16},{28,20},{32,40},... | collective-permute-start | bytes 20 | tf_op jit(solution)/shard_map/ppermute | solution.py:110
  158.4 5.5 %collective-permute-start.3 = (f32[]{:T(128)}, f32[]{:T(128)}, u32[]{:S(2)}, u32[]{:S(2)}) collective-permute-start(f32[]{:T(128)} %add.132), channel_id=1, source_target_pairs={{0,8},{4,12},{8,0},{12,4},{16,24},{20,28},{24,16},{28,20},{32,40},... | collective-permute-start | bytes 20 | tf_op jit(solution)/shard_map/ppermute | solution.py:110
  162.5 6.4 %collective-permute-start.19 = (f32[]{:T(128)}, f32[]{:T(128)}, u32[]{:S(2)}, u32[]{:S(2)}) collective-permute-start(f32[]{:T(128)} %add.143), channel_id=1, source_target_pairs={{0,16},{4,20},{8,24},{12,28},{16,0},{20,4},{24,8},{28,12},{32,48},... | collective-permute-start | bytes 20 | tf_op jit(solution)/shard_map/ppermute | solution.py:110
  164.6 6.4 %collective-permute-start.4 = (f32[]{:T(128)}, f32[]{:T(128)}, u32[]{:S(2)}, u32[]{:S(2)}) collective-permute-start(f32[]{:T(128)} %add.133), channel_id=1, source_target_pairs={{0,16},{4,20},{8,24},{12,28},{16,0},{20,4},{24,8},{28,12},{32,48},... | collective-permute-start | bytes 20 | tf_op jit(solution)/shard_map/ppermute | solution.py:110
  169.6 9.4 %collective-permute-start.20 = (f32[]{:T(128)}, f32[]{:T(128)}, u32[]{:S(2)}, u32[]{:S(2)}) collective-permute-start(f32[]{:T(128)} %add.144), channel_id=1, source_target_pairs={{0,32},{4,36},{8,40},{12,44},{16,48},{20,52},{24,56},{28,60},{32,0... | collective-permute-start | bytes 20 | tf_op jit(solution)/shard_map/ppermute | solution.py:110
  171.6 10.5 %collective-permute-start.5 = (f32[]{:T(128)}, f32[]{:T(128)}, u32[]{:S(2)}, u32[]{:S(2)}) collective-permute-start(f32[]{:T(128)} %add.134), channel_id=1, source_target_pairs={{0,32},{4,36},{8,40},{12,44},{16,48},{20,52},{24,56},{28,60},{32,0... | collective-permute-start | bytes 20 | tf_op jit(solution)/shard_map/ppermute | solution.py:110
  179.6 7.6 %collective-permute-start.21 = (f32[]{:T(128)}, f32[]{:T(128)}, u32[]{:S(2)}, u32[]{:S(2)}) collective-permute-start(f32[]{:T(128)} %add.145), channel_id=1, source_target_pairs={{0,64},{4,68},{8,72},{12,76},{16,80},{20,84},{24,88},{28,92},{32,9... | collective-permute-start | bytes 20 | tf_op jit(solution)/shard_map/ppermute | solution.py:110
  182.8 14.1 %collective-permute-start.6 = (f32[]{:T(128)}, f32[]{:T(128)}, u32[]{:S(2)}, u32[]{:S(2)}) collective-permute-start(f32[]{:T(128)} %add.135), channel_id=1, source_target_pairs={{0,64},{4,68},{8,72},{12,76},{16,80},{20,84},{24,88},{28,92},{32,9... | collective-permute-start | bytes 20 | tf_op jit(solution)/shard_map/ppermute | solution.py:110
  188.0 11.1 %collective-permute-start.22 = (f32[]{:T(128)}, f32[]{:T(128)}, u32[]{:S(2)}, u32[]{:S(2)}) collective-permute-start(f32[]{:T(128)} %add.146), channel_id=1, source_target_pairs={{0,128},{4,132},{8,136},{12,140},{16,144},{20,148},{24,152},{28,15... | collective-permute-start | bytes 20 | tf_op jit(solution)/shard_map/ppermute | solution.py:110
  197.6 5.1 %collective-permute-start.7 = (f32[]{:T(128)}, f32[]{:T(128)}, u32[]{:S(2)}, u32[]{:S(2)}) collective-permute-start(f32[]{:T(128)} %add.136), channel_id=1, source_target_pairs={{0,128},{4,132},{8,136},{12,140},{16,144},{20,148},{24,152},{28,15... | collective-permute-start | bytes 20 | tf_op jit(solution)/shard_map/ppermute | solution.py:110
  204.2 3.6 %collective-permute-start.23 = (f32[]{:T(128)}, f32[]{:T(128)}, u32[]{:S(2)}, u32[]{:S(2)}) collective-permute-start(f32[]{:T(128)} %multiply_reduce_fusion.1), channel_id=1, source_target_pairs={{0,1},{1,0},{2,3},{3,2},{4,5},{5,4},{6,7},{7,6},{8,9},{9,8},{10,11... | collective-permute-start | bytes 20 | tf_op jit(solution)/shard_map/ppermute | solution.py:110
  209.2 5.1 %collective-permute-start.24 = (f32[]{:T(128)}, f32[]{:T(128)}, u32[]{:S(2)}, u32[]{:S(2)}) collective-permute-start(f32[]{:T(128)} %add.148), channel_id=1, source_target_pairs={{0,2},{1,3},{2,0},{3,1},{4,6},{5,7},{6,4},{7,5},{8,10},{9,11},{10,... | collective-permute-start | bytes 20 | tf_op jit(solution)/shard_map/ppermute | solution.py:110
  214.9 1.2 collective-permute-start.25
  216.8 3.6 %collective-permute-start.26 = (f32[]{:T(128)}, f32[]{:T(128)}, u32[]{:S(2)}, u32[]{:S(2)}) collective-permute-start(f32[]{:T(128)} %add.150), channel_id=1, source_target_pairs={{0,8},{4,12},{8,0},{12,4},{16,24},{20,28},{24,16},{28,20},{32,40},... | collective-permute-start | bytes 20 | tf_op jit(solution)/shard_map/ppermute | solution.py:110
  221.0 4.5 %collective-permute-start.27 = (f32[]{:T(128)}, f32[]{:T(128)}, u32[]{:S(2)}, u32[]{:S(2)}) collective-permute-start(f32[]{:T(128)} %add.151), channel_id=1, source_target_pairs={{0,16},{4,20},{8,24},{12,28},{16,0},{20,4},{24,8},{28,12},{32,48},... | collective-permute-start | bytes 20 | tf_op jit(solution)/shard_map/ppermute | solution.py:110
  226.2 7.5 %collective-permute-start.28 = (f32[]{:T(128)}, f32[]{:T(128)}, u32[]{:S(2)}, u32[]{:S(2)}) collective-permute-start(f32[]{:T(128)} %add.152), channel_id=1, source_target_pairs={{0,32},{4,36},{8,40},{12,44},{16,48},{20,52},{24,56},{28,60},{32,0... | collective-permute-start | bytes 20 | tf_op jit(solution)/shard_map/ppermute | solution.py:110
  234.4 4.2 %collective-permute-start.29 = (f32[]{:T(128)}, f32[]{:T(128)}, u32[]{:S(2)}, u32[]{:S(2)}) collective-permute-start(f32[]{:T(128)} %add.153), channel_id=1, source_target_pairs={{0,64},{4,68},{8,72},{12,76},{16,80},{20,84},{24,88},{28,92},{32,9... | collective-permute-start | bytes 20 | tf_op jit(solution)/shard_map/ppermute | solution.py:110
  239.2 5.1 %collective-permute-start.30 = (f32[]{:T(128)}, f32[]{:T(128)}, u32[]{:S(2)}, u32[]{:S(2)}) collective-permute-start(f32[]{:T(128)} %add.154), channel_id=1, source_target_pairs={{0,128},{4,132},{8,136},{12,140},{16,144},{20,148},{24,152},{28,15... | collective-permute-start | bytes 20 | tf_op jit(solution)/shard_map/ppermute | solution.py:110
  246.0 16.5 %collective-permute-start.33 = (bf16[64,3072]{1,0:T(8,128)(2,1)S(1)}, bf16[64,3072]{1,0:T(8,128)(2,1)S(1)}, u32[]{:S(2)}, u32[]{:S(2)}) collective-permute-start(bf16[64,3072]{1,0:T(8,128)(2,1)S(1)} %get-tuple-element.10), channel_id=1, source_target_pairs={{3,0},{0,1},{1,2},{2,3},{7,4},{4,5},{5,6},{6,7},{11,8},{8,9},{9,10... | collective-permute-start | bytes 1179656 | tf_op jit(solution)/shard_map/ppermute | solution.py:120
  246.0 16.5 %collective-permute-start.32 = (bf16[64,3072]{1,0:T(8,128)(2,1)S(1)}, bf16[64,3072]{1,0:T(8,128)(2,1)S(1)}, u32[]{:S(2)}, u32[]{:S(2)}) collective-permute-start(bf16[64,3072]{1,0:T(8,128)(2,1)S(1)} %get-tuple-element.10), channel_id=1, source_target_pairs={{2,0},{3,1},{0,2},{1,3},{6,4},{7,5},{4,6},{5,7},{10,8},{11,9},{8,1... | collective-permute-start | bytes 1179656 | tf_op jit(solution)/shard_map/ppermute | solution.py:120
  248.1 15.1 %collective-permute-start.31 = (bf16[64,3072]{1,0:T(8,128)(2,1)S(1)}, bf16[64,3072]{1,0:T(8,128)(2,1)S(1)}, u32[]{:S(2)}, u32[]{:S(2)}) collective-permute-start(bf16[64,3072]{1,0:T(8,128)(2,1)S(1)} %get-tuple-element.10), channel_id=1, source_target_pairs={{1,0},{2,1},{3,2},{0,3},{5,4},{6,5},{7,6},{4,7},{9,8},{10,9},{11,1... | collective-permute-start | bytes 1179656 | tf_op jit(solution)/shard_map/ppermute | solution.py:120
  264.2 8.9 %collective-permute-start.34 = (bf16[64,1408]{1,0:T(8,128)(2,1)S(1)}, bf16[64,1408]{1,0:T(8,128)(2,1)S(1)}, u32[]{:S(2)}, u32[]{:S(2)}) collective-permute-start(bf16[64,1408]{1,0:T(8,128)(2,1)S(1)} %get-tuple-element.18), channel_id=1, source_target_pairs={{0,4},{4,8},{8,12},{12,16},{16,20},{20,24},{24,28},{28,32},{32,36}... | collective-permute-start | bytes 540680 | tf_op jit(solution)/shard_map/ppermute | solution.py:97
  266.1 8.8 %collective-permute-start.35 = (bf16[64,1408]{1,0:T(8,128)(2,1)S(1)}, bf16[64,1408]{1,0:T(8,128)(2,1)S(1)}, u32[]{:S(2)}, u32[]{:S(2)}) collective-permute-start(bf16[64,1408]{1,0:T(8,128)(2,1)S(1)} %get-tuple-element.19), channel_id=1, source_target_pairs={{4,0},{8,4},{12,8},{16,12},{20,16},{24,20},{28,24},{32,28},{36,32}... | collective-permute-start | bytes 540680 | tf_op jit(solution)/shard_map/ppermute | solution.py:100
  284.9 43.0 %copy-start.3 = (f32[64,3072]{1,0:T(8,128)S(1)}, f32[64,3072]{1,0:T(8,128)}, u32[]{:S(2)}) copy-start(f32[64,3072]{1,0:T(8,128)} %shard_map.88) | copy-start | bytes 2359300
  287.0 3.8 %collective-permute-start.36 = (f32[]{:T(128)}, f32[]{:T(128)}, u32[]{:S(2)}, u32[]{:S(2)}) collective-permute-start(f32[]{:T(128)} %multiply_reduce_fusion), channel_id=1, source_target_pairs={{0,1},{1,0},{2,3},{3,2},{4,5},{5,4},{6,7},{7,6},{8,9},{9,8},{10,11... | collective-permute-start | bytes 20 | tf_op jit(solution)/shard_map/ppermute | solution.py:110
  292.0 5.2 %collective-permute-start.37 = (f32[]{:T(128)}, f32[]{:T(128)}, u32[]{:S(2)}, u32[]{:S(2)}) collective-permute-start(f32[]{:T(128)} %add.157), channel_id=1, source_target_pairs={{0,2},{1,3},{2,0},{3,1},{4,6},{5,7},{6,4},{7,5},{8,10},{9,11},{10,... | collective-permute-start | bytes 20 | tf_op jit(solution)/shard_map/ppermute | solution.py:110
  297.9 1.3 collective-permute-start.38
  299.8 3.7 %collective-permute-start.39 = (f32[]{:T(128)}, f32[]{:T(128)}, u32[]{:S(2)}, u32[]{:S(2)}) collective-permute-start(f32[]{:T(128)} %add.159), channel_id=1, source_target_pairs={{0,8},{4,12},{8,0},{12,4},{16,24},{20,28},{24,16},{28,20},{32,40},... | collective-permute-start | bytes 20 | tf_op jit(solution)/shard_map/ppermute | solution.py:110
  304.2 4.6 %collective-permute-start.40 = (f32[]{:T(128)}, f32[]{:T(128)}, u32[]{:S(2)}, u32[]{:S(2)}) collective-permute-start(f32[]{:T(128)} %add.160), channel_id=1, source_target_pairs={{0,16},{4,20},{8,24},{12,28},{16,0},{20,4},{24,8},{28,12},{32,48},... | collective-permute-start | bytes 20 | tf_op jit(solution)/shard_map/ppermute | solution.py:110
  309.4 7.6 %collective-permute-start.41 = (f32[]{:T(128)}, f32[]{:T(128)}, u32[]{:S(2)}, u32[]{:S(2)}) collective-permute-start(f32[]{:T(128)} %add.161), channel_id=1, source_target_pairs={{0,32},{4,36},{8,40},{12,44},{16,48},{20,52},{24,56},{28,60},{32,0... | collective-permute-start | bytes 20 | tf_op jit(solution)/shard_map/ppermute | solution.py:110
  317.7 3.7 %collective-permute-start.42 = (f32[]{:T(128)}, f32[]{:T(128)}, u32[]{:S(2)}, u32[]{:S(2)}) collective-permute-start(f32[]{:T(128)} %add.162), channel_id=1, source_target_pairs={{0,64},{4,68},{8,72},{12,76},{16,80},{20,84},{24,88},{28,92},{32,9... | collective-permute-start | bytes 20 | tf_op jit(solution)/shard_map/ppermute | solution.py:110
  322.1 5.2 %collective-permute-start.43 = (f32[]{:T(128)}, f32[]{:T(128)}, u32[]{:S(2)}, u32[]{:S(2)}) collective-permute-start(f32[]{:T(128)} %add.163), channel_id=1, source_target_pairs={{0,128},{4,132},{8,136},{12,140},{16,144},{20,148},{24,152},{28,15... | collective-permute-start | bytes 20 | tf_op jit(solution)/shard_map/ppermute | solution.py:110
  (4 other events, 18.1 us)

commit v3 on v2

--- a/solution.py
+++ b/solution.py
@@ -12,33 +12,37 @@
 AMPLITUDE = 0.05
 
 
-def tile_kernel(begin_ref, count_ref, own_ref, win_ref, out_ref, *, slots, dims, runs):
+def tile_kernel(begin_ref, count_ref, own_ref, win_ref, out_ref, *, slots, runs):
     b = pl.program_id(0)
     start = begin_ref[b]
     count = count_ref[b]
     own = own_ref[0]
+    parts = jnp.concatenate([win_ref[start + s] for s in range(slots)], axis=1)
+    cross = jnp.dot(
+        own * -2.0, parts, precision=lax.Precision.HIGHEST, preferred_element_type=jnp.float32
+    )
+    own_sq = jnp.sum(own * own, axis=1, keepdims=True)
+    part_sq = jnp.sum(parts * parts, axis=0, keepdims=True)
     for s in range(slots):
+        cols = slice(s * runs, (s + 1) * runs)
+
         @pl.when(s < count)
         def _():
-            part = win_ref[start + s]
-            squared = jnp.zeros((runs, runs), jnp.float32)
-            for d in range(dims):
-                diff = own[:, d:d + 1] - part[d:d + 1, :]
-                squared = squared + diff * diff
-            radius_frac = jnp.sqrt(squared) / SUPPORT
+            squared = jnp.maximum((own_sq + part_sq[:, cols]) + cross[:, cols], 0.0)
+            radius_frac = jnp.sqrt(squared) * (1.0 / SUPPORT)
             remain = jnp.maximum(1.0 - radius_frac, 0.0)
             cubed = remain * remain * remain
             val = cubed * cubed * (6.0 * radius_frac + 1.0)
-            out_ref[0, :, s * runs:(s + 1) * runs] = val.astype(out_ref.dtype)
+            out_ref[0, :, cols] = val.astype(out_ref.dtype)
 
         @pl.when(s >= count)
         def _():
-            out_ref[0, :, s * runs:(s + 1) * runs] = jnp.zeros((runs, runs), out_ref.dtype)
+            out_ref[0, :, cols] = jnp.zeros((runs, runs), out_ref.dtype)
 
 
 def build_tiles(begin, count, own_t, win_c, slots):
     blocks, runs, dpad = own_t.shape
-    kern = functools.partial(tile_kernel, slots=slots, dims=dpad, runs=runs)
+    kern = functools.partial(tile_kernel, slots=slots, runs=runs)
     return pl.pallas_call(
         kern,
         grid_spec=pltpu.PrefetchScalarGridSpec(
@@ -130,14 +134,13 @@
     slot_limit = block_nbrs.shape[1]
     halo = slot_limit - 1
     device_pos = lax.axis_index("samp")
-    chan_pos = lax.axis_index("chan")
     local_perm = run_perm - device_pos * runs_local
     sorted_coords = jnp.take(coords, local_perm, axis=1)
     sorted_loads = jnp.take(loads, local_perm, axis=1)
-    norm_now = global_sum(jnp.sum(sorted_loads * sorted_loads))
-    full_factor = lax.all_gather(coreg_factor, "chan", axis=0, tiled=True)
-    coreg_rows = jnp.dot(coreg_factor, full_factor.T, precision=lax.Precision.HIGHEST)
-    coreg_perm = jnp.roll(coreg_rows, -chan_pos * chan_local, axis=1)
+    norm_local = jnp.sum(sorted_loads * sorted_loads)
+    coreg_perm = jnp.dot(
+        coreg_factor, gather_chan(coreg_factor).T, precision=lax.Precision.HIGHEST
+    )
     reach_runs = halo * block_runs
     window_blocks = blocks_local + 2 * halo
     widened_coords = extended(sorted_coords, "samp", 1, reach_runs)
@@ -165,7 +168,13 @@
         widened = extended(mixed_b, "samp", 1, reach_runs)
         win_v = widened.reshape(chan_local, window_blocks, block_runs).transpose(1, 0, 2)
         mapped = apply_operator(begin, win_v, tiles, direction, noise_col, 4)
-        step_size = norm_now / global_sum(jnp.sum(direction * mapped))
+        curvature = jnp.sum(direction * mapped)
+        if iteration == 0:
+            sums = global_sum(jnp.stack([norm_local, curvature]))
+            norm_now, curvature = sums[0], sums[1]
+        else:
+            curvature = global_sum(curvature)
+        step_size = norm_now / curvature
         iterate = iterate + step_size * direction
         remainder = remainder - step_size * mapped
         if iteration + 1 < ITERS:

time: 350 us -> 288 us (0.82); the launches traced: 351 us -> 285 us
  Pallas kernels: 79.8 us -> 49.2 us
  starting transfers between devices: 116 us -> 88.4 us
  blocking collectives: 12.2 us -> 0 us
  waiting for transfers between devices: 55.3 us -> 66.7 us
  between operations: 25 us -> 14.4 us
  other arithmetic: 14.8 us -> 18.8 us
    pallas_call x1, Pallas kernels: 62 us -> 31.3 us  [build_tiles(): pl.pallas_call(kern, grid_spec=pltpu.PrefetchScalarGridSpec(num_scalar_pr...]
    ppermute x32 -> x24, starting transfers between devices: 82.7 us -> 52.1 us  [global_sum(): value = value + lax.ppermute(value, axis, pairs)]
    all_gather x1 -> x0, blocking collectives: 12.2 us -> none  [per_device(): full_factor = lax.all_gather(coreg_factor, 'chan', axis=0, tiled=True)]
    ppermute x32 -> x24, waiting for transfers between devices: 39.2 us -> 51.3 us  [global_sum(): value = value + lax.ppermute(value, axis, pairs)]
    ppermute x6 -> x9, starting transfers between devices: 9.92 us -> 13.2 us  [gather_chan(): parts.append(lax.ppermute(rounded, 'chan', pairs))]
    ppermute x6 -> x9, waiting for transfers between devices: 13 us -> 12.4 us  [gather_chan(): parts.append(lax.ppermute(rounded, 'chan', pairs))]
  transfers between devices with their start and end apart: 44 -> 39, of which waited for: 22 -> 29; matrix products, arithmetic and copies ran while one was open for 5% -> 10% of each run, Pallas kernels for 18% -> 11%
where the time goes in v3:
time: 288 us; the launch traced here: 285 us
  starting transfers between devices  88.4 us (31%)
  waiting for transfers between devices  66.7 us (23%)
  Pallas kernels  49.2 us (17%)
  local copies, waits for them, and re-layouts  44.3 us (15%)
  other arithmetic  18.8 us (7%)
  between operations  14.4 us (5%)
  matrix products  3.58 us (1%)
    ppermute x24, starting transfers between devices, global_sum(): value = value + lax.ppermute(value, axis, pairs)  52.1 us
    ppermute x24, waiting for transfers between devices, global_sum(): value = value + lax.ppermute(value, axis, pairs)  51.3 us
    pallas_call x1, Pallas kernels, build_tiles(): pl.pallas_call(kern, grid_spec=pltpu.PrefetchScalarGridSpec(num_scalar_pr...  31.3 us
    pallas_call x2, Pallas kernels, apply_operator(): pl.pallas_call(kern, grid_spec=pltpu.PrefetchScalarGridSpec(num_scalar_pr...  17.9 us
    ppermute x3, starting transfers between devices, extended(): lax.ppermute(lax.slice_in_dim(block, 0, width, axis=dim), axis, backward)  17.4 us
    ppermute x9, starting transfers between devices, gather_chan(): parts.append(lax.ppermute(rounded, 'chan', pairs))  13.2 us
    ppermute x9, waiting for transfers between devices, gather_chan(): parts.append(lax.ppermute(rounded, 'chan', pairs))  12.4 us
    gather x2, local copies, waits for them, and re-layouts, per_device(): sorted_loads = jnp.take(loads, local_perm, axis=1)  8.57 us
  transfers between devices with their start and end apart: 39, of which 29 were waited for; matrix products, arithmetic and copies ran while one was open for 10% of the time, Pallas kernels for 11%

profile of v3, /device:TPU:2, one launch (start us, length us, event | category | flops | bytes accessed | tf_op | source)
XLA Modules:
  0.0 285.3 jit_solution(17392539270268022057)
XLA Ops:
  0.6 3.3 %collective-permute-start.1 = (f32[64,256]{1,0:T(8,128)}, f32[64,256]{1,0:T(8,128)S(1)}, u32[]{:S(2)}, u32[]{:S(2)}) collective-permute-start(f32[64,256]{1,0:T(8,128)} %param.9), channel_id=1, source_target_pairs={{2,0},{3,1},{0,2},{1,3},{6,4},{7,5},{4,6},{5,7},{10,8},{11,9},{8,1... | collective-permute-start | bytes 196616 | tf_op jit(solution)/shard_map/ppermute | solution.py:124
  5.7 1.6 copy.31
  7.3 8.1 %gather_fusion = f32[3072,64]{1,0:T(8,128)S(1)} fusion(f32[64,3072]{0,1:T(8,128)S(1)} %copy.31, s32[3072]{0:T(1024)S(1)} %broadcast_clamp_fusion), kind=kCustom, calls=%fused_computation | custom fusion | bytes 1585152 | tf_op jit(solution)/shard_map/jit(_take)/gather | solution.py:139
  18.7 2.6 collective-permute-start.3
  21.8 8.1 %gather_fusion.1 = f32[3072,6]{1,0:T(8,128)S(1)} fusion(f32[6,3072]{0,1:T(8,128)S(1)} %copy.34, s32[3072]{0:T(1024)S(1)} %broadcast_clamp_fusion), kind=kCustom, calls=%fused_computation.1 | custom fusion | bytes 159744 | tf_op jit(solution)/shard_map/jit(_take)/gather | solution.py:138
  36.0 1.9 collective-permute-start.8
  39.5 5.9 %collective-permute-start.9 = (f32[6,1408]{1,0:T(8,128)S(1)}, f32[6,1408]{1,0:T(8,128)S(1)}, u32[]{:S(2)}, u32[]{:S(2)}) collective-permute-start(f32[6,1408]{1,0:T(8,128)S(1)} %get-tuple-element.23), channel_id=1, source_target_pairs={{4,0},{8,4},{12,8},{16,12},{20,16},{24,20},{28,24},{32,28},{36,32}... | collective-permute-start | bytes 101384 | tf_op jit(solution)/shard_map/ppermute | solution.py:104
  45.8 2.3 convolution_convert_fusion.1
  48.1 1.9 collective-permute-start.6
  50.0 5.8 %collective-permute-start.7 = (bf16[64,1408]{1,0:T(8,128)(2,1)S(1)}, bf16[64,1408]{1,0:T(8,128)(2,1)S(1)}, u32[]{:S(2)}, u32[]{:S(2)}) collective-permute-start(bf16[64,1408]{1,0:T(8,128)(2,1)S(1)} %get-tuple-element.21), channel_id=1, source_target_pairs={{4,0},{8,4},{12,8},{16,12},{20,16},{24,20},{28,24},{32,28},{36,32}... | collective-permute-start | bytes 540680 | tf_op jit(solution)/shard_map/ppermute | solution.py:104
  56.5 31.3 %shard_map.86.tile_ref = bf16[24,128,1536]{2,1,0:T(8,128)(2,1)} custom-call(s32[24]{0:T(128)} %clamp_bitcast_fusion.begin_ref, s32[24]{0:T(128)} %count_ref.1, f32[24,128,8]{2,1,0:T(8,128)} %pad_bitcast_fusion.own_ref, f32[46,8,128]{2,1,0:T(8,128)} %pad_bitcast_fusion.1.win_ref), custom_call_target="tpu_custom_call" | custom-call | tf_op jit(solution)/shard_map/pallas_call | solution.py:46
  88.9 8.9 %shard_map.87 = f32[64,3072]{1,0:T(8,128)} custom-call(s32[24]{0:T(128)} %clamp_bitcast_fusion.begin_ref, bf16[46,64,128]{2,1,0:T(8,128)(2,1)} %bitcast_bitcast_fusion.1.win_ref, bf16[24,128,1536]{2,1,0:T(8,128)(2,1)} %shard_map.86.tile_ref, f32[64,3072]{1,0:T(8,128)} %get-tuple-element.13.p_ref, f32[64,1]{1,0:T(8,128)} %copy.39.noise_ref), custom_call_target="tpu_custom_call" | custom-call | tf_op jit(solution)/shard_map/pallas_call | solution.py:80
  97.9 2.0 multiply_reduce_fusion.3
  101.3 3.4 %collective-permute-done.10 = f32[2]{0:T(128)S(1)} collective-permute-done((f32[2]{0:T(128)S(1)}, f32[2]{0:T(128)S(1)}, u32[]{:S(2)}, u32[]{:S(2)}) %collective-permute-start.10) | collective-permute-done | bytes 40 | tf_op jit(solution)/shard_map/ppermute | solution.py:114
  107.1 4.1 %collective-permute-done.11 = f32[2]{0:T(128)S(1)} collective-permute-done((f32[2]{0:T(128)S(1)}, f32[2]{0:T(128)S(1)}, u32[]{:S(2)}, u32[]{:S(2)}) %collective-permute-start.11) | collective-permute-done | bytes 40 | tf_op jit(solution)/shard_map/ppermute | solution.py:114
  113.7 3.5 %collective-permute-done.13 = f32[2]{0:T(128)S(1)} collective-permute-done((f32[2]{0:T(128)S(1)}, f32[2]{0:T(128)S(1)}, u32[]{:S(2)}, u32[]{:S(2)}) %collective-permute-start.13) | collective-permute-done | bytes 40 | tf_op jit(solution)/shard_map/ppermute | solution.py:114
  117.2 4.4 %collective-permute-done.14 = f32[2]{0:T(128)S(1)} collective-permute-done((f32[2]{0:T(128)S(1)}, f32[2]{0:T(128)S(1)}, u32[]{:S(2)}, u32[]{:S(2)}) %collective-permute-start.14) | collective-permute-done | bytes 40 | tf_op jit(solution)/shard_map/ppermute | solution.py:114
  121.7 5.0 %collective-permute-start.15 = (f32[2]{0:T(128)S(1)}, f32[2]{0:T(128)S(1)}, u32[]{:S(2)}, u32[]{:S(2)}) collective-permute-start(f32[2]{0:T(128)S(1)} %add.100), channel_id=1, source_target_pairs={{0,32},{4,36},{8,40},{12,44},{16,48},{20,52},{24,56},{28,60},{32,0... | collective-permute-start | bytes 32 | tf_op jit(solution)/shard_map/ppermute | solution.py:114
  126.7 2.4 collective-permute-done.15
  130.0 2.6 collective-permute-done.16
  132.7 2.5 collective-permute-start.17
  135.2 2.6 collective-permute-done.17
  141.3 2.9 %collective-permute-done.18 = f32[]{:T(128)} collective-permute-done((f32[]{:T(128)}, f32[]{:T(128)}, u32[]{:S(2)}, u32[]{:S(2)}) %collective-permute-start.18) | collective-permute-done | bytes 36 | tf_op jit(solution)/shard_map/ppermute | solution.py:114
  145.5 3.2 %collective-permute-start.19 = (f32[]{:T(128)}, f32[]{:T(128)}, u32[]{:S(2)}, u32[]{:S(2)}) collective-permute-start(f32[]{:T(128)} %add.104), channel_id=1, source_target_pairs={{0,2},{1,3},{2,0},{3,1},{4,6},{5,7},{6,4},{7,5},{8,10},{9,11},{10,... | collective-permute-start | bytes 20 | tf_op jit(solution)/shard_map/ppermute | solution.py:114
  148.7 2.1 collective-permute-done.19
  154.7 2.3 collective-permute-done.21
  159.1 3.2 %collective-permute-done.22 = f32[]{:T(128)} collective-permute-done((f32[]{:T(128)}, f32[]{:T(128)}, u32[]{:S(2)}, u32[]{:S(2)}) %collective-permute-start.22) | collective-permute-done | bytes 36 | tf_op jit(solution)/shard_map/ppermute | solution.py:114
  163.0 6.4 %collective-permute-start.23 = (f32[]{:T(128)}, f32[]{:T(128)}, u32[]{:S(2)}, u32[]{:S(2)}) collective-permute-start(f32[]{:T(128)} %add.108), channel_id=1, source_target_pairs={{0,32},{4,36},{8,40},{12,44},{16,48},{20,52},{24,56},{28,60},{32,0... | collective-permute-start | bytes 20 | tf_op jit(solution)/shard_map/ppermute | solution.py:114
  171.3 2.3 collective-permute-start.24
  175.6 3.9 %collective-permute-start.25 = (f32[]{:T(128)}, f32[]{:T(128)}, u32[]{:S(2)}, u32[]{:S(2)}) collective-permute-start(f32[]{:T(128)} %add.110), channel_id=1, source_target_pairs={{0,128},{4,132},{8,136},{12,140},{16,144},{20,148},{24,152},{28,15... | collective-permute-start | bytes 20 | tf_op jit(solution)/shard_map/ppermute | solution.py:114
  184.1 2.9 %collective-permute-start.27 = (bf16[64,3072]{1,0:T(8,128)(2,1)S(1)}, bf16[64,3072]{1,0:T(8,128)(2,1)S(1)}, u32[]{:S(2)}, u32[]{:S(2)}) collective-permute-start(bf16[64,3072]{1,0:T(8,128)(2,1)S(1)} %get-tuple-element.10), channel_id=1, source_target_pairs={{2,0},{3,1},{0,2},{1,3},{6,4},{7,5},{4,6},{5,7},{10,8},{11,9},{8,1... | collective-permute-start | bytes 1179656 | tf_op jit(solution)/shard_map/ppermute | solution.py:124
  187.6 6.6 %collective-permute-done.28 = bf16[64,3072]{1,0:T(8,128)(2,1)S(1)} collective-permute-done((bf16[64,3072]{1,0:T(8,128)(2,1)S(1)}, bf16[64,3072]{1,0:T(8,128)(2,1)S(1)}, u32[]{:S(2)}, u32[]{:S(2)}) %collective-permute-start.28) | collective-permute-done | bytes 393248 | tf_op jit(solution)/shard_map/ppermute | solution.py:124
  194.2 4.2 %collective-permute-done.27 = bf16[64,3072]{1,0:T(8,128)(2,1)S(1)} collective-permute-done((bf16[64,3072]{1,0:T(8,128)(2,1)S(1)}, bf16[64,3072]{1,0:T(8,128)(2,1)S(1)}, u32[]{:S(2)}, u32[]{:S(2)}) %collective-permute-start.27) | collective-permute-done | bytes 393248 | tf_op jit(solution)/shard_map/ppermute | solution.py:124
  199.4 1.9 collective-permute-start.29
  201.3 5.8 %collective-permute-start.30 = (bf16[64,1408]{1,0:T(8,128)(2,1)S(1)}, bf16[64,1408]{1,0:T(8,128)(2,1)S(1)}, u32[]{:S(2)}, u32[]{:S(2)}) collective-permute-start(bf16[64,1408]{1,0:T(8,128)(2,1)S(1)} %get-tuple-element.19), channel_id=1, source_target_pairs={{4,0},{8,4},{12,8},{16,12},{20,16},{24,20},{28,24},{32,28},{36,32}... | collective-permute-start | bytes 540680 | tf_op jit(solution)/shard_map/ppermute | solution.py:104
  208.3 1.8 collective-permute-done.30
  211.2 8.9 %shard_map.88 = f32[64,3072]{1,0:T(8,128)} custom-call(s32[24]{0:T(128)} %clamp_bitcast_fusion.begin_ref, bf16[46,64,128]{2,1,0:T(8,128)(2,1)} %bitcast_bitcast_fusion.win_ref, bf16[24,128,1536]{2,1,0:T(8,128)(2,1)} %shard_map.86.tile_ref, f32[64,3072]{1,0:T(8,128)} %get-tuple-element.11.p_ref, f32[64,1]{1,0:T(8,128)} %copy.39.noise_ref), custom_call_target="tpu_custom_call" | custom-call | tf_op jit(solution)/shard_map/pallas_call | solution.py:80
  220.2 2.0 multiply_reduce_fusion
  223.4 2.4 collective-permute-done.31
  227.1 3.3 %collective-permute-start.32 = (f32[]{:T(128)}, f32[]{:T(128)}, u32[]{:S(2)}, u32[]{:S(2)}) collective-permute-start(f32[]{:T(128)} %add.113), channel_id=1, source_target_pairs={{0,2},{1,3},{2,0},{3,1},{4,6},{5,7},{6,4},{7,5},{8,10},{9,11},{10,... | collective-permute-start | bytes 20 | tf_op jit(solution)/shard_map/ppermute | solution.py:114
  230.3 1.8 collective-permute-done.32
  236.2 2.2 collective-permute-done.34
  239.0 3.3 %collective-permute-start.35 = (f32[]{:T(128)}, f32[]{:T(128)}, u32[]{:S(2)}, u32[]{:S(2)}) collective-permute-start(f32[]{:T(128)} %add.116), channel_id=1, source_target_pairs={{0,16},{4,20},{8,24},{12,28},{16,0},{20,4},{24,8},{28,12},{32,48},... | collective-permute-start | bytes 20 | tf_op jit(solution)/shard_map/ppermute | solution.py:114
  244.1 6.1 %collective-permute-start.36 = (f32[]{:T(128)}, f32[]{:T(128)}, u32[]{:S(2)}, u32[]{:S(2)}) collective-permute-start(f32[]{:T(128)} %add.117), channel_id=1, source_target_pairs={{0,32},{4,36},{8,40},{12,44},{16,48},{20,52},{24,56},{28,60},{32,0... | collective-permute-start | bytes 20 | tf_op jit(solution)/shard_map/ppermute | solution.py:114
  252.2 2.1 collective-permute-start.37
  256.4 3.6 %collective-permute-start.38 = (f32[]{:T(128)}, f32[]{:T(128)}, u32[]{:S(2)}, u32[]{:S(2)}) collective-permute-start(f32[]{:T(128)} %add.119), channel_id=1, source_target_pairs={{0,128},{4,132},{8,136},{12,140},{16,144},{20,148},{24,152},{28,15... | collective-permute-start | bytes 20 | tf_op jit(solution)/shard_map/ppermute | solution.py:114
  265.2 8.5 %scatter_custom_fusion.1 = f32[64,3072]{0,1:T(8,128)S(1)} fusion(s32[3072]{0:T(1024)S(1)} %get-tuple-element.15, f32[3072,64]{1,0:T(8,128)S(1)} %copy.43, f32[]{:T(128)} %constant.16.clone.1), kind=kCustom, calls=%fused_computation.32 | custom fusion | bytes 786436 | tf_op jit(solution)/shard_map/scatter | solution.py:185
  275.5 8.5 %scatter_custom_fusion = f32[64,3072]{0,1:T(8,128)S(1)} fusion(s32[3072]{0:T(1024)S(1)} %get-tuple-element.15, f32[3072,64]{1,0:T(8,128)S(1)} %copy.42, f32[]{:T(128)} %constant.16.clone.1), kind=kCustom, calls=%fused_computation.34 | custom fusion | bytes 786436 | tf_op jit(solution)/shard_map/scatter | solution.py:184
  (94 shorter events, 54.4 us)
Async XLA Ops:
  0.6 33.3 %collective-permute-start.1 = (f32[64,256]{1,0:T(8,128)}, f32[64,256]{1,0:T(8,128)S(1)}, u32[]{:S(2)}, u32[]{:S(2)}) collective-permute-start(f32[64,256]{1,0:T(8,128)} %param.9), channel_id=1, source_target_pairs={{2,0},{3,1},{0,2},{1,3},{6,4},{7,5},{4,6},{5,7},{10,8},{11,9},{8,1... | collective-permute-start | bytes 196616 | tf_op jit(solution)/shard_map/ppermute | solution.py:124
  3.9 32.1 %collective-permute-start = (f32[64,256]{1,0:T(8,128)}, f32[64,256]{1,0:T(8,128)S(1)}, u32[]{:S(2)}, u32[]{:S(2)}) collective-permute-start(f32[64,256]{1,0:T(8,128)} %param.9), channel_id=1, source_target_pairs={{1,0},{2,1},{3,2},{0,3},{5,4},{6,5},{7,6},{4,7},{9,8},{10,9},{11,1... | collective-permute-start | bytes 196616 | tf_op jit(solution)/shard_map/ppermute | solution.py:124
  15.9 5.4 %copy-start.5 = (f32[6,3072]{1,0:T(8,128)S(1)}, f32[6,3072]{1,0:T(8,128)}, u32[]{:S(2)}) copy-start(f32[6,3072]{1,0:T(8,128)} %param.8) | copy-start | bytes 221188
  17.0 28.8 %collective-permute-start.5 = (bf16[64,3072]{1,0:T(8,128)(2,1)}, bf16[64,3072]{1,0:T(8,128)(2,1)}, u32[]{:S(2)}, u32[]{:S(2)}) collective-permute-start(bf16[64,3072]{1,0:T(8,128)(2,1)} %get-tuple-element.12), channel_id=1, source_target_pairs={{3,0},{0,1},{1,2},{2,3},{7,4},{4,5},{5,6},{6,7},{11,8},{8,9},{9,10... | collective-permute-start | bytes 1179656 | tf_op jit(solution)/shard_map/ppermute | solution.py:124
  18.0 27.8 %collective-permute-start.4 = (bf16[64,3072]{1,0:T(8,128)(2,1)}, bf16[64,3072]{1,0:T(8,128)(2,1)}, u32[]{:S(2)}, u32[]{:S(2)}) collective-permute-start(bf16[64,3072]{1,0:T(8,128)(2,1)} %get-tuple-element.12), channel_id=1, source_target_pairs={{2,0},{3,1},{0,2},{1,3},{6,4},{7,5},{4,6},{5,7},{10,8},{11,9},{8,1... | collective-permute-start | bytes 1179656 | tf_op jit(solution)/shard_map/ppermute | solution.py:124
  18.7 27.1 %collective-permute-start.3 = (bf16[64,3072]{1,0:T(8,128)(2,1)}, bf16[64,3072]{1,0:T(8,128)(2,1)}, u32[]{:S(2)}, u32[]{:S(2)}) collective-permute-start(bf16[64,3072]{1,0:T(8,128)(2,1)} %get-tuple-element.12), channel_id=1, source_target_pairs={{1,0},{2,1},{3,2},{0,3},{5,4},{6,5},{7,6},{4,7},{9,8},{10,9},{11,1... | collective-permute-start | bytes 1179656 | tf_op jit(solution)/shard_map/ppermute | solution.py:124
  32.0 1.9 copy-start.7
  33.9 1.4 copy-start.6
  33.9 5.6 %collective-permute-start.2 = (f32[64,256]{1,0:T(8,128)S(1)}, f32[64,256]{1,0:T(8,128)S(1)}, u32[]{:S(2)}, u32[]{:S(2)}) collective-permute-start(f32[64,256]{1,0:T(8,128)S(1)} %copy-done.7), channel_id=1, source_target_pairs={{3,0},{0,1},{1,2},{2,3},{7,4},{4,5},{5,6},{6,7},{11,8},{8,9},{9,10... | collective-permute-start | bytes 196616 | tf_op jit(solution)/shard_map/ppermute | solution.py:124
  36.0 19.8 %collective-permute-start.8 = (f32[6,1408]{1,0:T(8,128)S(1)}, f32[6,1408]{1,0:T(8,128)S(1)}, u32[]{:S(2)}, u32[]{:S(2)}) collective-permute-start(f32[6,1408]{1,0:T(8,128)S(1)} %get-tuple-element.22), channel_id=1, source_target_pairs={{0,4},{4,8},{8,12},{12,16},{16,20},{20,24},{24,28},{28,32},{32,36}... | collective-permute-start | bytes 101384 | tf_op jit(solution)/shard_map/ppermute | solution.py:101
  39.5 16.3 %collective-permute-start.9 = (f32[6,1408]{1,0:T(8,128)S(1)}, f32[6,1408]{1,0:T(8,128)S(1)}, u32[]{:S(2)}, u32[]{:S(2)}) collective-permute-start(f32[6,1408]{1,0:T(8,128)S(1)} %get-tuple-element.23), channel_id=1, source_target_pairs={{4,0},{8,4},{12,8},{16,12},{20,16},{24,20},{28,24},{32,28},{36,32}... | collective-permute-start | bytes 101384 | tf_op jit(solution)/shard_map/ppermute | solution.py:104
  48.1 39.7 %collective-permute-start.6 = (bf16[64,1408]{1,0:T(8,128)(2,1)S(1)}, bf16[64,1408]{1,0:T(8,128)(2,1)S(1)}, u32[]{:S(2)}, u32[]{:S(2)}) collective-permute-start(bf16[64,1408]{1,0:T(8,128)(2,1)S(1)} %get-tuple-element.20), channel_id=1, source_target_pairs={{0,4},{4,8},{8,12},{12,16},{16,20},{20,24},{24,28},{28,32},{32,36}... | collective-permute-start | bytes 540680 | tf_op jit(solution)/shard_map/ppermute | solution.py:101
  50.0 37.8 %collective-permute-start.7 = (bf16[64,1408]{1,0:T(8,128)(2,1)S(1)}, bf16[64,1408]{1,0:T(8,128)(2,1)S(1)}, u32[]{:S(2)}, u32[]{:S(2)}) collective-permute-start(bf16[64,1408]{1,0:T(8,128)(2,1)S(1)} %get-tuple-element.21), channel_id=1, source_target_pairs={{4,0},{8,4},{12,8},{16,12},{20,16},{24,20},{28,24},{32,28},{36,32}... | collective-permute-start | bytes 540680 | tf_op jit(solution)/shard_map/ppermute | solution.py:104
  88.9 9.0 %copy-start = (f32[64,3072]{1,0:T(8,128)S(1)}, f32[64,3072]{1,0:T(8,128)}, u32[]{:S(2)}) copy-start(f32[64,3072]{1,0:T(8,128)} %get-tuple-element.13.p_ref) | copy-start | bytes 2359300
  97.9 41.8 %copy-start.1 = (f32[64,3072]{1,0:T(8,128)S(1)}, f32[64,3072]{1,0:T(8,128)}, u32[]{:S(2)}) copy-start(f32[64,3072]{1,0:T(8,128)} %shard_map.87) | copy-start | bytes 2359300
  101.2 3.6 %collective-permute-start.10 = (f32[2]{0:T(128)S(1)}, f32[2]{0:T(128)S(1)}, u32[]{:S(2)}, u32[]{:S(2)}) collective-permute-start(f32[2]{0:T(128)S(1)} %pad_maximum_fusion), channel_id=1, source_target_pairs={{0,1},{1,0},{2,3},{3,2},{4,5},{5,4},{6,7},{7,6},{8,9},{9,8},{10,11... | collective-permute-start | bytes 32 | tf_op jit(solution)/shard_map/ppermute | solution.py:114
  106.1 5.1 %collective-permute-start.11 = (f32[2]{0:T(128)S(1)}, f32[2]{0:T(128)S(1)}, u32[]{:S(2)}, u32[]{:S(2)}) collective-permute-start(f32[2]{0:T(128)S(1)} %fusion.38), channel_id=1, source_target_pairs={{0,2},{1,3},{2,0},{3,1},{4,6},{5,7},{6,4},{7,5},{8,10},{9,11},{10,... | collective-permute-start | bytes 32 | tf_op jit(solution)/shard_map/ppermute | solution.py:114
  112.5 1.1 collective-permute-start.12
  113.7 3.5 %collective-permute-start.13 = (f32[2]{0:T(128)S(1)}, f32[2]{0:T(128)S(1)}, u32[]{:S(2)}, u32[]{:S(2)}) collective-permute-start(f32[2]{0:T(128)S(1)} %add.98), channel_id=1, source_target_pairs={{0,8},{4,12},{8,0},{12,4},{16,24},{20,28},{24,16},{28,20},{32,40},... | collective-permute-start | bytes 32 | tf_op jit(solution)/shard_map/ppermute | solution.py:114
  117.2 4.4 %collective-permute-start.14 = (f32[2]{0:T(128)S(1)}, f32[2]{0:T(128)S(1)}, u32[]{:S(2)}, u32[]{:S(2)}) collective-permute-start(f32[2]{0:T(128)S(1)} %add.99), channel_id=1, source_target_pairs={{0,16},{4,20},{8,24},{12,28},{16,0},{20,4},{24,8},{28,12},{32,48},... | collective-permute-start | bytes 32 | tf_op jit(solution)/shard_map/ppermute | solution.py:114
  121.7 7.4 %collective-permute-start.15 = (f32[2]{0:T(128)S(1)}, f32[2]{0:T(128)S(1)}, u32[]{:S(2)}, u32[]{:S(2)}) collective-permute-start(f32[2]{0:T(128)S(1)} %add.100), channel_id=1, source_target_pairs={{0,32},{4,36},{8,40},{12,44},{16,48},{20,52},{24,56},{28,60},{32,0... | collective-permute-start | bytes 32 | tf_op jit(solution)/shard_map/ppermute | solution.py:114
  129.1 3.5 %collective-permute-start.16 = (f32[2]{0:T(128)S(1)}, f32[2]{0:T(128)S(1)}, u32[]{:S(2)}, u32[]{:S(2)}) collective-permute-start(f32[2]{0:T(128)S(1)} %add.101), channel_id=1, source_target_pairs={{0,64},{4,68},{8,72},{12,76},{16,80},{20,84},{24,88},{28,92},{32,9... | collective-permute-start | bytes 32 | tf_op jit(solution)/shard_map/ppermute | solution.py:114
  132.7 5.0 %collective-permute-start.17 = (f32[2]{0:T(128)S(1)}, f32[2]{0:T(128)S(1)}, u32[]{:S(2)}, u32[]{:S(2)}) collective-permute-start(f32[2]{0:T(128)S(1)} %add.102), channel_id=1, source_target_pairs={{0,128},{4,132},{8,136},{12,140},{16,144},{20,148},{24,152},{28,15... | collective-permute-start | bytes 32 | tf_op jit(solution)/shard_map/ppermute | solution.py:114
  140.4 3.8 %collective-permute-start.18 = (f32[]{:T(128)}, f32[]{:T(128)}, u32[]{:S(2)}, u32[]{:S(2)}) collective-permute-start(f32[]{:T(128)} %multiply_reduce_fusion.1), channel_id=1, source_target_pairs={{0,1},{1,0},{2,3},{3,2},{4,5},{5,4},{6,7},{7,6},{8,9},{9,8},{10,11... | collective-permute-start | bytes 20 | tf_op jit(solution)/shard_map/ppermute | solution.py:114
  145.5 5.2 %collective-permute-start.19 = (f32[]{:T(128)}, f32[]{:T(128)}, u32[]{:S(2)}, u32[]{:S(2)}) collective-permute-start(f32[]{:T(128)} %add.104), channel_id=1, source_target_pairs={{0,2},{1,3},{2,0},{3,1},{4,6},{5,7},{6,4},{7,5},{8,10},{9,11},{10,... | collective-permute-start | bytes 20 | tf_op jit(solution)/shard_map/ppermute | solution.py:114
  151.4 1.3 collective-permute-start.20
  153.3 3.7 %collective-permute-start.21 = (f32[]{:T(128)}, f32[]{:T(128)}, u32[]{:S(2)}, u32[]{:S(2)}) collective-permute-start(f32[]{:T(128)} %add.106), channel_id=1, source_target_pairs={{0,8},{4,12},{8,0},{12,4},{16,24},{20,28},{24,16},{28,20},{32,40},... | collective-permute-start | bytes 20 | tf_op jit(solution)/shard_map/ppermute | solution.py:114
  157.7 4.6 %collective-permute-start.22 = (f32[]{:T(128)}, f32[]{:T(128)}, u32[]{:S(2)}, u32[]{:S(2)}) collective-permute-start(f32[]{:T(128)} %add.107), channel_id=1, source_target_pairs={{0,16},{4,20},{8,24},{12,28},{16,0},{20,4},{24,8},{28,12},{32,48},... | collective-permute-start | bytes 20 | tf_op jit(solution)/shard_map/ppermute | solution.py:114
  163.0 7.6 %collective-permute-start.23 = (f32[]{:T(128)}, f32[]{:T(128)}, u32[]{:S(2)}, u32[]{:S(2)}) collective-permute-start(f32[]{:T(128)} %add.108), channel_id=1, source_target_pairs={{0,32},{4,36},{8,40},{12,44},{16,48},{20,52},{24,56},{28,60},{32,0... | collective-permute-start | bytes 20 | tf_op jit(solution)/shard_map/ppermute | solution.py:114
  171.3 3.7 %collective-permute-start.24 = (f32[]{:T(128)}, f32[]{:T(128)}, u32[]{:S(2)}, u32[]{:S(2)}) collective-permute-start(f32[]{:T(128)} %add.109), channel_id=1, source_target_pairs={{0,64},{4,68},{8,72},{12,76},{16,80},{20,84},{24,88},{28,92},{32,9... | collective-permute-start | bytes 20 | tf_op jit(solution)/shard_map/ppermute | solution.py:114
  175.6 5.2 %collective-permute-start.25 = (f32[]{:T(128)}, f32[]{:T(128)}, u32[]{:S(2)}, u32[]{:S(2)}) collective-permute-start(f32[]{:T(128)} %add.110), channel_id=1, source_target_pairs={{0,128},{4,132},{8,136},{12,140},{16,144},{20,148},{24,152},{28,15... | collective-permute-start | bytes 20 | tf_op jit(solution)/shard_map/ppermute | solution.py:114
  183.2 11.0 %collective-permute-start.28 = (bf16[64,3072]{1,0:T(8,128)(2,1)S(1)}, bf16[64,3072]{1,0:T(8,128)(2,1)S(1)}, u32[]{:S(2)}, u32[]{:S(2)}) collective-permute-start(bf16[64,3072]{1,0:T(8,128)(2,1)S(1)} %get-tuple-element.10), channel_id=1, source_target_pairs={{3,0},{0,1},{1,2},{2,3},{7,4},{4,5},{5,6},{6,7},{11,8},{8,9},{9,10... | collective-permute-start | bytes 1179656 | tf_op jit(solution)/shard_map/ppermute | solution.py:124
  184.1 14.3 %collective-permute-start.27 = (bf16[64,3072]{1,0:T(8,128)(2,1)S(1)}, bf16[64,3072]{1,0:T(8,128)(2,1)S(1)}, u32[]{:S(2)}, u32[]{:S(2)}) collective-permute-start(bf16[64,3072]{1,0:T(8,128)(2,1)S(1)} %get-tuple-element.10), channel_id=1, source_target_pairs={{2,0},{3,1},{0,2},{1,3},{6,4},{7,5},{4,6},{5,7},{10,8},{11,9},{8,1... | collective-permute-start | bytes 1179656 | tf_op jit(solution)/shard_map/ppermute | solution.py:124
  187.0 11.4 %collective-permute-start.26 = (bf16[64,3072]{1,0:T(8,128)(2,1)S(1)}, bf16[64,3072]{1,0:T(8,128)(2,1)S(1)}, u32[]{:S(2)}, u32[]{:S(2)}) collective-permute-start(bf16[64,3072]{1,0:T(8,128)(2,1)S(1)} %get-tuple-element.10), channel_id=1, source_target_pairs={{1,0},{2,1},{3,2},{0,3},{5,4},{6,5},{7,6},{4,7},{9,8},{10,9},{11,1... | collective-permute-start | bytes 1179656 | tf_op jit(solution)/shard_map/ppermute | solution.py:124
  199.4 8.9 %collective-permute-start.29 = (bf16[64,1408]{1,0:T(8,128)(2,1)S(1)}, bf16[64,1408]{1,0:T(8,128)(2,1)S(1)}, u32[]{:S(2)}, u32[]{:S(2)}) collective-permute-start(bf16[64,1408]{1,0:T(8,128)(2,1)S(1)} %get-tuple-element.18), channel_id=1, source_target_pairs={{0,4},{4,8},{8,12},{12,16},{16,20},{20,24},{24,28},{28,32},{32,36}... | collective-permute-start | bytes 540680 | tf_op jit(solution)/shard_map/ppermute | solution.py:101
  201.3 8.8 %collective-permute-start.30 = (bf16[64,1408]{1,0:T(8,128)(2,1)S(1)}, bf16[64,1408]{1,0:T(8,128)(2,1)S(1)}, u32[]{:S(2)}, u32[]{:S(2)}) collective-permute-start(bf16[64,1408]{1,0:T(8,128)(2,1)S(1)} %get-tuple-element.19), channel_id=1, source_target_pairs={{4,0},{8,4},{12,8},{16,12},{20,16},{24,20},{28,24},{32,28},{36,32}... | collective-permute-start | bytes 540680 | tf_op jit(solution)/shard_map/ppermute | solution.py:104
  211.2 9.0 %copy-start.2 = (f32[64,3072]{1,0:T(8,128)S(1)}, f32[64,3072]{1,0:T(8,128)}, u32[]{:S(2)}) copy-start(f32[64,3072]{1,0:T(8,128)} %get-tuple-element.11.p_ref) | copy-start | bytes 2359300
  220.2 42.0 %copy-start.3 = (f32[64,3072]{1,0:T(8,128)S(1)}, f32[64,3072]{1,0:T(8,128)}, u32[]{:S(2)}) copy-start(f32[64,3072]{1,0:T(8,128)} %shard_map.88) | copy-start | bytes 2359300
  222.2 3.6 %collective-permute-start.31 = (f32[]{:T(128)}, f32[]{:T(128)}, u32[]{:S(2)}, u32[]{:S(2)}) collective-permute-start(f32[]{:T(128)} %multiply_reduce_fusion), channel_id=1, source_target_pairs={{0,1},{1,0},{2,3},{3,2},{4,5},{5,4},{6,7},{7,6},{8,9},{9,8},{10,11... | collective-permute-start | bytes 20 | tf_op jit(solution)/shard_map/ppermute | solution.py:114
  227.1 5.1 %collective-permute-start.32 = (f32[]{:T(128)}, f32[]{:T(128)}, u32[]{:S(2)}, u32[]{:S(2)}) collective-permute-start(f32[]{:T(128)} %add.113), channel_id=1, source_target_pairs={{0,2},{1,3},{2,0},{3,1},{4,6},{5,7},{6,4},{7,5},{8,10},{9,11},{10,... | collective-permute-start | bytes 20 | tf_op jit(solution)/shard_map/ppermute | solution.py:114
  232.8 1.4 collective-permute-start.33
  234.8 3.6 %collective-permute-start.34 = (f32[]{:T(128)}, f32[]{:T(128)}, u32[]{:S(2)}, u32[]{:S(2)}) collective-permute-start(f32[]{:T(128)} %add.115), channel_id=1, source_target_pairs={{0,8},{4,12},{8,0},{12,4},{16,24},{20,28},{24,16},{28,20},{32,40},... | collective-permute-start | bytes 20 | tf_op jit(solution)/shard_map/ppermute | solution.py:114
  239.0 4.5 %collective-permute-start.35 = (f32[]{:T(128)}, f32[]{:T(128)}, u32[]{:S(2)}, u32[]{:S(2)}) collective-permute-start(f32[]{:T(128)} %add.116), channel_id=1, source_target_pairs={{0,16},{4,20},{8,24},{12,28},{16,0},{20,4},{24,8},{28,12},{32,48},... | collective-permute-start | bytes 20 | tf_op jit(solution)/shard_map/ppermute | solution.py:114
  244.1 7.5 %collective-permute-start.36 = (f32[]{:T(128)}, f32[]{:T(128)}, u32[]{:S(2)}, u32[]{:S(2)}) collective-permute-start(f32[]{:T(128)} %add.117), channel_id=1, source_target_pairs={{0,32},{4,36},{8,40},{12,44},{16,48},{20,52},{24,56},{28,60},{32,0... | collective-permute-start | bytes 20 | tf_op jit(solution)/shard_map/ppermute | solution.py:114
  252.2 3.6 %collective-permute-start.37 = (f32[]{:T(128)}, f32[]{:T(128)}, u32[]{:S(2)}, u32[]{:S(2)}) collective-permute-start(f32[]{:T(128)} %add.118), channel_id=1, source_target_pairs={{0,64},{4,68},{8,72},{12,76},{16,80},{20,84},{24,88},{28,92},{32,9... | collective-permute-start | bytes 20 | tf_op jit(solution)/shard_map/ppermute | solution.py:114
  256.4 5.1 %collective-permute-start.38 = (f32[]{:T(128)}, f32[]{:T(128)}, u32[]{:S(2)}, u32[]{:S(2)}) collective-permute-start(f32[]{:T(128)} %add.119), channel_id=1, source_target_pairs={{0,128},{4,132},{8,136},{12,140},{16,144},{20,148},{24,152},{28,15... | collective-permute-start | bytes 20 | tf_op jit(solution)/shard_map/ppermute | solution.py:114
  273.7 1.3 copy-start.4

commit v4 on v3

--- a/solution.py
+++ b/solution.py
@@ -135,8 +135,9 @@
     halo = slot_limit - 1
     device_pos = lax.axis_index("samp")
     local_perm = run_perm - device_pos * runs_local
-    sorted_coords = jnp.take(coords, local_perm, axis=1)
-    sorted_loads = jnp.take(loads, local_perm, axis=1)
+    sorted_both = jnp.take(jnp.concatenate([coords, loads], axis=0), local_perm, axis=1)
+    sorted_coords = sorted_both[:dims]
+    sorted_loads = sorted_both[dims:]
     norm_local = jnp.sum(sorted_loads * sorted_loads)
     coreg_perm = jnp.dot(
         coreg_factor, gather_chan(coreg_factor).T, precision=lax.Precision.HIGHEST
@@ -169,6 +170,10 @@
         win_v = widened.reshape(chan_local, window_blocks, block_runs).transpose(1, 0, 2)
         mapped = apply_operator(begin, win_v, tiles, direction, noise_col, 4)
         curvature = jnp.sum(direction * mapped)
+        if iteration + 1 == ITERS:
+            stacked = jnp.concatenate([iterate, remainder, direction, mapped], axis=0)
+            unsorted = jnp.zeros_like(stacked).at[:, local_perm].set(stacked)
+            iterate, remainder, direction, mapped = jnp.split(unsorted, 4, axis=0)
         if iteration == 0:
             sums = global_sum(jnp.stack([norm_local, curvature]))
             norm_now, curvature = sums[0], sums[1]
@@ -181,9 +186,7 @@
             norm_next = global_sum(jnp.sum(remainder * remainder))
             direction = remainder + norm_next / norm_now * direction
             norm_now = norm_next
-    solution = jnp.zeros_like(iterate).at[:, local_perm].set(iterate)
-    residual = jnp.zeros_like(remainder).at[:, local_perm].set(remainder)
-    return (solution, residual)
+    return (iterate, remainder)
 
 
 def solution(mesh):

time: 288 us -> 290 us (level)
  waiting for transfers between devices: 66.7 us -> 81.2 us
  starting transfers between devices: 88.4 us -> 78.9 us
  local copies, waits for them, and re-layouts: 44.3 us -> 38.6 us
    ppermute x9, waiting for transfers between devices: 12.4 us -> 22.2 us  [gather_chan(): parts.append(lax.ppermute(rounded, 'chan', pairs))]
    ppermute x24, starting transfers between devices: 52.1 us -> 43.8 us  [global_sum(): value = value + lax.ppermute(value, axis, pairs)]
    gather x3 -> x2, local copies, waits for them, and re-layouts: 16.7 us -> 9.54 us  [per_device(): jnp.take(jnp.concatenate([coords, loads], axis=0), local_perm, axis=1)]
    ppermute x24, waiting for transfers between devices: 51.3 us -> 56 us  [global_sum(): value = value + lax.ppermute(value, axis, pairs)]
    concatenate x0 -> x2, other arithmetic: none -> 3.46 us  [the longest x1 1.88 us: per_device(): jnp.concatenate([coords, loads], axis=0)]
    unnamed x20 -> x22, local copies, waits for them, and re-layouts: 4.8 us -> 7.51 us
    scatter x2 -> x1, local copies, waits for them, and re-layouts: 17 us -> 14.4 us  [per_device(): unsorted = jnp.zeros_like(stacked).at[:, local_perm].set(stacked)]
  transfers between devices with their start and end apart: 39 -> 39, of which waited for: 29 -> 28; matrix products, arithmetic and copies ran while one was open for 10% -> 14% of each run, Pallas kernels for 11% -> 11%
where the time goes in v4:
time: 290 us; the launch traced here: 287 us
  waiting for transfers between devices  81.2 us (28%)
  starting transfers between devices  78.9 us (27%)
  Pallas kernels  49.8 us (17%)
  local copies, waits for them, and re-layouts  38.6 us (13%)
  other arithmetic  21.7 us (7%)
  between operations  13.7 us (5%)
  matrix products  3.46 us (1%)
    ppermute x24, waiting for transfers between devices, global_sum(): value = value + lax.ppermute(value, axis, pairs)  56 us
    ppermute x24, starting transfers between devices, global_sum(): value = value + lax.ppermute(value, axis, pairs)  43.8 us
    pallas_call x1, Pallas kernels, build_tiles(): pl.pallas_call(kern, grid_spec=pltpu.PrefetchScalarGridSpec(num_scalar_pr...  32.1 us
    ppermute x9, waiting for transfers between devices, gather_chan(): parts.append(lax.ppermute(rounded, 'chan', pairs))  22.2 us
    pallas_call x2, Pallas kernels, apply_operator(): pl.pallas_call(kern, grid_spec=pltpu.PrefetchScalarGridSpec(num_scalar_pr...  17.8 us
    ppermute x3, starting transfers between devices, extended(): lax.ppermute(lax.slice_in_dim(block, 0, width, axis=dim), axis, backward)  17.3 us
    scatter x1, local copies, waits for them, and re-layouts, per_device(): unsorted = jnp.zeros_like(stacked).at[:, local_perm].set(stacked)  14.4 us
    ppermute x9, starting transfers between devices, gather_chan(): parts.append(lax.ppermute(rounded, 'chan', pairs))  12.1 us
  transfers between devices with their start and end apart: 39, of which 28 were waited for; matrix products, arithmetic and copies ran while one was open for 14% of the time, Pallas kernels for 11%

profile of v4, /device:TPU:2, one launch (start us, length us, event | category | flops | bytes accessed | tf_op | source)
XLA Modules:
  0.0 287.3 jit_solution(6417782648891981186)
XLA Ops:
  0.6 3.3 %collective-permute-start.1 = (f32[64,256]{1,0:T(8,128)}, f32[64,256]{1,0:T(8,128)S(1)}, u32[]{:S(2)}, u32[]{:S(2)}) collective-permute-start(f32[64,256]{1,0:T(8,128)} %param.9), channel_id=1, source_target_pairs={{2,0},{3,1},{0,2},{1,3},{6,4},{7,5},{4,6},{5,7},{10,8},{11,9},{8,1... | collective-permute-start | bytes 196616 | tf_op jit(solution)/shard_map/ppermute | solution.py:124
  9.0 1.9 pad_maximum_fusion
  10.9 8.1 %gather_fusion = f32[3072,70]{1,0:T(8,128)S(1)} fusion(f32[70,3072]{0,1:T(8,128)S(1)} %pad_maximum_fusion, s32[3072]{0:T(1024)S(1)} %broadcast_clamp_fusion), kind=kCustom, calls=%fused_computation | custom fusion | bytes 1732608 | tf_op jit(solution)/shard_map/jit(_take)/gather | solution.py:138
  23.6 2.5 collective-permute-start.3
  30.9 1.9 collective-permute-start.8
  32.8 10.4 %collective-permute-done.2 = f32[64,256]{1,0:T(8,128)S(1)} collective-permute-done((f32[64,256]{1,0:T(8,128)S(1)}, f32[64,256]{1,0:T(8,128)S(1)}, u32[]{:S(2)}, u32[]{:S(2)}) %collective-permute-start.2) | collective-permute-done | bytes 65568 | tf_op jit(solution)/shard_map/ppermute | solution.py:124
  43.2 5.8 %collective-permute-start.9 = (f32[6,1408]{1,0:T(8,128)S(1)}, f32[6,1408]{1,0:T(8,128)S(1)}, u32[]{:S(2)}, u32[]{:S(2)}) collective-permute-start(f32[6,1408]{1,0:T(8,128)S(1)} %get-tuple-element.18), channel_id=1, source_target_pairs={{4,0},{8,4},{12,8},{16,12},{20,16},{24,20},{28,24},{32,28},{36,32}... | collective-permute-start | bytes 101384 | tf_op jit(solution)/shard_map/ppermute | solution.py:104
  49.4 2.2 convolution_convert_fusion.1
  51.6 1.9 collective-permute-start.6
  53.5 5.8 %collective-permute-start.7 = (bf16[64,1408]{1,0:T(8,128)(2,1)S(1)}, bf16[64,1408]{1,0:T(8,128)(2,1)S(1)}, u32[]{:S(2)}, u32[]{:S(2)}) collective-permute-start(bf16[64,1408]{1,0:T(8,128)(2,1)S(1)} %get-tuple-element.22), channel_id=1, source_target_pairs={{4,0},{8,4},{12,8},{16,12},{20,16},{24,20},{28,24},{32,28},{36,32}... | collective-permute-start | bytes 540680 | tf_op jit(solution)/shard_map/ppermute | solution.py:104
  60.0 32.1 %shard_map.86.tile_ref = bf16[24,128,1536]{2,1,0:T(8,128)(2,1)} custom-call(s32[24]{0:T(128)} %clamp_bitcast_fusion.begin_ref, s32[24]{0:T(128)} %count_ref.1, f32[24,128,8]{2,1,0:T(8,128)} %pad_bitcast_fusion.own_ref, f32[46,8,128]{2,1,0:T(8,128)} %pad_bitcast_fusion.1.win_ref), custom_call_target="tpu_custom_call" | custom-call | tf_op jit(solution)/shard_map/pallas_call | solution.py:46
  93.2 8.8 %shard_map.87 = f32[64,3072]{1,0:T(8,128)} custom-call(s32[24]{0:T(128)} %clamp_bitcast_fusion.begin_ref, bf16[46,64,128]{2,1,0:T(8,128)(2,1)} %bitcast_bitcast_fusion.1.win_ref, bf16[24,128,1536]{2,1,0:T(8,128)(2,1)} %shard_map.86.tile_ref, f32[64,3072]{1,0:T(8,128)} %slice.48.p_ref, f32[64,1]{1,0:T(8,128)} %copy.25.noise_ref), custom_call_target="tpu_custom_call" | custom-call | tf_op jit(solution)/shard_map/pallas_call | solution.py:80
  102.0 2.0 multiply_reduce_fusion.3
  105.4 3.5 %collective-permute-done.10 = f32[2]{0:T(128)S(1)} collective-permute-done((f32[2]{0:T(128)S(1)}, f32[2]{0:T(128)S(1)}, u32[]{:S(2)}, u32[]{:S(2)}) %collective-permute-start.10) | collective-permute-done | bytes 40 | tf_op jit(solution)/shard_map/ppermute | solution.py:114
  110.3 5.0 %collective-permute-done.11 = f32[2]{0:T(128)S(1)} collective-permute-done((f32[2]{0:T(128)S(1)}, f32[2]{0:T(128)S(1)}, u32[]{:S(2)}, u32[]{:S(2)}) %collective-permute-start.11) | collective-permute-done | bytes 40 | tf_op jit(solution)/shard_map/ppermute | solution.py:114
  117.8 3.5 %collective-permute-done.13 = f32[2]{0:T(128)S(1)} collective-permute-done((f32[2]{0:T(128)S(1)}, f32[2]{0:T(128)S(1)}, u32[]{:S(2)}, u32[]{:S(2)}) %collective-permute-start.13) | collective-permute-done | bytes 40 | tf_op jit(solution)/shard_map/ppermute | solution.py:114
  121.4 4.4 %collective-permute-done.14 = f32[2]{0:T(128)S(1)} collective-permute-done((f32[2]{0:T(128)S(1)}, f32[2]{0:T(128)S(1)}, u32[]{:S(2)}, u32[]{:S(2)}) %collective-permute-start.14) | collective-permute-done | bytes 40 | tf_op jit(solution)/shard_map/ppermute | solution.py:114
  125.8 3.7 %collective-permute-start.15 = (f32[2]{0:T(128)S(1)}, f32[2]{0:T(128)S(1)}, u32[]{:S(2)}, u32[]{:S(2)}) collective-permute-start(f32[2]{0:T(128)S(1)} %add.99), channel_id=1, source_target_pairs={{0,32},{4,36},{8,40},{12,44},{16,48},{20,52},{24,56},{28,60},{32,0... | collective-permute-start | bytes 32 | tf_op jit(solution)/shard_map/ppermute | solution.py:114
  129.5 3.7 %collective-permute-done.15 = f32[2]{0:T(128)S(1)} collective-permute-done((f32[2]{0:T(128)S(1)}, f32[2]{0:T(128)S(1)}, u32[]{:S(2)}, u32[]{:S(2)}) %collective-permute-start.15) | collective-permute-done | bytes 40 | tf_op jit(solution)/shard_map/ppermute | solution.py:114
  133.6 3.2 %collective-permute-done.16 = f32[2]{0:T(128)S(1)} collective-permute-done((f32[2]{0:T(128)S(1)}, f32[2]{0:T(128)S(1)}, u32[]{:S(2)}, u32[]{:S(2)}) %collective-permute-start.16) | collective-permute-done | bytes 40 | tf_op jit(solution)/shard_map/ppermute | solution.py:114
  136.8 2.1 collective-permute-start.17
  138.9 2.9 %collective-permute-done.17 = f32[2]{0:T(128)S(1)} collective-permute-done((f32[2]{0:T(128)S(1)}, f32[2]{0:T(128)S(1)}, u32[]{:S(2)}, u32[]{:S(2)}) %collective-permute-start.17) | collective-permute-done | bytes 40 | tf_op jit(solution)/shard_map/ppermute | solution.py:114
  144.6 3.8 %collective-permute-done.18 = f32[]{:T(128)} collective-permute-done((f32[]{:T(128)}, f32[]{:T(128)}, u32[]{:S(2)}, u32[]{:S(2)}) %collective-permute-start.18) | collective-permute-done | bytes 36 | tf_op jit(solution)/shard_map/ppermute | solution.py:114
  150.9 3.8 %collective-permute-done.19 = f32[]{:T(128)} collective-permute-done((f32[]{:T(128)}, f32[]{:T(128)}, u32[]{:S(2)}, u32[]{:S(2)}) %collective-permute-start.19) | collective-permute-done | bytes 36 | tf_op jit(solution)/shard_map/ppermute | solution.py:114
  158.6 2.3 collective-permute-done.21
  162.9 3.2 %collective-permute-done.22 = f32[]{:T(128)} collective-permute-done((f32[]{:T(128)}, f32[]{:T(128)}, u32[]{:S(2)}, u32[]{:S(2)}) %collective-permute-start.22) | collective-permute-done | bytes 36 | tf_op jit(solution)/shard_map/ppermute | solution.py:114
  166.7 5.7 %collective-permute-start.23 = (f32[]{:T(128)}, f32[]{:T(128)}, u32[]{:S(2)}, u32[]{:S(2)}) collective-permute-start(f32[]{:T(128)} %add.107), channel_id=1, source_target_pairs={{0,32},{4,36},{8,40},{12,44},{16,48},{20,52},{24,56},{28,60},{32,0... | collective-permute-start | bytes 20 | tf_op jit(solution)/shard_map/ppermute | solution.py:114
  172.4 2.0 collective-permute-done.23
  174.9 1.9 collective-permute-start.24
  176.8 1.8 collective-permute-done.24
  179.2 3.5 %collective-permute-start.25 = (f32[]{:T(128)}, f32[]{:T(128)}, u32[]{:S(2)}, u32[]{:S(2)}) collective-permute-start(f32[]{:T(128)} %add.109), channel_id=1, source_target_pairs={{0,128},{4,132},{8,136},{12,140},{16,144},{20,148},{24,152},{28,15... | collective-permute-start | bytes 20 | tf_op jit(solution)/shard_map/ppermute | solution.py:114
  188.1 2.1 collective-permute-start.26
  190.2 11.1 %collective-permute-done.28 = bf16[64,3072]{1,0:T(8,128)(2,1)S(1)} collective-permute-done((bf16[64,3072]{1,0:T(8,128)(2,1)S(1)}, bf16[64,3072]{1,0:T(8,128)(2,1)S(1)}, u32[]{:S(2)}, u32[]{:S(2)}) %collective-permute-start.28) | collective-permute-done | bytes 393248 | tf_op jit(solution)/shard_map/ppermute | solution.py:124
  203.0 1.9 collective-permute-start.29
  204.9 5.8 %collective-permute-start.30 = (bf16[64,1408]{1,0:T(8,128)(2,1)S(1)}, bf16[64,1408]{1,0:T(8,128)(2,1)S(1)}, u32[]{:S(2)}, u32[]{:S(2)}) collective-permute-start(bf16[64,1408]{1,0:T(8,128)(2,1)S(1)} %get-tuple-element.20), channel_id=1, source_target_pairs={{4,0},{8,4},{12,8},{16,12},{20,16},{24,20},{28,24},{32,28},{36,32}... | collective-permute-start | bytes 540680 | tf_op jit(solution)/shard_map/ppermute | solution.py:104
  214.7 9.0 %shard_map.88 = f32[64,3072]{1,0:T(8,128)} custom-call(s32[24]{0:T(128)} %clamp_bitcast_fusion.begin_ref, bf16[46,64,128]{2,1,0:T(8,128)(2,1)} %bitcast_bitcast_fusion.win_ref, bf16[24,128,1536]{2,1,0:T(8,128)(2,1)} %shard_map.86.tile_ref, f32[64,3072]{1,0:T(8,128)} %get-tuple-element.9.p_ref, f32[64,1]{1,0:T(8,128)} %copy.25.noise_ref), custom_call_target="tpu_custom_call" | custom-call | tf_op jit(solution)/shard_map/pallas_call | solution.py:80
  223.7 2.1 multiply_reduce_fusion
  227.4 2.3 copy.28
  229.9 14.4 %scatter_custom_fusion = f32[256,3072]{0,1:T(8,128)S(1)} fusion(s32[3072]{0:T(1024)S(1)} %get-tuple-element.13, f32[3072,256]{1,0:T(8,128)} %copy.28, f32[]{:T(128)} %constant.10.clone.1), kind=kCustom, calls=%fused_computation.25 | custom fusion | bytes 3146240 | tf_op jit(solution)/shard_map/scatter | solution.py:175
  245.5 5.0 %collective-permute-start.32 = (f32[]{:T(128)}, f32[]{:T(128)}, u32[]{:S(2)}, u32[]{:S(2)}) collective-permute-start(f32[]{:T(128)} %add.112), channel_id=1, source_target_pairs={{0,2},{1,3},{2,0},{3,1},{4,6},{5,7},{6,4},{7,5},{8,10},{9,11},{10,... | collective-permute-start | bytes 20 | tf_op jit(solution)/shard_map/ppermute | solution.py:114
  254.5 2.2 collective-permute-done.34
  257.3 3.2 %collective-permute-start.35 = (f32[]{:T(128)}, f32[]{:T(128)}, u32[]{:S(2)}, u32[]{:S(2)}) collective-permute-start(f32[]{:T(128)} %add.115), channel_id=1, source_target_pairs={{0,16},{4,20},{8,24},{12,28},{16,0},{20,4},{24,8},{28,12},{32,48},... | collective-permute-start | bytes 20 | tf_op jit(solution)/shard_map/ppermute | solution.py:114
  262.4 5.1 %collective-permute-start.36 = (f32[]{:T(128)}, f32[]{:T(128)}, u32[]{:S(2)}, u32[]{:S(2)}) collective-permute-start(f32[]{:T(128)} %add.116), channel_id=1, source_target_pairs={{0,32},{4,36},{8,40},{12,44},{16,48},{20,52},{24,56},{28,60},{32,0... | collective-permute-start | bytes 20 | tf_op jit(solution)/shard_map/ppermute | solution.py:114
  267.5 2.4 collective-permute-done.36
  270.6 2.0 collective-permute-start.37
  274.8 3.5 %collective-permute-start.38 = (f32[]{:T(128)}, f32[]{:T(128)}, u32[]{:S(2)}, u32[]{:S(2)}) collective-permute-start(f32[]{:T(128)} %add.118), channel_id=1, source_target_pairs={{0,128},{4,132},{8,136},{12,140},{16,144},{20,148},{24,152},{28,15... | collective-permute-start | bytes 20 | tf_op jit(solution)/shard_map/ppermute | solution.py:114
  280.5 2.6 fusion
  283.1 2.9 copy.30
  (96 shorter events, 49.4 us)
Async XLA Ops:
  0.6 6.7 %copy-start.6 = (f32[6,3072]{1,0:T(8,128)S(1)}, f32[6,3072]{1,0:T(8,128)}, u32[]{:S(2)}) copy-start(f32[6,3072]{1,0:T(8,128)} %param.8) | copy-start | bytes 221188
  0.6 27.2 %collective-permute-start.1 = (f32[64,256]{1,0:T(8,128)}, f32[64,256]{1,0:T(8,128)S(1)}, u32[]{:S(2)}, u32[]{:S(2)}) collective-permute-start(f32[64,256]{1,0:T(8,128)} %param.9), channel_id=1, source_target_pairs={{2,0},{3,1},{0,2},{1,3},{6,4},{7,5},{4,6},{5,7},{10,8},{11,9},{8,1... | collective-permute-start | bytes 196616 | tf_op jit(solution)/shard_map/ppermute | solution.py:124
  3.9 27.0 %collective-permute-start = (f32[64,256]{1,0:T(8,128)}, f32[64,256]{1,0:T(8,128)S(1)}, u32[]{:S(2)}, u32[]{:S(2)}) collective-permute-start(f32[64,256]{1,0:T(8,128)} %param.9), channel_id=1, source_target_pairs={{1,0},{2,1},{3,2},{0,3},{5,4},{6,5},{7,6},{4,7},{9,8},{10,9},{11,1... | collective-permute-start | bytes 196616 | tf_op jit(solution)/shard_map/ppermute | solution.py:124
  21.7 6.2 %copy-start.8 = (f32[64,256]{1,0:T(8,128)S(1)}, f32[64,256]{1,0:T(8,128)}, u32[]{:S(2)}) copy-start(f32[64,256]{1,0:T(8,128)} %param.9) | copy-start | bytes 196612
  21.8 27.6 %collective-permute-start.5 = (bf16[64,3072]{1,0:T(8,128)(2,1)S(1)}, bf16[64,3072]{1,0:T(8,128)(2,1)}, u32[]{:S(2)}, u32[]{:S(2)}) collective-permute-start(bf16[64,3072]{1,0:T(8,128)(2,1)S(1)} %slice.63), channel_id=1, source_target_pairs={{3,0},{0,1},{1,2},{2,3},{7,4},{4,5},{5,6},{6,7},{11,8},{8,9},{9,10... | collective-permute-start | bytes 1179656 | tf_op jit(solution)/shard_map/ppermute | solution.py:124
  22.8 26.5 %collective-permute-start.4 = (bf16[64,3072]{1,0:T(8,128)(2,1)S(1)}, bf16[64,3072]{1,0:T(8,128)(2,1)}, u32[]{:S(2)}, u32[]{:S(2)}) collective-permute-start(bf16[64,3072]{1,0:T(8,128)(2,1)S(1)} %slice.63), channel_id=1, source_target_pairs={{2,0},{3,1},{0,2},{1,3},{6,4},{7,5},{4,6},{5,7},{10,8},{11,9},{8,1... | collective-permute-start | bytes 1179656 | tf_op jit(solution)/shard_map/ppermute | solution.py:124
  23.6 25.7 %collective-permute-start.3 = (bf16[64,3072]{1,0:T(8,128)(2,1)S(1)}, bf16[64,3072]{1,0:T(8,128)(2,1)}, u32[]{:S(2)}, u32[]{:S(2)}) collective-permute-start(bf16[64,3072]{1,0:T(8,128)(2,1)S(1)} %slice.63), channel_id=1, source_target_pairs={{1,0},{2,1},{3,2},{0,3},{5,4},{6,5},{7,6},{4,7},{9,8},{10,9},{11,1... | collective-permute-start | bytes 1179656 | tf_op jit(solution)/shard_map/ppermute | solution.py:124
  27.9 15.3 %collective-permute-start.2 = (f32[64,256]{1,0:T(8,128)S(1)}, f32[64,256]{1,0:T(8,128)S(1)}, u32[]{:S(2)}, u32[]{:S(2)}) collective-permute-start(f32[64,256]{1,0:T(8,128)S(1)} %copy-done.8), channel_id=1, source_target_pairs={{3,0},{0,1},{1,2},{2,3},{7,4},{4,5},{5,6},{6,7},{11,8},{8,9},{9,10... | collective-permute-start | bytes 196616 | tf_op jit(solution)/shard_map/ppermute | solution.py:124
  29.2 0.9 copy-start.7
  30.9 28.4 %collective-permute-start.8 = (f32[6,1408]{1,0:T(8,128)S(1)}, f32[6,1408]{1,0:T(8,128)S(1)}, u32[]{:S(2)}, u32[]{:S(2)}) collective-permute-start(f32[6,1408]{1,0:T(8,128)S(1)} %get-tuple-element.17), channel_id=1, source_target_pairs={{0,4},{4,8},{8,12},{12,16},{16,20},{20,24},{24,28},{28,32},{32,36}... | collective-permute-start | bytes 101384 | tf_op jit(solution)/shard_map/ppermute | solution.py:101
  43.2 16.1 %collective-permute-start.9 = (f32[6,1408]{1,0:T(8,128)S(1)}, f32[6,1408]{1,0:T(8,128)S(1)}, u32[]{:S(2)}, u32[]{:S(2)}) collective-permute-start(f32[6,1408]{1,0:T(8,128)S(1)} %get-tuple-element.18), channel_id=1, source_target_pairs={{4,0},{8,4},{12,8},{16,12},{20,16},{24,20},{28,24},{32,28},{36,32}... | collective-permute-start | bytes 101384 | tf_op jit(solution)/shard_map/ppermute | solution.py:104
  51.6 40.5 %collective-permute-start.6 = (bf16[64,1408]{1,0:T(8,128)(2,1)S(1)}, bf16[64,1408]{1,0:T(8,128)(2,1)S(1)}, u32[]{:S(2)}, u32[]{:S(2)}) collective-permute-start(bf16[64,1408]{1,0:T(8,128)(2,1)S(1)} %get-tuple-element.21), channel_id=1, source_target_pairs={{0,4},{4,8},{8,12},{12,16},{16,20},{20,24},{24,28},{28,32},{32,36}... | collective-permute-start | bytes 540680 | tf_op jit(solution)/shard_map/ppermute | solution.py:101
  53.5 38.6 %collective-permute-start.7 = (bf16[64,1408]{1,0:T(8,128)(2,1)S(1)}, bf16[64,1408]{1,0:T(8,128)(2,1)S(1)}, u32[]{:S(2)}, u32[]{:S(2)}) collective-permute-start(bf16[64,1408]{1,0:T(8,128)(2,1)S(1)} %get-tuple-element.22), channel_id=1, source_target_pairs={{4,0},{8,4},{12,8},{16,12},{20,16},{24,20},{28,24},{32,28},{36,32}... | collective-permute-start | bytes 540680 | tf_op jit(solution)/shard_map/ppermute | solution.py:104
  102.0 41.8 %copy-start.3 = (f32[64,3072]{1,0:T(8,128)S(1)}, f32[64,3072]{1,0:T(8,128)}, u32[]{:S(2)}) copy-start(f32[64,3072]{1,0:T(8,128)} %shard_map.87) | copy-start | bytes 2359300
  105.4 3.6 %collective-permute-start.10 = (f32[2]{0:T(128)S(1)}, f32[2]{0:T(128)S(1)}, u32[]{:S(2)}, u32[]{:S(2)}) collective-permute-start(f32[2]{0:T(128)S(1)} %pad_maximum_fusion.1), channel_id=1, source_target_pairs={{0,1},{1,0},{2,3},{3,2},{4,5},{5,4},{6,7},{7,6},{8,9},{9,8},{10,11... | collective-permute-start | bytes 32 | tf_op jit(solution)/shard_map/ppermute | solution.py:114
  110.3 5.1 %collective-permute-start.11 = (f32[2]{0:T(128)S(1)}, f32[2]{0:T(128)S(1)}, u32[]{:S(2)}, u32[]{:S(2)}) collective-permute-start(f32[2]{0:T(128)S(1)} %fusion.37), channel_id=1, source_target_pairs={{0,2},{1,3},{2,0},{3,1},{4,6},{5,7},{6,4},{7,5},{8,10},{9,11},{10,... | collective-permute-start | bytes 32 | tf_op jit(solution)/shard_map/ppermute | solution.py:114
  116.7 1.1 collective-permute-start.12
  117.8 3.5 %collective-permute-start.13 = (f32[2]{0:T(128)S(1)}, f32[2]{0:T(128)S(1)}, u32[]{:S(2)}, u32[]{:S(2)}) collective-permute-start(f32[2]{0:T(128)S(1)} %add.97), channel_id=1, source_target_pairs={{0,8},{4,12},{8,0},{12,4},{16,24},{20,28},{24,16},{28,20},{32,40},... | collective-permute-start | bytes 32 | tf_op jit(solution)/shard_map/ppermute | solution.py:114
  121.4 4.4 %collective-permute-start.14 = (f32[2]{0:T(128)S(1)}, f32[2]{0:T(128)S(1)}, u32[]{:S(2)}, u32[]{:S(2)}) collective-permute-start(f32[2]{0:T(128)S(1)} %add.98), channel_id=1, source_target_pairs={{0,16},{4,20},{8,24},{12,28},{16,0},{20,4},{24,8},{28,12},{32,48},... | collective-permute-start | bytes 32 | tf_op jit(solution)/shard_map/ppermute | solution.py:114
  125.8 7.4 %collective-permute-start.15 = (f32[2]{0:T(128)S(1)}, f32[2]{0:T(128)S(1)}, u32[]{:S(2)}, u32[]{:S(2)}) collective-permute-start(f32[2]{0:T(128)S(1)} %add.99), channel_id=1, source_target_pairs={{0,32},{4,36},{8,40},{12,44},{16,48},{20,52},{24,56},{28,60},{32,0... | collective-permute-start | bytes 32 | tf_op jit(solution)/shard_map/ppermute | solution.py:114
  133.3 3.5 %collective-permute-start.16 = (f32[2]{0:T(128)S(1)}, f32[2]{0:T(128)S(1)}, u32[]{:S(2)}, u32[]{:S(2)}) collective-permute-start(f32[2]{0:T(128)S(1)} %add.100), channel_id=1, source_target_pairs={{0,64},{4,68},{8,72},{12,76},{16,80},{20,84},{24,88},{28,92},{32,9... | collective-permute-start | bytes 32 | tf_op jit(solution)/shard_map/ppermute | solution.py:114
  136.8 5.0 %collective-permute-start.17 = (f32[2]{0:T(128)S(1)}, f32[2]{0:T(128)S(1)}, u32[]{:S(2)}, u32[]{:S(2)}) collective-permute-start(f32[2]{0:T(128)S(1)} %add.101), channel_id=1, source_target_pairs={{0,128},{4,132},{8,136},{12,140},{16,144},{20,148},{24,152},{28,15... | collective-permute-start | bytes 32 | tf_op jit(solution)/shard_map/ppermute | solution.py:114
  144.6 58.4 %copy-start.4 = (f32[64,3072]{1,0:T(8,128)}, f32[64,3072]{1,0:T(8,128)S(1)}, u32[]{:S(2)}) copy-start(f32[64,3072]{1,0:T(8,128)S(1)} %get-tuple-element.11) | copy-start | bytes 2359300
  144.6 3.8 %collective-permute-start.18 = (f32[]{:T(128)}, f32[]{:T(128)}, u32[]{:S(2)}, u32[]{:S(2)}) collective-permute-start(f32[]{:T(128)} %get-tuple-element.10), channel_id=1, source_target_pairs={{0,1},{1,0},{2,3},{3,2},{4,5},{5,4},{6,7},{7,6},{8,9},{9,8},{10,11... | collective-permute-start | bytes 20 | tf_op jit(solution)/shard_map/ppermute | solution.py:114
  149.5 5.2 %collective-permute-start.19 = (f32[]{:T(128)}, f32[]{:T(128)}, u32[]{:S(2)}, u32[]{:S(2)}) collective-permute-start(f32[]{:T(128)} %add.103), channel_id=1, source_target_pairs={{0,2},{1,3},{2,0},{3,1},{4,6},{5,7},{6,4},{7,5},{8,10},{9,11},{10,... | collective-permute-start | bytes 20 | tf_op jit(solution)/shard_map/ppermute | solution.py:114
  155.3 1.3 collective-permute-start.20
  157.2 3.7 %collective-permute-start.21 = (f32[]{:T(128)}, f32[]{:T(128)}, u32[]{:S(2)}, u32[]{:S(2)}) collective-permute-start(f32[]{:T(128)} %add.105), channel_id=1, source_target_pairs={{0,8},{4,12},{8,0},{12,4},{16,24},{20,28},{24,16},{28,20},{32,40},... | collective-permute-start | bytes 20 | tf_op jit(solution)/shard_map/ppermute | solution.py:114
  161.5 4.6 %collective-permute-start.22 = (f32[]{:T(128)}, f32[]{:T(128)}, u32[]{:S(2)}, u32[]{:S(2)}) collective-permute-start(f32[]{:T(128)} %add.106), channel_id=1, source_target_pairs={{0,16},{4,20},{8,24},{12,28},{16,0},{20,4},{24,8},{28,12},{32,48},... | collective-permute-start | bytes 20 | tf_op jit(solution)/shard_map/ppermute | solution.py:114
  166.7 7.6 %collective-permute-start.23 = (f32[]{:T(128)}, f32[]{:T(128)}, u32[]{:S(2)}, u32[]{:S(2)}) collective-permute-start(f32[]{:T(128)} %add.107), channel_id=1, source_target_pairs={{0,32},{4,36},{8,40},{12,44},{16,48},{20,52},{24,56},{28,60},{32,0... | collective-permute-start | bytes 20 | tf_op jit(solution)/shard_map/ppermute | solution.py:114
  174.9 3.7 %collective-permute-start.24 = (f32[]{:T(128)}, f32[]{:T(128)}, u32[]{:S(2)}, u32[]{:S(2)}) collective-permute-start(f32[]{:T(128)} %add.108), channel_id=1, source_target_pairs={{0,64},{4,68},{8,72},{12,76},{16,80},{20,84},{24,88},{28,92},{32,9... | collective-permute-start | bytes 20 | tf_op jit(solution)/shard_map/ppermute | solution.py:114
  179.2 5.2 %collective-permute-start.25 = (f32[]{:T(128)}, f32[]{:T(128)}, u32[]{:S(2)}, u32[]{:S(2)}) collective-permute-start(f32[]{:T(128)} %add.109), channel_id=1, source_target_pairs={{0,128},{4,132},{8,136},{12,140},{16,144},{20,148},{24,152},{28,15... | collective-permute-start | bytes 20 | tf_op jit(solution)/shard_map/ppermute | solution.py:114
  187.0 14.4 %collective-permute-start.28 = (bf16[64,3072]{1,0:T(8,128)(2,1)S(1)}, bf16[64,3072]{1,0:T(8,128)(2,1)S(1)}, u32[]{:S(2)}, u32[]{:S(2)}) collective-permute-start(bf16[64,3072]{1,0:T(8,128)(2,1)S(1)} %get-tuple-element.8), channel_id=1, source_target_pairs={{3,0},{0,1},{1,2},{2,3},{7,4},{4,5},{5,6},{6,7},{11,8},{8,9},{9,10... | collective-permute-start | bytes 1179656 | tf_op jit(solution)/shard_map/ppermute | solution.py:124
  187.0 14.4 %collective-permute-start.27 = (bf16[64,3072]{1,0:T(8,128)(2,1)S(1)}, bf16[64,3072]{1,0:T(8,128)(2,1)S(1)}, u32[]{:S(2)}, u32[]{:S(2)}) collective-permute-start(bf16[64,3072]{1,0:T(8,128)(2,1)S(1)} %get-tuple-element.8), channel_id=1, source_target_pairs={{2,0},{3,1},{0,2},{1,3},{6,4},{7,5},{4,6},{5,7},{10,8},{11,9},{8,1... | collective-permute-start | bytes 1179656 | tf_op jit(solution)/shard_map/ppermute | solution.py:124
  188.1 13.9 %collective-permute-start.26 = (bf16[64,3072]{1,0:T(8,128)(2,1)S(1)}, bf16[64,3072]{1,0:T(8,128)(2,1)S(1)}, u32[]{:S(2)}, u32[]{:S(2)}) collective-permute-start(bf16[64,3072]{1,0:T(8,128)(2,1)S(1)} %get-tuple-element.8), channel_id=1, source_target_pairs={{1,0},{2,1},{3,2},{0,3},{5,4},{6,5},{7,6},{4,7},{9,8},{10,9},{11,1... | collective-permute-start | bytes 1179656 | tf_op jit(solution)/shard_map/ppermute | solution.py:124
  203.0 8.9 %collective-permute-start.29 = (bf16[64,1408]{1,0:T(8,128)(2,1)S(1)}, bf16[64,1408]{1,0:T(8,128)(2,1)S(1)}, u32[]{:S(2)}, u32[]{:S(2)}) collective-permute-start(bf16[64,1408]{1,0:T(8,128)(2,1)S(1)} %get-tuple-element.19), channel_id=1, source_target_pairs={{0,4},{4,8},{8,12},{12,16},{16,20},{20,24},{24,28},{28,32},{32,36}... | collective-permute-start | bytes 540680 | tf_op jit(solution)/shard_map/ppermute | solution.py:101
  204.9 8.8 %collective-permute-start.30 = (bf16[64,1408]{1,0:T(8,128)(2,1)S(1)}, bf16[64,1408]{1,0:T(8,128)(2,1)S(1)}, u32[]{:S(2)}, u32[]{:S(2)}) collective-permute-start(bf16[64,1408]{1,0:T(8,128)(2,1)S(1)} %get-tuple-element.20), channel_id=1, source_target_pairs={{4,0},{8,4},{12,8},{16,12},{20,16},{24,20},{28,24},{32,28},{36,32}... | collective-permute-start | bytes 540680 | tf_op jit(solution)/shard_map/ppermute | solution.py:104
  214.7 9.0 %copy-start = (f32[64,3072]{1,0:T(8,128)S(1)}, f32[64,3072]{1,0:T(8,128)}, u32[]{:S(2)}) copy-start(f32[64,3072]{1,0:T(8,128)} %get-tuple-element.9.p_ref) | copy-start | bytes 2359300
  223.7 2.1 copy-start.1
  223.7 2.1 copy-start.2
  229.7 14.6 %collective-permute-start.31 = (f32[]{:T(128)}, f32[]{:T(128)}, u32[]{:S(2)}, u32[]{:S(2)}) collective-permute-start(f32[]{:T(128)} %multiply_reduce_fusion), channel_id=1, source_target_pairs={{0,1},{1,0},{2,3},{3,2},{4,5},{5,4},{6,7},{7,6},{8,9},{9,8},{10,11... | collective-permute-start | bytes 20 | tf_op jit(solution)/shard_map/ppermute | solution.py:114
  245.5 5.1 %collective-permute-start.32 = (f32[]{:T(128)}, f32[]{:T(128)}, u32[]{:S(2)}, u32[]{:S(2)}) collective-permute-start(f32[]{:T(128)} %add.112), channel_id=1, source_target_pairs={{0,2},{1,3},{2,0},{3,1},{4,6},{5,7},{6,4},{7,5},{8,10},{9,11},{10,... | collective-permute-start | bytes 20 | tf_op jit(solution)/shard_map/ppermute | solution.py:114
  251.3 1.2 collective-permute-start.33
  253.1 3.6 %collective-permute-start.34 = (f32[]{:T(128)}, f32[]{:T(128)}, u32[]{:S(2)}, u32[]{:S(2)}) collective-permute-start(f32[]{:T(128)} %add.114), channel_id=1, source_target_pairs={{0,8},{4,12},{8,0},{12,4},{16,24},{20,28},{24,16},{28,20},{32,40},... | collective-permute-start | bytes 20 | tf_op jit(solution)/shard_map/ppermute | solution.py:114
  257.3 4.5 %collective-permute-start.35 = (f32[]{:T(128)}, f32[]{:T(128)}, u32[]{:S(2)}, u32[]{:S(2)}) collective-permute-start(f32[]{:T(128)} %add.115), channel_id=1, source_target_pairs={{0,16},{4,20},{8,24},{12,28},{16,0},{20,4},{24,8},{28,12},{32,48},... | collective-permute-start | bytes 20 | tf_op jit(solution)/shard_map/ppermute | solution.py:114
  262.4 7.5 %collective-permute-start.36 = (f32[]{:T(128)}, f32[]{:T(128)}, u32[]{:S(2)}, u32[]{:S(2)}) collective-permute-start(f32[]{:T(128)} %add.116), channel_id=1, source_target_pairs={{0,32},{4,36},{8,40},{12,44},{16,48},{20,52},{24,56},{28,60},{32,0... | collective-permute-start | bytes 20 | tf_op jit(solution)/shard_map/ppermute | solution.py:114
  270.6 3.6 %collective-permute-start.37 = (f32[]{:T(128)}, f32[]{:T(128)}, u32[]{:S(2)}, u32[]{:S(2)}) collective-permute-start(f32[]{:T(128)} %add.117), channel_id=1, source_target_pairs={{0,64},{4,68},{8,72},{12,76},{16,80},{20,84},{24,88},{28,92},{32,9... | collective-permute-start | bytes 20 | tf_op jit(solution)/shard_map/ppermute | solution.py:114
  274.8 5.1 %collective-permute-start.38 = (f32[]{:T(128)}, f32[]{:T(128)}, u32[]{:S(2)}, u32[]{:S(2)}) collective-permute-start(f32[]{:T(128)} %add.118), channel_id=1, source_target_pairs={{0,128},{4,132},{8,136},{12,140},{16,144},{20,148},{24,152},{28,15... | collective-permute-start | bytes 20 | tf_op jit(solution)/shard_map/ppermute | solution.py:114
  283.1 2.9 copy-start.5

commit v5 on v4

--- a/solution.py
+++ b/solution.py
@@ -18,17 +18,13 @@
     count = count_ref[b]
     own = own_ref[0]
     parts = jnp.concatenate([win_ref[start + s] for s in range(slots)], axis=1)
-    cross = jnp.dot(
-        own * -2.0, parts, precision=lax.Precision.HIGHEST, preferred_element_type=jnp.float32
-    )
-    own_sq = jnp.sum(own * own, axis=1, keepdims=True)
-    part_sq = jnp.sum(parts * parts, axis=0, keepdims=True)
+    cross = jnp.dot(own, parts, precision=lax.Precision.HIGHEST, preferred_element_type=jnp.float32)
     for s in range(slots):
         cols = slice(s * runs, (s + 1) * runs)
 
         @pl.when(s < count)
         def _():
-            squared = jnp.maximum((own_sq + part_sq[:, cols]) + cross[:, cols], 0.0)
+            squared = jnp.maximum(cross[:, cols], 0.0)
             radius_frac = jnp.sqrt(squared) * (1.0 / SUPPORT)
             remain = jnp.maximum(1.0 - radius_frac, 0.0)
             cubed = remain * remain * remain
@@ -145,16 +141,20 @@
     reach_runs = halo * block_runs
     window_blocks = blocks_local + 2 * halo
     widened_coords = extended(sorted_coords, "samp", 1, reach_runs)
-    win_c = jnp.pad(
-        widened_coords.reshape(dims, window_blocks, block_runs), ((0, dpad - dims), (0, 0), (0, 0))
-    ).transpose(1, 0, 2)
-    own_t = jnp.pad(
-        sorted_coords.reshape(dims, blocks_local, block_runs), ((0, dpad - dims), (0, 0), (0, 0))
-    ).transpose(1, 2, 0)
+    part_sq = jnp.sum(widened_coords * widened_coords, axis=0, keepdims=True)
+    win_c = jnp.concatenate(
+        [widened_coords, jnp.ones_like(part_sq), part_sq], axis=0
+    ).reshape(dpad, window_blocks, block_runs).transpose(1, 0, 2)
+    own_sq = jnp.sum(sorted_coords * sorted_coords, axis=0, keepdims=True)
+    own_t = jnp.concatenate(
+        [sorted_coords * -2.0, own_sq, jnp.ones_like(own_sq)], axis=0
+    ).reshape(dpad, blocks_local, block_runs).transpose(1, 2, 0)
     begin = jnp.clip(
         block_nbrs[:, 0] - (device_pos * blocks_local - halo), 0, window_blocks - slot_limit
     ).astype(jnp.int32)
-    tiles = build_tiles(begin, nbr_count.astype(jnp.int32), own_t, win_c, slot_limit)
+    counts = nbr_count.astype(jnp.int32)
+    half = blocks_local // 2
+    tiles_lo = build_tiles(begin[:half], counts[:half], own_t[:half], win_c, slot_limit)
     noise_col = noise[:, None]
     iterate = jnp.zeros_like(sorted_loads)
     remainder = sorted_loads
@@ -162,6 +162,12 @@
     for iteration in range(ITERS):
         rounded = direction.astype(jnp.bfloat16)
         gathered = gather_chan(rounded)
+        if iteration == 0:
+            tiles_lo, gathered, coreg_perm = lax.optimization_barrier(
+                (tiles_lo, gathered, coreg_perm)
+            )
+            tiles_hi = build_tiles(begin[half:], counts[half:], own_t[half:], win_c, slot_limit)
+            tiles = jnp.concatenate([tiles_lo, tiles_hi], axis=0)
         mixed = jnp.dot(
             coreg_perm, gathered.astype(jnp.float32), precision=lax.Precision.HIGHEST
         )
@@ -171,9 +177,10 @@
         mapped = apply_operator(begin, win_v, tiles, direction, noise_col, 4)
         curvature = jnp.sum(direction * mapped)
         if iteration + 1 == ITERS:
-            stacked = jnp.concatenate([iterate, remainder, direction, mapped], axis=0)
+            stacked = jnp.concatenate([direction, mapped], axis=0)
             unsorted = jnp.zeros_like(stacked).at[:, local_perm].set(stacked)
-            iterate, remainder, direction, mapped = jnp.split(unsorted, 4, axis=0)
+            direction, mapped = jnp.split(unsorted, 2, axis=0)
+            iterate, remainder = jnp.split(early, 2, axis=0)
         if iteration == 0:
             sums = global_sum(jnp.stack([norm_local, curvature]))
             norm_now, curvature = sums[0], sums[1]
@@ -182,6 +189,9 @@
         step_size = norm_now / curvature
         iterate = iterate + step_size * direction
         remainder = remainder - step_size * mapped
+        if iteration + 2 == ITERS:
+            both = jnp.concatenate([iterate, remainder], axis=0)
+            early = jnp.zeros_like(both).at[:, local_perm].set(both)
         if iteration + 1 < ITERS:
             norm_next = global_sum(jnp.sum(remainder * remainder))
             direction = remainder + norm_next / norm_now * direction

time: 290 us -> 299 us (1.031)
  other arithmetic: 21.7 us -> 31 us
  starting transfers between devices: 78.9 us -> 72.1 us
  local copies, waits for them, and re-layouts: 38.6 us -> 44.7 us
    ppermute x24, waiting for transfers between devices: 56 us -> 66.6 us  [global_sum(): value = value + lax.ppermute(value, axis, pairs)]
    concatenate x1 -> x6, other arithmetic: 1.58 us -> 10.7 us  [the longest x1 6.55 us: per_device(): tiles = jnp.concatenate([tiles_lo, tiles_hi], axis=0)]
    scatter x0 -> x1, local copies, waits for them, and re-layouts: none -> 8.5 us  [per_device(): early = jnp.zeros_like(both).at[:, local_perm].set(both)]
    ppermute x24, starting transfers between devices: 43.8 us -> 35.7 us  [global_sum(): value = value + lax.ppermute(value, axis, pairs)]
    ppermute x9, waiting for transfers between devices: 22.2 us -> 15.8 us  [gather_chan(): parts.append(lax.ppermute(rounded, 'chan', pairs))]
    scatter x1, local copies, waits for them, and re-layouts: 14.4 us -> 8.83 us  [per_device(): unsorted = jnp.zeros_like(stacked).at[:, local_perm].set(stacked)]
    pallas_call x1 -> x2, Pallas kernels: 32.1 us -> 32.7 us  [build_tiles(): pl.pallas_call(kern, grid_spec=pltpu.PrefetchScalarGridSpec(num_scalar_pr...]
    unnamed x22 -> x29, local copies, waits for them, and re-layouts: 7.51 us -> 7.57 us
  transfers between devices with their start and end apart: 39 -> 39, of which waited for: 28 -> 28; matrix products, arithmetic and copies ran while one was open for 14% -> 8% of each run, Pallas kernels for 11% -> 11%
where the time goes in v5:
time: 299 us; the launch traced here: 298 us
  waiting for transfers between devices  82.8 us (28%)
  starting transfers between devices  72.1 us (24%)
  Pallas kernels  50.4 us (17%)
  local copies, waits for them, and re-layouts  44.7 us (15%)
  other arithmetic  31 us (10%)
  between operations  14.8 us (5%)
    ppermute x24, waiting for transfers between devices, global_sum(): value = value + lax.ppermute(value, axis, pairs)  66.6 us
    ppermute x24, starting transfers between devices, global_sum(): value = value + lax.ppermute(value, axis, pairs)  35.7 us
    pallas_call x2, Pallas kernels, build_tiles(): pl.pallas_call(kern, grid_spec=pltpu.PrefetchScalarGridSpec(num_scalar_pr...  32.7 us
    ppermute x3, starting transfers between devices, extended(): lax.ppermute(lax.slice_in_dim(block, 0, width, axis=dim), axis, backward)  17.8 us
    pallas_call x2, Pallas kernels, apply_operator(): pl.pallas_call(kern, grid_spec=pltpu.PrefetchScalarGridSpec(num_scalar_pr...  17.8 us
    ppermute x9, waiting for transfers between devices, gather_chan(): parts.append(lax.ppermute(rounded, 'chan', pairs))  15.8 us
    ppermute x9, starting transfers between devices, gather_chan(): parts.append(lax.ppermute(rounded, 'chan', pairs))  12.1 us
    gather x2, local copies, waits for them, and re-layouts, per_device(): jnp.take(jnp.concatenate([coords, loads], axis=0), local_perm, axis=1)  9.54 us
  transfers between devices with their start and end apart: 39, of which 28 were waited for; matrix products, arithmetic and copies ran while one was open for 8% of the time, Pallas kernels for 11%

profile of v5, /device:TPU:2, one launch (start us, length us, event | category | flops | bytes accessed | tf_op | source)
XLA Modules:
  0.0 298.0 jit_solution(9060850023629324047)
XLA Ops:
  4.0 1.9 pad_maximum_fusion.1
  5.9 8.1 %gather_fusion = f32[3072,70]{1,0:T(8,128)S(1)} fusion(f32[70,3072]{0,1:T(8,128)S(1)} %pad_maximum_fusion.1, s32[3072]{0:T(1024)S(1)} %broadcast_clamp_fusion), kind=kCustom, calls=%fused_computation | custom fusion | bytes 1732608 | tf_op jit(solution)/shard_map/jit(_take)/gather | solution.py:134
  18.4 2.9 collective-permute-start.3
  23.3 6.3 %collective-permute-start.1 = (f32[6,1408]{1,0:T(8,128)}, f32[6,1408]{1,0:T(8,128)S(1)}, u32[]{:S(2)}, u32[]{:S(2)}) collective-permute-start(f32[6,1408]{1,0:T(8,128)} %get-tuple-element.28), channel_id=1, source_target_pairs={{4,0},{8,4},{12,8},{16,12},{20,16},{24,20},{28,24},{32,28},{36,32}... | collective-permute-start | bytes 101384 | tf_op jit(solution)/shard_map/ppermute | solution.py:100
  29.6 1.9 collective-permute-start
  40.1 3.6 %collective-permute-done.7 = f32[64,256]{1,0:T(8,128)S(1)} collective-permute-done((f32[64,256]{1,0:T(8,128)S(1)}, f32[64,256]{1,0:T(8,128)S(1)}, u32[]{:S(2)}, u32[]{:S(2)}) %collective-permute-start.7) | collective-permute-done | bytes 65568 | tf_op jit(solution)/shard_map/ppermute | solution.py:120
  44.5 17.0 %shard_map.86 = bf16[12,128,1536]{2,1,0:T(8,128)(2,1)} custom-call(s32[12]{0:T(128)} %get-tuple-element.43.begin_ref, s32[12]{0:T(128)} %get-tuple-element.41.count_ref, f32[12,128,8]{2,1,0:T(8,128)} %get-tuple-element.25.own_ref, f32[46,8,128]{2,1,0:T(8,128)} %maximum_bitcast_fusion.4.win_ref), custom_call_target="tpu_custom_call" | custom-call | tf_op jit(solution)/shard_map/pallas_call | solution.py:42
  61.6 15.6 %shard_map.87 = bf16[12,128,1536]{2,1,0:T(8,128)(2,1)} custom-call(s32[12]{0:T(128)} %get-tuple-element.42.begin_ref, s32[12]{0:T(128)} %get-tuple-element.40.count_ref, f32[12,128,8]{2,1,0:T(8,128)} %get-tuple-element.24.own_ref, f32[46,8,128]{2,1,0:T(8,128)} %maximum_bitcast_fusion.4.win_ref), custom_call_target="tpu_custom_call" | custom-call | tf_op jit(solution)/shard_map/pallas_call | solution.py:42
  80.0 9.6 %collective-permute-start.9 = (bf16[64,1408]{1,0:T(8,128)(2,1)S(1)}, bf16[64,1408]{1,0:T(8,128)(2,1)S(1)}, u32[]{:S(2)}, u32[]{:S(2)}) collective-permute-start(bf16[64,1408]{1,0:T(8,128)(2,1)S(1)} %get-tuple-element.35), channel_id=1, source_target_pairs={{4,0},{8,4},{12,8},{16,12},{20,16},{24,20},{28,24},{32,28},{36,32}... | collective-permute-start | bytes 540680 | tf_op jit(solution)/shard_map/ppermute | solution.py:100
  89.6 1.9 collective-permute-start.8
  91.5 6.5 %pad_maximum_fusion.tile_ref = bf16[24,128,1536]{2,1,0:T(8,128)(2,1)} fusion(bf16[12,128,1536]{2,1,0:T(8,128)(2,1)} %shard_map.87, bf16[12,128,1536]{2,1,0:T(8,128)(2,1)S(1)} %copy-done), kind=kLoop, calls=%fused_computation.3 | loop fusion | flops 4718592 | bytes 18874368 | tf_op jit(solution)/shard_map/concatenate | solution.py:170
  99.6 8.8 %shard_map.88 = f32[64,3072]{1,0:T(8,128)} custom-call(s32[24]{0:T(128)} %fusion.36.begin_ref, bf16[46,64,128]{2,1,0:T(8,128)(2,1)} %bitcast_bitcast_fusion.1.win_ref, bf16[24,128,1536]{2,1,0:T(8,128)(2,1)} %pad_maximum_fusion.tile_ref, f32[64,3072]{1,0:T(8,128)} %slice.80.p_ref, f32[64,1]{1,0:T(8,128)} %copy.40.noise_ref), custom_call_target="tpu_custom_call" | custom-call | tf_op jit(solution)/shard_map/pallas_call | solution.py:76
  108.4 2.0 multiply_reduce_fusion.3
  117.5 4.4 %collective-permute-done.11 = f32[2]{0:T(128)S(1)} collective-permute-done((f32[2]{0:T(128)S(1)}, f32[2]{0:T(128)S(1)}, u32[]{:S(2)}, u32[]{:S(2)}) %collective-permute-start.11) | collective-permute-done | bytes 40 | tf_op jit(solution)/shard_map/ppermute | solution.py:110
  124.4 3.5 %collective-permute-done.13 = f32[2]{0:T(128)S(1)} collective-permute-done((f32[2]{0:T(128)S(1)}, f32[2]{0:T(128)S(1)}, u32[]{:S(2)}, u32[]{:S(2)}) %collective-permute-start.13) | collective-permute-done | bytes 40 | tf_op jit(solution)/shard_map/ppermute | solution.py:110
  128.0 4.4 %collective-permute-done.14 = f32[2]{0:T(128)S(1)} collective-permute-done((f32[2]{0:T(128)S(1)}, f32[2]{0:T(128)S(1)}, u32[]{:S(2)}, u32[]{:S(2)}) %collective-permute-start.14) | collective-permute-done | bytes 40 | tf_op jit(solution)/shard_map/ppermute | solution.py:110
  132.6 7.2 %collective-permute-done.15 = f32[2]{0:T(128)S(1)} collective-permute-done((f32[2]{0:T(128)S(1)}, f32[2]{0:T(128)S(1)}, u32[]{:S(2)}, u32[]{:S(2)}) %collective-permute-start.15) | collective-permute-done | bytes 40 | tf_op jit(solution)/shard_map/ppermute | solution.py:110
  139.8 3.5 %collective-permute-done.16 = f32[2]{0:T(128)S(1)} collective-permute-done((f32[2]{0:T(128)S(1)}, f32[2]{0:T(128)S(1)}, u32[]{:S(2)}, u32[]{:S(2)}) %collective-permute-start.16) | collective-permute-done | bytes 40 | tf_op jit(solution)/shard_map/ppermute | solution.py:110
  143.4 2.1 collective-permute-start.17
  145.5 3.0 collective-permute-done.17
  152.9 1.9 collective-permute-done.18
  156.1 2.0 collective-permute-start.19
  158.1 3.0 %collective-permute-done.19 = f32[]{:T(128)} collective-permute-done((f32[]{:T(128)}, f32[]{:T(128)}, u32[]{:S(2)}, u32[]{:S(2)}) %collective-permute-start.19) | collective-permute-done | bytes 36 | tf_op jit(solution)/shard_map/ppermute | solution.py:110
  165.1 2.2 collective-permute-done.21
  169.4 3.1 %collective-permute-done.22 = f32[]{:T(128)} collective-permute-done((f32[]{:T(128)}, f32[]{:T(128)}, u32[]{:S(2)}, u32[]{:S(2)}) %collective-permute-start.22) | collective-permute-done | bytes 36 | tf_op jit(solution)/shard_map/ppermute | solution.py:110
  174.7 5.9 %collective-permute-done.23 = f32[]{:T(128)} collective-permute-done((f32[]{:T(128)}, f32[]{:T(128)}, u32[]{:S(2)}, u32[]{:S(2)}) %collective-permute-start.23) | collective-permute-done | bytes 36 | tf_op jit(solution)/shard_map/ppermute | solution.py:110
  182.7 2.2 collective-permute-done.24
  185.5 3.5 %collective-permute-start.25 = (f32[]{:T(128)}, f32[]{:T(128)}, u32[]{:S(2)}, u32[]{:S(2)}) collective-permute-start(f32[]{:T(128)} %add.102), channel_id=1, source_target_pairs={{0,128},{4,132},{8,136},{12,140},{16,144},{20,148},{24,152},{28,15... | collective-permute-start | bytes 20 | tf_op jit(solution)/shard_map/ppermute | solution.py:110
  195.4 2.1 collective-permute-start.26
  197.5 11.5 %collective-permute-done.28 = bf16[64,3072]{1,0:T(8,128)(2,1)S(1)} collective-permute-done((bf16[64,3072]{1,0:T(8,128)(2,1)S(1)}, bf16[64,3072]{1,0:T(8,128)(2,1)S(1)}, u32[]{:S(2)}, u32[]{:S(2)}) %collective-permute-start.28) | collective-permute-done | bytes 393248 | tf_op jit(solution)/shard_map/ppermute | solution.py:120
  211.3 1.9 collective-permute-start.30
  213.2 2.6 collective-permute-start.29
  216.4 8.5 %scatter_custom_fusion = f32[128,3072]{0,1:T(8,128)S(1)} fusion(s32[3072]{0:T(1024)S(1)} %get-tuple-element.21, f32[3072,128]{1,0:T(8,128)S(1)} %copy.41, f32[]{:T(128)} %constant.12.clone.1), kind=kCustom, calls=%fused_computation.31 | custom fusion | bytes 1572868 | tf_op jit(solution)/shard_map/scatter | solution.py:194
  225.0 2.1 bitcast_bitcast_fusion.win_ref
  227.1 8.9 %shard_map.89 = f32[64,3072]{1,0:T(8,128)} custom-call(s32[24]{0:T(128)} %fusion.36.begin_ref, bf16[46,64,128]{2,1,0:T(8,128)(2,1)} %bitcast_bitcast_fusion.win_ref, bf16[24,128,1536]{2,1,0:T(8,128)(2,1)} %pad_maximum_fusion.tile_ref, f32[64,3072]{1,0:T(8,128)} %get-tuple-element.17.p_ref, f32[64,1]{1,0:T(8,128)} %copy.40.noise_ref), custom_call_target="tpu_custom_call" | custom-call | tf_op jit(solution)/shard_map/pallas_call | solution.py:76
  236.0 2.5 maximum_bitcast_fusion.1
  239.4 3.0 %copy.44 = f32[3072,128]{1,0:T(8,128)} copy(f32[3072,128]{0,1:T(8,128)} %maximum_bitcast_fusion.1) | data formatting | bytes 3145728 | tf_op jit(solution)/shard_map/concatenate | solution.py:180
  242.4 8.8 %scatter_custom_fusion.1 = f32[128,3072]{0,1:T(8,128)S(1)} fusion(s32[3072]{0:T(1024)S(1)} %get-tuple-element.21, f32[3072,128]{1,0:T(8,128)} %copy.44, f32[]{:T(128)} %constant.12.clone.1), kind=kCustom, calls=%fused_computation.29 | custom fusion | bytes 1573376 | tf_op jit(solution)/shard_map/scatter | solution.py:181
  252.8 2.2 collective-permute-done.31
  256.3 3.5 %collective-permute-start.32 = (f32[]{:T(128)}, f32[]{:T(128)}, u32[]{:S(2)}, u32[]{:S(2)}) collective-permute-start(f32[]{:T(128)} %add.105), channel_id=1, source_target_pairs={{0,2},{1,3},{2,0},{3,1},{4,6},{5,7},{6,4},{7,5},{8,10},{9,11},{10,... | collective-permute-start | bytes 20 | tf_op jit(solution)/shard_map/ppermute | solution.py:110
  265.5 1.9 collective-permute-done.34
  269.7 2.8 collective-permute-done.35
  273.1 1.9 collective-permute-start.36
  275.1 5.6 %collective-permute-done.36 = f32[]{:T(128)} collective-permute-done((f32[]{:T(128)}, f32[]{:T(128)}, u32[]{:S(2)}, u32[]{:S(2)}) %collective-permute-start.36) | collective-permute-done | bytes 36 | tf_op jit(solution)/shard_map/ppermute | solution.py:110
  281.3 2.1 collective-permute-start.37
  285.5 3.5 %collective-permute-start.38 = (f32[]{:T(128)}, f32[]{:T(128)}, u32[]{:S(2)}, u32[]{:S(2)}) collective-permute-start(f32[]{:T(128)} %add.111), channel_id=1, source_target_pairs={{0,128},{4,132},{8,136},{12,140},{16,144},{20,148},{24,152},{28,15... | collective-permute-start | bytes 20 | tf_op jit(solution)/shard_map/ppermute | solution.py:110
  291.2 2.6 fusion
  293.8 2.9 copy.45
  (116 shorter events, 64.0 us)
Async XLA Ops:
  0.6 1.7 copy-start.5
  0.6 3.3 %copy-start.8 = (s32[3072]{0:T(1024)S(1)}, s32[3072]{0:T(1024)}, u32[]{:S(2)}) copy-start(s32[3072]{0:T(1024)} %param.11) | copy-start | bytes 36868
  16.8 60.8 %collective-permute-start.4 = (bf16[64,3072]{1,0:T(8,128)(2,1)S(1)}, bf16[64,3072]{1,0:T(8,128)(2,1)S(1)}, u32[]{:S(2)}, u32[]{:S(2)}) collective-permute-start(bf16[64,3072]{1,0:T(8,128)(2,1)S(1)} %slice.101), channel_id=1, source_target_pairs={{3,0},{0,1},{1,2},{2,3},{7,4},{4,5},{5,6},{6,7},{11,8},{8,9},{9,10... | collective-permute-start | bytes 1179656 | tf_op jit(solution)/shard_map/ppermute | solution.py:120
  18.4 59.2 %collective-permute-start.3 = (bf16[64,3072]{1,0:T(8,128)(2,1)S(1)}, bf16[64,3072]{1,0:T(8,128)(2,1)}, u32[]{:S(2)}, u32[]{:S(2)}) collective-permute-start(bf16[64,3072]{1,0:T(8,128)(2,1)S(1)} %slice.101), channel_id=1, source_target_pairs={{2,0},{3,1},{0,2},{1,3},{6,4},{7,5},{4,6},{5,7},{10,8},{11,9},{8,1... | collective-permute-start | bytes 1179656 | tf_op jit(solution)/shard_map/ppermute | solution.py:120
  21.3 56.3 %collective-permute-start.2 = (bf16[64,3072]{1,0:T(8,128)(2,1)S(1)}, bf16[64,3072]{1,0:T(8,128)(2,1)}, u32[]{:S(2)}, u32[]{:S(2)}) collective-permute-start(bf16[64,3072]{1,0:T(8,128)(2,1)S(1)} %slice.101), channel_id=1, source_target_pairs={{1,0},{2,1},{3,2},{0,3},{5,4},{6,5},{7,6},{4,7},{9,8},{10,9},{11,1... | collective-permute-start | bytes 1179656 | tf_op jit(solution)/shard_map/ppermute | solution.py:120
  23.3 15.0 %collective-permute-start.1 = (f32[6,1408]{1,0:T(8,128)}, f32[6,1408]{1,0:T(8,128)S(1)}, u32[]{:S(2)}, u32[]{:S(2)}) collective-permute-start(f32[6,1408]{1,0:T(8,128)} %get-tuple-element.28), channel_id=1, source_target_pairs={{4,0},{8,4},{12,8},{16,12},{20,16},{24,20},{28,24},{32,28},{36,32}... | collective-permute-start | bytes 101384 | tf_op jit(solution)/shard_map/ppermute | solution.py:100
  29.6 9.4 %collective-permute-start = (f32[6,1408]{1,0:T(8,128)}, f32[6,1408]{1,0:T(8,128)S(1)}, u32[]{:S(2)}, u32[]{:S(2)}) collective-permute-start(f32[6,1408]{1,0:T(8,128)} %get-tuple-element.27), channel_id=1, source_target_pairs={{0,4},{4,8},{8,12},{12,16},{16,20},{20,24},{24,28},{28,32},{32,36}... | collective-permute-start | bytes 101384 | tf_op jit(solution)/shard_map/ppermute | solution.py:97
  36.0 2.3 copy-start.11
  38.3 5.5 %collective-permute-start.7 = (f32[64,256]{1,0:T(8,128)S(1)}, f32[64,256]{1,0:T(8,128)S(1)}, u32[]{:S(2)}, u32[]{:S(2)}) collective-permute-start(f32[64,256]{1,0:T(8,128)S(1)} %copy-done.11), channel_id=1, source_target_pairs={{3,0},{0,1},{1,2},{2,3},{7,4},{4,5},{5,6},{6,7},{11,8},{8,9},{9,10... | collective-permute-start | bytes 196616 | tf_op jit(solution)/shard_map/ppermute | solution.py:120
  39.0 38.2 %collective-permute-start.6 = (f32[64,256]{1,0:T(8,128)S(1)}, f32[64,256]{1,0:T(8,128)S(1)}, u32[]{:S(2)}, u32[]{:S(2)}) collective-permute-start(f32[64,256]{1,0:T(8,128)S(1)} %copy-done.11), channel_id=1, source_target_pairs={{2,0},{3,1},{0,2},{1,3},{6,4},{7,5},{4,6},{5,7},{10,8},{11,9},{8,1... | collective-permute-start | bytes 196616 | tf_op jit(solution)/shard_map/ppermute | solution.py:120
  43.8 33.4 %collective-permute-start.5 = (f32[64,256]{1,0:T(8,128)S(1)}, f32[64,256]{1,0:T(8,128)S(1)}, u32[]{:S(2)}, u32[]{:S(2)}) collective-permute-start(f32[64,256]{1,0:T(8,128)S(1)} %copy-done.11), channel_id=1, source_target_pairs={{1,0},{2,1},{3,2},{0,3},{5,4},{6,5},{7,6},{4,7},{9,8},{10,9},{11,1... | collective-permute-start | bytes 196616 | tf_op jit(solution)/shard_map/ppermute | solution.py:120
  77.6 13.9 %copy-start = (bf16[12,128,1536]{2,1,0:T(8,128)(2,1)S(1)}, bf16[12,128,1536]{2,1,0:T(8,128)(2,1)}, u32[]{:S(2)}) copy-start(bf16[12,128,1536]{2,1,0:T(8,128)(2,1)} %shard_map.86) | copy-start | bytes 14155780
  80.0 18.1 %collective-permute-start.9 = (bf16[64,1408]{1,0:T(8,128)(2,1)S(1)}, bf16[64,1408]{1,0:T(8,128)(2,1)S(1)}, u32[]{:S(2)}, u32[]{:S(2)}) collective-permute-start(bf16[64,1408]{1,0:T(8,128)(2,1)S(1)} %get-tuple-element.35), channel_id=1, source_target_pairs={{4,0},{8,4},{12,8},{16,12},{20,16},{24,20},{28,24},{32,28},{36,32}... | collective-permute-start | bytes 540680 | tf_op jit(solution)/shard_map/ppermute | solution.py:100
  89.6 8.9 %collective-permute-start.8 = (bf16[64,1408]{1,0:T(8,128)(2,1)S(1)}, bf16[64,1408]{1,0:T(8,128)(2,1)S(1)}, u32[]{:S(2)}, u32[]{:S(2)}) collective-permute-start(bf16[64,1408]{1,0:T(8,128)(2,1)S(1)} %get-tuple-element.34), channel_id=1, source_target_pairs={{0,4},{4,8},{8,12},{12,16},{16,20},{20,24},{24,28},{28,32},{32,36}... | collective-permute-start | bytes 540680 | tf_op jit(solution)/shard_map/ppermute | solution.py:97
  108.4 41.9 %copy-start.3 = (f32[64,3072]{1,0:T(8,128)S(1)}, f32[64,3072]{1,0:T(8,128)}, u32[]{:S(2)}) copy-start(f32[64,3072]{1,0:T(8,128)} %shard_map.88) | copy-start | bytes 2359300
  111.8 3.6 %collective-permute-start.10 = (f32[2]{0:T(128)S(1)}, f32[2]{0:T(128)S(1)}, u32[]{:S(2)}, u32[]{:S(2)}) collective-permute-start(f32[2]{0:T(128)S(1)} %pad_maximum_fusion.4), channel_id=1, source_target_pairs={{0,1},{1,0},{2,3},{3,2},{4,5},{5,4},{6,7},{7,6},{8,9},{9,8},{10,11... | collective-permute-start | bytes 32 | tf_op jit(solution)/shard_map/ppermute | solution.py:110
  116.7 5.3 %collective-permute-start.11 = (f32[2]{0:T(128)S(1)}, f32[2]{0:T(128)S(1)}, u32[]{:S(2)}, u32[]{:S(2)}) collective-permute-start(f32[2]{0:T(128)S(1)} %fusion.35), channel_id=1, source_target_pairs={{0,2},{1,3},{2,0},{3,1},{4,6},{5,7},{6,4},{7,5},{8,10},{9,11},{10,... | collective-permute-start | bytes 32 | tf_op jit(solution)/shard_map/ppermute | solution.py:110
  123.3 1.1 collective-permute-start.12
  124.4 3.5 %collective-permute-start.13 = (f32[2]{0:T(128)S(1)}, f32[2]{0:T(128)S(1)}, u32[]{:S(2)}, u32[]{:S(2)}) collective-permute-start(f32[2]{0:T(128)S(1)} %add.90), channel_id=1, source_target_pairs={{0,8},{4,12},{8,0},{12,4},{16,24},{20,28},{24,16},{28,20},{32,40},... | collective-permute-start | bytes 32 | tf_op jit(solution)/shard_map/ppermute | solution.py:110
  127.9 4.4 %collective-permute-start.14 = (f32[2]{0:T(128)S(1)}, f32[2]{0:T(128)S(1)}, u32[]{:S(2)}, u32[]{:S(2)}) collective-permute-start(f32[2]{0:T(128)S(1)} %add.91), channel_id=1, source_target_pairs={{0,16},{4,20},{8,24},{12,28},{16,0},{20,4},{24,8},{28,12},{32,48},... | collective-permute-start | bytes 32 | tf_op jit(solution)/shard_map/ppermute | solution.py:110
  132.4 7.4 %collective-permute-start.15 = (f32[2]{0:T(128)S(1)}, f32[2]{0:T(128)S(1)}, u32[]{:S(2)}, u32[]{:S(2)}) collective-permute-start(f32[2]{0:T(128)S(1)} %add.92), channel_id=1, source_target_pairs={{0,32},{4,36},{8,40},{12,44},{16,48},{20,52},{24,56},{28,60},{32,0... | collective-permute-start | bytes 32 | tf_op jit(solution)/shard_map/ppermute | solution.py:110
  139.8 3.5 %collective-permute-start.16 = (f32[2]{0:T(128)S(1)}, f32[2]{0:T(128)S(1)}, u32[]{:S(2)}, u32[]{:S(2)}) collective-permute-start(f32[2]{0:T(128)S(1)} %add.93), channel_id=1, source_target_pairs={{0,64},{4,68},{8,72},{12,76},{16,80},{20,84},{24,88},{28,92},{32,9... | collective-permute-start | bytes 32 | tf_op jit(solution)/shard_map/ppermute | solution.py:110
  143.4 5.0 %collective-permute-start.17 = (f32[2]{0:T(128)S(1)}, f32[2]{0:T(128)S(1)}, u32[]{:S(2)}, u32[]{:S(2)}) collective-permute-start(f32[2]{0:T(128)S(1)} %add.94), channel_id=1, source_target_pairs={{0,128},{4,132},{8,136},{12,140},{16,144},{20,148},{24,152},{28,15... | collective-permute-start | bytes 32 | tf_op jit(solution)/shard_map/ppermute | solution.py:110
  151.1 3.6 %collective-permute-start.18 = (f32[]{:T(128)}, f32[]{:T(128)}, u32[]{:S(2)}, u32[]{:S(2)}) collective-permute-start(f32[]{:T(128)} %get-tuple-element.18), channel_id=1, source_target_pairs={{0,1},{1,0},{2,3},{3,2},{4,5},{5,4},{6,7},{7,6},{8,9},{9,8},{10,11... | collective-permute-start | bytes 20 | tf_op jit(solution)/shard_map/ppermute | solution.py:110
  156.1 5.1 %collective-permute-start.19 = (f32[]{:T(128)}, f32[]{:T(128)}, u32[]{:S(2)}, u32[]{:S(2)}) collective-permute-start(f32[]{:T(128)} %add.96), channel_id=1, source_target_pairs={{0,2},{1,3},{2,0},{3,1},{4,6},{5,7},{6,4},{7,5},{8,10},{9,11},{10,... | collective-permute-start | bytes 20 | tf_op jit(solution)/shard_map/ppermute | solution.py:110
  161.9 1.2 collective-permute-start.20
  163.7 3.6 %collective-permute-start.21 = (f32[]{:T(128)}, f32[]{:T(128)}, u32[]{:S(2)}, u32[]{:S(2)}) collective-permute-start(f32[]{:T(128)} %add.98), channel_id=1, source_target_pairs={{0,8},{4,12},{8,0},{12,4},{16,24},{20,28},{24,16},{28,20},{32,40},... | collective-permute-start | bytes 20 | tf_op jit(solution)/shard_map/ppermute | solution.py:110
  168.0 4.5 %collective-permute-start.22 = (f32[]{:T(128)}, f32[]{:T(128)}, u32[]{:S(2)}, u32[]{:S(2)}) collective-permute-start(f32[]{:T(128)} %add.99), channel_id=1, source_target_pairs={{0,16},{4,20},{8,24},{12,28},{16,0},{20,4},{24,8},{28,12},{32,48},... | collective-permute-start | bytes 20 | tf_op jit(solution)/shard_map/ppermute | solution.py:110
  173.1 7.5 %collective-permute-start.23 = (f32[]{:T(128)}, f32[]{:T(128)}, u32[]{:S(2)}, u32[]{:S(2)}) collective-permute-start(f32[]{:T(128)} %add.100), channel_id=1, source_target_pairs={{0,32},{4,36},{8,40},{12,44},{16,48},{20,52},{24,56},{28,60},{32,0... | collective-permute-start | bytes 20 | tf_op jit(solution)/shard_map/ppermute | solution.py:110
  181.3 3.6 %collective-permute-start.24 = (f32[]{:T(128)}, f32[]{:T(128)}, u32[]{:S(2)}, u32[]{:S(2)}) collective-permute-start(f32[]{:T(128)} %add.101), channel_id=1, source_target_pairs={{0,64},{4,68},{8,72},{12,76},{16,80},{20,84},{24,88},{28,92},{32,9... | collective-permute-start | bytes 20 | tf_op jit(solution)/shard_map/ppermute | solution.py:110
  185.5 5.1 %collective-permute-start.25 = (f32[]{:T(128)}, f32[]{:T(128)}, u32[]{:S(2)}, u32[]{:S(2)}) collective-permute-start(f32[]{:T(128)} %add.102), channel_id=1, source_target_pairs={{0,128},{4,132},{8,136},{12,140},{16,144},{20,148},{24,152},{28,15... | collective-permute-start | bytes 20 | tf_op jit(solution)/shard_map/ppermute | solution.py:110
  192.0 17.6 %copy-start.7 = (f32[64,256]{1,0:T(8,128)S(1)}, f32[64,256]{1,0:T(8,128)}, u32[]{:S(2)}) copy-start(f32[64,256]{1,0:T(8,128)} %copy-done.6) | copy-start | bytes 196612
  193.0 15.9 %collective-permute-start.28 = (bf16[64,3072]{1,0:T(8,128)(2,1)S(1)}, bf16[64,3072]{1,0:T(8,128)(2,1)S(1)}, u32[]{:S(2)}, u32[]{:S(2)}) collective-permute-start(bf16[64,3072]{1,0:T(8,128)(2,1)S(1)} %get-tuple-element.16), channel_id=1, source_target_pairs={{3,0},{0,1},{1,2},{2,3},{7,4},{4,5},{5,6},{6,7},{11,8},{8,9},{9,10... | collective-permute-start | bytes 1179656 | tf_op jit(solution)/shard_map/ppermute | solution.py:120
  194.8 14.1 %collective-permute-start.27 = (bf16[64,3072]{1,0:T(8,128)(2,1)S(1)}, bf16[64,3072]{1,0:T(8,128)(2,1)S(1)}, u32[]{:S(2)}, u32[]{:S(2)}) collective-permute-start(bf16[64,3072]{1,0:T(8,128)(2,1)S(1)} %get-tuple-element.16), channel_id=1, source_target_pairs={{2,0},{3,1},{0,2},{1,3},{6,4},{7,5},{4,6},{5,7},{10,8},{11,9},{8,1... | collective-permute-start | bytes 1179656 | tf_op jit(solution)/shard_map/ppermute | solution.py:120
  195.4 14.2 %collective-permute-start.26 = (bf16[64,3072]{1,0:T(8,128)(2,1)S(1)}, bf16[64,3072]{1,0:T(8,128)(2,1)S(1)}, u32[]{:S(2)}, u32[]{:S(2)}) collective-permute-start(bf16[64,3072]{1,0:T(8,128)(2,1)S(1)} %get-tuple-element.16), channel_id=1, source_target_pairs={{1,0},{2,1},{3,2},{0,3},{5,4},{6,5},{7,6},{4,7},{9,8},{10,9},{11,1... | collective-permute-start | bytes 1179656 | tf_op jit(solution)/shard_map/ppermute | solution.py:120
  211.3 13.7 %collective-permute-start.30 = (bf16[64,1408]{1,0:T(8,128)(2,1)}, bf16[64,1408]{1,0:T(8,128)(2,1)}, u32[]{:S(2)}, u32[]{:S(2)}) collective-permute-start(bf16[64,1408]{1,0:T(8,128)(2,1)} %get-tuple-element.33), channel_id=1, source_target_pairs={{4,0},{8,4},{12,8},{16,12},{20,16},{24,20},{28,24},{32,28},{36,32}... | collective-permute-start | bytes 540680 | tf_op jit(solution)/shard_map/ppermute | solution.py:100
  213.2 11.8 %collective-permute-start.29 = (bf16[64,1408]{1,0:T(8,128)(2,1)}, bf16[64,1408]{1,0:T(8,128)(2,1)}, u32[]{:S(2)}, u32[]{:S(2)}) collective-permute-start(bf16[64,1408]{1,0:T(8,128)(2,1)} %get-tuple-element.32), channel_id=1, source_target_pairs={{0,4},{4,8},{8,12},{12,16},{16,20},{20,24},{24,28},{28,32},{32,36}... | collective-permute-start | bytes 540680 | tf_op jit(solution)/shard_map/ppermute | solution.py:97
  227.1 8.9 %copy-start.1 = (f32[64,3072]{1,0:T(8,128)S(1)}, f32[64,3072]{1,0:T(8,128)}, u32[]{:S(2)}) copy-start(f32[64,3072]{1,0:T(8,128)} %get-tuple-element.17.p_ref) | copy-start | bytes 2359300
  236.0 2.5 copy-start.2
  251.3 3.7 %collective-permute-start.31 = (f32[]{:T(128)}, f32[]{:T(128)}, u32[]{:S(2)}, u32[]{:S(2)}) collective-permute-start(f32[]{:T(128)} %multiply_reduce_fusion), channel_id=1, source_target_pairs={{0,1},{1,0},{2,3},{3,2},{4,5},{5,4},{6,7},{7,6},{8,9},{9,8},{10,11... | collective-permute-start | bytes 20 | tf_op jit(solution)/shard_map/ppermute | solution.py:110
  256.3 5.1 %collective-permute-start.32 = (f32[]{:T(128)}, f32[]{:T(128)}, u32[]{:S(2)}, u32[]{:S(2)}) collective-permute-start(f32[]{:T(128)} %add.105), channel_id=1, source_target_pairs={{0,2},{1,3},{2,0},{3,1},{4,6},{5,7},{6,4},{7,5},{8,10},{9,11},{10,... | collective-permute-start | bytes 20 | tf_op jit(solution)/shard_map/ppermute | solution.py:110
  262.0 1.2 collective-permute-start.33
  263.8 3.6 %collective-permute-start.34 = (f32[]{:T(128)}, f32[]{:T(128)}, u32[]{:S(2)}, u32[]{:S(2)}) collective-permute-start(f32[]{:T(128)} %add.107), channel_id=1, source_target_pairs={{0,8},{4,12},{8,0},{12,4},{16,24},{20,28},{24,16},{28,20},{32,40},... | collective-permute-start | bytes 20 | tf_op jit(solution)/shard_map/ppermute | solution.py:110
  268.0 4.5 %collective-permute-start.35 = (f32[]{:T(128)}, f32[]{:T(128)}, u32[]{:S(2)}, u32[]{:S(2)}) collective-permute-start(f32[]{:T(128)} %add.108), channel_id=1, source_target_pairs={{0,16},{4,20},{8,24},{12,28},{16,0},{20,4},{24,8},{28,12},{32,48},... | collective-permute-start | bytes 20 | tf_op jit(solution)/shard_map/ppermute | solution.py:110
  273.1 7.5 %collective-permute-start.36 = (f32[]{:T(128)}, f32[]{:T(128)}, u32[]{:S(2)}, u32[]{:S(2)}) collective-permute-start(f32[]{:T(128)} %add.109), channel_id=1, source_target_pairs={{0,32},{4,36},{8,40},{12,44},{16,48},{20,52},{24,56},{28,60},{32,0... | collective-permute-start | bytes 20 | tf_op jit(solution)/shard_map/ppermute | solution.py:110
  281.3 3.6 %collective-permute-start.37 = (f32[]{:T(128)}, f32[]{:T(128)}, u32[]{:S(2)}, u32[]{:S(2)}) collective-permute-start(f32[]{:T(128)} %add.110), channel_id=1, source_target_pairs={{0,64},{4,68},{8,72},{12,76},{16,80},{20,84},{24,88},{28,92},{32,9... | collective-permute-start | bytes 20 | tf_op jit(solution)/shard_map/ppermute | solution.py:110
  285.5 5.1 %collective-permute-start.38 = (f32[]{:T(128)}, f32[]{:T(128)}, u32[]{:S(2)}, u32[]{:S(2)}) collective-permute-start(f32[]{:T(128)} %add.111), channel_id=1, source_target_pairs={{0,128},{4,132},{8,136},{12,140},{16,144},{20,148},{24,152},{28,15... | collective-permute-start | bytes 20 | tf_op jit(solution)/shard_map/ppermute | solution.py:110
  293.8 2.9 copy-start.4
  (3 other events, 4.3 us)

commit v6 on v5

--- a/solution.py
+++ b/solution.py
@@ -17,14 +17,16 @@
     start = begin_ref[b]
     count = count_ref[b]
     own = own_ref[0]
-    parts = jnp.concatenate([win_ref[start + s] for s in range(slots)], axis=1)
-    cross = jnp.dot(own, parts, precision=lax.Precision.HIGHEST, preferred_element_type=jnp.float32)
     for s in range(slots):
         cols = slice(s * runs, (s + 1) * runs)
 
         @pl.when(s < count)
         def _():
-            squared = jnp.maximum(cross[:, cols], 0.0)
+            cross = jnp.dot(
+                own, win_ref[start + s], precision=lax.Precision.HIGHEST,
+                preferred_element_type=jnp.float32,
+            )
+            squared = jnp.maximum(cross, 0.0)
             radius_frac = jnp.sqrt(squared) * (1.0 / SUPPORT)
             remain = jnp.maximum(1.0 - radius_frac, 0.0)
             cubed = remain * remain * remain
@@ -152,9 +154,7 @@
     begin = jnp.clip(
         block_nbrs[:, 0] - (device_pos * blocks_local - halo), 0, window_blocks - slot_limit
     ).astype(jnp.int32)
-    counts = nbr_count.astype(jnp.int32)
-    half = blocks_local // 2
-    tiles_lo = build_tiles(begin[:half], counts[:half], own_t[:half], win_c, slot_limit)
+    tiles = build_tiles(begin, nbr_count.astype(jnp.int32), own_t, win_c, slot_limit)
     noise_col = noise[:, None]
     iterate = jnp.zeros_like(sorted_loads)
     remainder = sorted_loads
@@ -162,12 +162,6 @@
     for iteration in range(ITERS):
         rounded = direction.astype(jnp.bfloat16)
         gathered = gather_chan(rounded)
-        if iteration == 0:
-            tiles_lo, gathered, coreg_perm = lax.optimization_barrier(
-                (tiles_lo, gathered, coreg_perm)
-            )
-            tiles_hi = build_tiles(begin[half:], counts[half:], own_t[half:], win_c, slot_limit)
-            tiles = jnp.concatenate([tiles_lo, tiles_hi], axis=0)
         mixed = jnp.dot(
             coreg_perm, gathered.astype(jnp.float32), precision=lax.Precision.HIGHEST
         )
@@ -177,10 +171,9 @@
         mapped = apply_operator(begin, win_v, tiles, direction, noise_col, 4)
         curvature = jnp.sum(direction * mapped)
         if iteration + 1 == ITERS:
-            stacked = jnp.concatenate([direction, mapped], axis=0)
+            stacked = jnp.concatenate([iterate, remainder, direction, mapped], axis=0)
             unsorted = jnp.zeros_like(stacked).at[:, local_perm].set(stacked)
-            direction, mapped = jnp.split(unsorted, 2, axis=0)
-            iterate, remainder = jnp.split(early, 2, axis=0)
+            iterate, remainder, direction, mapped = jnp.split(unsorted, 4, axis=0)
         if iteration == 0:
             sums = global_sum(jnp.stack([norm_local, curvature]))
             norm_now, curvature = sums[0], sums[1]
@@ -189,9 +182,6 @@
         step_size = norm_now / curvature
         iterate = iterate + step_size * direction
         remainder = remainder - step_size * mapped
-        if iteration + 2 == ITERS:
-            both = jnp.concatenate([iterate, remainder], axis=0)
-            early = jnp.zeros_like(both).at[:, local_perm].set(both)
         if iteration + 1 < ITERS:
             norm_next = global_sum(jnp.sum(remainder * remainder))
             direction = remainder + norm_next / norm_now * direction

time: 299 us -> 315 us (1.054); the launches traced: 298 us -> 311 us
  starting transfers between devices: 72.1 us -> 102 us
  waiting for transfers between devices: 82.8 us -> 64.3 us
  Pallas kernels: 50.4 us -> 66.9 us
  other arithmetic: 31 us -> 22.5 us
  local copies, waits for them, and re-layouts: 44.7 us -> 38 us
    ppermute x24, starting transfers between devices: 35.7 us -> 67.5 us  [global_sum(): value = value + lax.ppermute(value, axis, pairs)]
    ppermute x24, waiting for transfers between devices: 66.6 us -> 39.4 us  [global_sum(): value = value + lax.ppermute(value, axis, pairs)]
    pallas_call x2 -> x1, Pallas kernels: 32.7 us -> 49.2 us  [build_tiles(): pl.pallas_call(kern, grid_spec=pltpu.PrefetchScalarGridSpec(num_scalar_pr...]
    concatenate x4 -> x1, other arithmetic: 10.6 us -> 1.58 us  [per_device(): stacked = jnp.concatenate([iterate, remainder, direction, mapped], axis=0)]
    scatter x1 -> x0, local copies, waits for them, and re-layouts: 8.5 us -> none  [per_device(): early = jnp.zeros_like(both).at[:, local_perm].set(both)]
    ppermute x3, waiting for transfers between devices: 0.44 us -> 7.02 us  [extended(): lax.ppermute(lax.slice_in_dim(block, block.shape[dim] - width, None, axis...]
    scatter x1, local copies, waits for them, and re-layouts: 8.83 us -> 14.4 us  [per_device(): unsorted = jnp.zeros_like(stacked).at[:, local_perm].set(stacked)]
    ppermute x3, starting transfers between devices: 17.8 us -> 14 us  [extended(): lax.ppermute(lax.slice_in_dim(block, 0, width, axis=dim), axis, backward)]
  transfers between devices with their start and end apart: 39 -> 39, of which waited for: 28 -> 31; matrix products, arithmetic and copies ran while one was open for 8% -> 7% of each run, Pallas kernels for 11% -> 16%
where the time goes in v6:
time: 315 us; the launch traced here: 311 us
  starting transfers between devices  102 us (32%)
  Pallas kernels  66.9 us (21%)
  waiting for transfers between devices  64.3 us (20%)
  local copies, waits for them, and re-layouts  38 us (12%)
  other arithmetic  22.5 us (7%)
  between operations  14.2 us (5%)
  matrix products  3.22 us (1%)
    ppermute x24, starting transfers between devices, global_sum(): value = value + lax.ppermute(value, axis, pairs)  67.5 us
    pallas_call x1, Pallas kernels, build_tiles(): pl.pallas_call(kern, grid_spec=pltpu.PrefetchScalarGridSpec(num_scalar_pr...  49.2 us
    ppermute x24, waiting for transfers between devices, global_sum(): value = value + lax.ppermute(value, axis, pairs)  39.4 us
    pallas_call x2, Pallas kernels, apply_operator(): pl.pallas_call(kern, grid_spec=pltpu.PrefetchScalarGridSpec(num_scalar_pr...  17.8 us
    ppermute x9, waiting for transfers between devices, gather_chan(): parts.append(lax.ppermute(rounded, 'chan', pairs))  16.2 us
    scatter x1, local copies, waits for them, and re-layouts, per_device(): unsorted = jnp.zeros_like(stacked).at[:, local_perm].set(stacked)  14.4 us
    ppermute x9, starting transfers between devices, gather_chan(): parts.append(lax.ppermute(rounded, 'chan', pairs))  14.3 us
    ppermute x3, starting transfers between devices, extended(): lax.ppermute(lax.slice_in_dim(block, 0, width, axis=dim), axis, backward)  14 us
  transfers between devices with their start and end apart: 39, of which 31 were waited for; matrix products, arithmetic and copies ran while one was open for 7% of the time, Pallas kernels for 16%

profile of v6, /device:TPU:2, one launch (start us, length us, event | category | flops | bytes accessed | tf_op | source)
XLA Modules:
  0.0 310.8 jit_solution(5401747775779313974)
XLA Ops:
  3.0 1.7 copy.32
  4.7 1.9 pad_maximum_fusion
  6.6 8.1 %gather_fusion = f32[3072,70]{1,0:T(8,128)S(1)} fusion(f32[70,3072]{0,1:T(8,128)S(1)} %pad_maximum_fusion, s32[3072]{0:T(1024)S(1)} %broadcast_clamp_fusion), kind=kCustom, calls=%fused_computation | custom fusion | bytes 1732608 | tf_op jit(solution)/shard_map/jit(_take)/gather | solution.py:136
  19.2 2.9 collective-permute-start.4
  23.8 1.9 collective-permute-start.8
  25.9 5.8 %collective-permute-done.8 = f32[6,1408]{1,0:T(8,128)S(1)} collective-permute-done((f32[6,1408]{1,0:T(8,128)S(1)}, f32[6,1408]{1,0:T(8,128)S(1)}, u32[]{:S(2)}, u32[]{:S(2)}) %collective-permute-start.8) | collective-permute-done | bytes 33824 | tf_op jit(solution)/shard_map/ppermute | solution.py:99
  31.7 2.5 collective-permute-start.9
  38.8 3.0 collective-permute-start
  43.7 3.6 %collective-permute-done.2 = f32[64,256]{1,0:T(8,128)S(1)} collective-permute-done((f32[64,256]{1,0:T(8,128)S(1)}, f32[64,256]{1,0:T(8,128)S(1)}, u32[]{:S(2)}, u32[]{:S(2)}) %collective-permute-start.2) | collective-permute-done | bytes 65568 | tf_op jit(solution)/shard_map/ppermute | solution.py:122
  47.7 1.9 convolution_convert_fusion.1
  49.6 1.9 collective-permute-start.6
  51.6 5.8 %collective-permute-start.7 = (bf16[64,1408]{1,0:T(8,128)(2,1)S(1)}, bf16[64,1408]{1,0:T(8,128)(2,1)S(1)}, u32[]{:S(2)}, u32[]{:S(2)}) collective-permute-start(bf16[64,1408]{1,0:T(8,128)(2,1)S(1)} %get-tuple-element.27), channel_id=1, source_target_pairs={{4,0},{8,4},{12,8},{16,12},{20,16},{24,20},{28,24},{32,28},{36,32}... | collective-permute-start | bytes 540680 | tf_op jit(solution)/shard_map/ppermute | solution.py:102
  58.1 49.2 %shard_map.86.tile_ref = bf16[24,128,1536]{2,1,0:T(8,128)(2,1)} custom-call(s32[24]{0:T(128)} %clamp_bitcast_fusion.begin_ref, s32[24]{0:T(128)} %count_ref.1, f32[24,128,8]{2,1,0:T(8,128)} %bitcast.42, f32[46,8,128]{2,1,0:T(8,128)} %maximum_bitcast_fusion.3.win_ref), custom_call_target="tpu_custom_call" | custom-call | tf_op jit(solution)/shard_map/pallas_call | solution.py:44
  108.4 8.8 %shard_map.87 = f32[64,3072]{1,0:T(8,128)} custom-call(s32[24]{0:T(128)} %clamp_bitcast_fusion.begin_ref, bf16[46,64,128]{2,1,0:T(8,128)(2,1)} %bitcast_bitcast_fusion.1.win_ref, bf16[24,128,1536]{2,1,0:T(8,128)(2,1)} %shard_map.86.tile_ref, f32[64,3072]{1,0:T(8,128)} %slice.48.p_ref, f32[64,1]{1,0:T(8,128)} %copy.38.noise_ref), custom_call_target="tpu_custom_call" | custom-call | tf_op jit(solution)/shard_map/pallas_call | solution.py:78
  117.2 2.0 multiply_reduce_fusion.3
  120.5 3.5 %collective-permute-done.10 = f32[2]{0:T(128)S(1)} collective-permute-done((f32[2]{0:T(128)S(1)}, f32[2]{0:T(128)S(1)}, u32[]{:S(2)}, u32[]{:S(2)}) %collective-permute-start.10) | collective-permute-done | bytes 40 | tf_op jit(solution)/shard_map/ppermute | solution.py:112
  125.4 5.0 %collective-permute-done.11 = f32[2]{0:T(128)S(1)} collective-permute-done((f32[2]{0:T(128)S(1)}, f32[2]{0:T(128)S(1)}, u32[]{:S(2)}, u32[]{:S(2)}) %collective-permute-start.11) | collective-permute-done | bytes 40 | tf_op jit(solution)/shard_map/ppermute | solution.py:112
  132.8 3.5 %collective-permute-done.13 = f32[2]{0:T(128)S(1)} collective-permute-done((f32[2]{0:T(128)S(1)}, f32[2]{0:T(128)S(1)}, u32[]{:S(2)}, u32[]{:S(2)}) %collective-permute-start.13) | collective-permute-done | bytes 40 | tf_op jit(solution)/shard_map/ppermute | solution.py:112
  136.4 4.4 %collective-permute-done.14 = f32[2]{0:T(128)S(1)} collective-permute-done((f32[2]{0:T(128)S(1)}, f32[2]{0:T(128)S(1)}, u32[]{:S(2)}, u32[]{:S(2)}) %collective-permute-start.14) | collective-permute-done | bytes 40 | tf_op jit(solution)/shard_map/ppermute | solution.py:112
  140.8 5.9 %collective-permute-start.15 = (f32[2]{0:T(128)S(1)}, f32[2]{0:T(128)S(1)}, u32[]{:S(2)}, u32[]{:S(2)}) collective-permute-start(f32[2]{0:T(128)S(1)} %add.95), channel_id=1, source_target_pairs={{0,32},{4,36},{8,40},{12,44},{16,48},{20,52},{24,56},{28,60},{32,0... | collective-permute-start | bytes 32 | tf_op jit(solution)/shard_map/ppermute | solution.py:112
  148.3 3.6 %collective-permute-start.16 = (f32[2]{0:T(128)S(1)}, f32[2]{0:T(128)S(1)}, u32[]{:S(2)}, u32[]{:S(2)}) collective-permute-start(f32[2]{0:T(128)S(1)} %add.96), channel_id=1, source_target_pairs={{0,64},{4,68},{8,72},{12,76},{16,80},{20,84},{24,88},{28,92},{32,9... | collective-permute-start | bytes 32 | tf_op jit(solution)/shard_map/ppermute | solution.py:112
  153.4 6.4 %collective-permute-start.17 = (f32[2]{0:T(128)S(1)}, f32[2]{0:T(128)S(1)}, u32[]{:S(2)}, u32[]{:S(2)}) collective-permute-start(f32[2]{0:T(128)S(1)} %add.97), channel_id=1, source_target_pairs={{0,128},{4,132},{8,136},{12,140},{16,144},{20,148},{24,152},{28,15... | collective-permute-start | bytes 32 | tf_op jit(solution)/shard_map/ppermute | solution.py:112
  165.5 2.3 collective-permute-done.18
  169.1 2.9 collective-permute-start.19
  172.0 2.3 collective-permute-done.19
  178.3 2.3 collective-permute-done.21
  181.3 4.3 %collective-permute-start.22 = (f32[]{:T(128)}, f32[]{:T(128)}, u32[]{:S(2)}, u32[]{:S(2)}) collective-permute-start(f32[]{:T(128)} %add.102), channel_id=1, source_target_pairs={{0,16},{4,20},{8,24},{12,28},{16,0},{20,4},{24,8},{28,12},{32,48},... | collective-permute-start | bytes 20 | tf_op jit(solution)/shard_map/ppermute | solution.py:112
  186.6 7.3 %collective-permute-start.23 = (f32[]{:T(128)}, f32[]{:T(128)}, u32[]{:S(2)}, u32[]{:S(2)}) collective-permute-start(f32[]{:T(128)} %add.103), channel_id=1, source_target_pairs={{0,32},{4,36},{8,40},{12,44},{16,48},{20,52},{24,56},{28,60},{32,0... | collective-permute-start | bytes 20 | tf_op jit(solution)/shard_map/ppermute | solution.py:112
  194.9 4.0 %collective-permute-start.24 = (f32[]{:T(128)}, f32[]{:T(128)}, u32[]{:S(2)}, u32[]{:S(2)}) collective-permute-start(f32[]{:T(128)} %add.104), channel_id=1, source_target_pairs={{0,64},{4,68},{8,72},{12,76},{16,80},{20,84},{24,88},{28,92},{32,9... | collective-permute-start | bytes 20 | tf_op jit(solution)/shard_map/ppermute | solution.py:112
  199.9 4.3 %collective-permute-start.25 = (f32[]{:T(128)}, f32[]{:T(128)}, u32[]{:S(2)}, u32[]{:S(2)}) collective-permute-start(f32[]{:T(128)} %add.105), channel_id=1, source_target_pairs={{0,128},{4,132},{8,136},{12,140},{16,144},{20,148},{24,152},{28,15... | collective-permute-start | bytes 20 | tf_op jit(solution)/shard_map/ppermute | solution.py:112
  209.2 1.8 collective-permute-start.27
  211.8 6.9 %collective-permute-done.28 = bf16[64,3072]{1,0:T(8,128)(2,1)S(1)} collective-permute-done((bf16[64,3072]{1,0:T(8,128)(2,1)S(1)}, bf16[64,3072]{1,0:T(8,128)(2,1)S(1)}, u32[]{:S(2)}, u32[]{:S(2)}) %collective-permute-start.28) | collective-permute-done | bytes 393248 | tf_op jit(solution)/shard_map/ppermute | solution.py:122
  218.7 4.2 %collective-permute-done.27 = bf16[64,3072]{1,0:T(8,128)(2,1)S(1)} collective-permute-done((bf16[64,3072]{1,0:T(8,128)(2,1)S(1)}, bf16[64,3072]{1,0:T(8,128)(2,1)S(1)}, u32[]{:S(2)}, u32[]{:S(2)}) %collective-permute-start.27) | collective-permute-done | bytes 393248 | tf_op jit(solution)/shard_map/ppermute | solution.py:122
  224.5 1.9 collective-permute-start.29
  226.5 5.8 %collective-permute-start.30 = (bf16[64,1408]{1,0:T(8,128)(2,1)S(1)}, bf16[64,1408]{1,0:T(8,128)(2,1)S(1)}, u32[]{:S(2)}, u32[]{:S(2)}) collective-permute-start(bf16[64,1408]{1,0:T(8,128)(2,1)S(1)} %get-tuple-element.25), channel_id=1, source_target_pairs={{4,0},{8,4},{12,8},{16,12},{20,16},{24,20},{28,24},{32,28},{36,32}... | collective-permute-start | bytes 540680 | tf_op jit(solution)/shard_map/ppermute | solution.py:102
  233.5 1.8 collective-permute-done.30
  236.3 8.9 %shard_map.88 = f32[64,3072]{1,0:T(8,128)} custom-call(s32[24]{0:T(128)} %clamp_bitcast_fusion.begin_ref, bf16[46,64,128]{2,1,0:T(8,128)(2,1)} %bitcast_bitcast_fusion.win_ref, bf16[24,128,1536]{2,1,0:T(8,128)(2,1)} %shard_map.86.tile_ref, f32[64,3072]{1,0:T(8,128)} %get-tuple-element.11.p_ref, f32[64,1]{1,0:T(8,128)} %copy.38.noise_ref), custom_call_target="tpu_custom_call" | custom-call | tf_op jit(solution)/shard_map/pallas_call | solution.py:78
  245.3 2.1 multiply_reduce_fusion
  249.0 2.3 copy.41
  252.4 14.4 %scatter_custom_fusion = f32[256,3072]{0,1:T(8,128)S(1)} fusion(s32[3072]{0:T(1024)S(1)} %get-tuple-element.15, f32[3072,256]{1,0:T(8,128)} %copy.41, f32[]{:T(128)} %constant.12.clone.1), kind=kCustom, calls=%fused_computation.24 | custom fusion | bytes 3146240 | tf_op jit(solution)/shard_map/scatter | solution.py:175
  268.0 4.3 %collective-permute-start.32 = (f32[]{:T(128)}, f32[]{:T(128)}, u32[]{:S(2)}, u32[]{:S(2)}) collective-permute-start(f32[]{:T(128)} %add.108), channel_id=1, source_target_pairs={{0,2},{1,3},{2,0},{3,1},{4,6},{5,7},{6,4},{7,5},{8,10},{9,11},{10,... | collective-permute-start | bytes 20 | tf_op jit(solution)/shard_map/ppermute | solution.py:112
  277.3 2.3 collective-permute-done.34
  280.2 3.6 %collective-permute-start.35 = (f32[]{:T(128)}, f32[]{:T(128)}, u32[]{:S(2)}, u32[]{:S(2)}) collective-permute-start(f32[]{:T(128)} %add.111), channel_id=1, source_target_pairs={{0,16},{4,20},{8,24},{12,28},{16,0},{20,4},{24,8},{28,12},{32,48},... | collective-permute-start | bytes 20 | tf_op jit(solution)/shard_map/ppermute | solution.py:112
  285.5 6.1 %collective-permute-start.36 = (f32[]{:T(128)}, f32[]{:T(128)}, u32[]{:S(2)}, u32[]{:S(2)}) collective-permute-start(f32[]{:T(128)} %add.112), channel_id=1, source_target_pairs={{0,32},{4,36},{8,40},{12,44},{16,48},{20,52},{24,56},{28,60},{32,0... | collective-permute-start | bytes 20 | tf_op jit(solution)/shard_map/ppermute | solution.py:112
  293.7 2.7 collective-permute-start.37
  298.1 4.3 %collective-permute-start.38 = (f32[]{:T(128)}, f32[]{:T(128)}, u32[]{:S(2)}, u32[]{:S(2)}) collective-permute-start(f32[]{:T(128)} %add.114), channel_id=1, source_target_pairs={{0,128},{4,132},{8,136},{12,140},{16,144},{20,148},{24,152},{28,15... | collective-permute-start | bytes 20 | tf_op jit(solution)/shard_map/ppermute | solution.py:112
  304.0 2.6 fusion
  306.6 2.9 copy.43
  (100 shorter events, 54.1 us)
Async XLA Ops:
  0.6 2.4 copy-start.6
  16.2 7.3 %copy-start.8 = (f32[64,256]{1,0:T(8,128)S(1)}, f32[64,256]{1,0:T(8,128)}, u32[]{:S(2)}) copy-start(f32[64,256]{1,0:T(8,128)} %param.9) | copy-start | bytes 196612
  17.4 19.0 %copy-start.7 = (f32[64]{0:T(128)S(1)}, f32[64]{0:T(128)}, u32[]{:S(2)}) copy-start(f32[64]{0:T(128)} %param.10) | copy-start | bytes 772
  17.5 30.1 %collective-permute-start.5 = (bf16[64,3072]{1,0:T(8,128)(2,1)S(1)}, bf16[64,3072]{1,0:T(8,128)(2,1)S(1)}, u32[]{:S(2)}, u32[]{:S(2)}) collective-permute-start(bf16[64,3072]{1,0:T(8,128)(2,1)S(1)} %slice.65), channel_id=1, source_target_pairs={{3,0},{0,1},{1,2},{2,3},{7,4},{4,5},{5,6},{6,7},{11,8},{8,9},{9,10... | collective-permute-start | bytes 1179656 | tf_op jit(solution)/shard_map/ppermute | solution.py:122
  19.2 28.5 %collective-permute-start.4 = (bf16[64,3072]{1,0:T(8,128)(2,1)S(1)}, bf16[64,3072]{1,0:T(8,128)(2,1)S(1)}, u32[]{:S(2)}, u32[]{:S(2)}) collective-permute-start(bf16[64,3072]{1,0:T(8,128)(2,1)S(1)} %slice.65), channel_id=1, source_target_pairs={{2,0},{3,1},{0,2},{1,3},{6,4},{7,5},{4,6},{5,7},{10,8},{11,9},{8,1... | collective-permute-start | bytes 1179656 | tf_op jit(solution)/shard_map/ppermute | solution.py:122
  22.1 25.6 %collective-permute-start.3 = (bf16[64,3072]{1,0:T(8,128)(2,1)S(1)}, bf16[64,3072]{1,0:T(8,128)(2,1)}, u32[]{:S(2)}, u32[]{:S(2)}) collective-permute-start(bf16[64,3072]{1,0:T(8,128)(2,1)S(1)} %slice.65), channel_id=1, source_target_pairs={{1,0},{2,1},{3,2},{0,3},{5,4},{6,5},{7,6},{4,7},{9,8},{10,9},{11,1... | collective-permute-start | bytes 1179656 | tf_op jit(solution)/shard_map/ppermute | solution.py:122
  23.4 18.4 %collective-permute-start.1 = (f32[64,256]{1,0:T(8,128)S(1)}, f32[64,256]{1,0:T(8,128)S(1)}, u32[]{:S(2)}, u32[]{:S(2)}) collective-permute-start(f32[64,256]{1,0:T(8,128)S(1)} %copy-done.8), channel_id=1, source_target_pairs={{2,0},{3,1},{0,2},{1,3},{6,4},{7,5},{4,6},{5,7},{10,8},{11,9},{8,1... | collective-permute-start | bytes 196616 | tf_op jit(solution)/shard_map/ppermute | solution.py:122
  23.8 7.9 %collective-permute-start.8 = (f32[6,1408]{1,0:T(8,128)S(1)}, f32[6,1408]{1,0:T(8,128)S(1)}, u32[]{:S(2)}, u32[]{:S(2)}) collective-permute-start(f32[6,1408]{1,0:T(8,128)S(1)} %get-tuple-element.19), channel_id=1, source_target_pairs={{0,4},{4,8},{8,12},{12,16},{16,20},{20,24},{24,28},{28,32},{32,36}... | collective-permute-start | bytes 101384 | tf_op jit(solution)/shard_map/ppermute | solution.py:99
  31.7 7.1 %collective-permute-start.9 = (f32[6,1408]{1,0:T(8,128)S(1)}, f32[6,1408]{1,0:T(8,128)S(1)}, u32[]{:S(2)}, u32[]{:S(2)}) collective-permute-start(f32[6,1408]{1,0:T(8,128)S(1)} %get-tuple-element.20), channel_id=1, source_target_pairs={{4,0},{8,4},{12,8},{16,12},{20,16},{24,20},{28,24},{32,28},{36,32}... | collective-permute-start | bytes 101384 | tf_op jit(solution)/shard_map/ppermute | solution.py:102
  38.8 4.9 %collective-permute-start = (f32[64,256]{1,0:T(8,128)S(1)}, f32[64,256]{1,0:T(8,128)S(1)}, u32[]{:S(2)}, u32[]{:S(2)}) collective-permute-start(f32[64,256]{1,0:T(8,128)S(1)} %copy-done.8), channel_id=1, source_target_pairs={{1,0},{2,1},{3,2},{0,3},{5,4},{6,5},{7,6},{4,7},{9,8},{10,9},{11,1... | collective-permute-start | bytes 196616 | tf_op jit(solution)/shard_map/ppermute | solution.py:122
  41.8 5.5 %collective-permute-start.2 = (f32[64,256]{1,0:T(8,128)S(1)}, f32[64,256]{1,0:T(8,128)S(1)}, u32[]{:S(2)}, u32[]{:S(2)}) collective-permute-start(f32[64,256]{1,0:T(8,128)S(1)} %copy-done.8), channel_id=1, source_target_pairs={{3,0},{0,1},{1,2},{2,3},{7,4},{4,5},{5,6},{6,7},{11,8},{8,9},{9,10... | collective-permute-start | bytes 196616 | tf_op jit(solution)/shard_map/ppermute | solution.py:122
  49.6 57.6 %collective-permute-start.6 = (bf16[64,1408]{1,0:T(8,128)(2,1)S(1)}, bf16[64,1408]{1,0:T(8,128)(2,1)S(1)}, u32[]{:S(2)}, u32[]{:S(2)}) collective-permute-start(bf16[64,1408]{1,0:T(8,128)(2,1)S(1)} %get-tuple-element.26), channel_id=1, source_target_pairs={{0,4},{4,8},{8,12},{12,16},{16,20},{20,24},{24,28},{28,32},{32,36}... | collective-permute-start | bytes 540680 | tf_op jit(solution)/shard_map/ppermute | solution.py:99
  51.6 55.7 %collective-permute-start.7 = (bf16[64,1408]{1,0:T(8,128)(2,1)S(1)}, bf16[64,1408]{1,0:T(8,128)(2,1)S(1)}, u32[]{:S(2)}, u32[]{:S(2)}) collective-permute-start(bf16[64,1408]{1,0:T(8,128)(2,1)S(1)} %get-tuple-element.27), channel_id=1, source_target_pairs={{4,0},{8,4},{12,8},{16,12},{20,16},{24,20},{28,24},{32,28},{36,32}... | collective-permute-start | bytes 540680 | tf_op jit(solution)/shard_map/ppermute | solution.py:102
  117.2 46.0 %copy-start.3 = (f32[64,3072]{1,0:T(8,128)S(1)}, f32[64,3072]{1,0:T(8,128)}, u32[]{:S(2)}) copy-start(f32[64,3072]{1,0:T(8,128)} %shard_map.87) | copy-start | bytes 2359300
  120.5 3.6 %collective-permute-start.10 = (f32[2]{0:T(128)S(1)}, f32[2]{0:T(128)S(1)}, u32[]{:S(2)}, u32[]{:S(2)}) collective-permute-start(f32[2]{0:T(128)S(1)} %pad_maximum_fusion.2), channel_id=1, source_target_pairs={{0,1},{1,0},{2,3},{3,2},{4,5},{5,4},{6,7},{7,6},{8,9},{9,8},{10,11... | collective-permute-start | bytes 32 | tf_op jit(solution)/shard_map/ppermute | solution.py:112
  125.3 5.1 %collective-permute-start.11 = (f32[2]{0:T(128)S(1)}, f32[2]{0:T(128)S(1)}, u32[]{:S(2)}, u32[]{:S(2)}) collective-permute-start(f32[2]{0:T(128)S(1)} %fusion.39), channel_id=1, source_target_pairs={{0,2},{1,3},{2,0},{3,1},{4,6},{5,7},{6,4},{7,5},{8,10},{9,11},{10,... | collective-permute-start | bytes 32 | tf_op jit(solution)/shard_map/ppermute | solution.py:112
  131.7 1.1 collective-permute-start.12
  132.8 3.5 %collective-permute-start.13 = (f32[2]{0:T(128)S(1)}, f32[2]{0:T(128)S(1)}, u32[]{:S(2)}, u32[]{:S(2)}) collective-permute-start(f32[2]{0:T(128)S(1)} %add.93), channel_id=1, source_target_pairs={{0,8},{4,12},{8,0},{12,4},{16,24},{20,28},{24,16},{28,20},{32,40},... | collective-permute-start | bytes 32 | tf_op jit(solution)/shard_map/ppermute | solution.py:112
  136.4 4.4 %collective-permute-start.14 = (f32[2]{0:T(128)S(1)}, f32[2]{0:T(128)S(1)}, u32[]{:S(2)}, u32[]{:S(2)}) collective-permute-start(f32[2]{0:T(128)S(1)} %add.94), channel_id=1, source_target_pairs={{0,16},{4,20},{8,24},{12,28},{16,0},{20,4},{24,8},{28,12},{32,48},... | collective-permute-start | bytes 32 | tf_op jit(solution)/shard_map/ppermute | solution.py:112
  140.8 7.5 %collective-permute-start.15 = (f32[2]{0:T(128)S(1)}, f32[2]{0:T(128)S(1)}, u32[]{:S(2)}, u32[]{:S(2)}) collective-permute-start(f32[2]{0:T(128)S(1)} %add.95), channel_id=1, source_target_pairs={{0,32},{4,36},{8,40},{12,44},{16,48},{20,52},{24,56},{28,60},{32,0... | collective-permute-start | bytes 32 | tf_op jit(solution)/shard_map/ppermute | solution.py:112
  148.3 5.2 %collective-permute-start.16 = (f32[2]{0:T(128)S(1)}, f32[2]{0:T(128)S(1)}, u32[]{:S(2)}, u32[]{:S(2)}) collective-permute-start(f32[2]{0:T(128)S(1)} %add.96), channel_id=1, source_target_pairs={{0,64},{4,68},{8,72},{12,76},{16,80},{20,84},{24,88},{28,92},{32,9... | collective-permute-start | bytes 32 | tf_op jit(solution)/shard_map/ppermute | solution.py:112
  153.4 7.9 %collective-permute-start.17 = (f32[2]{0:T(128)S(1)}, f32[2]{0:T(128)S(1)}, u32[]{:S(2)}, u32[]{:S(2)}) collective-permute-start(f32[2]{0:T(128)S(1)} %add.97), channel_id=1, source_target_pairs={{0,128},{4,132},{8,136},{12,140},{16,144},{20,148},{24,152},{28,15... | collective-permute-start | bytes 32 | tf_op jit(solution)/shard_map/ppermute | solution.py:112
  164.0 60.5 %copy-start.4 = (f32[64,3072]{1,0:T(8,128)}, f32[64,3072]{1,0:T(8,128)S(1)}, u32[]{:S(2)}) copy-start(f32[64,3072]{1,0:T(8,128)S(1)} %get-tuple-element.13) | copy-start | bytes 2359300
  164.0 3.8 %collective-permute-start.18 = (f32[]{:T(128)}, f32[]{:T(128)}, u32[]{:S(2)}, u32[]{:S(2)}) collective-permute-start(f32[]{:T(128)} %get-tuple-element.12), channel_id=1, source_target_pairs={{0,1},{1,0},{2,3},{3,2},{4,5},{5,4},{6,7},{7,6},{8,9},{9,8},{10,11... | collective-permute-start | bytes 20 | tf_op jit(solution)/shard_map/ppermute | solution.py:112
  169.1 5.2 %collective-permute-start.19 = (f32[]{:T(128)}, f32[]{:T(128)}, u32[]{:S(2)}, u32[]{:S(2)}) collective-permute-start(f32[]{:T(128)} %add.99), channel_id=1, source_target_pairs={{0,2},{1,3},{2,0},{3,1},{4,6},{5,7},{6,4},{7,5},{8,10},{9,11},{10,... | collective-permute-start | bytes 20 | tf_op jit(solution)/shard_map/ppermute | solution.py:112
  175.0 1.3 collective-permute-start.20
  177.0 3.7 %collective-permute-start.21 = (f32[]{:T(128)}, f32[]{:T(128)}, u32[]{:S(2)}, u32[]{:S(2)}) collective-permute-start(f32[]{:T(128)} %add.101), channel_id=1, source_target_pairs={{0,8},{4,12},{8,0},{12,4},{16,24},{20,28},{24,16},{28,20},{32,40},... | collective-permute-start | bytes 20 | tf_op jit(solution)/shard_map/ppermute | solution.py:112
  181.3 4.6 %collective-permute-start.22 = (f32[]{:T(128)}, f32[]{:T(128)}, u32[]{:S(2)}, u32[]{:S(2)}) collective-permute-start(f32[]{:T(128)} %add.102), channel_id=1, source_target_pairs={{0,16},{4,20},{8,24},{12,28},{16,0},{20,4},{24,8},{28,12},{32,48},... | collective-permute-start | bytes 20 | tf_op jit(solution)/shard_map/ppermute | solution.py:112
  186.6 7.6 %collective-permute-start.23 = (f32[]{:T(128)}, f32[]{:T(128)}, u32[]{:S(2)}, u32[]{:S(2)}) collective-permute-start(f32[]{:T(128)} %add.103), channel_id=1, source_target_pairs={{0,32},{4,36},{8,40},{12,44},{16,48},{20,52},{24,56},{28,60},{32,0... | collective-permute-start | bytes 20 | tf_op jit(solution)/shard_map/ppermute | solution.py:112
  194.9 4.3 %collective-permute-start.24 = (f32[]{:T(128)}, f32[]{:T(128)}, u32[]{:S(2)}, u32[]{:S(2)}) collective-permute-start(f32[]{:T(128)} %add.104), channel_id=1, source_target_pairs={{0,64},{4,68},{8,72},{12,76},{16,80},{20,84},{24,88},{28,92},{32,9... | collective-permute-start | bytes 20 | tf_op jit(solution)/shard_map/ppermute | solution.py:112
  199.9 5.2 %collective-permute-start.25 = (f32[]{:T(128)}, f32[]{:T(128)}, u32[]{:S(2)}, u32[]{:S(2)}) collective-permute-start(f32[]{:T(128)} %add.105), channel_id=1, source_target_pairs={{0,128},{4,132},{8,136},{12,140},{16,144},{20,148},{24,152},{28,15... | collective-permute-start | bytes 20 | tf_op jit(solution)/shard_map/ppermute | solution.py:112
  207.7 11.0 %collective-permute-start.28 = (bf16[64,3072]{1,0:T(8,128)(2,1)S(1)}, bf16[64,3072]{1,0:T(8,128)(2,1)S(1)}, u32[]{:S(2)}, u32[]{:S(2)}) collective-permute-start(bf16[64,3072]{1,0:T(8,128)(2,1)S(1)} %get-tuple-element.10), channel_id=1, source_target_pairs={{3,0},{0,1},{1,2},{2,3},{7,4},{4,5},{5,6},{6,7},{11,8},{8,9},{9,10... | collective-permute-start | bytes 1179656 | tf_op jit(solution)/shard_map/ppermute | solution.py:122
  209.2 13.8 %collective-permute-start.27 = (bf16[64,3072]{1,0:T(8,128)(2,1)S(1)}, bf16[64,3072]{1,0:T(8,128)(2,1)S(1)}, u32[]{:S(2)}, u32[]{:S(2)}) collective-permute-start(bf16[64,3072]{1,0:T(8,128)(2,1)S(1)} %get-tuple-element.10), channel_id=1, source_target_pairs={{2,0},{3,1},{0,2},{1,3},{6,4},{7,5},{4,6},{5,7},{10,8},{11,9},{8,1... | collective-permute-start | bytes 1179656 | tf_op jit(solution)/shard_map/ppermute | solution.py:122
  211.0 12.6 %collective-permute-start.26 = (bf16[64,3072]{1,0:T(8,128)(2,1)S(1)}, bf16[64,3072]{1,0:T(8,128)(2,1)S(1)}, u32[]{:S(2)}, u32[]{:S(2)}) collective-permute-start(bf16[64,3072]{1,0:T(8,128)(2,1)S(1)} %get-tuple-element.10), channel_id=1, source_target_pairs={{1,0},{2,1},{3,2},{0,3},{5,4},{6,5},{7,6},{4,7},{9,8},{10,9},{11,1... | collective-permute-start | bytes 1179656 | tf_op jit(solution)/shard_map/ppermute | solution.py:122
  224.5 8.9 %collective-permute-start.29 = (bf16[64,1408]{1,0:T(8,128)(2,1)S(1)}, bf16[64,1408]{1,0:T(8,128)(2,1)S(1)}, u32[]{:S(2)}, u32[]{:S(2)}) collective-permute-start(bf16[64,1408]{1,0:T(8,128)(2,1)S(1)} %get-tuple-element.24), channel_id=1, source_target_pairs={{0,4},{4,8},{8,12},{12,16},{16,20},{20,24},{24,28},{28,32},{32,36}... | collective-permute-start | bytes 540680 | tf_op jit(solution)/shard_map/ppermute | solution.py:99
  226.5 8.8 %collective-permute-start.30 = (bf16[64,1408]{1,0:T(8,128)(2,1)S(1)}, bf16[64,1408]{1,0:T(8,128)(2,1)S(1)}, u32[]{:S(2)}, u32[]{:S(2)}) collective-permute-start(bf16[64,1408]{1,0:T(8,128)(2,1)S(1)} %get-tuple-element.25), channel_id=1, source_target_pairs={{4,0},{8,4},{12,8},{16,12},{20,16},{24,20},{28,24},{32,28},{36,32}... | collective-permute-start | bytes 540680 | tf_op jit(solution)/shard_map/ppermute | solution.py:102
  236.3 9.0 %copy-start = (f32[64,3072]{1,0:T(8,128)S(1)}, f32[64,3072]{1,0:T(8,128)}, u32[]{:S(2)}) copy-start(f32[64,3072]{1,0:T(8,128)} %get-tuple-element.11.p_ref) | copy-start | bytes 2359300
  245.2 2.1 copy-start.1
  245.2 2.1 copy-start.2
  251.3 15.5 %collective-permute-start.31 = (f32[]{:T(128)}, f32[]{:T(128)}, u32[]{:S(2)}, u32[]{:S(2)}) collective-permute-start(f32[]{:T(128)} %multiply_reduce_fusion), channel_id=1, source_target_pairs={{0,1},{1,0},{2,3},{3,2},{4,5},{5,4},{6,7},{7,6},{8,9},{9,8},{10,11... | collective-permute-start | bytes 20 | tf_op jit(solution)/shard_map/ppermute | solution.py:112
  268.0 5.2 %collective-permute-start.32 = (f32[]{:T(128)}, f32[]{:T(128)}, u32[]{:S(2)}, u32[]{:S(2)}) collective-permute-start(f32[]{:T(128)} %add.108), channel_id=1, source_target_pairs={{0,2},{1,3},{2,0},{3,1},{4,6},{5,7},{6,4},{7,5},{8,10},{9,11},{10,... | collective-permute-start | bytes 20 | tf_op jit(solution)/shard_map/ppermute | solution.py:112
  273.9 1.3 collective-permute-start.33
  275.9 3.7 %collective-permute-start.34 = (f32[]{:T(128)}, f32[]{:T(128)}, u32[]{:S(2)}, u32[]{:S(2)}) collective-permute-start(f32[]{:T(128)} %add.110), channel_id=1, source_target_pairs={{0,8},{4,12},{8,0},{12,4},{16,24},{20,28},{24,16},{28,20},{32,40},... | collective-permute-start | bytes 20 | tf_op jit(solution)/shard_map/ppermute | solution.py:112
  280.2 4.6 %collective-permute-start.35 = (f32[]{:T(128)}, f32[]{:T(128)}, u32[]{:S(2)}, u32[]{:S(2)}) collective-permute-start(f32[]{:T(128)} %add.111), channel_id=1, source_target_pairs={{0,16},{4,20},{8,24},{12,28},{16,0},{20,4},{24,8},{28,12},{32,48},... | collective-permute-start | bytes 20 | tf_op jit(solution)/shard_map/ppermute | solution.py:112
  285.5 7.6 %collective-permute-start.36 = (f32[]{:T(128)}, f32[]{:T(128)}, u32[]{:S(2)}, u32[]{:S(2)}) collective-permute-start(f32[]{:T(128)} %add.112), channel_id=1, source_target_pairs={{0,32},{4,36},{8,40},{12,44},{16,48},{20,52},{24,56},{28,60},{32,0... | collective-permute-start | bytes 20 | tf_op jit(solution)/shard_map/ppermute | solution.py:112
  293.7 3.7 %collective-permute-start.37 = (f32[]{:T(128)}, f32[]{:T(128)}, u32[]{:S(2)}, u32[]{:S(2)}) collective-permute-start(f32[]{:T(128)} %add.113), channel_id=1, source_target_pairs={{0,64},{4,68},{8,72},{12,76},{16,80},{20,84},{24,88},{28,92},{32,9... | collective-permute-start | bytes 20 | tf_op jit(solution)/shard_map/ppermute | solution.py:112
  298.1 5.2 %collective-permute-start.38 = (f32[]{:T(128)}, f32[]{:T(128)}, u32[]{:S(2)}, u32[]{:S(2)}) collective-permute-start(f32[]{:T(128)} %add.114), channel_id=1, source_target_pairs={{0,128},{4,132},{8,136},{12,140},{16,144},{20,148},{24,152},{28,15... | collective-permute-start | bytes 20 | tf_op jit(solution)/shard_map/ppermute | solution.py:112
  306.6 2.9 copy-start.5

commit v7 on v4

--- a/solution.py
+++ b/solution.py
@@ -162,6 +162,8 @@
     for iteration in range(ITERS):
         rounded = direction.astype(jnp.bfloat16)
         gathered = gather_chan(rounded)
+        if iteration == 0:
+            tiles, gathered, coreg_perm = lax.optimization_barrier((tiles, gathered, coreg_perm))
         mixed = jnp.dot(
             coreg_perm, gathered.astype(jnp.float32), precision=lax.Precision.HIGHEST
         )

time: 290 us -> 291 us (level)
  starting transfers between devices: 78.9 us -> 99.8 us
  waiting for transfers between devices: 81.2 us -> 61.7 us
    ppermute x24, starting transfers between devices: 43.8 us -> 58.3 us  [global_sum(): value = value + lax.ppermute(value, axis, pairs)]
    ppermute x24, waiting for transfers between devices: 56 us -> 42.3 us  [global_sum(): value = value + lax.ppermute(value, axis, pairs)]
    ppermute x9, waiting for transfers between devices: 22.2 us -> 15 us  [gather_chan(): parts.append(lax.ppermute(rounded, 'chan', pairs))]
    ppermute x3, starting transfers between devices: 17.3 us -> 21.6 us  [extended(): lax.ppermute(lax.slice_in_dim(block, 0, width, axis=dim), axis, backward)]
    unnamed x22 -> x20, local copies, waits for them, and re-layouts: 7.51 us -> 7.27 us
  transfers between devices with their start and end apart: 39 -> 39, of which waited for: 28 -> 29; matrix products, arithmetic and copies ran while one was open for 14% -> 9% of each run, Pallas kernels for 11% -> 11%
where the time goes in v7:
time: 291 us; the launch traced here: 289 us
  starting transfers between devices  99.8 us (34%)
  waiting for transfers between devices  61.7 us (21%)
  Pallas kernels  48.6 us (17%)
  local copies, waits for them, and re-layouts  38.4 us (13%)
  other arithmetic  23 us (8%)
  between operations  14 us (5%)
  matrix products  3.15 us (1%)
    ppermute x24, starting transfers between devices, global_sum(): value = value + lax.ppermute(value, axis, pairs)  58.3 us
    ppermute x24, waiting for transfers between devices, global_sum(): value = value + lax.ppermute(value, axis, pairs)  42.3 us
    pallas_call x1, Pallas kernels, build_tiles(): pl.pallas_call(kern, grid_spec=pltpu.PrefetchScalarGridSpec(num_scalar_pr...  30.9 us
    ppermute x3, starting transfers between devices, extended(): lax.ppermute(lax.slice_in_dim(block, 0, width, axis=dim), axis, backward)  21.6 us
    pallas_call x2, Pallas kernels, apply_operator(): pl.pallas_call(kern, grid_spec=pltpu.PrefetchScalarGridSpec(num_scalar_pr...  17.8 us
    ppermute x9, waiting for transfers between devices, gather_chan(): parts.append(lax.ppermute(rounded, 'chan', pairs))  15 us
    scatter x1, local copies, waits for them, and re-layouts, per_device(): unsorted = jnp.zeros_like(stacked).at[:, local_perm].set(stacked)  14.4 us
    ppermute x9, starting transfers between devices, gather_chan(): parts.append(lax.ppermute(rounded, 'chan', pairs))  14.1 us
  transfers between devices with their start and end apart: 39, of which 29 were waited for; matrix products, arithmetic and copies ran while one was open for 9% of the time, Pallas kernels for 11%

profile of v7, /device:TPU:2, one launch (start us, length us, event | category | flops | bytes accessed | tf_op | source)
XLA Modules:
  0.0 288.6 jit_solution(8193644748116728235)
XLA Ops:
  4.5 1.9 pad_maximum_fusion
  6.4 8.1 %gather_fusion = f32[3072,70]{1,0:T(8,128)S(1)} fusion(f32[70,3072]{0,1:T(8,128)S(1)} %pad_maximum_fusion, s32[3072]{0:T(1024)S(1)} %broadcast_clamp_fusion), kind=kCustom, calls=%fused_computation | custom fusion | bytes 1732608 | tf_op jit(solution)/shard_map/jit(_take)/gather | solution.py:138
  17.3 3.1 %collective-permute-start.2 = (bf16[64,3072]{1,0:T(8,128)(2,1)S(1)}, bf16[64,3072]{1,0:T(8,128)(2,1)S(1)}, u32[]{:S(2)}, u32[]{:S(2)}) collective-permute-start(bf16[64,3072]{1,0:T(8,128)(2,1)S(1)} %slice.63), channel_id=1, source_target_pairs={{1,0},{2,1},{3,2},{0,3},{5,4},{6,5},{7,6},{4,7},{9,8},{10,9},{11,1... | collective-permute-start | bytes 1179656 | tf_op jit(solution)/shard_map/ppermute | solution.py:124
  22.0 1.9 collective-permute-start
  23.9 6.3 %collective-permute-start.1 = (f32[6,1408]{1,0:T(8,128)S(1)}, f32[6,1408]{1,0:T(8,128)S(1)}, u32[]{:S(2)}, u32[]{:S(2)}) collective-permute-start(f32[6,1408]{1,0:T(8,128)S(1)} %get-tuple-element.24), channel_id=1, source_target_pairs={{4,0},{8,4},{12,8},{16,12},{20,16},{24,20},{28,24},{32,28},{36,32}... | collective-permute-start | bytes 101384 | tf_op jit(solution)/shard_map/ppermute | solution.py:104
  33.2 2.3 collective-permute-start.5
  37.2 2.9 %collective-permute-done.5 = f32[64,256]{1,0:T(8,128)S(1)} collective-permute-done((f32[64,256]{1,0:T(8,128)}, f32[64,256]{1,0:T(8,128)S(1)}, u32[]{:S(2)}, u32[]{:S(2)}) %collective-permute-start.5) | collective-permute-done | bytes 65568 | tf_op jit(solution)/shard_map/ppermute | solution.py:124
  42.0 30.9 %shard_map.86.tile_ref = bf16[24,128,1536]{2,1,0:T(8,128)(2,1)} custom-call(s32[24]{0:T(128)} %clamp_bitcast_fusion.begin_ref, s32[24]{0:T(128)} %count_ref.1, f32[24,128,8]{2,1,0:T(8,128)} %pad_bitcast_fusion.own_ref, f32[46,8,128]{2,1,0:T(8,128)} %pad_bitcast_fusion.1.win_ref), custom_call_target="tpu_custom_call" | custom-call | tf_op jit(solution)/shard_map/pallas_call | solution.py:46
  76.4 2.0 collective-permute-start.8
  78.4 9.5 %collective-permute-start.9 = (bf16[64,1408]{1,0:T(8,128)(2,1)S(1)}, bf16[64,1408]{1,0:T(8,128)(2,1)S(1)}, u32[]{:S(2)}, u32[]{:S(2)}) collective-permute-start(bf16[64,1408]{1,0:T(8,128)(2,1)S(1)} %get-tuple-element.28), channel_id=1, source_target_pairs={{4,0},{8,4},{12,8},{16,12},{20,16},{24,20},{28,24},{32,28},{36,32}... | collective-permute-start | bytes 540680 | tf_op jit(solution)/shard_map/ppermute | solution.py:104
  92.1 8.8 %shard_map.87 = f32[64,3072]{1,0:T(8,128)} custom-call(s32[24]{0:T(128)} %clamp_bitcast_fusion.begin_ref, bf16[46,64,128]{2,1,0:T(8,128)(2,1)} %bitcast_bitcast_fusion.1.win_ref, bf16[24,128,1536]{2,1,0:T(8,128)(2,1)} %shard_map.86.tile_ref, f32[64,3072]{1,0:T(8,128)} %slice.48.p_ref, f32[64,1]{1,0:T(8,128)} %copy.25.noise_ref), custom_call_target="tpu_custom_call" | custom-call | tf_op jit(solution)/shard_map/pallas_call | solution.py:80
  100.9 2.0 multiply_reduce_fusion.3
  104.5 3.3 %collective-permute-done.10 = f32[2]{0:T(128)S(1)} collective-permute-done((f32[2]{0:T(128)S(1)}, f32[2]{0:T(128)S(1)}, u32[]{:S(2)}, u32[]{:S(2)}) %collective-permute-start.10) | collective-permute-done | bytes 40 | tf_op jit(solution)/shard_map/ppermute | solution.py:114
  109.1 2.8 collective-permute-start.11
  111.9 2.3 collective-permute-done.11
  116.7 3.5 %collective-permute-done.13 = f32[2]{0:T(128)S(1)} collective-permute-done((f32[2]{0:T(128)S(1)}, f32[2]{0:T(128)S(1)}, u32[]{:S(2)}, u32[]{:S(2)}) %collective-permute-start.13) | collective-permute-done | bytes 40 | tf_op jit(solution)/shard_map/ppermute | solution.py:114
  120.2 2.2 collective-permute-start.14
  122.4 2.2 collective-permute-done.14
  124.7 5.1 %collective-permute-start.15 = (f32[2]{0:T(128)S(1)}, f32[2]{0:T(128)S(1)}, u32[]{:S(2)}, u32[]{:S(2)}) collective-permute-start(f32[2]{0:T(128)S(1)} %add.99), channel_id=1, source_target_pairs={{0,32},{4,36},{8,40},{12,44},{16,48},{20,52},{24,56},{28,60},{32,0... | collective-permute-start | bytes 32 | tf_op jit(solution)/shard_map/ppermute | solution.py:114
  129.8 2.3 collective-permute-done.15
  132.1 3.5 %collective-permute-done.16 = f32[2]{0:T(128)S(1)} collective-permute-done((f32[2]{0:T(128)S(1)}, f32[2]{0:T(128)S(1)}, u32[]{:S(2)}, u32[]{:S(2)}) %collective-permute-start.16) | collective-permute-done | bytes 40 | tf_op jit(solution)/shard_map/ppermute | solution.py:114
  135.7 2.3 collective-permute-start.17
  138.0 2.7 collective-permute-done.17
  143.8 3.5 %collective-permute-done.18 = f32[]{:T(128)} collective-permute-done((f32[]{:T(128)}, f32[]{:T(128)}, u32[]{:S(2)}, u32[]{:S(2)}) %collective-permute-start.18) | collective-permute-done | bytes 36 | tf_op jit(solution)/shard_map/ppermute | solution.py:114
  148.5 4.1 %collective-permute-start.19 = (f32[]{:T(128)}, f32[]{:T(128)}, u32[]{:S(2)}, u32[]{:S(2)}) collective-permute-start(f32[]{:T(128)} %add.103), channel_id=1, source_target_pairs={{0,2},{1,3},{2,0},{3,1},{4,6},{5,7},{6,4},{7,5},{8,10},{9,11},{10,... | collective-permute-start | bytes 20 | tf_op jit(solution)/shard_map/ppermute | solution.py:114
  156.4 2.7 collective-permute-start.21
  160.7 3.6 %collective-permute-start.22 = (f32[]{:T(128)}, f32[]{:T(128)}, u32[]{:S(2)}, u32[]{:S(2)}) collective-permute-start(f32[]{:T(128)} %add.106), channel_id=1, source_target_pairs={{0,16},{4,20},{8,24},{12,28},{16,0},{20,4},{24,8},{28,12},{32,48},... | collective-permute-start | bytes 20 | tf_op jit(solution)/shard_map/ppermute | solution.py:114
  166.0 6.5 %collective-permute-start.23 = (f32[]{:T(128)}, f32[]{:T(128)}, u32[]{:S(2)}, u32[]{:S(2)}) collective-permute-start(f32[]{:T(128)} %add.107), channel_id=1, source_target_pairs={{0,32},{4,36},{8,40},{12,44},{16,48},{20,52},{24,56},{28,60},{32,0... | collective-permute-start | bytes 20 | tf_op jit(solution)/shard_map/ppermute | solution.py:114
  174.2 2.4 collective-permute-start.24
  178.6 3.7 %collective-permute-start.25 = (f32[]{:T(128)}, f32[]{:T(128)}, u32[]{:S(2)}, u32[]{:S(2)}) collective-permute-start(f32[]{:T(128)} %add.109), channel_id=1, source_target_pairs={{0,128},{4,132},{8,136},{12,140},{16,144},{20,148},{24,152},{28,15... | collective-permute-start | bytes 20 | tf_op jit(solution)/shard_map/ppermute | solution.py:114
  190.7 8.4 %collective-permute-done.26 = bf16[64,3072]{1,0:T(8,128)(2,1)S(1)} collective-permute-done((bf16[64,3072]{1,0:T(8,128)(2,1)S(1)}, bf16[64,3072]{1,0:T(8,128)(2,1)S(1)}, u32[]{:S(2)}, u32[]{:S(2)}) %collective-permute-start.26) | collective-permute-done | bytes 393248 | tf_op jit(solution)/shard_map/ppermute | solution.py:124
  199.1 3.7 %collective-permute-done.28 = bf16[64,3072]{1,0:T(8,128)(2,1)S(1)} collective-permute-done((bf16[64,3072]{1,0:T(8,128)(2,1)S(1)}, bf16[64,3072]{1,0:T(8,128)(2,1)S(1)}, u32[]{:S(2)}, u32[]{:S(2)}) %collective-permute-start.28) | collective-permute-done | bytes 393248 | tf_op jit(solution)/shard_map/ppermute | solution.py:124
  203.8 1.9 collective-permute-start.29
  205.7 5.8 %collective-permute-start.30 = (bf16[64,1408]{1,0:T(8,128)(2,1)S(1)}, bf16[64,1408]{1,0:T(8,128)(2,1)S(1)}, u32[]{:S(2)}, u32[]{:S(2)}) collective-permute-start(bf16[64,1408]{1,0:T(8,128)(2,1)S(1)} %get-tuple-element.26), channel_id=1, source_target_pairs={{4,0},{8,4},{12,8},{16,12},{20,16},{24,20},{28,24},{32,28},{36,32}... | collective-permute-start | bytes 540680 | tf_op jit(solution)/shard_map/ppermute | solution.py:104
  212.7 1.8 collective-permute-done.30
  215.5 9.0 %shard_map.88 = f32[64,3072]{1,0:T(8,128)} custom-call(s32[24]{0:T(128)} %clamp_bitcast_fusion.begin_ref, bf16[46,64,128]{2,1,0:T(8,128)(2,1)} %bitcast_bitcast_fusion.win_ref, bf16[24,128,1536]{2,1,0:T(8,128)(2,1)} %shard_map.86.tile_ref, f32[64,3072]{1,0:T(8,128)} %get-tuple-element.15.p_ref, f32[64,1]{1,0:T(8,128)} %copy.25.noise_ref), custom_call_target="tpu_custom_call" | custom-call | tf_op jit(solution)/shard_map/pallas_call | solution.py:80
  224.5 2.1 multiply_reduce_fusion
  228.2 2.4 copy.28
  230.6 14.4 %scatter_custom_fusion = f32[256,3072]{0,1:T(8,128)S(1)} fusion(s32[3072]{0:T(1024)S(1)} %get-tuple-element.19, f32[3072,256]{1,0:T(8,128)} %copy.28, f32[]{:T(128)} %constant.10.clone.1), kind=kCustom, calls=%fused_computation.19 | custom fusion | bytes 3146240 | tf_op jit(solution)/shard_map/scatter | solution.py:177
  246.2 3.5 %collective-permute-start.32 = (f32[]{:T(128)}, f32[]{:T(128)}, u32[]{:S(2)}, u32[]{:S(2)}) collective-permute-start(f32[]{:T(128)} %add.112), channel_id=1, source_target_pairs={{0,2},{1,3},{2,0},{3,1},{4,6},{5,7},{6,4},{7,5},{8,10},{9,11},{10,... | collective-permute-start | bytes 20 | tf_op jit(solution)/shard_map/ppermute | solution.py:114
  249.6 1.8 collective-permute-done.32
  255.3 2.3 collective-permute-done.34
  258.2 3.6 %collective-permute-start.35 = (f32[]{:T(128)}, f32[]{:T(128)}, u32[]{:S(2)}, u32[]{:S(2)}) collective-permute-start(f32[]{:T(128)} %add.115), channel_id=1, source_target_pairs={{0,16},{4,20},{8,24},{12,28},{16,0},{20,4},{24,8},{28,12},{32,48},... | collective-permute-start | bytes 20 | tf_op jit(solution)/shard_map/ppermute | solution.py:114
  263.4 6.1 %collective-permute-start.36 = (f32[]{:T(128)}, f32[]{:T(128)}, u32[]{:S(2)}, u32[]{:S(2)}) collective-permute-start(f32[]{:T(128)} %add.116), channel_id=1, source_target_pairs={{0,32},{4,36},{8,40},{12,44},{16,48},{20,52},{24,56},{28,60},{32,0... | collective-permute-start | bytes 20 | tf_op jit(solution)/shard_map/ppermute | solution.py:114
  273.1 2.3 collective-permute-done.37
  276.0 4.3 %collective-permute-start.38 = (f32[]{:T(128)}, f32[]{:T(128)}, u32[]{:S(2)}, u32[]{:S(2)}) collective-permute-start(f32[]{:T(128)} %add.118), channel_id=1, source_target_pairs={{0,128},{4,132},{8,136},{12,140},{16,144},{20,148},{24,152},{28,15... | collective-permute-start | bytes 20 | tf_op jit(solution)/shard_map/ppermute | solution.py:114
  281.8 2.6 fusion
  284.5 2.9 copy.29
  (95 shorter events, 57.4 us)
Async XLA Ops:
  0.6 2.2 copy-start.6
  17.3 56.9 %collective-permute-start.2 = (bf16[64,3072]{1,0:T(8,128)(2,1)S(1)}, bf16[64,3072]{1,0:T(8,128)(2,1)S(1)}, u32[]{:S(2)}, u32[]{:S(2)}) collective-permute-start(bf16[64,3072]{1,0:T(8,128)(2,1)S(1)} %slice.63), channel_id=1, source_target_pairs={{1,0},{2,1},{3,2},{0,3},{5,4},{6,5},{7,6},{4,7},{9,8},{10,9},{11,1... | collective-permute-start | bytes 1179656 | tf_op jit(solution)/shard_map/ppermute | solution.py:124
  20.4 53.8 %collective-permute-start.3 = (bf16[64,3072]{1,0:T(8,128)(2,1)S(1)}, bf16[64,3072]{1,0:T(8,128)(2,1)}, u32[]{:S(2)}, u32[]{:S(2)}) collective-permute-start(bf16[64,3072]{1,0:T(8,128)(2,1)S(1)} %slice.63), channel_id=1, source_target_pairs={{2,0},{3,1},{0,2},{1,3},{6,4},{7,5},{4,6},{5,7},{10,8},{11,9},{8,1... | collective-permute-start | bytes 1179656 | tf_op jit(solution)/shard_map/ppermute | solution.py:124
  21.0 53.2 %collective-permute-start.4 = (bf16[64,3072]{1,0:T(8,128)(2,1)S(1)}, bf16[64,3072]{1,0:T(8,128)(2,1)}, u32[]{:S(2)}, u32[]{:S(2)}) collective-permute-start(bf16[64,3072]{1,0:T(8,128)(2,1)S(1)} %slice.63), channel_id=1, source_target_pairs={{3,0},{0,1},{1,2},{2,3},{7,4},{4,5},{5,6},{6,7},{11,8},{8,9},{9,10... | collective-permute-start | bytes 1179656 | tf_op jit(solution)/shard_map/ppermute | solution.py:124
  22.0 11.2 %collective-permute-start = (f32[6,1408]{1,0:T(8,128)S(1)}, f32[6,1408]{1,0:T(8,128)S(1)}, u32[]{:S(2)}, u32[]{:S(2)}) collective-permute-start(f32[6,1408]{1,0:T(8,128)S(1)} %get-tuple-element.23), channel_id=1, source_target_pairs={{0,4},{4,8},{8,12},{12,16},{16,20},{20,24},{24,28},{28,32},{32,36}... | collective-permute-start | bytes 101384 | tf_op jit(solution)/shard_map/ppermute | solution.py:101
  23.9 11.6 %collective-permute-start.1 = (f32[6,1408]{1,0:T(8,128)S(1)}, f32[6,1408]{1,0:T(8,128)S(1)}, u32[]{:S(2)}, u32[]{:S(2)}) collective-permute-start(f32[6,1408]{1,0:T(8,128)S(1)} %get-tuple-element.24), channel_id=1, source_target_pairs={{4,0},{8,4},{12,8},{16,12},{20,16},{24,20},{28,24},{32,28},{36,32}... | collective-permute-start | bytes 101384 | tf_op jit(solution)/shard_map/ppermute | solution.py:104
  33.2 6.9 %collective-permute-start.5 = (f32[64,256]{1,0:T(8,128)}, f32[64,256]{1,0:T(8,128)S(1)}, u32[]{:S(2)}, u32[]{:S(2)}) collective-permute-start(f32[64,256]{1,0:T(8,128)} %param.9), channel_id=1, source_target_pairs={{1,0},{2,1},{3,2},{0,3},{5,4},{6,5},{7,6},{4,7},{9,8},{10,9},{11,1... | collective-permute-start | bytes 196616 | tf_op jit(solution)/shard_map/ppermute | solution.py:124
  35.4 37.4 %collective-permute-start.6 = (f32[64,256]{1,0:T(8,128)}, f32[64,256]{1,0:T(8,128)S(1)}, u32[]{:S(2)}, u32[]{:S(2)}) collective-permute-start(f32[64,256]{1,0:T(8,128)} %param.9), channel_id=1, source_target_pairs={{2,0},{3,1},{0,2},{1,3},{6,4},{7,5},{4,6},{5,7},{10,8},{11,9},{8,1... | collective-permute-start | bytes 196616 | tf_op jit(solution)/shard_map/ppermute | solution.py:124
  40.1 32.8 %collective-permute-start.7 = (f32[64,256]{1,0:T(8,128)}, f32[64,256]{1,0:T(8,128)S(1)}, u32[]{:S(2)}, u32[]{:S(2)}) collective-permute-start(f32[64,256]{1,0:T(8,128)} %param.9), channel_id=1, source_target_pairs={{3,0},{0,1},{1,2},{2,3},{7,4},{4,5},{5,6},{6,7},{11,8},{8,9},{9,10... | collective-permute-start | bytes 196616 | tf_op jit(solution)/shard_map/ppermute | solution.py:124
  76.4 12.5 %copy-start.7 = (f32[64]{0:T(128)S(1)}, f32[64]{0:T(128)}, u32[]{:S(2)}) copy-start(f32[64]{0:T(128)} %param.10) | copy-start | bytes 772
  76.4 13.2 %collective-permute-start.8 = (bf16[64,1408]{1,0:T(8,128)(2,1)S(1)}, bf16[64,1408]{1,0:T(8,128)(2,1)S(1)}, u32[]{:S(2)}, u32[]{:S(2)}) collective-permute-start(bf16[64,1408]{1,0:T(8,128)(2,1)S(1)} %get-tuple-element.27), channel_id=1, source_target_pairs={{0,4},{4,8},{8,12},{12,16},{16,20},{20,24},{24,28},{28,32},{32,36}... | collective-permute-start | bytes 540680 | tf_op jit(solution)/shard_map/ppermute | solution.py:101
  78.4 12.5 %collective-permute-start.9 = (bf16[64,1408]{1,0:T(8,128)(2,1)S(1)}, bf16[64,1408]{1,0:T(8,128)(2,1)S(1)}, u32[]{:S(2)}, u32[]{:S(2)}) collective-permute-start(bf16[64,1408]{1,0:T(8,128)(2,1)S(1)} %get-tuple-element.28), channel_id=1, source_target_pairs={{4,0},{8,4},{12,8},{16,12},{20,16},{24,20},{28,24},{32,28},{36,32}... | collective-permute-start | bytes 540680 | tf_op jit(solution)/shard_map/ppermute | solution.py:104
  100.9 41.8 %copy-start.3 = (f32[64,3072]{1,0:T(8,128)S(1)}, f32[64,3072]{1,0:T(8,128)}, u32[]{:S(2)}) copy-start(f32[64,3072]{1,0:T(8,128)} %shard_map.87) | copy-start | bytes 2359300
  104.2 3.6 %collective-permute-start.10 = (f32[2]{0:T(128)S(1)}, f32[2]{0:T(128)S(1)}, u32[]{:S(2)}, u32[]{:S(2)}) collective-permute-start(f32[2]{0:T(128)S(1)} %pad_maximum_fusion.2), channel_id=1, source_target_pairs={{0,1},{1,0},{2,3},{3,2},{4,5},{5,4},{6,7},{7,6},{8,9},{9,8},{10,11... | collective-permute-start | bytes 32 | tf_op jit(solution)/shard_map/ppermute | solution.py:114
  109.1 5.1 %collective-permute-start.11 = (f32[2]{0:T(128)S(1)}, f32[2]{0:T(128)S(1)}, u32[]{:S(2)}, u32[]{:S(2)}) collective-permute-start(f32[2]{0:T(128)S(1)} %fusion.29), channel_id=1, source_target_pairs={{0,2},{1,3},{2,0},{3,1},{4,6},{5,7},{6,4},{7,5},{8,10},{9,11},{10,... | collective-permute-start | bytes 32 | tf_op jit(solution)/shard_map/ppermute | solution.py:114
  115.5 1.1 collective-permute-start.12
  116.7 3.5 %collective-permute-start.13 = (f32[2]{0:T(128)S(1)}, f32[2]{0:T(128)S(1)}, u32[]{:S(2)}, u32[]{:S(2)}) collective-permute-start(f32[2]{0:T(128)S(1)} %add.97), channel_id=1, source_target_pairs={{0,8},{4,12},{8,0},{12,4},{16,24},{20,28},{24,16},{28,20},{32,40},... | collective-permute-start | bytes 32 | tf_op jit(solution)/shard_map/ppermute | solution.py:114
  120.2 4.4 %collective-permute-start.14 = (f32[2]{0:T(128)S(1)}, f32[2]{0:T(128)S(1)}, u32[]{:S(2)}, u32[]{:S(2)}) collective-permute-start(f32[2]{0:T(128)S(1)} %add.98), channel_id=1, source_target_pairs={{0,16},{4,20},{8,24},{12,28},{16,0},{20,4},{24,8},{28,12},{32,48},... | collective-permute-start | bytes 32 | tf_op jit(solution)/shard_map/ppermute | solution.py:114
  124.7 7.4 %collective-permute-start.15 = (f32[2]{0:T(128)S(1)}, f32[2]{0:T(128)S(1)}, u32[]{:S(2)}, u32[]{:S(2)}) collective-permute-start(f32[2]{0:T(128)S(1)} %add.99), channel_id=1, source_target_pairs={{0,32},{4,36},{8,40},{12,44},{16,48},{20,52},{24,56},{28,60},{32,0... | collective-permute-start | bytes 32 | tf_op jit(solution)/shard_map/ppermute | solution.py:114
  132.1 3.5 %collective-permute-start.16 = (f32[2]{0:T(128)S(1)}, f32[2]{0:T(128)S(1)}, u32[]{:S(2)}, u32[]{:S(2)}) collective-permute-start(f32[2]{0:T(128)S(1)} %add.100), channel_id=1, source_target_pairs={{0,64},{4,68},{8,72},{12,76},{16,80},{20,84},{24,88},{28,92},{32,9... | collective-permute-start | bytes 32 | tf_op jit(solution)/shard_map/ppermute | solution.py:114
  135.7 5.0 %collective-permute-start.17 = (f32[2]{0:T(128)S(1)}, f32[2]{0:T(128)S(1)}, u32[]{:S(2)}, u32[]{:S(2)}) collective-permute-start(f32[2]{0:T(128)S(1)} %add.101), channel_id=1, source_target_pairs={{0,128},{4,132},{8,136},{12,140},{16,144},{20,148},{24,152},{28,15... | collective-permute-start | bytes 32 | tf_op jit(solution)/shard_map/ppermute | solution.py:114
  143.5 60.3 %copy-start.4 = (f32[64,3072]{1,0:T(8,128)}, f32[64,3072]{1,0:T(8,128)S(1)}, u32[]{:S(2)}) copy-start(f32[64,3072]{1,0:T(8,128)S(1)} %get-tuple-element.17) | copy-start | bytes 2359300
  143.5 3.8 %collective-permute-start.18 = (f32[]{:T(128)}, f32[]{:T(128)}, u32[]{:S(2)}, u32[]{:S(2)}) collective-permute-start(f32[]{:T(128)} %get-tuple-element.16), channel_id=1, source_target_pairs={{0,1},{1,0},{2,3},{3,2},{4,5},{5,4},{6,7},{7,6},{8,9},{9,8},{10,11... | collective-permute-start | bytes 20 | tf_op jit(solution)/shard_map/ppermute | solution.py:114
  148.5 5.2 %collective-permute-start.19 = (f32[]{:T(128)}, f32[]{:T(128)}, u32[]{:S(2)}, u32[]{:S(2)}) collective-permute-start(f32[]{:T(128)} %add.103), channel_id=1, source_target_pairs={{0,2},{1,3},{2,0},{3,1},{4,6},{5,7},{6,4},{7,5},{8,10},{9,11},{10,... | collective-permute-start | bytes 20 | tf_op jit(solution)/shard_map/ppermute | solution.py:114
  154.4 1.3 collective-permute-start.20
  156.4 3.7 %collective-permute-start.21 = (f32[]{:T(128)}, f32[]{:T(128)}, u32[]{:S(2)}, u32[]{:S(2)}) collective-permute-start(f32[]{:T(128)} %add.105), channel_id=1, source_target_pairs={{0,8},{4,12},{8,0},{12,4},{16,24},{20,28},{24,16},{28,20},{32,40},... | collective-permute-start | bytes 20 | tf_op jit(solution)/shard_map/ppermute | solution.py:114
  160.7 4.6 %collective-permute-start.22 = (f32[]{:T(128)}, f32[]{:T(128)}, u32[]{:S(2)}, u32[]{:S(2)}) collective-permute-start(f32[]{:T(128)} %add.106), channel_id=1, source_target_pairs={{0,16},{4,20},{8,24},{12,28},{16,0},{20,4},{24,8},{28,12},{32,48},... | collective-permute-start | bytes 20 | tf_op jit(solution)/shard_map/ppermute | solution.py:114
  166.0 7.6 %collective-permute-start.23 = (f32[]{:T(128)}, f32[]{:T(128)}, u32[]{:S(2)}, u32[]{:S(2)}) collective-permute-start(f32[]{:T(128)} %add.107), channel_id=1, source_target_pairs={{0,32},{4,36},{8,40},{12,44},{16,48},{20,52},{24,56},{28,60},{32,0... | collective-permute-start | bytes 20 | tf_op jit(solution)/shard_map/ppermute | solution.py:114
  174.2 3.7 %collective-permute-start.24 = (f32[]{:T(128)}, f32[]{:T(128)}, u32[]{:S(2)}, u32[]{:S(2)}) collective-permute-start(f32[]{:T(128)} %add.108), channel_id=1, source_target_pairs={{0,64},{4,68},{8,72},{12,76},{16,80},{20,84},{24,88},{28,92},{32,9... | collective-permute-start | bytes 20 | tf_op jit(solution)/shard_map/ppermute | solution.py:114
  178.6 5.2 %collective-permute-start.25 = (f32[]{:T(128)}, f32[]{:T(128)}, u32[]{:S(2)}, u32[]{:S(2)}) collective-permute-start(f32[]{:T(128)} %add.109), channel_id=1, source_target_pairs={{0,128},{4,132},{8,136},{12,140},{16,144},{20,148},{24,152},{28,15... | collective-permute-start | bytes 20 | tf_op jit(solution)/shard_map/ppermute | solution.py:114
  186.5 12.6 %collective-permute-start.26 = (bf16[64,3072]{1,0:T(8,128)(2,1)S(1)}, bf16[64,3072]{1,0:T(8,128)(2,1)S(1)}, u32[]{:S(2)}, u32[]{:S(2)}) collective-permute-start(bf16[64,3072]{1,0:T(8,128)(2,1)S(1)} %get-tuple-element.14), channel_id=1, source_target_pairs={{1,0},{2,1},{3,2},{0,3},{5,4},{6,5},{7,6},{4,7},{9,8},{10,9},{11,1... | collective-permute-start | bytes 1179656 | tf_op jit(solution)/shard_map/ppermute | solution.py:124
  188.1 11.0 %collective-permute-start.27 = (bf16[64,3072]{1,0:T(8,128)(2,1)S(1)}, bf16[64,3072]{1,0:T(8,128)(2,1)S(1)}, u32[]{:S(2)}, u32[]{:S(2)}) collective-permute-start(bf16[64,3072]{1,0:T(8,128)(2,1)S(1)} %get-tuple-element.14), channel_id=1, source_target_pairs={{2,0},{3,1},{0,2},{1,3},{6,4},{7,5},{4,6},{5,7},{10,8},{11,9},{8,1... | collective-permute-start | bytes 1179656 | tf_op jit(solution)/shard_map/ppermute | solution.py:124
  189.2 13.5 %collective-permute-start.28 = (bf16[64,3072]{1,0:T(8,128)(2,1)S(1)}, bf16[64,3072]{1,0:T(8,128)(2,1)S(1)}, u32[]{:S(2)}, u32[]{:S(2)}) collective-permute-start(bf16[64,3072]{1,0:T(8,128)(2,1)S(1)} %get-tuple-element.14), channel_id=1, source_target_pairs={{3,0},{0,1},{1,2},{2,3},{7,4},{4,5},{5,6},{6,7},{11,8},{8,9},{9,10... | collective-permute-start | bytes 1179656 | tf_op jit(solution)/shard_map/ppermute | solution.py:124
  203.8 8.9 %collective-permute-start.29 = (bf16[64,1408]{1,0:T(8,128)(2,1)S(1)}, bf16[64,1408]{1,0:T(8,128)(2,1)S(1)}, u32[]{:S(2)}, u32[]{:S(2)}) collective-permute-start(bf16[64,1408]{1,0:T(8,128)(2,1)S(1)} %get-tuple-element.25), channel_id=1, source_target_pairs={{0,4},{4,8},{8,12},{12,16},{16,20},{20,24},{24,28},{28,32},{32,36}... | collective-permute-start | bytes 540680 | tf_op jit(solution)/shard_map/ppermute | solution.py:101
  205.7 8.8 %collective-permute-start.30 = (bf16[64,1408]{1,0:T(8,128)(2,1)S(1)}, bf16[64,1408]{1,0:T(8,128)(2,1)S(1)}, u32[]{:S(2)}, u32[]{:S(2)}) collective-permute-start(bf16[64,1408]{1,0:T(8,128)(2,1)S(1)} %get-tuple-element.26), channel_id=1, source_target_pairs={{4,0},{8,4},{12,8},{16,12},{20,16},{24,20},{28,24},{32,28},{36,32}... | collective-permute-start | bytes 540680 | tf_op jit(solution)/shard_map/ppermute | solution.py:104
  215.5 9.0 %copy-start = (f32[64,3072]{1,0:T(8,128)S(1)}, f32[64,3072]{1,0:T(8,128)}, u32[]{:S(2)}) copy-start(f32[64,3072]{1,0:T(8,128)} %get-tuple-element.15.p_ref) | copy-start | bytes 2359300
  224.5 2.1 copy-start.1
  224.5 2.1 copy-start.2
  226.6 18.4 %collective-permute-start.31 = (f32[]{:T(128)}, f32[]{:T(128)}, u32[]{:S(2)}, u32[]{:S(2)}) collective-permute-start(f32[]{:T(128)} %multiply_reduce_fusion), channel_id=1, source_target_pairs={{0,1},{1,0},{2,3},{3,2},{4,5},{5,4},{6,7},{7,6},{8,9},{9,8},{10,11... | collective-permute-start | bytes 20 | tf_op jit(solution)/shard_map/ppermute | solution.py:114
  246.2 5.2 %collective-permute-start.32 = (f32[]{:T(128)}, f32[]{:T(128)}, u32[]{:S(2)}, u32[]{:S(2)}) collective-permute-start(f32[]{:T(128)} %add.112), channel_id=1, source_target_pairs={{0,2},{1,3},{2,0},{3,1},{4,6},{5,7},{6,4},{7,5},{8,10},{9,11},{10,... | collective-permute-start | bytes 20 | tf_op jit(solution)/shard_map/ppermute | solution.py:114
  252.0 1.3 collective-permute-start.33
  253.9 3.7 %collective-permute-start.34 = (f32[]{:T(128)}, f32[]{:T(128)}, u32[]{:S(2)}, u32[]{:S(2)}) collective-permute-start(f32[]{:T(128)} %add.114), channel_id=1, source_target_pairs={{0,8},{4,12},{8,0},{12,4},{16,24},{20,28},{24,16},{28,20},{32,40},... | collective-permute-start | bytes 20 | tf_op jit(solution)/shard_map/ppermute | solution.py:114
  258.2 4.6 %collective-permute-start.35 = (f32[]{:T(128)}, f32[]{:T(128)}, u32[]{:S(2)}, u32[]{:S(2)}) collective-permute-start(f32[]{:T(128)} %add.115), channel_id=1, source_target_pairs={{0,16},{4,20},{8,24},{12,28},{16,0},{20,4},{24,8},{28,12},{32,48},... | collective-permute-start | bytes 20 | tf_op jit(solution)/shard_map/ppermute | solution.py:114
  263.4 7.6 %collective-permute-start.36 = (f32[]{:T(128)}, f32[]{:T(128)}, u32[]{:S(2)}, u32[]{:S(2)}) collective-permute-start(f32[]{:T(128)} %add.116), channel_id=1, source_target_pairs={{0,32},{4,36},{8,40},{12,44},{16,48},{20,52},{24,56},{28,60},{32,0... | collective-permute-start | bytes 20 | tf_op jit(solution)/shard_map/ppermute | solution.py:114
  271.7 3.7 %collective-permute-start.37 = (f32[]{:T(128)}, f32[]{:T(128)}, u32[]{:S(2)}, u32[]{:S(2)}) collective-permute-start(f32[]{:T(128)} %add.117), channel_id=1, source_target_pairs={{0,64},{4,68},{8,72},{12,76},{16,80},{20,84},{24,88},{28,92},{32,9... | collective-permute-start | bytes 20 | tf_op jit(solution)/shard_map/ppermute | solution.py:114
  276.0 5.2 %collective-permute-start.38 = (f32[]{:T(128)}, f32[]{:T(128)}, u32[]{:S(2)}, u32[]{:S(2)}) collective-permute-start(f32[]{:T(128)} %add.118), channel_id=1, source_target_pairs={{0,128},{4,132},{8,136},{12,140},{16,144},{20,148},{24,152},{28,15... | collective-permute-start | bytes 20 | tf_op jit(solution)/shard_map/ppermute | solution.py:114
  284.5 2.9 copy-start.5

commit v8 on v7

--- a/solution.py
+++ b/solution.py
@@ -16,32 +16,34 @@
     b = pl.program_id(0)
     start = begin_ref[b]
     count = count_ref[b]
-    own = own_ref[0]
-    parts = jnp.concatenate([win_ref[start + s] for s in range(slots)], axis=1)
+    own = own_ref[...]
+    parts = jnp.concatenate([win_ref[start + s] for s in range(slots)], axis=0)
     cross = jnp.dot(
-        own * -2.0, parts, precision=lax.Precision.HIGHEST, preferred_element_type=jnp.float32
-    )
-    own_sq = jnp.sum(own * own, axis=1, keepdims=True)
-    part_sq = jnp.sum(parts * parts, axis=0, keepdims=True)
+        parts, own * -2.0, precision=lax.Precision.HIGHEST, preferred_element_type=jnp.float32
+    )
+    own_sq = jnp.sum(own * own, axis=0, keepdims=True)
+    part_sq = jnp.sum(parts * parts, axis=1, keepdims=True)
     for s in range(slots):
-        cols = slice(s * runs, (s + 1) * runs)
+        rows = slice(s * runs, (s + 1) * runs)
 
         @pl.when(s < count)
         def _():
-            squared = jnp.maximum((own_sq + part_sq[:, cols]) + cross[:, cols], 0.0)
+            squared = jnp.maximum((own_sq + part_sq[rows]) + cross[rows], 0.0)
             radius_frac = jnp.sqrt(squared) * (1.0 / SUPPORT)
             remain = jnp.maximum(1.0 - radius_frac, 0.0)
             cubed = remain * remain * remain
             val = cubed * cubed * (6.0 * radius_frac + 1.0)
-            out_ref[0, :, cols] = val.astype(out_ref.dtype)
+            out_ref[0, rows, :] = val.astype(out_ref.dtype)
 
         @pl.when(s >= count)
         def _():
-            out_ref[0, :, cols] = jnp.zeros((runs, runs), out_ref.dtype)
-
-
-def build_tiles(begin, count, own_t, win_c, slots):
-    blocks, runs, dpad = own_t.shape
+            out_ref[0, rows, :] = jnp.zeros((runs, runs), out_ref.dtype)
+
+
+def build_tiles(begin, count, own_c, win_c, slots):
+    dpad, total = own_c.shape
+    runs = win_c.shape[1]
+    blocks = total // runs
     kern = functools.partial(tile_kernel, slots=slots, runs=runs)
     return pl.pallas_call(
         kern,
@@ -49,13 +51,13 @@
             num_scalar_prefetch=2,
             grid=(blocks,),
             in_specs=[
-                pl.BlockSpec((1, runs, dpad), lambda b, *_: (b, 0, 0)),
+                pl.BlockSpec((dpad, runs), lambda b, *_: (0, b)),
                 pl.BlockSpec(win_c.shape, lambda b, *_: (0, 0, 0)),
             ],
-            out_specs=pl.BlockSpec((1, runs, slots * runs), lambda b, *_: (b, 0, 0)),
+            out_specs=pl.BlockSpec((1, slots * runs, runs), lambda b, *_: (b, 0, 0)),
         ),
-        out_shape=jax.ShapeDtypeStruct((blocks, runs, slots * runs), jnp.bfloat16),
-    )(begin, count, own_t, win_c)
+        out_shape=jax.ShapeDtypeStruct((blocks, slots * runs, runs), jnp.bfloat16),
+    )(begin, count, own_c, win_c)
 
 
 def apply_kernel(begin_ref, win_ref, tile_ref, p_ref, noise_ref, out_ref, *, per_step, slots, runs):
@@ -65,15 +67,13 @@
         start = begin_ref[g * per_step + k]
         vals = win_ref[pl.ds(start, slots)]
         cat = jnp.concatenate([vals[s] for s in range(slots)], axis=1)
-        acc = lax.dot_general(
-            cat, tile_ref[k], (((1,), (1,)), ((), ())), preferred_element_type=jnp.float32
-        )
+        acc = jnp.dot(cat, tile_ref[k], preferred_element_type=jnp.float32)
         cols = slice(k * runs, (k + 1) * runs)
         out_ref[:, cols] = AMPLITUDE * acc + noise * p_ref[:, cols]
 
 
 def apply_operator(begin, win_v, tiles, direction, noise_col, per_step):
-    blocks, runs, width = tiles.shape
+    blocks, width, runs = tiles.shape
     slots = width // runs
     chans, total = direction.shape
     kern = functools.partial(apply_kernel, per_step=per_step, slots=slots, runs=runs)
@@ -84,7 +84,7 @@
             grid=(blocks // per_step,),
             in_specs=[
                 pl.BlockSpec(win_v.shape, lambda g, *_: (0, 0, 0)),
-                pl.BlockSpec((per_step, runs, width), lambda g, *_: (g, 0, 0)),
+                pl.BlockSpec((per_step, width, runs), lambda g, *_: (g, 0, 0)),
                 pl.BlockSpec((chans, per_step * runs), lambda g, *_: (0, g)),
                 pl.BlockSpec((chans, 1), lambda g, *_: (0, 0)),
             ],
@@ -147,14 +147,12 @@
     widened_coords = extended(sorted_coords, "samp", 1, reach_runs)
     win_c = jnp.pad(
         widened_coords.reshape(dims, window_blocks, block_runs), ((0, dpad - dims), (0, 0), (0, 0))
-    ).transpose(1, 0, 2)
-    own_t = jnp.pad(
-        sorted_coords.reshape(dims, blocks_local, block_runs), ((0, dpad - dims), (0, 0), (0, 0))
     ).transpose(1, 2, 0)
+    own_c = jnp.pad(sorted_coords, ((0, dpad - dims), (0, 0)))
     begin = jnp.clip(
         block_nbrs[:, 0] - (device_pos * blocks_local - halo), 0, window_blocks - slot_limit
     ).astype(jnp.int32)
-    tiles = build_tiles(begin, nbr_count.astype(jnp.int32), own_t, win_c, slot_limit)
+    tiles = build_tiles(begin, nbr_count.astype(jnp.int32), own_c, win_c, slot_limit)
     noise_col = noise[:, None]
     iterate = jnp.zeros_like(sorted_loads)
     remainder = sorted_loads

time: 291 us -> 295 us (1.014)
  waiting for transfers between devices: 61.7 us -> 81.2 us
  starting transfers between devices: 99.8 us -> 82 us
  local copies, waits for them, and re-layouts: 38.4 us -> 42.3 us
    ppermute x3, waiting for transfers between devices: 1.24 us -> 14 us  [extended(): lax.ppermute(lax.slice_in_dim(block, block.shape[dim] - width, None, axis...]
    ppermute x24, starting transfers between devices: 58.3 us -> 47.3 us  [global_sum(): value = value + lax.ppermute(value, axis, pairs)]
    ppermute x24, waiting for transfers between devices: 42.3 us -> 52.6 us  [global_sum(): value = value + lax.ppermute(value, axis, pairs)]
    ppermute x3, starting transfers between devices: 21.6 us -> 15.5 us  [extended(): lax.ppermute(lax.slice_in_dim(block, 0, width, axis=dim), axis, backward)]
    transpose x1, local copies, waits for them, and re-layouts: 0.69 us -> 3.85 us  [per_device(): win_c = jnp.pad(widened_coords.reshape(dims, window_blocks, block_runs),...]
    unnamed x20 -> x26, local copies, waits for them, and re-layouts: 7.27 us -> 7.55 us
  transfers between devices with their start and end apart: 39 -> 39, of which waited for: 29 -> 30; matrix products, arithmetic and copies ran while one was open for 9% -> 8% of each run, Pallas kernels for 11% -> 10%
where the time goes in v8:
time: 295 us; the launch traced here: 292 us
  starting transfers between devices  82 us (28%)
  waiting for transfers between devices  81.2 us (28%)
  Pallas kernels  46.8 us (16%)
  local copies, waits for them, and re-layouts  42.3 us (14%)
  other arithmetic  22.3 us (8%)
  between operations  14.9 us (5%)
    ppermute x24, waiting for transfers between devices, global_sum(): value = value + lax.ppermute(value, axis, pairs)  52.6 us
    ppermute x24, starting transfers between devices, global_sum(): value = value + lax.ppermute(value, axis, pairs)  47.3 us
    pallas_call x1, Pallas kernels, build_tiles(): pl.pallas_call(kern, grid_spec=pltpu.PrefetchScalarGridSpec(num_scalar_pr...  30.5 us
    pallas_call x2, Pallas kernels, apply_operator(): pl.pallas_call(kern, grid_spec=pltpu.PrefetchScalarGridSpec(num_scalar_pr...  16.3 us
    ppermute x3, starting transfers between devices, extended(): lax.ppermute(lax.slice_in_dim(block, 0, width, axis=dim), axis, backward)  15.5 us
    scatter x1, local copies, waits for them, and re-layouts, per_device(): unsorted = jnp.zeros_like(stacked).at[:, local_perm].set(stacked)  14.4 us
    ppermute x3, waiting for transfers between devices, extended(): lax.ppermute(lax.slice_in_dim(block, block.shape[dim] - width, None, axis...  14 us
    ppermute x9, waiting for transfers between devices, gather_chan(): parts.append(lax.ppermute(rounded, 'chan', pairs))  13.9 us
  transfers between devices with their start and end apart: 39, of which 30 were waited for; matrix products, arithmetic and copies ran while one was open for 8% of the time, Pallas kernels for 10%

profile of v8, /device:TPU:2, one launch (start us, length us, event | category | flops | bytes accessed | tf_op | source)
XLA Modules:
  0.0 291.7 jit_solution(11997264263488657291)
XLA Ops:
  4.0 1.9 pad_maximum_fusion
  5.9 8.1 %gather_fusion = f32[3072,70]{1,0:T(8,128)S(1)} fusion(f32[70,3072]{0,1:T(8,128)S(1)} %pad_maximum_fusion, s32[3072]{0:T(1024)S(1)} %broadcast_clamp_fusion), kind=kCustom, calls=%fused_computation | custom fusion | bytes 1732608 | tf_op jit(solution)/shard_map/jit(_take)/gather | solution.py:138
  18.4 2.9 collective-permute-start.3
  22.7 6.3 %collective-permute-start.1 = (f32[6,1408]{1,0:T(8,128)S(1)}, f32[6,1408]{1,0:T(8,128)S(1)}, u32[]{:S(2)}, u32[]{:S(2)}) collective-permute-start(f32[6,1408]{1,0:T(8,128)S(1)} %get-tuple-element.24), channel_id=1, source_target_pairs={{4,0},{8,4},{12,8},{16,12},{20,16},{24,20},{28,24},{32,28},{36,32}... | collective-permute-start | bytes 101384 | tf_op jit(solution)/shard_map/ppermute | solution.py:104
  29.0 1.9 collective-permute-start
  33.8 2.8 collective-permute-done
  37.0 2.2 copy.29
  42.1 3.9 %pad_bitcast_fusion.win_ref = f32[46,128,8]{2,1,0:T(8,128)} fusion(f32[6,46,128]{0,2,1:T(8,128)} %bitcast.34), kind=kLoop, calls=%fused_computation.5 | loop fusion | bytes 329728 | tf_op jit(solution)/shard_map/transpose | solution.py:150
  45.9 30.5 %shard_map.86.tile_ref = bf16[24,1536,128]{2,1,0:T(8,128)(2,1)} custom-call(s32[24]{0:T(128)} %clamp_bitcast_fusion.begin_ref, s32[24]{0:T(128)} %count_ref.1, f32[8,3072]{1,0:T(8,128)} %slice_select_fusion.own_ref, f32[46,128,8]{2,1,0:T(8,128)} %pad_bitcast_fusion.win_ref), custom_call_target="tpu_custom_call" | custom-call | tf_op jit(solution)/shard_map/pallas_call | solution.py:48
  78.0 7.2 %collective-permute-start.9 = (bf16[64,1408]{1,0:T(8,128)(2,1)S(1)}, bf16[64,1408]{1,0:T(8,128)(2,1)S(1)}, u32[]{:S(2)}, u32[]{:S(2)}) collective-permute-start(bf16[64,1408]{1,0:T(8,128)(2,1)S(1)} %get-tuple-element.28), channel_id=1, source_target_pairs={{4,0},{8,4},{12,8},{16,12},{20,16},{24,20},{28,24},{32,28},{36,32}... | collective-permute-start | bytes 540680 | tf_op jit(solution)/shard_map/ppermute | solution.py:104
  85.2 1.9 collective-permute-start.8
  88.8 5.3 %collective-permute-done.8 = bf16[64,1408]{1,0:T(8,128)(2,1)S(1)} collective-permute-done((bf16[64,1408]{1,0:T(8,128)(2,1)S(1)}, bf16[64,1408]{1,0:T(8,128)(2,1)S(1)}, u32[]{:S(2)}, u32[]{:S(2)}) %collective-permute-start.8) | collective-permute-done | bytes 180256 | tf_op jit(solution)/shard_map/ppermute | solution.py:101
  95.2 8.1 %shard_map.87 = f32[64,3072]{1,0:T(8,128)} custom-call(s32[24]{0:T(128)} %clamp_bitcast_fusion.begin_ref, bf16[46,64,128]{2,1,0:T(8,128)(2,1)} %bitcast_bitcast_fusion.1.win_ref, bf16[24,1536,128]{2,1,0:T(8,128)(2,1)} %shard_map.86.tile_ref, f32[64,3072]{1,0:T(8,128)} %slice.52.p_ref, f32[64,1]{1,0:T(8,128)} %copy.23.noise_ref), custom_call_target="tpu_custom_call" | custom-call | tf_op jit(solution)/shard_map/pallas_call | solution.py:80
  103.3 2.1 multiply_reduce_fusion.3
  112.6 4.2 %collective-permute-done.11 = f32[2]{0:T(128)S(1)} collective-permute-done((f32[2]{0:T(128)S(1)}, f32[2]{0:T(128)S(1)}, u32[]{:S(2)}, u32[]{:S(2)}) %collective-permute-start.11) | collective-permute-done | bytes 40 | tf_op jit(solution)/shard_map/ppermute | solution.py:114
  119.4 3.5 %collective-permute-done.13 = f32[2]{0:T(128)S(1)} collective-permute-done((f32[2]{0:T(128)S(1)}, f32[2]{0:T(128)S(1)}, u32[]{:S(2)}, u32[]{:S(2)}) %collective-permute-start.13) | collective-permute-done | bytes 40 | tf_op jit(solution)/shard_map/ppermute | solution.py:114
  122.9 4.4 %collective-permute-done.14 = f32[2]{0:T(128)S(1)} collective-permute-done((f32[2]{0:T(128)S(1)}, f32[2]{0:T(128)S(1)}, u32[]{:S(2)}, u32[]{:S(2)}) %collective-permute-start.14) | collective-permute-done | bytes 40 | tf_op jit(solution)/shard_map/ppermute | solution.py:114
  127.4 2.9 collective-permute-start.15
  130.3 4.5 %collective-permute-done.15 = f32[2]{0:T(128)S(1)} collective-permute-done((f32[2]{0:T(128)S(1)}, f32[2]{0:T(128)S(1)}, u32[]{:S(2)}, u32[]{:S(2)}) %collective-permute-start.15) | collective-permute-done | bytes 40 | tf_op jit(solution)/shard_map/ppermute | solution.py:114
  134.8 3.5 %collective-permute-done.16 = f32[2]{0:T(128)S(1)} collective-permute-done((f32[2]{0:T(128)S(1)}, f32[2]{0:T(128)S(1)}, u32[]{:S(2)}, u32[]{:S(2)}) %collective-permute-start.16) | collective-permute-done | bytes 40 | tf_op jit(solution)/shard_map/ppermute | solution.py:114
  138.4 3.8 %collective-permute-start.17 = (f32[2]{0:T(128)S(1)}, f32[2]{0:T(128)S(1)}, u32[]{:S(2)}, u32[]{:S(2)}) collective-permute-start(f32[2]{0:T(128)S(1)} %add.99), channel_id=1, source_target_pairs={{0,128},{4,132},{8,136},{12,140},{16,144},{20,148},{24,152},{28,15... | collective-permute-start | bytes 32 | tf_op jit(solution)/shard_map/ppermute | solution.py:114
  148.2 1.9 collective-permute-done.18
  151.4 2.2 collective-permute-start.19
  153.6 2.8 collective-permute-done.19
  160.3 2.2 collective-permute-done.21
  164.5 3.1 %collective-permute-done.22 = f32[]{:T(128)} collective-permute-done((f32[]{:T(128)}, f32[]{:T(128)}, u32[]{:S(2)}, u32[]{:S(2)}) %collective-permute-start.22) | collective-permute-done | bytes 36 | tf_op jit(solution)/shard_map/ppermute | solution.py:114
  168.3 4.5 %collective-permute-start.23 = (f32[]{:T(128)}, f32[]{:T(128)}, u32[]{:S(2)}, u32[]{:S(2)}) collective-permute-start(f32[]{:T(128)} %add.105), channel_id=1, source_target_pairs={{0,32},{4,36},{8,40},{12,44},{16,48},{20,52},{24,56},{28,60},{32,0... | collective-permute-start | bytes 20 | tf_op jit(solution)/shard_map/ppermute | solution.py:114
  172.8 2.9 %collective-permute-done.23 = f32[]{:T(128)} collective-permute-done((f32[]{:T(128)}, f32[]{:T(128)}, u32[]{:S(2)}, u32[]{:S(2)}) %collective-permute-start.23) | collective-permute-done | bytes 36 | tf_op jit(solution)/shard_map/ppermute | solution.py:114
  176.4 2.1 collective-permute-start.24
  180.6 4.9 %collective-permute-start.25 = (f32[]{:T(128)}, f32[]{:T(128)}, u32[]{:S(2)}, u32[]{:S(2)}) collective-permute-start(f32[]{:T(128)} %add.107), channel_id=1, source_target_pairs={{0,128},{4,132},{8,136},{12,140},{16,144},{20,148},{24,152},{28,15... | collective-permute-start | bytes 20 | tf_op jit(solution)/shard_map/ppermute | solution.py:114
  191.0 1.8 collective-permute-start.26
  192.8 11.8 %collective-permute-done.28 = bf16[64,3072]{1,0:T(8,128)(2,1)S(1)} collective-permute-done((bf16[64,3072]{1,0:T(8,128)(2,1)S(1)}, bf16[64,3072]{1,0:T(8,128)(2,1)S(1)}, u32[]{:S(2)}, u32[]{:S(2)}) %collective-permute-start.28) | collective-permute-done | bytes 393248 | tf_op jit(solution)/shard_map/ppermute | solution.py:124
  206.2 1.9 collective-permute-start.30
  208.2 2.4 collective-permute-start.29
  211.1 5.9 %collective-permute-done.29 = bf16[64,1408]{1,0:T(8,128)(2,1)S(1)} collective-permute-done((bf16[64,1408]{1,0:T(8,128)(2,1)S(1)}, bf16[64,1408]{1,0:T(8,128)(2,1)S(1)}, u32[]{:S(2)}, u32[]{:S(2)}) %collective-permute-start.29) | collective-permute-done | bytes 180256 | tf_op jit(solution)/shard_map/ppermute | solution.py:101
  218.2 8.2 %shard_map.88 = f32[64,3072]{1,0:T(8,128)} custom-call(s32[24]{0:T(128)} %clamp_bitcast_fusion.begin_ref, bf16[46,64,128]{2,1,0:T(8,128)(2,1)} %bitcast_bitcast_fusion.win_ref, bf16[24,1536,128]{2,1,0:T(8,128)(2,1)} %shard_map.86.tile_ref, f32[64,3072]{1,0:T(8,128)} %get-tuple-element.15.p_ref, f32[64,1]{1,0:T(8,128)} %copy.23.noise_ref), custom_call_target="tpu_custom_call" | custom-call | tf_op jit(solution)/shard_map/pallas_call | solution.py:80
  226.4 2.1 multiply_reduce_fusion
  230.1 2.4 copy.26
  233.9 14.4 %scatter_custom_fusion = f32[256,3072]{0,1:T(8,128)S(1)} fusion(s32[3072]{0:T(1024)S(1)} %get-tuple-element.19, f32[3072,256]{1,0:T(8,128)} %copy.26, f32[]{:T(128)} %constant.11.clone.1), kind=kCustom, calls=%fused_computation.19 | custom fusion | bytes 3146240 | tf_op jit(solution)/shard_map/scatter | solution.py:175
  249.6 4.1 %collective-permute-start.32 = (f32[]{:T(128)}, f32[]{:T(128)}, u32[]{:S(2)}, u32[]{:S(2)}) collective-permute-start(f32[]{:T(128)} %add.110), channel_id=1, source_target_pairs={{0,2},{1,3},{2,0},{3,1},{4,6},{5,7},{6,4},{7,5},{8,10},{9,11},{10,... | collective-permute-start | bytes 20 | tf_op jit(solution)/shard_map/ppermute | solution.py:114
  258.6 2.2 collective-permute-done.34
  262.8 3.1 %collective-permute-done.35 = f32[]{:T(128)} collective-permute-done((f32[]{:T(128)}, f32[]{:T(128)}, u32[]{:S(2)}, u32[]{:S(2)}) %collective-permute-start.35) | collective-permute-done | bytes 36 | tf_op jit(solution)/shard_map/ppermute | solution.py:114
  266.6 3.6 %collective-permute-start.36 = (f32[]{:T(128)}, f32[]{:T(128)}, u32[]{:S(2)}, u32[]{:S(2)}) collective-permute-start(f32[]{:T(128)} %add.114), channel_id=1, source_target_pairs={{0,32},{4,36},{8,40},{12,44},{16,48},{20,52},{24,56},{28,60},{32,0... | collective-permute-start | bytes 20 | tf_op jit(solution)/shard_map/ppermute | solution.py:114
  270.3 3.8 %collective-permute-done.36 = f32[]{:T(128)} collective-permute-done((f32[]{:T(128)}, f32[]{:T(128)}, u32[]{:S(2)}, u32[]{:S(2)}) %collective-permute-start.36) | collective-permute-done | bytes 36 | tf_op jit(solution)/shard_map/ppermute | solution.py:114
  276.2 2.2 collective-permute-done.37
  279.0 4.6 %collective-permute-start.38 = (f32[]{:T(128)}, f32[]{:T(128)}, u32[]{:S(2)}, u32[]{:S(2)}) collective-permute-start(f32[]{:T(128)} %add.116), channel_id=1, source_target_pairs={{0,128},{4,132},{8,136},{12,140},{16,144},{20,148},{24,152},{28,15... | collective-permute-start | bytes 20 | tf_op jit(solution)/shard_map/ppermute | solution.py:114
  284.8 2.6 fusion
  287.5 2.9 copy.27
  (101 shorter events, 58.0 us)
Async XLA Ops:
  0.6 3.3 %copy-start.7 = (s32[3072]{0:T(1024)S(1)}, s32[3072]{0:T(1024)}, u32[]{:S(2)}) copy-start(s32[3072]{0:T(1024)} %param.11) | copy-start | bytes 36868
  15.4 15.5 %copy-start.9 = (pred[8]{0:T(512)(128)(4,1)S(1)}, pred[8]{0:T(512)(128)(4,1)}, u32[]{:S(2)}) copy-start(pred[8]{0:T(512)(128)(4,1)} %constant.38.clone.1) | copy-start | bytes 28
  15.4 17.5 %copy-start.10 = (f32[64,256]{1,0:T(8,128)S(1)}, f32[64,256]{1,0:T(8,128)}, u32[]{:S(2)}) copy-start(f32[64,256]{1,0:T(8,128)} %param.9) | copy-start | bytes 196612
  16.8 60.0 %collective-permute-start.4 = (bf16[64,3072]{1,0:T(8,128)(2,1)S(1)}, bf16[64,3072]{1,0:T(8,128)(2,1)S(1)}, u32[]{:S(2)}, u32[]{:S(2)}) collective-permute-start(bf16[64,3072]{1,0:T(8,128)(2,1)S(1)} %slice.69), channel_id=1, source_target_pairs={{3,0},{0,1},{1,2},{2,3},{7,4},{4,5},{5,6},{6,7},{11,8},{8,9},{9,10... | collective-permute-start | bytes 1179656 | tf_op jit(solution)/shard_map/ppermute | solution.py:124
  18.4 58.4 %collective-permute-start.3 = (bf16[64,3072]{1,0:T(8,128)(2,1)S(1)}, bf16[64,3072]{1,0:T(8,128)(2,1)S(1)}, u32[]{:S(2)}, u32[]{:S(2)}) collective-permute-start(bf16[64,3072]{1,0:T(8,128)(2,1)S(1)} %slice.69), channel_id=1, source_target_pairs={{2,0},{3,1},{0,2},{1,3},{6,4},{7,5},{4,6},{5,7},{10,8},{11,9},{8,1... | collective-permute-start | bytes 1179656 | tf_op jit(solution)/shard_map/ppermute | solution.py:124
  21.3 55.5 %collective-permute-start.2 = (bf16[64,3072]{1,0:T(8,128)(2,1)S(1)}, bf16[64,3072]{1,0:T(8,128)(2,1)S(1)}, u32[]{:S(2)}, u32[]{:S(2)}) collective-permute-start(bf16[64,3072]{1,0:T(8,128)(2,1)S(1)} %slice.69), channel_id=1, source_target_pairs={{1,0},{2,1},{3,2},{0,3},{5,4},{6,5},{7,6},{4,7},{9,8},{10,9},{11,1... | collective-permute-start | bytes 1179656 | tf_op jit(solution)/shard_map/ppermute | solution.py:124
  22.7 10.3 %collective-permute-start.1 = (f32[6,1408]{1,0:T(8,128)S(1)}, f32[6,1408]{1,0:T(8,128)S(1)}, u32[]{:S(2)}, u32[]{:S(2)}) collective-permute-start(f32[6,1408]{1,0:T(8,128)S(1)} %get-tuple-element.24), channel_id=1, source_target_pairs={{4,0},{8,4},{12,8},{16,12},{20,16},{24,20},{28,24},{32,28},{36,32}... | collective-permute-start | bytes 101384 | tf_op jit(solution)/shard_map/ppermute | solution.py:104
  29.0 7.5 %collective-permute-start = (f32[6,1408]{1,0:T(8,128)S(1)}, f32[6,1408]{1,0:T(8,128)S(1)}, u32[]{:S(2)}, u32[]{:S(2)}) collective-permute-start(f32[6,1408]{1,0:T(8,128)S(1)} %get-tuple-element.23), channel_id=1, source_target_pairs={{0,4},{4,8},{8,12},{12,16},{16,20},{20,24},{24,28},{28,32},{32,36}... | collective-permute-start | bytes 101384 | tf_op jit(solution)/shard_map/ppermute | solution.py:101
  33.0 7.7 %collective-permute-start.7 = (f32[64,256]{1,0:T(8,128)S(1)}, f32[64,256]{1,0:T(8,128)S(1)}, u32[]{:S(2)}, u32[]{:S(2)}) collective-permute-start(f32[64,256]{1,0:T(8,128)S(1)} %copy-done.10), channel_id=1, source_target_pairs={{3,0},{0,1},{1,2},{2,3},{7,4},{4,5},{5,6},{6,7},{11,8},{8,9},{9,10... | collective-permute-start | bytes 196616 | tf_op jit(solution)/shard_map/ppermute | solution.py:124
  36.5 39.9 %collective-permute-start.6 = (f32[64,256]{1,0:T(8,128)S(1)}, f32[64,256]{1,0:T(8,128)S(1)}, u32[]{:S(2)}, u32[]{:S(2)}) collective-permute-start(f32[64,256]{1,0:T(8,128)S(1)} %copy-done.10), channel_id=1, source_target_pairs={{2,0},{3,1},{0,2},{1,3},{6,4},{7,5},{4,6},{5,7},{10,8},{11,9},{8,1... | collective-permute-start | bytes 196616 | tf_op jit(solution)/shard_map/ppermute | solution.py:124
  40.7 35.7 %collective-permute-start.5 = (f32[64,256]{1,0:T(8,128)S(1)}, f32[64,256]{1,0:T(8,128)S(1)}, u32[]{:S(2)}, u32[]{:S(2)}) collective-permute-start(f32[64,256]{1,0:T(8,128)S(1)} %copy-done.10), channel_id=1, source_target_pairs={{1,0},{2,1},{3,2},{0,3},{5,4},{6,5},{7,6},{4,7},{9,8},{10,9},{11,1... | collective-permute-start | bytes 196616 | tf_op jit(solution)/shard_map/ppermute | solution.py:124
  77.9 10.1 %copy-start.8 = (f32[64]{0:T(128)S(1)}, f32[64]{0:T(128)}, u32[]{:S(2)}) copy-start(f32[64]{0:T(128)} %param.10) | copy-start | bytes 772
  78.0 10.8 %collective-permute-start.9 = (bf16[64,1408]{1,0:T(8,128)(2,1)S(1)}, bf16[64,1408]{1,0:T(8,128)(2,1)S(1)}, u32[]{:S(2)}, u32[]{:S(2)}) collective-permute-start(bf16[64,1408]{1,0:T(8,128)(2,1)S(1)} %get-tuple-element.28), channel_id=1, source_target_pairs={{4,0},{8,4},{12,8},{16,12},{20,16},{24,20},{28,24},{32,28},{36,32}... | collective-permute-start | bytes 540680 | tf_op jit(solution)/shard_map/ppermute | solution.py:104
  85.2 8.9 %collective-permute-start.8 = (bf16[64,1408]{1,0:T(8,128)(2,1)S(1)}, bf16[64,1408]{1,0:T(8,128)(2,1)S(1)}, u32[]{:S(2)}, u32[]{:S(2)}) collective-permute-start(bf16[64,1408]{1,0:T(8,128)(2,1)S(1)} %get-tuple-element.27), channel_id=1, source_target_pairs={{0,4},{4,8},{8,12},{12,16},{16,20},{20,24},{24,28},{28,32},{32,36}... | collective-permute-start | bytes 540680 | tf_op jit(solution)/shard_map/ppermute | solution.py:101
  103.3 42.4 %copy-start.3 = (f32[64,3072]{1,0:T(8,128)S(1)}, f32[64,3072]{1,0:T(8,128)}, u32[]{:S(2)}) copy-start(f32[64,3072]{1,0:T(8,128)} %shard_map.87) | copy-start | bytes 2359300
  106.8 3.6 %collective-permute-start.10 = (f32[2]{0:T(128)S(1)}, f32[2]{0:T(128)S(1)}, u32[]{:S(2)}, u32[]{:S(2)}) collective-permute-start(f32[2]{0:T(128)S(1)} %pad_maximum_fusion.3), channel_id=1, source_target_pairs={{0,1},{1,0},{2,3},{3,2},{4,5},{5,4},{6,7},{7,6},{8,9},{9,8},{10,11... | collective-permute-start | bytes 32 | tf_op jit(solution)/shard_map/ppermute | solution.py:114
  111.8 5.1 %collective-permute-start.11 = (f32[2]{0:T(128)S(1)}, f32[2]{0:T(128)S(1)}, u32[]{:S(2)}, u32[]{:S(2)}) collective-permute-start(f32[2]{0:T(128)S(1)} %fusion.29), channel_id=1, source_target_pairs={{0,2},{1,3},{2,0},{3,1},{4,6},{5,7},{6,4},{7,5},{8,10},{9,11},{10,... | collective-permute-start | bytes 32 | tf_op jit(solution)/shard_map/ppermute | solution.py:114
  118.2 1.1 collective-permute-start.12
  119.4 3.5 %collective-permute-start.13 = (f32[2]{0:T(128)S(1)}, f32[2]{0:T(128)S(1)}, u32[]{:S(2)}, u32[]{:S(2)}) collective-permute-start(f32[2]{0:T(128)S(1)} %add.95), channel_id=1, source_target_pairs={{0,8},{4,12},{8,0},{12,4},{16,24},{20,28},{24,16},{28,20},{32,40},... | collective-permute-start | bytes 32 | tf_op jit(solution)/shard_map/ppermute | solution.py:114
  122.9 4.4 %collective-permute-start.14 = (f32[2]{0:T(128)S(1)}, f32[2]{0:T(128)S(1)}, u32[]{:S(2)}, u32[]{:S(2)}) collective-permute-start(f32[2]{0:T(128)S(1)} %add.96), channel_id=1, source_target_pairs={{0,16},{4,20},{8,24},{12,28},{16,0},{20,4},{24,8},{28,12},{32,48},... | collective-permute-start | bytes 32 | tf_op jit(solution)/shard_map/ppermute | solution.py:114
  127.4 7.4 %collective-permute-start.15 = (f32[2]{0:T(128)S(1)}, f32[2]{0:T(128)S(1)}, u32[]{:S(2)}, u32[]{:S(2)}) collective-permute-start(f32[2]{0:T(128)S(1)} %add.97), channel_id=1, source_target_pairs={{0,32},{4,36},{8,40},{12,44},{16,48},{20,52},{24,56},{28,60},{32,0... | collective-permute-start | bytes 32 | tf_op jit(solution)/shard_map/ppermute | solution.py:114
  134.8 3.5 %collective-permute-start.16 = (f32[2]{0:T(128)S(1)}, f32[2]{0:T(128)S(1)}, u32[]{:S(2)}, u32[]{:S(2)}) collective-permute-start(f32[2]{0:T(128)S(1)} %add.98), channel_id=1, source_target_pairs={{0,64},{4,68},{8,72},{12,76},{16,80},{20,84},{24,88},{28,92},{32,9... | collective-permute-start | bytes 32 | tf_op jit(solution)/shard_map/ppermute | solution.py:114
  138.4 5.3 %collective-permute-start.17 = (f32[2]{0:T(128)S(1)}, f32[2]{0:T(128)S(1)}, u32[]{:S(2)}, u32[]{:S(2)}) collective-permute-start(f32[2]{0:T(128)S(1)} %add.99), channel_id=1, source_target_pairs={{0,128},{4,132},{8,136},{12,140},{16,144},{20,148},{24,152},{28,15... | collective-permute-start | bytes 32 | tf_op jit(solution)/shard_map/ppermute | solution.py:114
  146.5 59.8 %copy-start.4 = (f32[64,3072]{1,0:T(8,128)}, f32[64,3072]{1,0:T(8,128)S(1)}, u32[]{:S(2)}) copy-start(f32[64,3072]{1,0:T(8,128)S(1)} %get-tuple-element.17) | copy-start | bytes 2359300
  146.5 3.6 %collective-permute-start.18 = (f32[]{:T(128)}, f32[]{:T(128)}, u32[]{:S(2)}, u32[]{:S(2)}) collective-permute-start(f32[]{:T(128)} %get-tuple-element.16), channel_id=1, source_target_pairs={{0,1},{1,0},{2,3},{3,2},{4,5},{5,4},{6,7},{7,6},{8,9},{9,8},{10,11... | collective-permute-start | bytes 20 | tf_op jit(solution)/shard_map/ppermute | solution.py:114
  151.4 5.1 %collective-permute-start.19 = (f32[]{:T(128)}, f32[]{:T(128)}, u32[]{:S(2)}, u32[]{:S(2)}) collective-permute-start(f32[]{:T(128)} %add.101), channel_id=1, source_target_pairs={{0,2},{1,3},{2,0},{3,1},{4,6},{5,7},{6,4},{7,5},{8,10},{9,11},{10,... | collective-permute-start | bytes 20 | tf_op jit(solution)/shard_map/ppermute | solution.py:114
  157.1 1.2 collective-permute-start.20
  158.9 3.6 %collective-permute-start.21 = (f32[]{:T(128)}, f32[]{:T(128)}, u32[]{:S(2)}, u32[]{:S(2)}) collective-permute-start(f32[]{:T(128)} %add.103), channel_id=1, source_target_pairs={{0,8},{4,12},{8,0},{12,4},{16,24},{20,28},{24,16},{28,20},{32,40},... | collective-permute-start | bytes 20 | tf_op jit(solution)/shard_map/ppermute | solution.py:114
  163.1 4.5 %collective-permute-start.22 = (f32[]{:T(128)}, f32[]{:T(128)}, u32[]{:S(2)}, u32[]{:S(2)}) collective-permute-start(f32[]{:T(128)} %add.104), channel_id=1, source_target_pairs={{0,16},{4,20},{8,24},{12,28},{16,0},{20,4},{24,8},{28,12},{32,48},... | collective-permute-start | bytes 20 | tf_op jit(solution)/shard_map/ppermute | solution.py:114
  168.3 7.5 %collective-permute-start.23 = (f32[]{:T(128)}, f32[]{:T(128)}, u32[]{:S(2)}, u32[]{:S(2)}) collective-permute-start(f32[]{:T(128)} %add.105), channel_id=1, source_target_pairs={{0,32},{4,36},{8,40},{12,44},{16,48},{20,52},{24,56},{28,60},{32,0... | collective-permute-start | bytes 20 | tf_op jit(solution)/shard_map/ppermute | solution.py:114
  176.4 3.6 %collective-permute-start.24 = (f32[]{:T(128)}, f32[]{:T(128)}, u32[]{:S(2)}, u32[]{:S(2)}) collective-permute-start(f32[]{:T(128)} %add.106), channel_id=1, source_target_pairs={{0,64},{4,68},{8,72},{12,76},{16,80},{20,84},{24,88},{28,92},{32,9... | collective-permute-start | bytes 20 | tf_op jit(solution)/shard_map/ppermute | solution.py:114
  180.6 5.1 %collective-permute-start.25 = (f32[]{:T(128)}, f32[]{:T(128)}, u32[]{:S(2)}, u32[]{:S(2)}) collective-permute-start(f32[]{:T(128)} %add.107), channel_id=1, source_target_pairs={{0,128},{4,132},{8,136},{12,140},{16,144},{20,148},{24,152},{28,15... | collective-permute-start | bytes 20 | tf_op jit(solution)/shard_map/ppermute | solution.py:114
  188.4 16.2 %collective-permute-start.28 = (bf16[64,3072]{1,0:T(8,128)(2,1)S(1)}, bf16[64,3072]{1,0:T(8,128)(2,1)S(1)}, u32[]{:S(2)}, u32[]{:S(2)}) collective-permute-start(bf16[64,3072]{1,0:T(8,128)(2,1)S(1)} %get-tuple-element.14), channel_id=1, source_target_pairs={{3,0},{0,1},{1,2},{2,3},{7,4},{4,5},{5,6},{6,7},{11,8},{8,9},{9,10... | collective-permute-start | bytes 1179656 | tf_op jit(solution)/shard_map/ppermute | solution.py:124
  190.1 14.4 %collective-permute-start.27 = (bf16[64,3072]{1,0:T(8,128)(2,1)S(1)}, bf16[64,3072]{1,0:T(8,128)(2,1)S(1)}, u32[]{:S(2)}, u32[]{:S(2)}) collective-permute-start(bf16[64,3072]{1,0:T(8,128)(2,1)S(1)} %get-tuple-element.14), channel_id=1, source_target_pairs={{2,0},{3,1},{0,2},{1,3},{6,4},{7,5},{4,6},{5,7},{10,8},{11,9},{8,1... | collective-permute-start | bytes 1179656 | tf_op jit(solution)/shard_map/ppermute | solution.py:124
  191.0 14.3 %collective-permute-start.26 = (bf16[64,3072]{1,0:T(8,128)(2,1)S(1)}, bf16[64,3072]{1,0:T(8,128)(2,1)S(1)}, u32[]{:S(2)}, u32[]{:S(2)}) collective-permute-start(bf16[64,3072]{1,0:T(8,128)(2,1)S(1)} %get-tuple-element.14), channel_id=1, source_target_pairs={{1,0},{2,1},{3,2},{0,3},{5,4},{6,5},{7,6},{4,7},{9,8},{10,9},{11,1... | collective-permute-start | bytes 1179656 | tf_op jit(solution)/shard_map/ppermute | solution.py:124
  206.2 4.9 %collective-permute-start.30 = (bf16[64,1408]{1,0:T(8,128)(2,1)S(1)}, bf16[64,1408]{1,0:T(8,128)(2,1)S(1)}, u32[]{:S(2)}, u32[]{:S(2)}) collective-permute-start(bf16[64,1408]{1,0:T(8,128)(2,1)S(1)} %get-tuple-element.26), channel_id=1, source_target_pairs={{4,0},{8,4},{12,8},{16,12},{20,16},{24,20},{28,24},{32,28},{36,32}... | collective-permute-start | bytes 540680 | tf_op jit(solution)/shard_map/ppermute | solution.py:104
  208.2 8.9 %collective-permute-start.29 = (bf16[64,1408]{1,0:T(8,128)(2,1)S(1)}, bf16[64,1408]{1,0:T(8,128)(2,1)S(1)}, u32[]{:S(2)}, u32[]{:S(2)}) collective-permute-start(bf16[64,1408]{1,0:T(8,128)(2,1)S(1)} %get-tuple-element.25), channel_id=1, source_target_pairs={{0,4},{4,8},{8,12},{12,16},{16,20},{20,24},{24,28},{28,32},{32,36}... | collective-permute-start | bytes 540680 | tf_op jit(solution)/shard_map/ppermute | solution.py:101
  218.2 8.2 %copy-start = (f32[64,3072]{1,0:T(8,128)S(1)}, f32[64,3072]{1,0:T(8,128)}, u32[]{:S(2)}) copy-start(f32[64,3072]{1,0:T(8,128)} %get-tuple-element.15.p_ref) | copy-start | bytes 2359300
  226.4 2.1 copy-start.1
  232.5 15.8 %collective-permute-start.31 = (f32[]{:T(128)}, f32[]{:T(128)}, u32[]{:S(2)}, u32[]{:S(2)}) collective-permute-start(f32[]{:T(128)} %multiply_reduce_fusion), channel_id=1, source_target_pairs={{0,1},{1,0},{2,3},{3,2},{4,5},{5,4},{6,7},{7,6},{8,9},{9,8},{10,11... | collective-permute-start | bytes 20 | tf_op jit(solution)/shard_map/ppermute | solution.py:114
  249.6 5.1 %collective-permute-start.32 = (f32[]{:T(128)}, f32[]{:T(128)}, u32[]{:S(2)}, u32[]{:S(2)}) collective-permute-start(f32[]{:T(128)} %add.110), channel_id=1, source_target_pairs={{0,2},{1,3},{2,0},{3,1},{4,6},{5,7},{6,4},{7,5},{8,10},{9,11},{10,... | collective-permute-start | bytes 20 | tf_op jit(solution)/shard_map/ppermute | solution.py:114
  255.3 1.2 collective-permute-start.33
  257.2 3.6 %collective-permute-start.34 = (f32[]{:T(128)}, f32[]{:T(128)}, u32[]{:S(2)}, u32[]{:S(2)}) collective-permute-start(f32[]{:T(128)} %add.112), channel_id=1, source_target_pairs={{0,8},{4,12},{8,0},{12,4},{16,24},{20,28},{24,16},{28,20},{32,40},... | collective-permute-start | bytes 20 | tf_op jit(solution)/shard_map/ppermute | solution.py:114
  261.5 4.5 %collective-permute-start.35 = (f32[]{:T(128)}, f32[]{:T(128)}, u32[]{:S(2)}, u32[]{:S(2)}) collective-permute-start(f32[]{:T(128)} %add.113), channel_id=1, source_target_pairs={{0,16},{4,20},{8,24},{12,28},{16,0},{20,4},{24,8},{28,12},{32,48},... | collective-permute-start | bytes 20 | tf_op jit(solution)/shard_map/ppermute | solution.py:114
  266.6 7.5 %collective-permute-start.36 = (f32[]{:T(128)}, f32[]{:T(128)}, u32[]{:S(2)}, u32[]{:S(2)}) collective-permute-start(f32[]{:T(128)} %add.114), channel_id=1, source_target_pairs={{0,32},{4,36},{8,40},{12,44},{16,48},{20,52},{24,56},{28,60},{32,0... | collective-permute-start | bytes 20 | tf_op jit(solution)/shard_map/ppermute | solution.py:114
  274.8 3.6 %collective-permute-start.37 = (f32[]{:T(128)}, f32[]{:T(128)}, u32[]{:S(2)}, u32[]{:S(2)}) collective-permute-start(f32[]{:T(128)} %add.115), channel_id=1, source_target_pairs={{0,64},{4,68},{8,72},{12,76},{16,80},{20,84},{24,88},{28,92},{32,9... | collective-permute-start | bytes 20 | tf_op jit(solution)/shard_map/ppermute | solution.py:114
  279.0 5.1 %collective-permute-start.38 = (f32[]{:T(128)}, f32[]{:T(128)}, u32[]{:S(2)}, u32[]{:S(2)}) collective-permute-start(f32[]{:T(128)} %add.116), channel_id=1, source_target_pairs={{0,128},{4,132},{8,136},{12,140},{16,144},{20,148},{24,152},{28,15... | collective-permute-start | bytes 20 | tf_op jit(solution)/shard_map/ppermute | solution.py:114
  287.5 2.9 copy-start.5
  (2 other events, 3.8 us)

commit v9 on v7

--- a/solution.py
+++ b/solution.py
@@ -145,6 +145,7 @@
     reach_runs = halo * block_runs
     window_blocks = blocks_local + 2 * halo
     widened_coords = extended(sorted_coords, "samp", 1, reach_runs)
+    widened_coords, sorted_loads = lax.optimization_barrier((widened_coords, sorted_loads))
     win_c = jnp.pad(
         widened_coords.reshape(dims, window_blocks, block_runs), ((0, dpad - dims), (0, 0), (0, 0))
     ).transpose(1, 0, 2)

time: 291 us -> 284 us (0.976)
  starting transfers between devices: 99.8 us -> 81.7 us
  waiting for transfers between devices: 61.7 us -> 72.8 us
    ppermute x24, waiting for transfers between devices: 42.3 us -> 57 us  [global_sum(): value = value + lax.ppermute(value, axis, pairs)]
    ppermute x24, starting transfers between devices: 58.3 us -> 43.7 us  [global_sum(): value = value + lax.ppermute(value, axis, pairs)]
    ppermute x9, waiting for transfers between devices: 15 us -> 10.5 us  [gather_chan(): parts.append(lax.ppermute(rounded, 'chan', pairs))]
    ppermute x3, starting transfers between devices: 21.6 us -> 18.1 us  [extended(): lax.ppermute(lax.slice_in_dim(block, 0, width, axis=dim), axis, backward)]
    unnamed x20 -> x26, local copies, waits for them, and re-layouts: 7.27 us -> 7.51 us
  transfers between devices with their start and end apart: 39 -> 39, of which waited for: 29 -> 29; matrix products, arithmetic and copies ran while one was open for 9% -> 13% of each run, Pallas kernels for 11% -> 11%
where the time goes in v9:
time: 284 us; the launch traced here: 282 us
  starting transfers between devices  81.7 us (29%)
  waiting for transfers between devices  72.8 us (26%)
  Pallas kernels  50.3 us (18%)
  local copies, waits for them, and re-layouts  37.6 us (13%)
  other arithmetic  22.8 us (8%)
  between operations  14.2 us (5%)
    ppermute x24, waiting for transfers between devices, global_sum(): value = value + lax.ppermute(value, axis, pairs)  57 us
    ppermute x24, starting transfers between devices, global_sum(): value = value + lax.ppermute(value, axis, pairs)  43.7 us
    pallas_call x1, Pallas kernels, build_tiles(): pl.pallas_call(kern, grid_spec=pltpu.PrefetchScalarGridSpec(num_scalar_pr...  32.4 us
    ppermute x3, starting transfers between devices, extended(): lax.ppermute(lax.slice_in_dim(block, 0, width, axis=dim), axis, backward)  18.1 us
    pallas_call x2, Pallas kernels, apply_operator(): pl.pallas_call(kern, grid_spec=pltpu.PrefetchScalarGridSpec(num_scalar_pr...  17.9 us
    scatter x1, local copies, waits for them, and re-layouts, per_device(): unsorted = jnp.zeros_like(stacked).at[:, local_perm].set(stacked)  14.4 us
    ppermute x9, starting transfers between devices, gather_chan(): parts.append(lax.ppermute(rounded, 'chan', pairs))  14 us
    ppermute x9, waiting for transfers between devices, gather_chan(): parts.append(lax.ppermute(rounded, 'chan', pairs))  10.5 us
  transfers between devices with their start and end apart: 39, of which 29 were waited for; matrix products, arithmetic and copies ran while one was open for 13% of the time, Pallas kernels for 11%

profile of v9, /device:TPU:2, one launch (start us, length us, event | category | flops | bytes accessed | tf_op | source)
XLA Modules:
  0.0 281.7 jit_solution(17967845933822257690)
XLA Ops:
  0.6 3.3 %collective-permute-start.6 = (f32[64,256]{1,0:T(8,128)}, f32[64,256]{1,0:T(8,128)S(1)}, u32[]{:S(2)}, u32[]{:S(2)}) collective-permute-start(f32[64,256]{1,0:T(8,128)} %param.9), channel_id=1, source_target_pairs={{2,0},{3,1},{0,2},{1,3},{6,4},{7,5},{4,6},{5,7},{10,8},{11,9},{8,1... | collective-permute-start | bytes 196616 | tf_op jit(solution)/shard_map/ppermute | solution.py:124
  9.0 1.9 pad_maximum_fusion
  10.9 8.1 %gather_fusion = f32[3072,70]{1,0:T(8,128)S(1)} fusion(f32[70,3072]{0,1:T(8,128)S(1)} %pad_maximum_fusion, s32[3072]{0:T(1024)S(1)} %broadcast_clamp_fusion), kind=kCustom, calls=%fused_computation | custom fusion | bytes 1732608 | tf_op jit(solution)/shard_map/jit(_take)/gather | solution.py:138
  21.7 1.9 collective-permute-start
  23.6 6.6 %collective-permute-start.1 = (f32[6,1408]{1,0:T(8,128)S(1)}, f32[6,1408]{1,0:T(8,128)S(1)}, u32[]{:S(2)}, u32[]{:S(2)}) collective-permute-start(f32[6,1408]{1,0:T(8,128)S(1)} %get-tuple-element.27), channel_id=1, source_target_pairs={{4,0},{8,4},{12,8},{16,12},{20,16},{24,20},{28,24},{32,28},{36,32}... | collective-permute-start | bytes 101384 | tf_op jit(solution)/shard_map/ppermute | solution.py:104
  34.9 2.5 collective-permute-start.2
  39.4 32.4 %shard_map.86.tile_ref = bf16[24,128,1536]{2,1,0:T(8,128)(2,1)} custom-call(s32[24]{0:T(128)} %clamp_bitcast_fusion.begin_ref, s32[24]{0:T(128)} %count_ref.1, f32[24,128,8]{2,1,0:T(8,128)} %pad_bitcast_fusion.own_ref, f32[46,8,128]{2,1,0:T(8,128)} %pad_bitcast_fusion.1.win_ref), custom_call_target="tpu_custom_call" | custom-call | tf_op jit(solution)/shard_map/pallas_call | solution.py:46
  73.3 1.9 collective-permute-start.8
  75.2 5.8 %collective-permute-start.9 = (bf16[64,1408]{1,0:T(8,128)(2,1)S(1)}, bf16[64,1408]{1,0:T(8,128)(2,1)S(1)}, u32[]{:S(2)}, u32[]{:S(2)}) collective-permute-start(bf16[64,1408]{1,0:T(8,128)(2,1)S(1)} %get-tuple-element.32), channel_id=1, source_target_pairs={{4,0},{8,4},{12,8},{16,12},{20,16},{24,20},{28,24},{32,28},{36,32}... | collective-permute-start | bytes 540680 | tf_op jit(solution)/shard_map/ppermute | solution.py:104
  85.0 8.9 %shard_map.87 = f32[64,3072]{1,0:T(8,128)} custom-call(s32[24]{0:T(128)} %clamp_bitcast_fusion.begin_ref, bf16[46,64,128]{2,1,0:T(8,128)(2,1)} %bitcast_bitcast_fusion.1.win_ref, bf16[24,128,1536]{2,1,0:T(8,128)(2,1)} %shard_map.86.tile_ref, f32[64,3072]{1,0:T(8,128)} %copy-done, f32[64,1]{1,0:T(8,128)} %copy.25.noise_ref), custom_call_target="tpu_custom_call" | custom-call | tf_op jit(solution)/shard_map/pallas_call | solution.py:80
  94.0 2.0 multiply_reduce_fusion.2
  97.3 1.8 collective-permute-start.10
  102.3 2.7 collective-permute-start.11
  105.0 2.4 collective-permute-done.11
  109.8 3.5 %collective-permute-done.13 = f32[2]{0:T(128)S(1)} collective-permute-done((f32[2]{0:T(128)S(1)}, f32[2]{0:T(128)S(1)}, u32[]{:S(2)}, u32[]{:S(2)}) %collective-permute-start.13) | collective-permute-done | bytes 40 | tf_op jit(solution)/shard_map/ppermute | solution.py:114
  113.4 4.4 %collective-permute-done.14 = f32[2]{0:T(128)S(1)} collective-permute-done((f32[2]{0:T(128)S(1)}, f32[2]{0:T(128)S(1)}, u32[]{:S(2)}, u32[]{:S(2)}) %collective-permute-start.14) | collective-permute-done | bytes 40 | tf_op jit(solution)/shard_map/ppermute | solution.py:114
  117.8 2.8 %collective-permute-start.15 = (f32[2]{0:T(128)S(1)}, f32[2]{0:T(128)S(1)}, u32[]{:S(2)}, u32[]{:S(2)}) collective-permute-start(f32[2]{0:T(128)S(1)} %add.99), channel_id=1, source_target_pairs={{0,32},{4,36},{8,40},{12,44},{16,48},{20,52},{24,56},{28,60},{32,0... | collective-permute-start | bytes 32 | tf_op jit(solution)/shard_map/ppermute | solution.py:114
  120.7 4.6 %collective-permute-done.15 = f32[2]{0:T(128)S(1)} collective-permute-done((f32[2]{0:T(128)S(1)}, f32[2]{0:T(128)S(1)}, u32[]{:S(2)}, u32[]{:S(2)}) %collective-permute-start.15) | collective-permute-done | bytes 40 | tf_op jit(solution)/shard_map/ppermute | solution.py:114
  125.3 3.5 %collective-permute-done.16 = f32[2]{0:T(128)S(1)} collective-permute-done((f32[2]{0:T(128)S(1)}, f32[2]{0:T(128)S(1)}, u32[]{:S(2)}, u32[]{:S(2)}) %collective-permute-start.16) | collective-permute-done | bytes 40 | tf_op jit(solution)/shard_map/ppermute | solution.py:114
  130.0 3.8 %collective-permute-done.17 = f32[2]{0:T(128)S(1)} collective-permute-done((f32[2]{0:T(128)S(1)}, f32[2]{0:T(128)S(1)}, u32[]{:S(2)}, u32[]{:S(2)}) %collective-permute-start.17) | collective-permute-done | bytes 40 | tf_op jit(solution)/shard_map/ppermute | solution.py:114
  138.4 2.0 collective-permute-done.18
  141.6 4.1 %collective-permute-start.19 = (f32[]{:T(128)}, f32[]{:T(128)}, u32[]{:S(2)}, u32[]{:S(2)}) collective-permute-start(f32[]{:T(128)} %add.103), channel_id=1, source_target_pairs={{0,2},{1,3},{2,0},{3,1},{4,6},{5,7},{6,4},{7,5},{8,10},{9,11},{10,... | collective-permute-start | bytes 20 | tf_op jit(solution)/shard_map/ppermute | solution.py:114
  150.7 2.3 collective-permute-done.21
  155.0 3.2 %collective-permute-done.22 = f32[]{:T(128)} collective-permute-done((f32[]{:T(128)}, f32[]{:T(128)}, u32[]{:S(2)}, u32[]{:S(2)}) %collective-permute-start.22) | collective-permute-done | bytes 36 | tf_op jit(solution)/shard_map/ppermute | solution.py:114
  158.8 4.6 %collective-permute-start.23 = (f32[]{:T(128)}, f32[]{:T(128)}, u32[]{:S(2)}, u32[]{:S(2)}) collective-permute-start(f32[]{:T(128)} %add.107), channel_id=1, source_target_pairs={{0,32},{4,36},{8,40},{12,44},{16,48},{20,52},{24,56},{28,60},{32,0... | collective-permute-start | bytes 20 | tf_op jit(solution)/shard_map/ppermute | solution.py:114
  163.3 3.1 %collective-permute-done.23 = f32[]{:T(128)} collective-permute-done((f32[]{:T(128)}, f32[]{:T(128)}, u32[]{:S(2)}, u32[]{:S(2)}) %collective-permute-start.23) | collective-permute-done | bytes 36 | tf_op jit(solution)/shard_map/ppermute | solution.py:114
  168.4 2.3 collective-permute-done.24
  171.3 2.6 collective-permute-start.25
  173.9 2.6 collective-permute-done.25
  180.9 2.9 %collective-permute-start.27 = (bf16[64,3072]{1,0:T(8,128)(2,1)S(1)}, bf16[64,3072]{1,0:T(8,128)(2,1)S(1)}, u32[]{:S(2)}, u32[]{:S(2)}) collective-permute-start(bf16[64,3072]{1,0:T(8,128)(2,1)S(1)} %get-tuple-element.16), channel_id=1, source_target_pairs={{2,0},{3,1},{0,2},{1,3},{6,4},{7,5},{4,6},{5,7},{10,8},{11,9},{8,1... | collective-permute-start | bytes 1179656 | tf_op jit(solution)/shard_map/ppermute | solution.py:124
  184.4 6.3 %collective-permute-done.28 = bf16[64,3072]{1,0:T(8,128)(2,1)S(1)} collective-permute-done((bf16[64,3072]{1,0:T(8,128)(2,1)S(1)}, bf16[64,3072]{1,0:T(8,128)(2,1)S(1)}, u32[]{:S(2)}, u32[]{:S(2)}) %collective-permute-start.28) | collective-permute-done | bytes 393248 | tf_op jit(solution)/shard_map/ppermute | solution.py:124
  190.7 4.2 %collective-permute-done.27 = bf16[64,3072]{1,0:T(8,128)(2,1)S(1)} collective-permute-done((bf16[64,3072]{1,0:T(8,128)(2,1)S(1)}, bf16[64,3072]{1,0:T(8,128)(2,1)S(1)}, u32[]{:S(2)}, u32[]{:S(2)}) %collective-permute-start.27) | collective-permute-done | bytes 393248 | tf_op jit(solution)/shard_map/ppermute | solution.py:124
  195.9 1.9 collective-permute-start.29
  197.8 5.8 %collective-permute-start.30 = (bf16[64,1408]{1,0:T(8,128)(2,1)S(1)}, bf16[64,1408]{1,0:T(8,128)(2,1)S(1)}, u32[]{:S(2)}, u32[]{:S(2)}) collective-permute-start(bf16[64,1408]{1,0:T(8,128)(2,1)S(1)} %get-tuple-element.30), channel_id=1, source_target_pairs={{4,0},{8,4},{12,8},{16,12},{20,16},{24,20},{28,24},{32,28},{36,32}... | collective-permute-start | bytes 540680 | tf_op jit(solution)/shard_map/ppermute | solution.py:104
  207.7 8.9 %shard_map.88 = f32[64,3072]{1,0:T(8,128)} custom-call(s32[24]{0:T(128)} %clamp_bitcast_fusion.begin_ref, bf16[46,64,128]{2,1,0:T(8,128)(2,1)} %bitcast_bitcast_fusion.win_ref, bf16[24,128,1536]{2,1,0:T(8,128)(2,1)} %shard_map.86.tile_ref, f32[64,3072]{1,0:T(8,128)} %get-tuple-element.17.p_ref, f32[64,1]{1,0:T(8,128)} %copy.25.noise_ref), custom_call_target="tpu_custom_call" | custom-call | tf_op jit(solution)/shard_map/pallas_call | solution.py:80
  216.7 2.1 multiply_reduce_fusion
  220.4 2.4 copy.28
  223.9 14.4 %scatter_custom_fusion = f32[256,3072]{0,1:T(8,128)S(1)} fusion(s32[3072]{0:T(1024)S(1)} %get-tuple-element.21, f32[3072,256]{1,0:T(8,128)} %copy.28, f32[]{:T(128)} %constant.10.clone.1), kind=kCustom, calls=%fused_computation.19 | custom fusion | bytes 3146240 | tf_op jit(solution)/shard_map/scatter | solution.py:178
  239.6 3.8 %collective-permute-start.32 = (f32[]{:T(128)}, f32[]{:T(128)}, u32[]{:S(2)}, u32[]{:S(2)}) collective-permute-start(f32[]{:T(128)} %add.112), channel_id=1, source_target_pairs={{0,2},{1,3},{2,0},{3,1},{4,6},{5,7},{6,4},{7,5},{8,10},{9,11},{10,... | collective-permute-start | bytes 20 | tf_op jit(solution)/shard_map/ppermute | solution.py:114
  248.6 2.2 collective-permute-done.34
  253.2 2.7 collective-permute-done.35
  256.6 3.9 %collective-permute-start.36 = (f32[]{:T(128)}, f32[]{:T(128)}, u32[]{:S(2)}, u32[]{:S(2)}) collective-permute-start(f32[]{:T(128)} %add.116), channel_id=1, source_target_pairs={{0,32},{4,36},{8,40},{12,44},{16,48},{20,52},{24,56},{28,60},{32,0... | collective-permute-start | bytes 20 | tf_op jit(solution)/shard_map/ppermute | solution.py:114
  260.6 3.5 %collective-permute-done.36 = f32[]{:T(128)} collective-permute-done((f32[]{:T(128)}, f32[]{:T(128)}, u32[]{:S(2)}, u32[]{:S(2)}) %collective-permute-start.36) | collective-permute-done | bytes 36 | tf_op jit(solution)/shard_map/ppermute | solution.py:114
  266.2 2.2 collective-permute-done.37
  269.0 2.6 collective-permute-start.38
  271.6 2.5 collective-permute-done.38
  274.8 2.6 fusion
  277.5 2.9 %copy.30 = f32[64,3072]{1,0:T(8,128)} copy(f32[64,3072]{0,1:T(8,128)} %get-tuple-element.22) | data formatting | bytes 1572864
  (101 shorter events, 57.7 us)
Async XLA Ops:
  0.6 6.7 %copy-start.8 = (f32[6,3072]{1,0:T(8,128)S(1)}, f32[6,3072]{1,0:T(8,128)}, u32[]{:S(2)}) copy-start(f32[6,3072]{1,0:T(8,128)} %param.8) | copy-start | bytes 221188
  0.6 38.0 %collective-permute-start.6 = (f32[64,256]{1,0:T(8,128)}, f32[64,256]{1,0:T(8,128)S(1)}, u32[]{:S(2)}, u32[]{:S(2)}) collective-permute-start(f32[64,256]{1,0:T(8,128)} %param.9), channel_id=1, source_target_pairs={{2,0},{3,1},{0,2},{1,3},{6,4},{7,5},{4,6},{5,7},{10,8},{11,9},{8,1... | collective-permute-start | bytes 196616 | tf_op jit(solution)/shard_map/ppermute | solution.py:124
  3.9 67.8 %collective-permute-start.5 = (f32[64,256]{1,0:T(8,128)}, f32[64,256]{1,0:T(8,128)S(1)}, u32[]{:S(2)}, u32[]{:S(2)}) collective-permute-start(f32[64,256]{1,0:T(8,128)} %param.9), channel_id=1, source_target_pairs={{1,0},{2,1},{3,2},{0,3},{5,4},{6,5},{7,6},{4,7},{9,8},{10,9},{11,1... | collective-permute-start | bytes 196616 | tf_op jit(solution)/shard_map/ppermute | solution.py:124
  21.7 11.2 %collective-permute-start = (f32[6,1408]{1,0:T(8,128)S(1)}, f32[6,1408]{1,0:T(8,128)S(1)}, u32[]{:S(2)}, u32[]{:S(2)}) collective-permute-start(f32[6,1408]{1,0:T(8,128)S(1)} %get-tuple-element.26), channel_id=1, source_target_pairs={{0,4},{4,8},{8,12},{12,16},{16,20},{20,24},{24,28},{28,32},{32,36}... | collective-permute-start | bytes 101384 | tf_op jit(solution)/shard_map/ppermute | solution.py:101
  23.6 9.3 %collective-permute-start.1 = (f32[6,1408]{1,0:T(8,128)S(1)}, f32[6,1408]{1,0:T(8,128)S(1)}, u32[]{:S(2)}, u32[]{:S(2)}) collective-permute-start(f32[6,1408]{1,0:T(8,128)S(1)} %get-tuple-element.27), channel_id=1, source_target_pairs={{4,0},{8,4},{12,8},{16,12},{20,16},{24,20},{28,24},{32,28},{36,32}... | collective-permute-start | bytes 101384 | tf_op jit(solution)/shard_map/ppermute | solution.py:104
  33.0 39.1 %collective-permute-start.4 = (bf16[64,3072]{1,0:T(8,128)(2,1)S(1)}, bf16[64,3072]{1,0:T(8,128)(2,1)S(1)}, u32[]{:S(2)}, u32[]{:S(2)}) collective-permute-start(bf16[64,3072]{1,0:T(8,128)(2,1)S(1)} %convert_element_type.18), channel_id=1, source_target_pairs={{3,0},{0,1},{1,2},{2,3},{7,4},{4,5},{5,6},{6,7},{11,8},{8,9},{9,10... | collective-permute-start | bytes 1179656 | tf_op jit(solution)/shard_map/ppermute | solution.py:124
  34.0 38.1 %collective-permute-start.3 = (bf16[64,3072]{1,0:T(8,128)(2,1)S(1)}, bf16[64,3072]{1,0:T(8,128)(2,1)S(1)}, u32[]{:S(2)}, u32[]{:S(2)}) collective-permute-start(bf16[64,3072]{1,0:T(8,128)(2,1)S(1)} %convert_element_type.18), channel_id=1, source_target_pairs={{2,0},{3,1},{0,2},{1,3},{6,4},{7,5},{4,6},{5,7},{10,8},{11,9},{8,1... | collective-permute-start | bytes 1179656 | tf_op jit(solution)/shard_map/ppermute | solution.py:124
  34.9 37.3 %collective-permute-start.2 = (bf16[64,3072]{1,0:T(8,128)(2,1)S(1)}, bf16[64,3072]{1,0:T(8,128)(2,1)S(1)}, u32[]{:S(2)}, u32[]{:S(2)}) collective-permute-start(bf16[64,3072]{1,0:T(8,128)(2,1)S(1)} %convert_element_type.18), channel_id=1, source_target_pairs={{1,0},{2,1},{3,2},{0,3},{5,4},{6,5},{7,6},{4,7},{9,8},{10,9},{11,1... | collective-permute-start | bytes 1179656 | tf_op jit(solution)/shard_map/ppermute | solution.py:124
  38.7 33.1 %collective-permute-start.7 = (f32[64,256]{1,0:T(8,128)S(1)}, f32[64,256]{1,0:T(8,128)S(1)}, u32[]{:S(2)}, u32[]{:S(2)}) collective-permute-start(f32[64,256]{1,0:T(8,128)S(1)} %copy-done.10), channel_id=1, source_target_pairs={{3,0},{0,1},{1,2},{2,3},{7,4},{4,5},{5,6},{6,7},{11,8},{8,9},{9,10... | collective-permute-start | bytes 196616 | tf_op jit(solution)/shard_map/ppermute | solution.py:124
  72.3 8.7 %copy-start.9 = (f32[64]{0:T(128)S(1)}, f32[64]{0:T(128)}, u32[]{:S(2)}) copy-start(f32[64]{0:T(128)} %param.10) | copy-start | bytes 772
  73.3 8.9 %collective-permute-start.8 = (bf16[64,1408]{1,0:T(8,128)(2,1)S(1)}, bf16[64,1408]{1,0:T(8,128)(2,1)S(1)}, u32[]{:S(2)}, u32[]{:S(2)}) collective-permute-start(bf16[64,1408]{1,0:T(8,128)(2,1)S(1)} %get-tuple-element.31), channel_id=1, source_target_pairs={{0,4},{4,8},{8,12},{12,16},{16,20},{20,24},{24,28},{28,32},{32,36}... | collective-permute-start | bytes 540680 | tf_op jit(solution)/shard_map/ppermute | solution.py:101
  75.2 8.8 %collective-permute-start.9 = (bf16[64,1408]{1,0:T(8,128)(2,1)S(1)}, bf16[64,1408]{1,0:T(8,128)(2,1)S(1)}, u32[]{:S(2)}, u32[]{:S(2)}) collective-permute-start(bf16[64,1408]{1,0:T(8,128)(2,1)S(1)} %get-tuple-element.32), channel_id=1, source_target_pairs={{4,0},{8,4},{12,8},{16,12},{20,16},{24,20},{28,24},{32,28},{36,32}... | collective-permute-start | bytes 540680 | tf_op jit(solution)/shard_map/ppermute | solution.py:104
  85.0 8.9 %copy-start.1 = (f32[64,3072]{1,0:T(8,128)S(1)}, f32[64,3072]{1,0:T(8,128)}, u32[]{:S(2)}) copy-start(f32[64,3072]{1,0:T(8,128)} %copy-done) | copy-start | bytes 2359300
  94.0 41.8 %copy-start.5 = (f32[64,3072]{1,0:T(8,128)S(1)}, f32[64,3072]{1,0:T(8,128)}, u32[]{:S(2)}) copy-start(f32[64,3072]{1,0:T(8,128)} %shard_map.87) | copy-start | bytes 2359300
  97.3 3.6 %collective-permute-start.10 = (f32[2]{0:T(128)S(1)}, f32[2]{0:T(128)S(1)}, u32[]{:S(2)}, u32[]{:S(2)}) collective-permute-start(f32[2]{0:T(128)S(1)} %pad_maximum_fusion.3), channel_id=1, source_target_pairs={{0,1},{1,0},{2,3},{3,2},{4,5},{5,4},{6,7},{7,6},{8,9},{9,8},{10,11... | collective-permute-start | bytes 32 | tf_op jit(solution)/shard_map/ppermute | solution.py:114
  102.3 5.1 %collective-permute-start.11 = (f32[2]{0:T(128)S(1)}, f32[2]{0:T(128)S(1)}, u32[]{:S(2)}, u32[]{:S(2)}) collective-permute-start(f32[2]{0:T(128)S(1)} %fusion.29), channel_id=1, source_target_pairs={{0,2},{1,3},{2,0},{3,1},{4,6},{5,7},{6,4},{7,5},{8,10},{9,11},{10,... | collective-permute-start | bytes 32 | tf_op jit(solution)/shard_map/ppermute | solution.py:114
  108.7 1.1 collective-permute-start.12
  109.8 3.5 %collective-permute-start.13 = (f32[2]{0:T(128)S(1)}, f32[2]{0:T(128)S(1)}, u32[]{:S(2)}, u32[]{:S(2)}) collective-permute-start(f32[2]{0:T(128)S(1)} %add.97), channel_id=1, source_target_pairs={{0,8},{4,12},{8,0},{12,4},{16,24},{20,28},{24,16},{28,20},{32,40},... | collective-permute-start | bytes 32 | tf_op jit(solution)/shard_map/ppermute | solution.py:114
  113.4 4.4 %collective-permute-start.14 = (f32[2]{0:T(128)S(1)}, f32[2]{0:T(128)S(1)}, u32[]{:S(2)}, u32[]{:S(2)}) collective-permute-start(f32[2]{0:T(128)S(1)} %add.98), channel_id=1, source_target_pairs={{0,16},{4,20},{8,24},{12,28},{16,0},{20,4},{24,8},{28,12},{32,48},... | collective-permute-start | bytes 32 | tf_op jit(solution)/shard_map/ppermute | solution.py:114
  117.8 7.4 %collective-permute-start.15 = (f32[2]{0:T(128)S(1)}, f32[2]{0:T(128)S(1)}, u32[]{:S(2)}, u32[]{:S(2)}) collective-permute-start(f32[2]{0:T(128)S(1)} %add.99), channel_id=1, source_target_pairs={{0,32},{4,36},{8,40},{12,44},{16,48},{20,52},{24,56},{28,60},{32,0... | collective-permute-start | bytes 32 | tf_op jit(solution)/shard_map/ppermute | solution.py:114
  125.3 3.5 %collective-permute-start.16 = (f32[2]{0:T(128)S(1)}, f32[2]{0:T(128)S(1)}, u32[]{:S(2)}, u32[]{:S(2)}) collective-permute-start(f32[2]{0:T(128)S(1)} %add.100), channel_id=1, source_target_pairs={{0,64},{4,68},{8,72},{12,76},{16,80},{20,84},{24,88},{28,92},{32,9... | collective-permute-start | bytes 32 | tf_op jit(solution)/shard_map/ppermute | solution.py:114
  128.8 5.0 %collective-permute-start.17 = (f32[2]{0:T(128)S(1)}, f32[2]{0:T(128)S(1)}, u32[]{:S(2)}, u32[]{:S(2)}) collective-permute-start(f32[2]{0:T(128)S(1)} %add.101), channel_id=1, source_target_pairs={{0,128},{4,132},{8,136},{12,140},{16,144},{20,148},{24,152},{28,15... | collective-permute-start | bytes 32 | tf_op jit(solution)/shard_map/ppermute | solution.py:114
  136.6 42.5 %copy-start.6 = (f32[64,3072]{1,0:T(8,128)}, f32[64,3072]{1,0:T(8,128)S(1)}, u32[]{:S(2)}) copy-start(f32[64,3072]{1,0:T(8,128)S(1)} %get-tuple-element.19) | copy-start | bytes 2359300
  136.6 3.8 %collective-permute-start.18 = (f32[]{:T(128)}, f32[]{:T(128)}, u32[]{:S(2)}, u32[]{:S(2)}) collective-permute-start(f32[]{:T(128)} %get-tuple-element.18), channel_id=1, source_target_pairs={{0,1},{1,0},{2,3},{3,2},{4,5},{5,4},{6,7},{7,6},{8,9},{9,8},{10,11... | collective-permute-start | bytes 20 | tf_op jit(solution)/shard_map/ppermute | solution.py:114
  141.6 5.2 %collective-permute-start.19 = (f32[]{:T(128)}, f32[]{:T(128)}, u32[]{:S(2)}, u32[]{:S(2)}) collective-permute-start(f32[]{:T(128)} %add.103), channel_id=1, source_target_pairs={{0,2},{1,3},{2,0},{3,1},{4,6},{5,7},{6,4},{7,5},{8,10},{9,11},{10,... | collective-permute-start | bytes 20 | tf_op jit(solution)/shard_map/ppermute | solution.py:114
  147.4 1.3 collective-permute-start.20
  149.3 3.7 %collective-permute-start.21 = (f32[]{:T(128)}, f32[]{:T(128)}, u32[]{:S(2)}, u32[]{:S(2)}) collective-permute-start(f32[]{:T(128)} %add.105), channel_id=1, source_target_pairs={{0,8},{4,12},{8,0},{12,4},{16,24},{20,28},{24,16},{28,20},{32,40},... | collective-permute-start | bytes 20 | tf_op jit(solution)/shard_map/ppermute | solution.py:114
  153.6 4.6 %collective-permute-start.22 = (f32[]{:T(128)}, f32[]{:T(128)}, u32[]{:S(2)}, u32[]{:S(2)}) collective-permute-start(f32[]{:T(128)} %add.106), channel_id=1, source_target_pairs={{0,16},{4,20},{8,24},{12,28},{16,0},{20,4},{24,8},{28,12},{32,48},... | collective-permute-start | bytes 20 | tf_op jit(solution)/shard_map/ppermute | solution.py:114
  158.8 7.6 %collective-permute-start.23 = (f32[]{:T(128)}, f32[]{:T(128)}, u32[]{:S(2)}, u32[]{:S(2)}) collective-permute-start(f32[]{:T(128)} %add.107), channel_id=1, source_target_pairs={{0,32},{4,36},{8,40},{12,44},{16,48},{20,52},{24,56},{28,60},{32,0... | collective-permute-start | bytes 20 | tf_op jit(solution)/shard_map/ppermute | solution.py:114
  167.0 3.7 %collective-permute-start.24 = (f32[]{:T(128)}, f32[]{:T(128)}, u32[]{:S(2)}, u32[]{:S(2)}) collective-permute-start(f32[]{:T(128)} %add.108), channel_id=1, source_target_pairs={{0,64},{4,68},{8,72},{12,76},{16,80},{20,84},{24,88},{28,92},{32,9... | collective-permute-start | bytes 20 | tf_op jit(solution)/shard_map/ppermute | solution.py:114
  171.3 5.2 %collective-permute-start.25 = (f32[]{:T(128)}, f32[]{:T(128)}, u32[]{:S(2)}, u32[]{:S(2)}) collective-permute-start(f32[]{:T(128)} %add.109), channel_id=1, source_target_pairs={{0,128},{4,132},{8,136},{12,140},{16,144},{20,148},{24,152},{28,15... | collective-permute-start | bytes 20 | tf_op jit(solution)/shard_map/ppermute | solution.py:114
  179.1 11.6 %collective-permute-start.28 = (bf16[64,3072]{1,0:T(8,128)(2,1)S(1)}, bf16[64,3072]{1,0:T(8,128)(2,1)S(1)}, u32[]{:S(2)}, u32[]{:S(2)}) collective-permute-start(bf16[64,3072]{1,0:T(8,128)(2,1)S(1)} %get-tuple-element.16), channel_id=1, source_target_pairs={{3,0},{0,1},{1,2},{2,3},{7,4},{4,5},{5,6},{6,7},{11,8},{8,9},{9,10... | collective-permute-start | bytes 1179656 | tf_op jit(solution)/shard_map/ppermute | solution.py:124
  180.9 14.0 %collective-permute-start.27 = (bf16[64,3072]{1,0:T(8,128)(2,1)S(1)}, bf16[64,3072]{1,0:T(8,128)(2,1)S(1)}, u32[]{:S(2)}, u32[]{:S(2)}) collective-permute-start(bf16[64,3072]{1,0:T(8,128)(2,1)S(1)} %get-tuple-element.16), channel_id=1, source_target_pairs={{2,0},{3,1},{0,2},{1,3},{6,4},{7,5},{4,6},{5,7},{10,8},{11,9},{8,1... | collective-permute-start | bytes 1179656 | tf_op jit(solution)/shard_map/ppermute | solution.py:124
  183.8 11.1 %collective-permute-start.26 = (bf16[64,3072]{1,0:T(8,128)(2,1)S(1)}, bf16[64,3072]{1,0:T(8,128)(2,1)S(1)}, u32[]{:S(2)}, u32[]{:S(2)}) collective-permute-start(bf16[64,3072]{1,0:T(8,128)(2,1)S(1)} %get-tuple-element.16), channel_id=1, source_target_pairs={{1,0},{2,1},{3,2},{0,3},{5,4},{6,5},{7,6},{4,7},{9,8},{10,9},{11,1... | collective-permute-start | bytes 1179656 | tf_op jit(solution)/shard_map/ppermute | solution.py:124
  195.9 8.9 %collective-permute-start.29 = (bf16[64,1408]{1,0:T(8,128)(2,1)S(1)}, bf16[64,1408]{1,0:T(8,128)(2,1)S(1)}, u32[]{:S(2)}, u32[]{:S(2)}) collective-permute-start(bf16[64,1408]{1,0:T(8,128)(2,1)S(1)} %get-tuple-element.29), channel_id=1, source_target_pairs={{0,4},{4,8},{8,12},{12,16},{16,20},{20,24},{24,28},{28,32},{32,36}... | collective-permute-start | bytes 540680 | tf_op jit(solution)/shard_map/ppermute | solution.py:101
  197.8 8.8 %collective-permute-start.30 = (bf16[64,1408]{1,0:T(8,128)(2,1)S(1)}, bf16[64,1408]{1,0:T(8,128)(2,1)S(1)}, u32[]{:S(2)}, u32[]{:S(2)}) collective-permute-start(bf16[64,1408]{1,0:T(8,128)(2,1)S(1)} %get-tuple-element.30), channel_id=1, source_target_pairs={{4,0},{8,4},{12,8},{16,12},{20,16},{24,20},{28,24},{32,28},{36,32}... | collective-permute-start | bytes 540680 | tf_op jit(solution)/shard_map/ppermute | solution.py:104
  207.7 9.0 %copy-start.2 = (f32[64,3072]{1,0:T(8,128)S(1)}, f32[64,3072]{1,0:T(8,128)}, u32[]{:S(2)}) copy-start(f32[64,3072]{1,0:T(8,128)} %get-tuple-element.17.p_ref) | copy-start | bytes 2359300
  216.6 2.1 copy-start.3
  216.6 2.1 copy-start.4
  222.7 15.5 %collective-permute-start.31 = (f32[]{:T(128)}, f32[]{:T(128)}, u32[]{:S(2)}, u32[]{:S(2)}) collective-permute-start(f32[]{:T(128)} %multiply_reduce_fusion), channel_id=1, source_target_pairs={{0,1},{1,0},{2,3},{3,2},{4,5},{5,4},{6,7},{7,6},{8,9},{9,8},{10,11... | collective-permute-start | bytes 20 | tf_op jit(solution)/shard_map/ppermute | solution.py:114
  239.6 5.1 %collective-permute-start.32 = (f32[]{:T(128)}, f32[]{:T(128)}, u32[]{:S(2)}, u32[]{:S(2)}) collective-permute-start(f32[]{:T(128)} %add.112), channel_id=1, source_target_pairs={{0,2},{1,3},{2,0},{3,1},{4,6},{5,7},{6,4},{7,5},{8,10},{9,11},{10,... | collective-permute-start | bytes 20 | tf_op jit(solution)/shard_map/ppermute | solution.py:114
  245.3 1.2 collective-permute-start.33
  247.2 3.6 %collective-permute-start.34 = (f32[]{:T(128)}, f32[]{:T(128)}, u32[]{:S(2)}, u32[]{:S(2)}) collective-permute-start(f32[]{:T(128)} %add.114), channel_id=1, source_target_pairs={{0,8},{4,12},{8,0},{12,4},{16,24},{20,28},{24,16},{28,20},{32,40},... | collective-permute-start | bytes 20 | tf_op jit(solution)/shard_map/ppermute | solution.py:114
  251.5 4.5 %collective-permute-start.35 = (f32[]{:T(128)}, f32[]{:T(128)}, u32[]{:S(2)}, u32[]{:S(2)}) collective-permute-start(f32[]{:T(128)} %add.115), channel_id=1, source_target_pairs={{0,16},{4,20},{8,24},{12,28},{16,0},{20,4},{24,8},{28,12},{32,48},... | collective-permute-start | bytes 20 | tf_op jit(solution)/shard_map/ppermute | solution.py:114
  256.6 7.5 %collective-permute-start.36 = (f32[]{:T(128)}, f32[]{:T(128)}, u32[]{:S(2)}, u32[]{:S(2)}) collective-permute-start(f32[]{:T(128)} %add.116), channel_id=1, source_target_pairs={{0,32},{4,36},{8,40},{12,44},{16,48},{20,52},{24,56},{28,60},{32,0... | collective-permute-start | bytes 20 | tf_op jit(solution)/shard_map/ppermute | solution.py:114
  264.8 3.6 %collective-permute-start.37 = (f32[]{:T(128)}, f32[]{:T(128)}, u32[]{:S(2)}, u32[]{:S(2)}) collective-permute-start(f32[]{:T(128)} %add.117), channel_id=1, source_target_pairs={{0,64},{4,68},{8,72},{12,76},{16,80},{20,84},{24,88},{28,92},{32,9... | collective-permute-start | bytes 20 | tf_op jit(solution)/shard_map/ppermute | solution.py:114
  269.0 5.1 %collective-permute-start.38 = (f32[]{:T(128)}, f32[]{:T(128)}, u32[]{:S(2)}, u32[]{:S(2)}) collective-permute-start(f32[]{:T(128)} %add.118), channel_id=1, source_target_pairs={{0,128},{4,132},{8,136},{12,140},{16,144},{20,148},{24,152},{28,15... | collective-permute-start | bytes 20 | tf_op jit(solution)/shard_map/ppermute | solution.py:114
  277.5 2.9 %copy-start.7 = (f32[64,3072]{0,1:T(8,128)S(1)}, f32[64,3072]{0,1:T(8,128)}, u32[]{:S(2)}) copy-start(f32[64,3072]{0,1:T(8,128)} %get-tuple-element.23) | copy-start | bytes 2359300
  (2 other events, 3.2 us)

commit v10 on v9

--- a/solution.py
+++ b/solution.py
@@ -135,6 +135,9 @@
     halo = slot_limit - 1
     device_pos = lax.axis_index("samp")
     local_perm = run_perm - device_pos * runs_local
+    inverse_perm = jnp.zeros_like(local_perm).at[local_perm].set(
+        jnp.arange(runs_local, dtype=local_perm.dtype)
+    )
     sorted_both = jnp.take(jnp.concatenate([coords, loads], axis=0), local_perm, axis=1)
     sorted_coords = sorted_both[:dims]
     sorted_loads = sorted_both[dims:]
@@ -175,7 +178,7 @@
         curvature = jnp.sum(direction * mapped)
         if iteration + 1 == ITERS:
             stacked = jnp.concatenate([iterate, remainder, direction, mapped], axis=0)
-            unsorted = jnp.zeros_like(stacked).at[:, local_perm].set(stacked)
+            unsorted = jnp.take(stacked, inverse_perm, axis=1)
             iterate, remainder, direction, mapped = jnp.split(unsorted, 4, axis=0)
         if iteration == 0:
             sums = global_sum(jnp.stack([norm_local, curvature]))

time: 284 us -> 287 us (1.011)
  waiting for transfers between devices: 72.8 us -> 55.7 us
  local copies, waits for them, and re-layouts: 37.6 us -> 47.1 us
  starting transfers between devices: 81.7 us -> 87.9 us
  other arithmetic: 22.8 us -> 25.8 us
    gather x0 -> x1, local copies, waits for them, and re-layouts: none -> 12.3 us  [per_device(): unsorted = jnp.take(stacked, inverse_perm, axis=1)]
    ppermute x9, waiting for transfers between devices: 10.5 us -> 1.06 us  [gather_chan(): parts.append(lax.ppermute(rounded, 'chan', pairs))]
    ppermute x24, waiting for transfers between devices: 57 us -> 49.4 us  [global_sum(): value = value + lax.ppermute(value, axis, pairs)]
    ppermute x24, starting transfers between devices: 43.7 us -> 51 us  [global_sum(): value = value + lax.ppermute(value, axis, pairs)]
    select_n x0 -> x1, other arithmetic: none -> 2.97 us  [per_device(): unsorted = jnp.take(stacked, inverse_perm, axis=1)]
    unnamed x26 -> x22, local copies, waits for them, and re-layouts: 7.51 us -> 7.27 us
  transfers between devices with their start and end apart: 39 -> 39, of which waited for: 29 -> 28; matrix products, arithmetic and copies ran while one was open for 13% -> 19% of each run, Pallas kernels for 11% -> 12%
where the time goes in v10:
time: 287 us; the launch traced here: 285 us
  starting transfers between devices  87.9 us (31%)
  waiting for transfers between devices  55.7 us (19%)
  Pallas kernels  51.7 us (18%)
  local copies, waits for them, and re-layouts  47.1 us (16%)
  other arithmetic  25.8 us (9%)
  between operations  14 us (5%)
  matrix products  3.34 us (1%)
    ppermute x24, starting transfers between devices, global_sum(): value = value + lax.ppermute(value, axis, pairs)  51 us
    ppermute x24, waiting for transfers between devices, global_sum(): value = value + lax.ppermute(value, axis, pairs)  49.4 us
    pallas_call x1, Pallas kernels, build_tiles(): pl.pallas_call(kern, grid_spec=pltpu.PrefetchScalarGridSpec(num_scalar_pr...  33.8 us
    ppermute x3, starting transfers between devices, extended(): lax.ppermute(lax.slice_in_dim(block, 0, width, axis=dim), axis, backward)  18.1 us
    pallas_call x2, Pallas kernels, apply_operator(): pl.pallas_call(kern, grid_spec=pltpu.PrefetchScalarGridSpec(num_scalar_pr...  17.9 us
    ppermute x9, starting transfers between devices, gather_chan(): parts.append(lax.ppermute(rounded, 'chan', pairs))  12.9 us
    gather x1, local copies, waits for them, and re-layouts, per_device(): unsorted = jnp.take(stacked, inverse_perm, axis=1)  12.3 us
    scatter x1, local copies, waits for them, and re-layouts, per_device(): jnp.zeros_like(local_perm).at[local_perm]  11.8 us
  transfers between devices with their start and end apart: 39, of which 28 were waited for; matrix products, arithmetic and copies ran while one was open for 19% of the time, Pallas kernels for 12%

profile of v10, /device:TPU:2, one launch (start us, length us, event | category | flops | bytes accessed | tf_op | source)
XLA Modules:
  0.0 285.4 jit_solution(1518508105310801826)
XLA Ops:
  0.6 3.1 %collective-permute-start.5 = (f32[64,256]{1,0:T(8,128)}, f32[64,256]{1,0:T(8,128)S(1)}, u32[]{:S(2)}, u32[]{:S(2)}) collective-permute-start(f32[64,256]{1,0:T(8,128)} %param.9), channel_id=1, source_target_pairs={{1,0},{2,1},{3,2},{0,3},{5,4},{6,5},{7,6},{4,7},{9,8},{10,9},{11,1... | collective-permute-start | bytes 196616 | tf_op jit(solution)/shard_map/ppermute | solution.py:124
  8.1 1.9 pad_maximum_fusion.1
  10.0 8.1 %gather_fusion = f32[3072,70]{1,0:T(8,128)S(1)} fusion(f32[70,3072]{0,1:T(8,128)S(1)} %pad_maximum_fusion.1, s32[3072]{0:T(1024)S(1)} %broadcast_clamp_fusion), kind=kCustom, calls=%fused_computation | custom fusion | bytes 1732608 | tf_op jit(solution)/shard_map/jit(_take)/gather | solution.py:141
  20.8 1.9 collective-permute-start
  22.8 6.6 %collective-permute-start.1 = (f32[6,1408]{1,0:T(8,128)S(1)}, f32[6,1408]{1,0:T(8,128)S(1)}, u32[]{:S(2)}, u32[]{:S(2)}) collective-permute-start(f32[6,1408]{1,0:T(8,128)S(1)} %get-tuple-element.27), channel_id=1, source_target_pairs={{4,0},{8,4},{12,8},{16,12},{20,16},{24,20},{28,24},{32,28},{36,32}... | collective-permute-start | bytes 101384 | tf_op jit(solution)/shard_map/ppermute | solution.py:104
  33.3 2.0 collective-permute-start.3
  38.7 33.8 %shard_map.86.tile_ref = bf16[24,128,1536]{2,1,0:T(8,128)(2,1)} custom-call(s32[24]{0:T(128)} %clamp_bitcast_fusion.begin_ref, s32[24]{0:T(128)} %count_ref.1, f32[24,128,8]{2,1,0:T(8,128)} %pad_bitcast_fusion.own_ref, f32[46,8,128]{2,1,0:T(8,128)} %pad_bitcast_fusion.1.win_ref), custom_call_target="tpu_custom_call" | custom-call | tf_op jit(solution)/shard_map/pallas_call | solution.py:46
  74.0 1.9 collective-permute-start.8
  75.9 5.8 %collective-permute-start.9 = (bf16[64,1408]{1,0:T(8,128)(2,1)S(1)}, bf16[64,1408]{1,0:T(8,128)(2,1)S(1)}, u32[]{:S(2)}, u32[]{:S(2)}) collective-permute-start(bf16[64,1408]{1,0:T(8,128)(2,1)S(1)} %get-tuple-element.32), channel_id=1, source_target_pairs={{4,0},{8,4},{12,8},{16,12},{20,16},{24,20},{28,24},{32,28},{36,32}... | collective-permute-start | bytes 540680 | tf_op jit(solution)/shard_map/ppermute | solution.py:104
  85.8 8.9 %shard_map.87 = f32[64,3072]{1,0:T(8,128)} custom-call(s32[24]{0:T(128)} %clamp_bitcast_fusion.begin_ref, bf16[46,64,128]{2,1,0:T(8,128)(2,1)} %bitcast_bitcast_fusion.1.win_ref, bf16[24,128,1536]{2,1,0:T(8,128)(2,1)} %shard_map.86.tile_ref, f32[64,3072]{1,0:T(8,128)} %copy-done, f32[64,1]{1,0:T(8,128)} %copy.25.noise_ref), custom_call_target="tpu_custom_call" | custom-call | tf_op jit(solution)/shard_map/pallas_call | solution.py:80
  94.8 2.0 multiply_reduce_fusion.2
  99.7 2.0 collective-permute-done.10
  103.0 3.2 %collective-permute-start.11 = (f32[2]{0:T(128)S(1)}, f32[2]{0:T(128)S(1)}, u32[]{:S(2)}, u32[]{:S(2)}) collective-permute-start(f32[2]{0:T(128)S(1)} %fusion.30), channel_id=1, source_target_pairs={{0,2},{1,3},{2,0},{3,1},{4,6},{5,7},{6,4},{7,5},{8,10},{9,11},{10,... | collective-permute-start | bytes 32 | tf_op jit(solution)/shard_map/ppermute | solution.py:114
  110.6 3.5 %collective-permute-done.13 = f32[2]{0:T(128)S(1)} collective-permute-done((f32[2]{0:T(128)S(1)}, f32[2]{0:T(128)S(1)}, u32[]{:S(2)}, u32[]{:S(2)}) %collective-permute-start.13) | collective-permute-done | bytes 40 | tf_op jit(solution)/shard_map/ppermute | solution.py:114
  115.6 3.0 %collective-permute-done.14 = f32[2]{0:T(128)S(1)} collective-permute-done((f32[2]{0:T(128)S(1)}, f32[2]{0:T(128)S(1)}, u32[]{:S(2)}, u32[]{:S(2)}) %collective-permute-start.14) | collective-permute-done | bytes 40 | tf_op jit(solution)/shard_map/ppermute | solution.py:114
  118.6 4.7 %collective-permute-start.15 = (f32[2]{0:T(128)S(1)}, f32[2]{0:T(128)S(1)}, u32[]{:S(2)}, u32[]{:S(2)}) collective-permute-start(f32[2]{0:T(128)S(1)} %add.106), channel_id=1, source_target_pairs={{0,32},{4,36},{8,40},{12,44},{16,48},{20,52},{24,56},{28,60},{32,0... | collective-permute-start | bytes 32 | tf_op jit(solution)/shard_map/ppermute | solution.py:114
  123.3 2.7 collective-permute-done.15
  126.0 3.5 %collective-permute-done.16 = f32[2]{0:T(128)S(1)} collective-permute-done((f32[2]{0:T(128)S(1)}, f32[2]{0:T(128)S(1)}, u32[]{:S(2)}, u32[]{:S(2)}) %collective-permute-start.16) | collective-permute-done | bytes 40 | tf_op jit(solution)/shard_map/ppermute | solution.py:114
  130.1 4.5 %collective-permute-done.17 = f32[2]{0:T(128)S(1)} collective-permute-done((f32[2]{0:T(128)S(1)}, f32[2]{0:T(128)S(1)}, u32[]{:S(2)}, u32[]{:S(2)}) %collective-permute-start.17) | collective-permute-done | bytes 40 | tf_op jit(solution)/shard_map/ppermute | solution.py:114
  138.9 2.2 collective-permute-done.18
  142.3 4.6 %collective-permute-start.19 = (f32[]{:T(128)}, f32[]{:T(128)}, u32[]{:S(2)}, u32[]{:S(2)}) collective-permute-start(f32[]{:T(128)} %add.110), channel_id=1, source_target_pairs={{0,2},{1,3},{2,0},{3,1},{4,6},{5,7},{6,4},{7,5},{8,10},{9,11},{10,... | collective-permute-start | bytes 20 | tf_op jit(solution)/shard_map/ppermute | solution.py:114
  150.0 2.0 collective-permute-start.21
  154.3 2.9 %collective-permute-start.22 = (f32[]{:T(128)}, f32[]{:T(128)}, u32[]{:S(2)}, u32[]{:S(2)}) collective-permute-start(f32[]{:T(128)} %add.113), channel_id=1, source_target_pairs={{0,16},{4,20},{8,24},{12,28},{16,0},{20,4},{24,8},{28,12},{32,48},... | collective-permute-start | bytes 20 | tf_op jit(solution)/shard_map/ppermute | solution.py:114
  159.5 6.1 %collective-permute-start.23 = (f32[]{:T(128)}, f32[]{:T(128)}, u32[]{:S(2)}, u32[]{:S(2)}) collective-permute-start(f32[]{:T(128)} %add.114), channel_id=1, source_target_pairs={{0,32},{4,36},{8,40},{12,44},{16,48},{20,52},{24,56},{28,60},{32,0... | collective-permute-start | bytes 20 | tf_op jit(solution)/shard_map/ppermute | solution.py:114
  169.1 2.3 collective-permute-done.24
  172.0 2.0 collective-permute-start.25
  174.0 3.3 %collective-permute-done.25 = f32[]{:T(128)} collective-permute-done((f32[]{:T(128)}, f32[]{:T(128)}, u32[]{:S(2)}, u32[]{:S(2)}) %collective-permute-start.25) | collective-permute-done | bytes 36 | tf_op jit(solution)/shard_map/ppermute | solution.py:114
  179.6 3.0 %collective-permute-start.26 = (bf16[64,3072]{1,0:T(8,128)(2,1)S(1)}, bf16[64,3072]{1,0:T(8,128)(2,1)S(1)}, u32[]{:S(2)}, u32[]{:S(2)}) collective-permute-start(bf16[64,3072]{1,0:T(8,128)(2,1)S(1)} %get-tuple-element.16), channel_id=1, source_target_pairs={{1,0},{2,1},{3,2},{0,3},{5,4},{6,5},{7,6},{4,7},{9,8},{10,9},{11,1... | collective-permute-start | bytes 1179656 | tf_op jit(solution)/shard_map/ppermute | solution.py:124
  184.2 11.8 %scatter_custom_fusion = s32[3072]{0:T(1024)S(1)} fusion(s32[3072]{0:T(1024)S(1)} %get-tuple-element.21, s32[3072]{0:T(1024)S(1)} %iota.3, s32[]{:T(128)} %constant.22.clone.1), kind=kCustom, calls=%fused_computation.49 | custom fusion | bytes 12292 | tf_op jit(solution)/shard_map/scatter | solution.py:138
  197.1 2.0 convolution_convert_fusion
  199.1 1.9 collective-permute-start.29
  201.1 5.8 %collective-permute-start.30 = (bf16[64,1408]{1,0:T(8,128)(2,1)S(1)}, bf16[64,1408]{1,0:T(8,128)(2,1)S(1)}, u32[]{:S(2)}, u32[]{:S(2)}) collective-permute-start(bf16[64,1408]{1,0:T(8,128)(2,1)S(1)} %get-tuple-element.30), channel_id=1, source_target_pairs={{4,0},{8,4},{12,8},{16,12},{20,16},{24,20},{28,24},{32,28},{36,32}... | collective-permute-start | bytes 540680 | tf_op jit(solution)/shard_map/ppermute | solution.py:104
  210.9 8.9 %shard_map.88 = f32[64,3072]{1,0:T(8,128)} custom-call(s32[24]{0:T(128)} %clamp_bitcast_fusion.begin_ref, bf16[46,64,128]{2,1,0:T(8,128)(2,1)} %bitcast_bitcast_fusion.win_ref, bf16[24,128,1536]{2,1,0:T(8,128)(2,1)} %shard_map.86.tile_ref, f32[64,3072]{1,0:T(8,128)} %get-tuple-element.17.p_ref, f32[64,1]{1,0:T(8,128)} %copy.25.noise_ref), custom_call_target="tpu_custom_call" | custom-call | tf_op jit(solution)/shard_map/pallas_call | solution.py:80
  219.9 2.0 multiply_reduce_fusion
  222.8 1.9 pad_maximum_fusion
  224.6 2.4 copy.28
  227.0 12.3 %gather_fusion.1 = f32[3072,256]{1,0:T(8,128)} fusion(f32[256,3072]{0,1:T(8,128)S(1)} %copy.28, s32[3072]{0:T(1024)S(1)} %fusion.16), kind=kCustom, calls=%fused_computation.1 | custom fusion | bytes 6303744 | tf_op jit(solution)/shard_map/jit(_take)/gather | solution.py:181
  239.3 3.0 %select_bitcast_fusion = f32[256,3072]{0,1:T(8,128)S(1)} fusion(f32[3072,256]{1,0:T(8,128)} %gather_fusion.1, pred[3072]{0:T(1024)(128)(4,1)S(1)} %compare_and_fusion.1), kind=kLoop, calls=%fused_computation.6 | loop fusion | flops 786432 | bytes 6294528 | tf_op jit(solution)/shard_map/jit(_take)/select_n | solution.py:181
  243.6 3.2 %collective-permute-start.32 = (f32[]{:T(128)}, f32[]{:T(128)}, u32[]{:S(2)}, u32[]{:S(2)}) collective-permute-start(f32[]{:T(128)} %add.119), channel_id=1, source_target_pairs={{0,2},{1,3},{2,0},{3,1},{4,6},{5,7},{6,4},{7,5},{8,10},{9,11},{10,... | collective-permute-start | bytes 20 | tf_op jit(solution)/shard_map/ppermute | solution.py:114
  252.5 2.2 collective-permute-done.34
  255.4 3.0 %collective-permute-start.35 = (f32[]{:T(128)}, f32[]{:T(128)}, u32[]{:S(2)}, u32[]{:S(2)}) collective-permute-start(f32[]{:T(128)} %add.122), channel_id=1, source_target_pairs={{0,16},{4,20},{8,24},{12,28},{16,0},{20,4},{24,8},{28,12},{32,48},... | collective-permute-start | bytes 20 | tf_op jit(solution)/shard_map/ppermute | solution.py:114
  260.5 5.2 %collective-permute-start.36 = (f32[]{:T(128)}, f32[]{:T(128)}, u32[]{:S(2)}, u32[]{:S(2)}) collective-permute-start(f32[]{:T(128)} %add.123), channel_id=1, source_target_pairs={{0,32},{4,36},{8,40},{12,44},{16,48},{20,52},{24,56},{28,60},{32,0... | collective-permute-start | bytes 20 | tf_op jit(solution)/shard_map/ppermute | solution.py:114
  265.7 2.3 collective-permute-done.36
  270.0 2.2 collective-permute-done.37
  272.8 2.0 collective-permute-start.38
  274.8 3.1 %collective-permute-done.38 = f32[]{:T(128)} collective-permute-done((f32[]{:T(128)}, f32[]{:T(128)}, u32[]{:S(2)}, u32[]{:S(2)}) %collective-permute-start.38) | collective-permute-done | bytes 36 | tf_op jit(solution)/shard_map/ppermute | solution.py:114
  278.6 2.6 fusion
  281.2 2.9 %copy.29 = f32[64,3072]{1,0:T(8,128)} copy(f32[64,3072]{0,1:T(8,128)} %get-tuple-element.23) | data formatting | bytes 1572864
  (102 shorter events, 59.3 us)
Async XLA Ops:
  0.6 5.9 %copy-start.6 = (f32[64,3072]{1,0:T(8,128)S(1)}, f32[64,3072]{1,0:T(8,128)}, u32[]{:S(2)}) copy-start(f32[64,3072]{1,0:T(8,128)} %param.7) | copy-start | bytes 2359300
  0.6 37.2 %collective-permute-start.5 = (f32[64,256]{1,0:T(8,128)}, f32[64,256]{1,0:T(8,128)S(1)}, u32[]{:S(2)}, u32[]{:S(2)}) collective-permute-start(f32[64,256]{1,0:T(8,128)} %param.9), channel_id=1, source_target_pairs={{1,0},{2,1},{3,2},{0,3},{5,4},{6,5},{7,6},{4,7},{9,8},{10,9},{11,1... | collective-permute-start | bytes 196616 | tf_op jit(solution)/shard_map/ppermute | solution.py:124
  3.7 68.8 %collective-permute-start.6 = (f32[64,256]{1,0:T(8,128)}, f32[64,256]{1,0:T(8,128)S(1)}, u32[]{:S(2)}, u32[]{:S(2)}) collective-permute-start(f32[64,256]{1,0:T(8,128)} %param.9), channel_id=1, source_target_pairs={{2,0},{3,1},{0,2},{1,3},{6,4},{7,5},{4,6},{5,7},{10,8},{11,9},{8,1... | collective-permute-start | bytes 196616 | tf_op jit(solution)/shard_map/ppermute | solution.py:124
  20.8 11.2 %collective-permute-start = (f32[6,1408]{1,0:T(8,128)S(1)}, f32[6,1408]{1,0:T(8,128)S(1)}, u32[]{:S(2)}, u32[]{:S(2)}) collective-permute-start(f32[6,1408]{1,0:T(8,128)S(1)} %get-tuple-element.26), channel_id=1, source_target_pairs={{0,4},{4,8},{8,12},{12,16},{16,20},{20,24},{24,28},{28,32},{32,36}... | collective-permute-start | bytes 101384 | tf_op jit(solution)/shard_map/ppermute | solution.py:101
  22.8 9.3 %collective-permute-start.1 = (f32[6,1408]{1,0:T(8,128)S(1)}, f32[6,1408]{1,0:T(8,128)S(1)}, u32[]{:S(2)}, u32[]{:S(2)}) collective-permute-start(f32[6,1408]{1,0:T(8,128)S(1)} %get-tuple-element.27), channel_id=1, source_target_pairs={{4,0},{8,4},{12,8},{16,12},{20,16},{24,20},{28,24},{32,28},{36,32}... | collective-permute-start | bytes 101384 | tf_op jit(solution)/shard_map/ppermute | solution.py:104
  30.3 1.9 copy-start
  32.2 40.7 %collective-permute-start.2 = (bf16[64,3072]{1,0:T(8,128)(2,1)S(1)}, bf16[64,3072]{1,0:T(8,128)(2,1)S(1)}, u32[]{:S(2)}, u32[]{:S(2)}) collective-permute-start(bf16[64,3072]{1,0:T(8,128)(2,1)S(1)} %convert_element_type.18), channel_id=1, source_target_pairs={{1,0},{2,1},{3,2},{0,3},{5,4},{6,5},{7,6},{4,7},{9,8},{10,9},{11,1... | collective-permute-start | bytes 1179656 | tf_op jit(solution)/shard_map/ppermute | solution.py:124
  33.3 39.6 %collective-permute-start.3 = (bf16[64,3072]{1,0:T(8,128)(2,1)S(1)}, bf16[64,3072]{1,0:T(8,128)(2,1)S(1)}, u32[]{:S(2)}, u32[]{:S(2)}) collective-permute-start(bf16[64,3072]{1,0:T(8,128)(2,1)S(1)} %convert_element_type.18), channel_id=1, source_target_pairs={{2,0},{3,1},{0,2},{1,3},{6,4},{7,5},{4,6},{5,7},{10,8},{11,9},{8,1... | collective-permute-start | bytes 1179656 | tf_op jit(solution)/shard_map/ppermute | solution.py:124
  35.3 37.6 %collective-permute-start.4 = (bf16[64,3072]{1,0:T(8,128)(2,1)S(1)}, bf16[64,3072]{1,0:T(8,128)(2,1)S(1)}, u32[]{:S(2)}, u32[]{:S(2)}) collective-permute-start(bf16[64,3072]{1,0:T(8,128)(2,1)S(1)} %convert_element_type.18), channel_id=1, source_target_pairs={{3,0},{0,1},{1,2},{2,3},{7,4},{4,5},{5,6},{6,7},{11,8},{8,9},{9,10... | collective-permute-start | bytes 1179656 | tf_op jit(solution)/shard_map/ppermute | solution.py:124
  36.6 1.3 copy-start.8
  37.8 34.7 %collective-permute-start.7 = (f32[64,256]{1,0:T(8,128)S(1)}, f32[64,256]{1,0:T(8,128)S(1)}, u32[]{:S(2)}, u32[]{:S(2)}) collective-permute-start(f32[64,256]{1,0:T(8,128)S(1)} %copy-done.8), channel_id=1, source_target_pairs={{3,0},{0,1},{1,2},{2,3},{7,4},{4,5},{5,6},{6,7},{11,8},{8,9},{9,10... | collective-permute-start | bytes 196616 | tf_op jit(solution)/shard_map/ppermute | solution.py:124
  73.0 8.7 %copy-start.7 = (f32[64]{0:T(128)S(1)}, f32[64]{0:T(128)}, u32[]{:S(2)}) copy-start(f32[64]{0:T(128)} %param.10) | copy-start | bytes 772
  74.0 8.9 %collective-permute-start.8 = (bf16[64,1408]{1,0:T(8,128)(2,1)S(1)}, bf16[64,1408]{1,0:T(8,128)(2,1)S(1)}, u32[]{:S(2)}, u32[]{:S(2)}) collective-permute-start(bf16[64,1408]{1,0:T(8,128)(2,1)S(1)} %get-tuple-element.31), channel_id=1, source_target_pairs={{0,4},{4,8},{8,12},{12,16},{16,20},{20,24},{24,28},{28,32},{32,36}... | collective-permute-start | bytes 540680 | tf_op jit(solution)/shard_map/ppermute | solution.py:101
  75.9 8.8 %collective-permute-start.9 = (bf16[64,1408]{1,0:T(8,128)(2,1)S(1)}, bf16[64,1408]{1,0:T(8,128)(2,1)S(1)}, u32[]{:S(2)}, u32[]{:S(2)}) collective-permute-start(bf16[64,1408]{1,0:T(8,128)(2,1)S(1)} %get-tuple-element.32), channel_id=1, source_target_pairs={{4,0},{8,4},{12,8},{16,12},{20,16},{24,20},{28,24},{32,28},{36,32}... | collective-permute-start | bytes 540680 | tf_op jit(solution)/shard_map/ppermute | solution.py:104
  85.8 9.0 %copy-start.1 = (f32[64,3072]{1,0:T(8,128)S(1)}, f32[64,3072]{1,0:T(8,128)}, u32[]{:S(2)}) copy-start(f32[64,3072]{1,0:T(8,128)} %copy-done) | copy-start | bytes 2359300
  94.7 41.8 %copy-start.4 = (f32[64,3072]{1,0:T(8,128)S(1)}, f32[64,3072]{1,0:T(8,128)}, u32[]{:S(2)}) copy-start(f32[64,3072]{1,0:T(8,128)} %shard_map.87) | copy-start | bytes 2359300
  98.1 3.6 %collective-permute-start.10 = (f32[2]{0:T(128)S(1)}, f32[2]{0:T(128)S(1)}, u32[]{:S(2)}, u32[]{:S(2)}) collective-permute-start(f32[2]{0:T(128)S(1)} %pad_maximum_fusion.4), channel_id=1, source_target_pairs={{0,1},{1,0},{2,3},{3,2},{4,5},{5,4},{6,7},{7,6},{8,9},{9,8},{10,11... | collective-permute-start | bytes 32 | tf_op jit(solution)/shard_map/ppermute | solution.py:114
  103.0 5.1 %collective-permute-start.11 = (f32[2]{0:T(128)S(1)}, f32[2]{0:T(128)S(1)}, u32[]{:S(2)}, u32[]{:S(2)}) collective-permute-start(f32[2]{0:T(128)S(1)} %fusion.30), channel_id=1, source_target_pairs={{0,2},{1,3},{2,0},{3,1},{4,6},{5,7},{6,4},{7,5},{8,10},{9,11},{10,... | collective-permute-start | bytes 32 | tf_op jit(solution)/shard_map/ppermute | solution.py:114
  109.4 1.1 collective-permute-start.12
  110.6 3.5 %collective-permute-start.13 = (f32[2]{0:T(128)S(1)}, f32[2]{0:T(128)S(1)}, u32[]{:S(2)}, u32[]{:S(2)}) collective-permute-start(f32[2]{0:T(128)S(1)} %add.104), channel_id=1, source_target_pairs={{0,8},{4,12},{8,0},{12,4},{16,24},{20,28},{24,16},{28,20},{32,40},... | collective-permute-start | bytes 32 | tf_op jit(solution)/shard_map/ppermute | solution.py:114
  114.1 4.4 %collective-permute-start.14 = (f32[2]{0:T(128)S(1)}, f32[2]{0:T(128)S(1)}, u32[]{:S(2)}, u32[]{:S(2)}) collective-permute-start(f32[2]{0:T(128)S(1)} %add.105), channel_id=1, source_target_pairs={{0,16},{4,20},{8,24},{12,28},{16,0},{20,4},{24,8},{28,12},{32,48},... | collective-permute-start | bytes 32 | tf_op jit(solution)/shard_map/ppermute | solution.py:114
  118.6 7.4 %collective-permute-start.15 = (f32[2]{0:T(128)S(1)}, f32[2]{0:T(128)S(1)}, u32[]{:S(2)}, u32[]{:S(2)}) collective-permute-start(f32[2]{0:T(128)S(1)} %add.106), channel_id=1, source_target_pairs={{0,32},{4,36},{8,40},{12,44},{16,48},{20,52},{24,56},{28,60},{32,0... | collective-permute-start | bytes 32 | tf_op jit(solution)/shard_map/ppermute | solution.py:114
  126.0 3.5 %collective-permute-start.16 = (f32[2]{0:T(128)S(1)}, f32[2]{0:T(128)S(1)}, u32[]{:S(2)}, u32[]{:S(2)}) collective-permute-start(f32[2]{0:T(128)S(1)} %add.107), channel_id=1, source_target_pairs={{0,64},{4,68},{8,72},{12,76},{16,80},{20,84},{24,88},{28,92},{32,9... | collective-permute-start | bytes 32 | tf_op jit(solution)/shard_map/ppermute | solution.py:114
  129.6 5.0 %collective-permute-start.17 = (f32[2]{0:T(128)S(1)}, f32[2]{0:T(128)S(1)}, u32[]{:S(2)}, u32[]{:S(2)}) collective-permute-start(f32[2]{0:T(128)S(1)} %add.108), channel_id=1, source_target_pairs={{0,128},{4,132},{8,136},{12,140},{16,144},{20,148},{24,152},{28,15... | collective-permute-start | bytes 32 | tf_op jit(solution)/shard_map/ppermute | solution.py:114
  137.3 3.8 %collective-permute-start.18 = (f32[]{:T(128)}, f32[]{:T(128)}, u32[]{:S(2)}, u32[]{:S(2)}) collective-permute-start(f32[]{:T(128)} %get-tuple-element.18), channel_id=1, source_target_pairs={{0,1},{1,0},{2,3},{3,2},{4,5},{5,4},{6,7},{7,6},{8,9},{9,8},{10,11... | collective-permute-start | bytes 20 | tf_op jit(solution)/shard_map/ppermute | solution.py:114
  142.3 5.2 %collective-permute-start.19 = (f32[]{:T(128)}, f32[]{:T(128)}, u32[]{:S(2)}, u32[]{:S(2)}) collective-permute-start(f32[]{:T(128)} %add.110), channel_id=1, source_target_pairs={{0,2},{1,3},{2,0},{3,1},{4,6},{5,7},{6,4},{7,5},{8,10},{9,11},{10,... | collective-permute-start | bytes 20 | tf_op jit(solution)/shard_map/ppermute | solution.py:114
  148.1 1.3 collective-permute-start.20
  150.0 3.7 %collective-permute-start.21 = (f32[]{:T(128)}, f32[]{:T(128)}, u32[]{:S(2)}, u32[]{:S(2)}) collective-permute-start(f32[]{:T(128)} %add.112), channel_id=1, source_target_pairs={{0,8},{4,12},{8,0},{12,4},{16,24},{20,28},{24,16},{28,20},{32,40},... | collective-permute-start | bytes 20 | tf_op jit(solution)/shard_map/ppermute | solution.py:114
  154.3 4.6 %collective-permute-start.22 = (f32[]{:T(128)}, f32[]{:T(128)}, u32[]{:S(2)}, u32[]{:S(2)}) collective-permute-start(f32[]{:T(128)} %add.113), channel_id=1, source_target_pairs={{0,16},{4,20},{8,24},{12,28},{16,0},{20,4},{24,8},{28,12},{32,48},... | collective-permute-start | bytes 20 | tf_op jit(solution)/shard_map/ppermute | solution.py:114
  159.5 7.6 %collective-permute-start.23 = (f32[]{:T(128)}, f32[]{:T(128)}, u32[]{:S(2)}, u32[]{:S(2)}) collective-permute-start(f32[]{:T(128)} %add.114), channel_id=1, source_target_pairs={{0,32},{4,36},{8,40},{12,44},{16,48},{20,52},{24,56},{28,60},{32,0... | collective-permute-start | bytes 20 | tf_op jit(solution)/shard_map/ppermute | solution.py:114
  167.7 3.7 %collective-permute-start.24 = (f32[]{:T(128)}, f32[]{:T(128)}, u32[]{:S(2)}, u32[]{:S(2)}) collective-permute-start(f32[]{:T(128)} %add.115), channel_id=1, source_target_pairs={{0,64},{4,68},{8,72},{12,76},{16,80},{20,84},{24,88},{28,92},{32,9... | collective-permute-start | bytes 20 | tf_op jit(solution)/shard_map/ppermute | solution.py:114
  172.0 5.2 %collective-permute-start.25 = (f32[]{:T(128)}, f32[]{:T(128)}, u32[]{:S(2)}, u32[]{:S(2)}) collective-permute-start(f32[]{:T(128)} %add.116), channel_id=1, source_target_pairs={{0,128},{4,132},{8,136},{12,140},{16,144},{20,148},{24,152},{28,15... | collective-permute-start | bytes 20 | tf_op jit(solution)/shard_map/ppermute | solution.py:114
  179.6 16.4 %collective-permute-start.26 = (bf16[64,3072]{1,0:T(8,128)(2,1)S(1)}, bf16[64,3072]{1,0:T(8,128)(2,1)S(1)}, u32[]{:S(2)}, u32[]{:S(2)}) collective-permute-start(bf16[64,3072]{1,0:T(8,128)(2,1)S(1)} %get-tuple-element.16), channel_id=1, source_target_pairs={{1,0},{2,1},{3,2},{0,3},{5,4},{6,5},{7,6},{4,7},{9,8},{10,9},{11,1... | collective-permute-start | bytes 1179656 | tf_op jit(solution)/shard_map/ppermute | solution.py:124
  182.6 13.4 %collective-permute-start.27 = (bf16[64,3072]{1,0:T(8,128)(2,1)S(1)}, bf16[64,3072]{1,0:T(8,128)(2,1)}, u32[]{:S(2)}, u32[]{:S(2)}) collective-permute-start(bf16[64,3072]{1,0:T(8,128)(2,1)S(1)} %get-tuple-element.16), channel_id=1, source_target_pairs={{2,0},{3,1},{0,2},{1,3},{6,4},{7,5},{4,6},{5,7},{10,8},{11,9},{8,1... | collective-permute-start | bytes 1179656 | tf_op jit(solution)/shard_map/ppermute | solution.py:124
  183.2 13.8 %collective-permute-start.28 = (bf16[64,3072]{1,0:T(8,128)(2,1)S(1)}, bf16[64,3072]{1,0:T(8,128)(2,1)}, u32[]{:S(2)}, u32[]{:S(2)}) collective-permute-start(bf16[64,3072]{1,0:T(8,128)(2,1)S(1)} %get-tuple-element.16), channel_id=1, source_target_pairs={{3,0},{0,1},{1,2},{2,3},{7,4},{4,5},{5,6},{6,7},{11,8},{8,9},{9,10... | collective-permute-start | bytes 1179656 | tf_op jit(solution)/shard_map/ppermute | solution.py:124
  199.1 8.9 %collective-permute-start.29 = (bf16[64,1408]{1,0:T(8,128)(2,1)S(1)}, bf16[64,1408]{1,0:T(8,128)(2,1)S(1)}, u32[]{:S(2)}, u32[]{:S(2)}) collective-permute-start(bf16[64,1408]{1,0:T(8,128)(2,1)S(1)} %get-tuple-element.29), channel_id=1, source_target_pairs={{0,4},{4,8},{8,12},{12,16},{16,20},{20,24},{24,28},{28,32},{32,36}... | collective-permute-start | bytes 540680 | tf_op jit(solution)/shard_map/ppermute | solution.py:101
  201.1 8.8 %collective-permute-start.30 = (bf16[64,1408]{1,0:T(8,128)(2,1)S(1)}, bf16[64,1408]{1,0:T(8,128)(2,1)S(1)}, u32[]{:S(2)}, u32[]{:S(2)}) collective-permute-start(bf16[64,1408]{1,0:T(8,128)(2,1)S(1)} %get-tuple-element.30), channel_id=1, source_target_pairs={{4,0},{8,4},{12,8},{16,12},{20,16},{24,20},{28,24},{32,28},{36,32}... | collective-permute-start | bytes 540680 | tf_op jit(solution)/shard_map/ppermute | solution.py:104
  210.9 8.9 %copy-start.2 = (f32[64,3072]{1,0:T(8,128)S(1)}, f32[64,3072]{1,0:T(8,128)}, u32[]{:S(2)}) copy-start(f32[64,3072]{1,0:T(8,128)} %get-tuple-element.17.p_ref) | copy-start | bytes 2359300
  219.9 2.9 %copy-start.3 = (f32[64,3072]{1,0:T(8,128)S(1)}, f32[64,3072]{1,0:T(8,128)}, u32[]{:S(2)}) copy-start(f32[64,3072]{1,0:T(8,128)} %shard_map.88) | copy-start | bytes 2359300
  221.9 20.4 %collective-permute-start.31 = (f32[]{:T(128)}, f32[]{:T(128)}, u32[]{:S(2)}, u32[]{:S(2)}) collective-permute-start(f32[]{:T(128)} %multiply_reduce_fusion), channel_id=1, source_target_pairs={{0,1},{1,0},{2,3},{3,2},{4,5},{5,4},{6,7},{7,6},{8,9},{9,8},{10,11... | collective-permute-start | bytes 20 | tf_op jit(solution)/shard_map/ppermute | solution.py:114
  243.6 5.1 %collective-permute-start.32 = (f32[]{:T(128)}, f32[]{:T(128)}, u32[]{:S(2)}, u32[]{:S(2)}) collective-permute-start(f32[]{:T(128)} %add.119), channel_id=1, source_target_pairs={{0,2},{1,3},{2,0},{3,1},{4,6},{5,7},{6,4},{7,5},{8,10},{9,11},{10,... | collective-permute-start | bytes 20 | tf_op jit(solution)/shard_map/ppermute | solution.py:114
  249.3 1.2 collective-permute-start.33
  251.2 3.6 %collective-permute-start.34 = (f32[]{:T(128)}, f32[]{:T(128)}, u32[]{:S(2)}, u32[]{:S(2)}) collective-permute-start(f32[]{:T(128)} %add.121), channel_id=1, source_target_pairs={{0,8},{4,12},{8,0},{12,4},{16,24},{20,28},{24,16},{28,20},{32,40},... | collective-permute-start | bytes 20 | tf_op jit(solution)/shard_map/ppermute | solution.py:114
  255.4 4.5 %collective-permute-start.35 = (f32[]{:T(128)}, f32[]{:T(128)}, u32[]{:S(2)}, u32[]{:S(2)}) collective-permute-start(f32[]{:T(128)} %add.122), channel_id=1, source_target_pairs={{0,16},{4,20},{8,24},{12,28},{16,0},{20,4},{24,8},{28,12},{32,48},... | collective-permute-start | bytes 20 | tf_op jit(solution)/shard_map/ppermute | solution.py:114
  260.5 7.5 %collective-permute-start.36 = (f32[]{:T(128)}, f32[]{:T(128)}, u32[]{:S(2)}, u32[]{:S(2)}) collective-permute-start(f32[]{:T(128)} %add.123), channel_id=1, source_target_pairs={{0,32},{4,36},{8,40},{12,44},{16,48},{20,52},{24,56},{28,60},{32,0... | collective-permute-start | bytes 20 | tf_op jit(solution)/shard_map/ppermute | solution.py:114
  268.6 3.6 %collective-permute-start.37 = (f32[]{:T(128)}, f32[]{:T(128)}, u32[]{:S(2)}, u32[]{:S(2)}) collective-permute-start(f32[]{:T(128)} %add.124), channel_id=1, source_target_pairs={{0,64},{4,68},{8,72},{12,76},{16,80},{20,84},{24,88},{28,92},{32,9... | collective-permute-start | bytes 20 | tf_op jit(solution)/shard_map/ppermute | solution.py:114
  272.8 5.1 %collective-permute-start.38 = (f32[]{:T(128)}, f32[]{:T(128)}, u32[]{:S(2)}, u32[]{:S(2)}) collective-permute-start(f32[]{:T(128)} %add.125), channel_id=1, source_target_pairs={{0,128},{4,132},{8,136},{12,140},{16,144},{20,148},{24,152},{28,15... | collective-permute-start | bytes 20 | tf_op jit(solution)/shard_map/ppermute | solution.py:114
  281.2 2.9 %copy-start.5 = (f32[64,3072]{0,1:T(8,128)S(1)}, f32[64,3072]{0,1:T(8,128)}, u32[]{:S(2)}) copy-start(f32[64,3072]{0,1:T(8,128)} %get-tuple-element.22) | copy-start | bytes 2359300

commit v11 on v9

--- a/solution.py
+++ b/solution.py
@@ -19,7 +19,7 @@
     own = own_ref[0]
     parts = jnp.concatenate([win_ref[start + s] for s in range(slots)], axis=1)
     cross = jnp.dot(
-        own * -2.0, parts, precision=lax.Precision.HIGHEST, preferred_element_type=jnp.float32
+        own * -2.0, parts, precision=lax.Precision.HIGH, preferred_element_type=jnp.float32
     )
     own_sq = jnp.sum(own * own, axis=1, keepdims=True)
     part_sq = jnp.sum(parts * parts, axis=0, keepdims=True)

time: 284 us -> 278 us (0.979)
  starting transfers between devices: 81.7 us -> 101 us
  waiting for transfers between devices: 72.8 us -> 54.9 us
  Pallas kernels: 50.3 us -> 42.9 us
    ppermute x24, starting transfers between devices: 43.7 us -> 62.9 us  [global_sum(): value = value + lax.ppermute(value, axis, pairs)]
    ppermute x24, waiting for transfers between devices: 57 us -> 38.8 us  [global_sum(): value = value + lax.ppermute(value, axis, pairs)]
    pallas_call x1, Pallas kernels: 32.4 us -> 25 us  [build_tiles(): pl.pallas_call(kern, grid_spec=pltpu.PrefetchScalarGridSpec(num_scalar_pr...]
  transfers between devices with their start and end apart: 39 -> 39, of which waited for: 29 -> 29; matrix products, arithmetic and copies ran while one was open for 13% -> 13% of each run, Pallas kernels for 11% -> 9%
where the time goes in v11:
time: 278 us; the launch traced here: 276 us
  starting transfers between devices  101 us (36%)
  waiting for transfers between devices  54.9 us (20%)
  Pallas kernels  42.9 us (15%)
  local copies, waits for them, and re-layouts  37.6 us (14%)
  other arithmetic  22.8 us (8%)
  between operations  14.2 us (5%)
    ppermute x24, starting transfers between devices, global_sum(): value = value + lax.ppermute(value, axis, pairs)  62.9 us
    ppermute x24, waiting for transfers between devices, global_sum(): value = value + lax.ppermute(value, axis, pairs)  38.8 us
    pallas_call x1, Pallas kernels, build_tiles(): pl.pallas_call(kern, grid_spec=pltpu.PrefetchScalarGridSpec(num_scalar_pr...  25 us
    ppermute x3, starting transfers between devices, extended(): lax.ppermute(lax.slice_in_dim(block, 0, width, axis=dim), axis, backward)  18.1 us
    pallas_call x2, Pallas kernels, apply_operator(): pl.pallas_call(kern, grid_spec=pltpu.PrefetchScalarGridSpec(num_scalar_pr...  17.9 us
    scatter x1, local copies, waits for them, and re-layouts, per_device(): unsorted = jnp.zeros_like(stacked).at[:, local_perm].set(stacked)  14.4 us
    ppermute x9, starting transfers between devices, gather_chan(): parts.append(lax.ppermute(rounded, 'chan', pairs))  14.1 us
    ppermute x9, waiting for transfers between devices, gather_chan(): parts.append(lax.ppermute(rounded, 'chan', pairs))  10.8 us
  transfers between devices with their start and end apart: 39, of which 29 were waited for; matrix products, arithmetic and copies ran while one was open for 13% of the time, Pallas kernels for 9%

profile of v11, /device:TPU:2, one launch (start us, length us, event | category | flops | bytes accessed | tf_op | source)
XLA Modules:
  0.0 275.7 jit_solution(10209531225071278841)
XLA Ops:
  0.6 3.3 %collective-permute-start.6 = (f32[64,256]{1,0:T(8,128)}, f32[64,256]{1,0:T(8,128)S(1)}, u32[]{:S(2)}, u32[]{:S(2)}) collective-permute-start(f32[64,256]{1,0:T(8,128)} %param.9), channel_id=1, source_target_pairs={{2,0},{3,1},{0,2},{1,3},{6,4},{7,5},{4,6},{5,7},{10,8},{11,9},{8,1... | collective-permute-start | bytes 196616 | tf_op jit(solution)/shard_map/ppermute | solution.py:124
  9.0 1.9 pad_maximum_fusion
  10.9 8.1 %gather_fusion = f32[3072,70]{1,0:T(8,128)S(1)} fusion(f32[70,3072]{0,1:T(8,128)S(1)} %pad_maximum_fusion, s32[3072]{0:T(1024)S(1)} %broadcast_clamp_fusion), kind=kCustom, calls=%fused_computation | custom fusion | bytes 1732608 | tf_op jit(solution)/shard_map/jit(_take)/gather | solution.py:138
  21.7 1.9 collective-permute-start
  23.6 6.6 %collective-permute-start.1 = (f32[6,1408]{1,0:T(8,128)S(1)}, f32[6,1408]{1,0:T(8,128)S(1)}, u32[]{:S(2)}, u32[]{:S(2)}) collective-permute-start(f32[6,1408]{1,0:T(8,128)S(1)} %get-tuple-element.27), channel_id=1, source_target_pairs={{4,0},{8,4},{12,8},{16,12},{20,16},{24,20},{28,24},{32,28},{36,32}... | collective-permute-start | bytes 101384 | tf_op jit(solution)/shard_map/ppermute | solution.py:104
  34.9 2.5 collective-permute-start.2
  39.4 25.0 %shard_map.86.tile_ref = bf16[24,128,1536]{2,1,0:T(8,128)(2,1)} custom-call(s32[24]{0:T(128)} %clamp_bitcast_fusion.begin_ref, s32[24]{0:T(128)} %count_ref.1, f32[24,128,8]{2,1,0:T(8,128)} %pad_bitcast_fusion.own_ref, f32[46,8,128]{2,1,0:T(8,128)} %pad_bitcast_fusion.1.win_ref), custom_call_target="tpu_custom_call" | custom-call | tf_op jit(solution)/shard_map/pallas_call | solution.py:46
  65.9 1.9 collective-permute-start.8
  67.8 5.8 %collective-permute-start.9 = (bf16[64,1408]{1,0:T(8,128)(2,1)S(1)}, bf16[64,1408]{1,0:T(8,128)(2,1)S(1)}, u32[]{:S(2)}, u32[]{:S(2)}) collective-permute-start(bf16[64,1408]{1,0:T(8,128)(2,1)S(1)} %get-tuple-element.32), channel_id=1, source_target_pairs={{4,0},{8,4},{12,8},{16,12},{20,16},{24,20},{28,24},{32,28},{36,32}... | collective-permute-start | bytes 540680 | tf_op jit(solution)/shard_map/ppermute | solution.py:104
  77.7 8.9 %shard_map.87 = f32[64,3072]{1,0:T(8,128)} custom-call(s32[24]{0:T(128)} %clamp_bitcast_fusion.begin_ref, bf16[46,64,128]{2,1,0:T(8,128)(2,1)} %bitcast_bitcast_fusion.1.win_ref, bf16[24,128,1536]{2,1,0:T(8,128)(2,1)} %shard_map.86.tile_ref, f32[64,3072]{1,0:T(8,128)} %copy-done, f32[64,1]{1,0:T(8,128)} %copy.25.noise_ref), custom_call_target="tpu_custom_call" | custom-call | tf_op jit(solution)/shard_map/pallas_call | solution.py:80
  86.7 2.0 multiply_reduce_fusion.2
  90.0 1.8 collective-permute-start.10
  91.8 1.8 collective-permute-done.10
  94.9 2.7 collective-permute-start.11
  97.6 2.3 collective-permute-done.11
  102.5 3.5 %collective-permute-done.13 = f32[2]{0:T(128)S(1)} collective-permute-done((f32[2]{0:T(128)S(1)}, f32[2]{0:T(128)S(1)}, u32[]{:S(2)}, u32[]{:S(2)}) %collective-permute-start.13) | collective-permute-done | bytes 40 | tf_op jit(solution)/shard_map/ppermute | solution.py:114
  106.0 3.8 %collective-permute-start.14 = (f32[2]{0:T(128)S(1)}, f32[2]{0:T(128)S(1)}, u32[]{:S(2)}, u32[]{:S(2)}) collective-permute-start(f32[2]{0:T(128)S(1)} %add.98), channel_id=1, source_target_pairs={{0,16},{4,20},{8,24},{12,28},{16,0},{20,4},{24,8},{28,12},{32,48},... | collective-permute-start | bytes 32 | tf_op jit(solution)/shard_map/ppermute | solution.py:114
  111.4 6.1 %collective-permute-start.15 = (f32[2]{0:T(128)S(1)}, f32[2]{0:T(128)S(1)}, u32[]{:S(2)}, u32[]{:S(2)}) collective-permute-start(f32[2]{0:T(128)S(1)} %add.99), channel_id=1, source_target_pairs={{0,32},{4,36},{8,40},{12,44},{16,48},{20,52},{24,56},{28,60},{32,0... | collective-permute-start | bytes 32 | tf_op jit(solution)/shard_map/ppermute | solution.py:114
  119.0 3.5 %collective-permute-done.16 = f32[2]{0:T(128)S(1)} collective-permute-done((f32[2]{0:T(128)S(1)}, f32[2]{0:T(128)S(1)}, u32[]{:S(2)}, u32[]{:S(2)}) %collective-permute-start.16) | collective-permute-done | bytes 40 | tf_op jit(solution)/shard_map/ppermute | solution.py:114
  124.0 3.6 %collective-permute-done.17 = f32[2]{0:T(128)S(1)} collective-permute-done((f32[2]{0:T(128)S(1)}, f32[2]{0:T(128)S(1)}, u32[]{:S(2)}, u32[]{:S(2)}) %collective-permute-start.17) | collective-permute-done | bytes 40 | tf_op jit(solution)/shard_map/ppermute | solution.py:114
  130.3 1.8 collective-permute-start.18
  132.1 2.0 collective-permute-done.18
  135.3 4.1 %collective-permute-start.19 = (f32[]{:T(128)}, f32[]{:T(128)}, u32[]{:S(2)}, u32[]{:S(2)}) collective-permute-start(f32[]{:T(128)} %add.103), channel_id=1, source_target_pairs={{0,2},{1,3},{2,0},{3,1},{4,6},{5,7},{6,4},{7,5},{8,10},{9,11},{10,... | collective-permute-start | bytes 20 | tf_op jit(solution)/shard_map/ppermute | solution.py:114
  143.0 3.2 %collective-permute-start.21 = (f32[]{:T(128)}, f32[]{:T(128)}, u32[]{:S(2)}, u32[]{:S(2)}) collective-permute-start(f32[]{:T(128)} %add.105), channel_id=1, source_target_pairs={{0,8},{4,12},{8,0},{12,4},{16,24},{20,28},{24,16},{28,20},{32,40},... | collective-permute-start | bytes 20 | tf_op jit(solution)/shard_map/ppermute | solution.py:114
  147.3 4.1 %collective-permute-start.22 = (f32[]{:T(128)}, f32[]{:T(128)}, u32[]{:S(2)}, u32[]{:S(2)}) collective-permute-start(f32[]{:T(128)} %add.106), channel_id=1, source_target_pairs={{0,16},{4,20},{8,24},{12,28},{16,0},{20,4},{24,8},{28,12},{32,48},... | collective-permute-start | bytes 20 | tf_op jit(solution)/shard_map/ppermute | solution.py:114
  152.5 7.3 %collective-permute-start.23 = (f32[]{:T(128)}, f32[]{:T(128)}, u32[]{:S(2)}, u32[]{:S(2)}) collective-permute-start(f32[]{:T(128)} %add.107), channel_id=1, source_target_pairs={{0,32},{4,36},{8,40},{12,44},{16,48},{20,52},{24,56},{28,60},{32,0... | collective-permute-start | bytes 20 | tf_op jit(solution)/shard_map/ppermute | solution.py:114
  162.1 2.3 collective-permute-done.24
  165.0 2.9 %collective-permute-start.25 = (f32[]{:T(128)}, f32[]{:T(128)}, u32[]{:S(2)}, u32[]{:S(2)}) collective-permute-start(f32[]{:T(128)} %add.109), channel_id=1, source_target_pairs={{0,128},{4,132},{8,136},{12,140},{16,144},{20,148},{24,152},{28,15... | collective-permute-start | bytes 20 | tf_op jit(solution)/shard_map/ppermute | solution.py:114
  167.9 2.4 collective-permute-done.25
  172.8 1.8 collective-permute-start.28
  174.6 2.9 %collective-permute-start.27 = (bf16[64,3072]{1,0:T(8,128)(2,1)S(1)}, bf16[64,3072]{1,0:T(8,128)(2,1)S(1)}, u32[]{:S(2)}, u32[]{:S(2)}) collective-permute-start(bf16[64,3072]{1,0:T(8,128)(2,1)S(1)} %get-tuple-element.16), channel_id=1, source_target_pairs={{2,0},{3,1},{0,2},{1,3},{6,4},{7,5},{4,6},{5,7},{10,8},{11,9},{8,1... | collective-permute-start | bytes 1179656 | tf_op jit(solution)/shard_map/ppermute | solution.py:124
  178.2 6.6 %collective-permute-done.28 = bf16[64,3072]{1,0:T(8,128)(2,1)S(1)} collective-permute-done((bf16[64,3072]{1,0:T(8,128)(2,1)S(1)}, bf16[64,3072]{1,0:T(8,128)(2,1)S(1)}, u32[]{:S(2)}, u32[]{:S(2)}) %collective-permute-start.28) | collective-permute-done | bytes 393248 | tf_op jit(solution)/shard_map/ppermute | solution.py:124
  184.8 4.2 %collective-permute-done.27 = bf16[64,3072]{1,0:T(8,128)(2,1)S(1)} collective-permute-done((bf16[64,3072]{1,0:T(8,128)(2,1)S(1)}, bf16[64,3072]{1,0:T(8,128)(2,1)S(1)}, u32[]{:S(2)}, u32[]{:S(2)}) %collective-permute-start.27) | collective-permute-done | bytes 393248 | tf_op jit(solution)/shard_map/ppermute | solution.py:124
  190.0 1.9 collective-permute-start.29
  191.9 5.8 %collective-permute-start.30 = (bf16[64,1408]{1,0:T(8,128)(2,1)S(1)}, bf16[64,1408]{1,0:T(8,128)(2,1)S(1)}, u32[]{:S(2)}, u32[]{:S(2)}) collective-permute-start(bf16[64,1408]{1,0:T(8,128)(2,1)S(1)} %get-tuple-element.30), channel_id=1, source_target_pairs={{4,0},{8,4},{12,8},{16,12},{20,16},{24,20},{28,24},{32,28},{36,32}... | collective-permute-start | bytes 540680 | tf_op jit(solution)/shard_map/ppermute | solution.py:104
  201.8 8.9 %shard_map.88 = f32[64,3072]{1,0:T(8,128)} custom-call(s32[24]{0:T(128)} %clamp_bitcast_fusion.begin_ref, bf16[46,64,128]{2,1,0:T(8,128)(2,1)} %bitcast_bitcast_fusion.win_ref, bf16[24,128,1536]{2,1,0:T(8,128)(2,1)} %shard_map.86.tile_ref, f32[64,3072]{1,0:T(8,128)} %get-tuple-element.17.p_ref, f32[64,1]{1,0:T(8,128)} %copy.25.noise_ref), custom_call_target="tpu_custom_call" | custom-call | tf_op jit(solution)/shard_map/pallas_call | solution.py:80
  210.7 2.1 multiply_reduce_fusion
  214.4 2.4 copy.28
  217.9 14.4 %scatter_custom_fusion = f32[256,3072]{0,1:T(8,128)S(1)} fusion(s32[3072]{0:T(1024)S(1)} %get-tuple-element.21, f32[3072,256]{1,0:T(8,128)} %copy.28, f32[]{:T(128)} %constant.10.clone.1), kind=kCustom, calls=%fused_computation.19 | custom fusion | bytes 3146240 | tf_op jit(solution)/shard_map/scatter | solution.py:178
  233.6 3.8 %collective-permute-start.32 = (f32[]{:T(128)}, f32[]{:T(128)}, u32[]{:S(2)}, u32[]{:S(2)}) collective-permute-start(f32[]{:T(128)} %add.112), channel_id=1, source_target_pairs={{0,2},{1,3},{2,0},{3,1},{4,6},{5,7},{6,4},{7,5},{8,10},{9,11},{10,... | collective-permute-start | bytes 20 | tf_op jit(solution)/shard_map/ppermute | solution.py:114
  242.7 2.2 collective-permute-done.34
  245.5 3.9 %collective-permute-start.35 = (f32[]{:T(128)}, f32[]{:T(128)}, u32[]{:S(2)}, u32[]{:S(2)}) collective-permute-start(f32[]{:T(128)} %add.115), channel_id=1, source_target_pairs={{0,16},{4,20},{8,24},{12,28},{16,0},{20,4},{24,8},{28,12},{32,48},... | collective-permute-start | bytes 20 | tf_op jit(solution)/shard_map/ppermute | solution.py:114
  250.7 6.1 %collective-permute-start.36 = (f32[]{:T(128)}, f32[]{:T(128)}, u32[]{:S(2)}, u32[]{:S(2)}) collective-permute-start(f32[]{:T(128)} %add.116), channel_id=1, source_target_pairs={{0,32},{4,36},{8,40},{12,44},{16,48},{20,52},{24,56},{28,60},{32,0... | collective-permute-start | bytes 20 | tf_op jit(solution)/shard_map/ppermute | solution.py:114
  260.2 2.2 collective-permute-done.37
  263.1 2.5 collective-permute-start.38
  265.6 2.6 collective-permute-done.38
  268.9 2.6 fusion
  271.5 2.9 %copy.30 = f32[64,3072]{1,0:T(8,128)} copy(f32[64,3072]{0,1:T(8,128)} %get-tuple-element.22) | data formatting | bytes 1572864
  (101 shorter events, 54.5 us)
Async XLA Ops:
  0.6 6.7 %copy-start.8 = (f32[6,3072]{1,0:T(8,128)S(1)}, f32[6,3072]{1,0:T(8,128)}, u32[]{:S(2)}) copy-start(f32[6,3072]{1,0:T(8,128)} %param.8) | copy-start | bytes 221188
  0.6 38.0 %collective-permute-start.6 = (f32[64,256]{1,0:T(8,128)}, f32[64,256]{1,0:T(8,128)S(1)}, u32[]{:S(2)}, u32[]{:S(2)}) collective-permute-start(f32[64,256]{1,0:T(8,128)} %param.9), channel_id=1, source_target_pairs={{2,0},{3,1},{0,2},{1,3},{6,4},{7,5},{4,6},{5,7},{10,8},{11,9},{8,1... | collective-permute-start | bytes 196616 | tf_op jit(solution)/shard_map/ppermute | solution.py:124
  3.9 60.5 %collective-permute-start.5 = (f32[64,256]{1,0:T(8,128)}, f32[64,256]{1,0:T(8,128)S(1)}, u32[]{:S(2)}, u32[]{:S(2)}) collective-permute-start(f32[64,256]{1,0:T(8,128)} %param.9), channel_id=1, source_target_pairs={{1,0},{2,1},{3,2},{0,3},{5,4},{6,5},{7,6},{4,7},{9,8},{10,9},{11,1... | collective-permute-start | bytes 196616 | tf_op jit(solution)/shard_map/ppermute | solution.py:124
  21.7 11.2 %collective-permute-start = (f32[6,1408]{1,0:T(8,128)S(1)}, f32[6,1408]{1,0:T(8,128)S(1)}, u32[]{:S(2)}, u32[]{:S(2)}) collective-permute-start(f32[6,1408]{1,0:T(8,128)S(1)} %get-tuple-element.26), channel_id=1, source_target_pairs={{0,4},{4,8},{8,12},{12,16},{16,20},{20,24},{24,28},{28,32},{32,36}... | collective-permute-start | bytes 101384 | tf_op jit(solution)/shard_map/ppermute | solution.py:101
  23.6 9.3 %collective-permute-start.1 = (f32[6,1408]{1,0:T(8,128)S(1)}, f32[6,1408]{1,0:T(8,128)S(1)}, u32[]{:S(2)}, u32[]{:S(2)}) collective-permute-start(f32[6,1408]{1,0:T(8,128)S(1)} %get-tuple-element.27), channel_id=1, source_target_pairs={{4,0},{8,4},{12,8},{16,12},{20,16},{24,20},{28,24},{32,28},{36,32}... | collective-permute-start | bytes 101384 | tf_op jit(solution)/shard_map/ppermute | solution.py:104
  33.0 31.8 %collective-permute-start.4 = (bf16[64,3072]{1,0:T(8,128)(2,1)S(1)}, bf16[64,3072]{1,0:T(8,128)(2,1)S(1)}, u32[]{:S(2)}, u32[]{:S(2)}) collective-permute-start(bf16[64,3072]{1,0:T(8,128)(2,1)S(1)} %convert_element_type.18), channel_id=1, source_target_pairs={{3,0},{0,1},{1,2},{2,3},{7,4},{4,5},{5,6},{6,7},{11,8},{8,9},{9,10... | collective-permute-start | bytes 1179656 | tf_op jit(solution)/shard_map/ppermute | solution.py:124
  34.0 30.8 %collective-permute-start.3 = (bf16[64,3072]{1,0:T(8,128)(2,1)S(1)}, bf16[64,3072]{1,0:T(8,128)(2,1)S(1)}, u32[]{:S(2)}, u32[]{:S(2)}) collective-permute-start(bf16[64,3072]{1,0:T(8,128)(2,1)S(1)} %convert_element_type.18), channel_id=1, source_target_pairs={{2,0},{3,1},{0,2},{1,3},{6,4},{7,5},{4,6},{5,7},{10,8},{11,9},{8,1... | collective-permute-start | bytes 1179656 | tf_op jit(solution)/shard_map/ppermute | solution.py:124
  34.9 29.9 %collective-permute-start.2 = (bf16[64,3072]{1,0:T(8,128)(2,1)S(1)}, bf16[64,3072]{1,0:T(8,128)(2,1)S(1)}, u32[]{:S(2)}, u32[]{:S(2)}) collective-permute-start(bf16[64,3072]{1,0:T(8,128)(2,1)S(1)} %convert_element_type.18), channel_id=1, source_target_pairs={{1,0},{2,1},{3,2},{0,3},{5,4},{6,5},{7,6},{4,7},{9,8},{10,9},{11,1... | collective-permute-start | bytes 1179656 | tf_op jit(solution)/shard_map/ppermute | solution.py:124
  38.7 25.7 %collective-permute-start.7 = (f32[64,256]{1,0:T(8,128)S(1)}, f32[64,256]{1,0:T(8,128)S(1)}, u32[]{:S(2)}, u32[]{:S(2)}) collective-permute-start(f32[64,256]{1,0:T(8,128)S(1)} %copy-done.10), channel_id=1, source_target_pairs={{3,0},{0,1},{1,2},{2,3},{7,4},{4,5},{5,6},{6,7},{11,8},{8,9},{9,10... | collective-permute-start | bytes 196616 | tf_op jit(solution)/shard_map/ppermute | solution.py:124
  64.9 8.7 %copy-start.9 = (f32[64]{0:T(128)S(1)}, f32[64]{0:T(128)}, u32[]{:S(2)}) copy-start(f32[64]{0:T(128)} %param.10) | copy-start | bytes 772
  65.9 8.9 %collective-permute-start.8 = (bf16[64,1408]{1,0:T(8,128)(2,1)S(1)}, bf16[64,1408]{1,0:T(8,128)(2,1)S(1)}, u32[]{:S(2)}, u32[]{:S(2)}) collective-permute-start(bf16[64,1408]{1,0:T(8,128)(2,1)S(1)} %get-tuple-element.31), channel_id=1, source_target_pairs={{0,4},{4,8},{8,12},{12,16},{16,20},{20,24},{24,28},{28,32},{32,36}... | collective-permute-start | bytes 540680 | tf_op jit(solution)/shard_map/ppermute | solution.py:101
  67.8 8.8 %collective-permute-start.9 = (bf16[64,1408]{1,0:T(8,128)(2,1)S(1)}, bf16[64,1408]{1,0:T(8,128)(2,1)S(1)}, u32[]{:S(2)}, u32[]{:S(2)}) collective-permute-start(bf16[64,1408]{1,0:T(8,128)(2,1)S(1)} %get-tuple-element.32), channel_id=1, source_target_pairs={{4,0},{8,4},{12,8},{16,12},{20,16},{24,20},{28,24},{32,28},{36,32}... | collective-permute-start | bytes 540680 | tf_op jit(solution)/shard_map/ppermute | solution.py:104
  77.7 9.0 %copy-start.1 = (f32[64,3072]{1,0:T(8,128)S(1)}, f32[64,3072]{1,0:T(8,128)}, u32[]{:S(2)}) copy-start(f32[64,3072]{1,0:T(8,128)} %copy-done) | copy-start | bytes 2359300
  86.7 42.9 %copy-start.5 = (f32[64,3072]{1,0:T(8,128)S(1)}, f32[64,3072]{1,0:T(8,128)}, u32[]{:S(2)}) copy-start(f32[64,3072]{1,0:T(8,128)} %shard_map.87) | copy-start | bytes 2359300
  90.0 3.6 %collective-permute-start.10 = (f32[2]{0:T(128)S(1)}, f32[2]{0:T(128)S(1)}, u32[]{:S(2)}, u32[]{:S(2)}) collective-permute-start(f32[2]{0:T(128)S(1)} %pad_maximum_fusion.3), channel_id=1, source_target_pairs={{0,1},{1,0},{2,3},{3,2},{4,5},{5,4},{6,7},{7,6},{8,9},{9,8},{10,11... | collective-permute-start | bytes 32 | tf_op jit(solution)/shard_map/ppermute | solution.py:114
  94.9 5.1 %collective-permute-start.11 = (f32[2]{0:T(128)S(1)}, f32[2]{0:T(128)S(1)}, u32[]{:S(2)}, u32[]{:S(2)}) collective-permute-start(f32[2]{0:T(128)S(1)} %fusion.29), channel_id=1, source_target_pairs={{0,2},{1,3},{2,0},{3,1},{4,6},{5,7},{6,4},{7,5},{8,10},{9,11},{10,... | collective-permute-start | bytes 32 | tf_op jit(solution)/shard_map/ppermute | solution.py:114
  101.3 1.1 collective-permute-start.12
  102.5 3.5 %collective-permute-start.13 = (f32[2]{0:T(128)S(1)}, f32[2]{0:T(128)S(1)}, u32[]{:S(2)}, u32[]{:S(2)}) collective-permute-start(f32[2]{0:T(128)S(1)} %add.97), channel_id=1, source_target_pairs={{0,8},{4,12},{8,0},{12,4},{16,24},{20,28},{24,16},{28,20},{32,40},... | collective-permute-start | bytes 32 | tf_op jit(solution)/shard_map/ppermute | solution.py:114
  106.0 5.3 %collective-permute-start.14 = (f32[2]{0:T(128)S(1)}, f32[2]{0:T(128)S(1)}, u32[]{:S(2)}, u32[]{:S(2)}) collective-permute-start(f32[2]{0:T(128)S(1)} %add.98), channel_id=1, source_target_pairs={{0,16},{4,20},{8,24},{12,28},{16,0},{20,4},{24,8},{28,12},{32,48},... | collective-permute-start | bytes 32 | tf_op jit(solution)/shard_map/ppermute | solution.py:114
  111.4 7.6 %collective-permute-start.15 = (f32[2]{0:T(128)S(1)}, f32[2]{0:T(128)S(1)}, u32[]{:S(2)}, u32[]{:S(2)}) collective-permute-start(f32[2]{0:T(128)S(1)} %add.99), channel_id=1, source_target_pairs={{0,32},{4,36},{8,40},{12,44},{16,48},{20,52},{24,56},{28,60},{32,0... | collective-permute-start | bytes 32 | tf_op jit(solution)/shard_map/ppermute | solution.py:114
  119.0 3.5 %collective-permute-start.16 = (f32[2]{0:T(128)S(1)}, f32[2]{0:T(128)S(1)}, u32[]{:S(2)}, u32[]{:S(2)}) collective-permute-start(f32[2]{0:T(128)S(1)} %add.100), channel_id=1, source_target_pairs={{0,64},{4,68},{8,72},{12,76},{16,80},{20,84},{24,88},{28,92},{32,9... | collective-permute-start | bytes 32 | tf_op jit(solution)/shard_map/ppermute | solution.py:114
  122.5 5.0 %collective-permute-start.17 = (f32[2]{0:T(128)S(1)}, f32[2]{0:T(128)S(1)}, u32[]{:S(2)}, u32[]{:S(2)}) collective-permute-start(f32[2]{0:T(128)S(1)} %add.101), channel_id=1, source_target_pairs={{0,128},{4,132},{8,136},{12,140},{16,144},{20,148},{24,152},{28,15... | collective-permute-start | bytes 32 | tf_op jit(solution)/shard_map/ppermute | solution.py:114
  130.3 42.5 %copy-start.6 = (f32[64,3072]{1,0:T(8,128)}, f32[64,3072]{1,0:T(8,128)S(1)}, u32[]{:S(2)}) copy-start(f32[64,3072]{1,0:T(8,128)S(1)} %get-tuple-element.19) | copy-start | bytes 2359300
  130.3 3.8 %collective-permute-start.18 = (f32[]{:T(128)}, f32[]{:T(128)}, u32[]{:S(2)}, u32[]{:S(2)}) collective-permute-start(f32[]{:T(128)} %get-tuple-element.18), channel_id=1, source_target_pairs={{0,1},{1,0},{2,3},{3,2},{4,5},{5,4},{6,7},{7,6},{8,9},{9,8},{10,11... | collective-permute-start | bytes 20 | tf_op jit(solution)/shard_map/ppermute | solution.py:114
  135.3 5.2 %collective-permute-start.19 = (f32[]{:T(128)}, f32[]{:T(128)}, u32[]{:S(2)}, u32[]{:S(2)}) collective-permute-start(f32[]{:T(128)} %add.103), channel_id=1, source_target_pairs={{0,2},{1,3},{2,0},{3,1},{4,6},{5,7},{6,4},{7,5},{8,10},{9,11},{10,... | collective-permute-start | bytes 20 | tf_op jit(solution)/shard_map/ppermute | solution.py:114
  141.1 1.3 collective-permute-start.20
  143.0 3.7 %collective-permute-start.21 = (f32[]{:T(128)}, f32[]{:T(128)}, u32[]{:S(2)}, u32[]{:S(2)}) collective-permute-start(f32[]{:T(128)} %add.105), channel_id=1, source_target_pairs={{0,8},{4,12},{8,0},{12,4},{16,24},{20,28},{24,16},{28,20},{32,40},... | collective-permute-start | bytes 20 | tf_op jit(solution)/shard_map/ppermute | solution.py:114
  147.3 4.6 %collective-permute-start.22 = (f32[]{:T(128)}, f32[]{:T(128)}, u32[]{:S(2)}, u32[]{:S(2)}) collective-permute-start(f32[]{:T(128)} %add.106), channel_id=1, source_target_pairs={{0,16},{4,20},{8,24},{12,28},{16,0},{20,4},{24,8},{28,12},{32,48},... | collective-permute-start | bytes 20 | tf_op jit(solution)/shard_map/ppermute | solution.py:114
  152.5 7.6 %collective-permute-start.23 = (f32[]{:T(128)}, f32[]{:T(128)}, u32[]{:S(2)}, u32[]{:S(2)}) collective-permute-start(f32[]{:T(128)} %add.107), channel_id=1, source_target_pairs={{0,32},{4,36},{8,40},{12,44},{16,48},{20,52},{24,56},{28,60},{32,0... | collective-permute-start | bytes 20 | tf_op jit(solution)/shard_map/ppermute | solution.py:114
  160.7 3.7 %collective-permute-start.24 = (f32[]{:T(128)}, f32[]{:T(128)}, u32[]{:S(2)}, u32[]{:S(2)}) collective-permute-start(f32[]{:T(128)} %add.108), channel_id=1, source_target_pairs={{0,64},{4,68},{8,72},{12,76},{16,80},{20,84},{24,88},{28,92},{32,9... | collective-permute-start | bytes 20 | tf_op jit(solution)/shard_map/ppermute | solution.py:114
  165.0 5.2 %collective-permute-start.25 = (f32[]{:T(128)}, f32[]{:T(128)}, u32[]{:S(2)}, u32[]{:S(2)}) collective-permute-start(f32[]{:T(128)} %add.109), channel_id=1, source_target_pairs={{0,128},{4,132},{8,136},{12,140},{16,144},{20,148},{24,152},{28,15... | collective-permute-start | bytes 20 | tf_op jit(solution)/shard_map/ppermute | solution.py:114
  172.8 11.9 %collective-permute-start.28 = (bf16[64,3072]{1,0:T(8,128)(2,1)S(1)}, bf16[64,3072]{1,0:T(8,128)(2,1)S(1)}, u32[]{:S(2)}, u32[]{:S(2)}) collective-permute-start(bf16[64,3072]{1,0:T(8,128)(2,1)S(1)} %get-tuple-element.16), channel_id=1, source_target_pairs={{3,0},{0,1},{1,2},{2,3},{7,4},{4,5},{5,6},{6,7},{11,8},{8,9},{9,10... | collective-permute-start | bytes 1179656 | tf_op jit(solution)/shard_map/ppermute | solution.py:124
  174.6 14.4 %collective-permute-start.27 = (bf16[64,3072]{1,0:T(8,128)(2,1)S(1)}, bf16[64,3072]{1,0:T(8,128)(2,1)S(1)}, u32[]{:S(2)}, u32[]{:S(2)}) collective-permute-start(bf16[64,3072]{1,0:T(8,128)(2,1)S(1)} %get-tuple-element.16), channel_id=1, source_target_pairs={{2,0},{3,1},{0,2},{1,3},{6,4},{7,5},{4,6},{5,7},{10,8},{11,9},{8,1... | collective-permute-start | bytes 1179656 | tf_op jit(solution)/shard_map/ppermute | solution.py:124
  177.5 11.5 %collective-permute-start.26 = (bf16[64,3072]{1,0:T(8,128)(2,1)S(1)}, bf16[64,3072]{1,0:T(8,128)(2,1)S(1)}, u32[]{:S(2)}, u32[]{:S(2)}) collective-permute-start(bf16[64,3072]{1,0:T(8,128)(2,1)S(1)} %get-tuple-element.16), channel_id=1, source_target_pairs={{1,0},{2,1},{3,2},{0,3},{5,4},{6,5},{7,6},{4,7},{9,8},{10,9},{11,1... | collective-permute-start | bytes 1179656 | tf_op jit(solution)/shard_map/ppermute | solution.py:124
  190.0 8.9 %collective-permute-start.29 = (bf16[64,1408]{1,0:T(8,128)(2,1)S(1)}, bf16[64,1408]{1,0:T(8,128)(2,1)S(1)}, u32[]{:S(2)}, u32[]{:S(2)}) collective-permute-start(bf16[64,1408]{1,0:T(8,128)(2,1)S(1)} %get-tuple-element.29), channel_id=1, source_target_pairs={{0,4},{4,8},{8,12},{12,16},{16,20},{20,24},{24,28},{28,32},{32,36}... | collective-permute-start | bytes 540680 | tf_op jit(solution)/shard_map/ppermute | solution.py:101
  191.9 8.8 %collective-permute-start.30 = (bf16[64,1408]{1,0:T(8,128)(2,1)S(1)}, bf16[64,1408]{1,0:T(8,128)(2,1)S(1)}, u32[]{:S(2)}, u32[]{:S(2)}) collective-permute-start(bf16[64,1408]{1,0:T(8,128)(2,1)S(1)} %get-tuple-element.30), channel_id=1, source_target_pairs={{4,0},{8,4},{12,8},{16,12},{20,16},{24,20},{28,24},{32,28},{36,32}... | collective-permute-start | bytes 540680 | tf_op jit(solution)/shard_map/ppermute | solution.py:104
  201.8 8.9 %copy-start.2 = (f32[64,3072]{1,0:T(8,128)S(1)}, f32[64,3072]{1,0:T(8,128)}, u32[]{:S(2)}) copy-start(f32[64,3072]{1,0:T(8,128)} %get-tuple-element.17.p_ref) | copy-start | bytes 2359300
  210.7 2.1 copy-start.3
  210.7 2.1 copy-start.4
  216.8 15.6 %collective-permute-start.31 = (f32[]{:T(128)}, f32[]{:T(128)}, u32[]{:S(2)}, u32[]{:S(2)}) collective-permute-start(f32[]{:T(128)} %multiply_reduce_fusion), channel_id=1, source_target_pairs={{0,1},{1,0},{2,3},{3,2},{4,5},{5,4},{6,7},{7,6},{8,9},{9,8},{10,11... | collective-permute-start | bytes 20 | tf_op jit(solution)/shard_map/ppermute | solution.py:114
  233.6 5.1 %collective-permute-start.32 = (f32[]{:T(128)}, f32[]{:T(128)}, u32[]{:S(2)}, u32[]{:S(2)}) collective-permute-start(f32[]{:T(128)} %add.112), channel_id=1, source_target_pairs={{0,2},{1,3},{2,0},{3,1},{4,6},{5,7},{6,4},{7,5},{8,10},{9,11},{10,... | collective-permute-start | bytes 20 | tf_op jit(solution)/shard_map/ppermute | solution.py:114
  239.4 1.2 collective-permute-start.33
  241.3 3.6 %collective-permute-start.34 = (f32[]{:T(128)}, f32[]{:T(128)}, u32[]{:S(2)}, u32[]{:S(2)}) collective-permute-start(f32[]{:T(128)} %add.114), channel_id=1, source_target_pairs={{0,8},{4,12},{8,0},{12,4},{16,24},{20,28},{24,16},{28,20},{32,40},... | collective-permute-start | bytes 20 | tf_op jit(solution)/shard_map/ppermute | solution.py:114
  245.5 4.5 %collective-permute-start.35 = (f32[]{:T(128)}, f32[]{:T(128)}, u32[]{:S(2)}, u32[]{:S(2)}) collective-permute-start(f32[]{:T(128)} %add.115), channel_id=1, source_target_pairs={{0,16},{4,20},{8,24},{12,28},{16,0},{20,4},{24,8},{28,12},{32,48},... | collective-permute-start | bytes 20 | tf_op jit(solution)/shard_map/ppermute | solution.py:114
  250.7 7.5 %collective-permute-start.36 = (f32[]{:T(128)}, f32[]{:T(128)}, u32[]{:S(2)}, u32[]{:S(2)}) collective-permute-start(f32[]{:T(128)} %add.116), channel_id=1, source_target_pairs={{0,32},{4,36},{8,40},{12,44},{16,48},{20,52},{24,56},{28,60},{32,0... | collective-permute-start | bytes 20 | tf_op jit(solution)/shard_map/ppermute | solution.py:114
  258.9 3.6 %collective-permute-start.37 = (f32[]{:T(128)}, f32[]{:T(128)}, u32[]{:S(2)}, u32[]{:S(2)}) collective-permute-start(f32[]{:T(128)} %add.117), channel_id=1, source_target_pairs={{0,64},{4,68},{8,72},{12,76},{16,80},{20,84},{24,88},{28,92},{32,9... | collective-permute-start | bytes 20 | tf_op jit(solution)/shard_map/ppermute | solution.py:114
  263.1 5.1 %collective-permute-start.38 = (f32[]{:T(128)}, f32[]{:T(128)}, u32[]{:S(2)}, u32[]{:S(2)}) collective-permute-start(f32[]{:T(128)} %add.118), channel_id=1, source_target_pairs={{0,128},{4,132},{8,136},{12,140},{16,144},{20,148},{24,152},{28,15... | collective-permute-start | bytes 20 | tf_op jit(solution)/shard_map/ppermute | solution.py:114
  271.5 2.9 %copy-start.7 = (f32[64,3072]{0,1:T(8,128)S(1)}, f32[64,3072]{0,1:T(8,128)}, u32[]{:S(2)}) copy-start(f32[64,3072]{0,1:T(8,128)} %get-tuple-element.23) | copy-start | bytes 2359300
  (2 other events, 3.2 us)

commit v12 on v11

--- a/solution.py
+++ b/solution.py
@@ -12,47 +12,48 @@
 AMPLITUDE = 0.05
 
 
-def tile_kernel(begin_ref, count_ref, own_ref, win_ref, out_ref, *, slots, runs):
-    b = pl.program_id(0)
-    start = begin_ref[b]
-    count = count_ref[b]
-    own = own_ref[0]
-    parts = jnp.concatenate([win_ref[start + s] for s in range(slots)], axis=1)
-    cross = jnp.dot(
-        own * -2.0, parts, precision=lax.Precision.HIGH, preferred_element_type=jnp.float32
-    )
-    own_sq = jnp.sum(own * own, axis=1, keepdims=True)
-    part_sq = jnp.sum(parts * parts, axis=0, keepdims=True)
-    for s in range(slots):
-        cols = slice(s * runs, (s + 1) * runs)
-
-        @pl.when(s < count)
-        def _():
-            squared = jnp.maximum((own_sq + part_sq[:, cols]) + cross[:, cols], 0.0)
-            radius_frac = jnp.sqrt(squared) * (1.0 / SUPPORT)
-            remain = jnp.maximum(1.0 - radius_frac, 0.0)
-            cubed = remain * remain * remain
-            val = cubed * cubed * (6.0 * radius_frac + 1.0)
-            out_ref[0, :, cols] = val.astype(out_ref.dtype)
-
-        @pl.when(s >= count)
-        def _():
-            out_ref[0, :, cols] = jnp.zeros((runs, runs), out_ref.dtype)
-
-
-def build_tiles(begin, count, own_t, win_c, slots):
+def tile_kernel(begin_ref, count_ref, own_ref, win_ref, out_ref, *, slots, runs, per_step):
+    for k in range(per_step):
+        b = pl.program_id(0) * per_step + k
+        start = begin_ref[b]
+        count = count_ref[b]
+        own = own_ref[k]
+        parts = jnp.concatenate([win_ref[start + s] for s in range(slots)], axis=1)
+        cross = jnp.dot(
+            own * -2.0, parts, precision=lax.Precision.HIGH, preferred_element_type=jnp.float32
+        )
+        own_sq = jnp.sum(own * own, axis=1, keepdims=True)
+        part_sq = jnp.sum(parts * parts, axis=0, keepdims=True)
+        for s in range(slots):
+            cols = slice(s * runs, (s + 1) * runs)
+
+            @pl.when(s < count)
+            def _():
+                squared = jnp.maximum((own_sq + part_sq[:, cols]) + cross[:, cols], 0.0)
+                radius_frac = jnp.sqrt(squared) * (1.0 / SUPPORT)
+                remain = jnp.maximum(1.0 - radius_frac, 0.0)
+                cubed = remain * remain * remain
+                val = cubed * cubed * (6.0 * radius_frac + 1.0)
+                out_ref[k, :, cols] = val.astype(out_ref.dtype)
+
+            @pl.when(s >= count)
+            def _():
+                out_ref[k, :, cols] = jnp.zeros((runs, runs), out_ref.dtype)
+
+
+def build_tiles(begin, count, own_t, win_c, slots, per_step=2):
     blocks, runs, dpad = own_t.shape
-    kern = functools.partial(tile_kernel, slots=slots, runs=runs)
+    kern = functools.partial(tile_kernel, slots=slots, runs=runs, per_step=per_step)
     return pl.pallas_call(
         kern,
         grid_spec=pltpu.PrefetchScalarGridSpec(
             num_scalar_prefetch=2,
-            grid=(blocks,),
+            grid=(blocks // per_step,),
             in_specs=[
-                pl.BlockSpec((1, runs, dpad), lambda b, *_: (b, 0, 0)),
-                pl.BlockSpec(win_c.shape, lambda b, *_: (0, 0, 0)),
+                pl.BlockSpec((per_step, runs, dpad), lambda g, *_: (g, 0, 0)),
+                pl.BlockSpec(win_c.shape, lambda g, *_: (0, 0, 0)),
             ],
-            out_specs=pl.BlockSpec((1, runs, slots * runs), lambda b, *_: (b, 0, 0)),
+            out_specs=pl.BlockSpec((per_step, runs, slots * runs), lambda g, *_: (g, 0, 0)),
         ),
         out_shape=jax.ShapeDtypeStruct((blocks, runs, slots * runs), jnp.bfloat16),
     )(begin, count, own_t, win_c)

time: 278 us -> 276 us (level)
  starting transfers between devices: 101 us -> 92.1 us
  waiting for transfers between devices: 54.9 us -> 62.5 us
    ppermute x24, starting transfers between devices: 62.9 us -> 54.2 us  [global_sum(): value = value + lax.ppermute(value, axis, pairs)]
    ppermute x24, waiting for transfers between devices: 38.8 us -> 46.7 us  [global_sum(): value = value + lax.ppermute(value, axis, pairs)]
where the time goes in v12:
time: 276 us; the launch traced here: 275 us
  starting transfers between devices  92.1 us (33%)
  waiting for transfers between devices  62.5 us (23%)
  Pallas kernels  43.1 us (16%)
  local copies, waits for them, and re-layouts  37.6 us (14%)
  other arithmetic  22.8 us (8%)
  between operations  14.2 us (5%)
    ppermute x24, starting transfers between devices, global_sum(): value = value + lax.ppermute(value, axis, pairs)  54.2 us
    ppermute x24, waiting for transfers between devices, global_sum(): value = value + lax.ppermute(value, axis, pairs)  46.7 us
    pallas_call x1, Pallas kernels, build_tiles(): pl.pallas_call(kern, grid_spec=pltpu.PrefetchScalarGridSpec(num_scalar_pr...  25.2 us
    ppermute x3, starting transfers between devices, extended(): lax.ppermute(lax.slice_in_dim(block, 0, width, axis=dim), axis, backward)  18.1 us
    pallas_call x2, Pallas kernels, apply_operator(): pl.pallas_call(kern, grid_spec=pltpu.PrefetchScalarGridSpec(num_scalar_pr...  17.9 us
    scatter x1, local copies, waits for them, and re-layouts, per_device(): unsorted = jnp.zeros_like(stacked).at[:, local_perm].set(stacked)  14.4 us
    ppermute x9, starting transfers between devices, gather_chan(): parts.append(lax.ppermute(rounded, 'chan', pairs))  14 us
    ppermute x9, waiting for transfers between devices, gather_chan(): parts.append(lax.ppermute(rounded, 'chan', pairs))  10.5 us
  transfers between devices with their start and end apart: 39, of which 29 were waited for; matrix products, arithmetic and copies ran while one was open for 13% of the time, Pallas kernels for 9%

profile of v12, /device:TPU:2, one launch (start us, length us, event | category | flops | bytes accessed | tf_op | source)
XLA Modules:
  0.0 274.6 jit_solution(17159201259989313474)
XLA Ops:
  0.6 3.3 %collective-permute-start.6 = (f32[64,256]{1,0:T(8,128)}, f32[64,256]{1,0:T(8,128)S(1)}, u32[]{:S(2)}, u32[]{:S(2)}) collective-permute-start(f32[64,256]{1,0:T(8,128)} %param.9), channel_id=1, source_target_pairs={{2,0},{3,1},{0,2},{1,3},{6,4},{7,5},{4,6},{5,7},{10,8},{11,9},{8,1... | collective-permute-start | bytes 196616 | tf_op jit(solution)/shard_map/ppermute | solution.py:125
  9.0 1.9 pad_maximum_fusion
  10.9 8.1 %gather_fusion = f32[3072,70]{1,0:T(8,128)S(1)} fusion(f32[70,3072]{0,1:T(8,128)S(1)} %pad_maximum_fusion, s32[3072]{0:T(1024)S(1)} %broadcast_clamp_fusion), kind=kCustom, calls=%fused_computation | custom fusion | bytes 1732608 | tf_op jit(solution)/shard_map/jit(_take)/gather | solution.py:139
  21.7 1.9 collective-permute-start
  23.6 6.6 %collective-permute-start.1 = (f32[6,1408]{1,0:T(8,128)S(1)}, f32[6,1408]{1,0:T(8,128)S(1)}, u32[]{:S(2)}, u32[]{:S(2)}) collective-permute-start(f32[6,1408]{1,0:T(8,128)S(1)} %get-tuple-element.27), channel_id=1, source_target_pairs={{4,0},{8,4},{12,8},{16,12},{20,16},{24,20},{28,24},{32,28},{36,32}... | collective-permute-start | bytes 101384 | tf_op jit(solution)/shard_map/ppermute | solution.py:105
  34.9 2.5 collective-permute-start.2
  39.4 25.2 %shard_map.86.tile_ref = bf16[24,128,1536]{2,1,0:T(8,128)(2,1)} custom-call(s32[24]{0:T(128)} %clamp_bitcast_fusion.begin_ref, s32[24]{0:T(128)} %count_ref.1, f32[24,128,8]{2,1,0:T(8,128)} %pad_bitcast_fusion.own_ref, f32[46,8,128]{2,1,0:T(8,128)} %pad_bitcast_fusion.1.win_ref), custom_call_target="tpu_custom_call" | custom-call | tf_op jit(solution)/shard_map/pallas_call | solution.py:47
  66.0 1.9 collective-permute-start.8
  68.0 5.8 %collective-permute-start.9 = (bf16[64,1408]{1,0:T(8,128)(2,1)S(1)}, bf16[64,1408]{1,0:T(8,128)(2,1)S(1)}, u32[]{:S(2)}, u32[]{:S(2)}) collective-permute-start(bf16[64,1408]{1,0:T(8,128)(2,1)S(1)} %get-tuple-element.32), channel_id=1, source_target_pairs={{4,0},{8,4},{12,8},{16,12},{20,16},{24,20},{28,24},{32,28},{36,32}... | collective-permute-start | bytes 540680 | tf_op jit(solution)/shard_map/ppermute | solution.py:105
  77.8 8.9 %shard_map.87 = f32[64,3072]{1,0:T(8,128)} custom-call(s32[24]{0:T(128)} %clamp_bitcast_fusion.begin_ref, bf16[46,64,128]{2,1,0:T(8,128)(2,1)} %bitcast_bitcast_fusion.1.win_ref, bf16[24,128,1536]{2,1,0:T(8,128)(2,1)} %shard_map.86.tile_ref, f32[64,3072]{1,0:T(8,128)} %copy-done, f32[64,1]{1,0:T(8,128)} %copy.25.noise_ref), custom_call_target="tpu_custom_call" | custom-call | tf_op jit(solution)/shard_map/pallas_call | solution.py:81
  86.8 2.0 multiply_reduce_fusion.2
  90.1 1.8 collective-permute-start.10
  95.1 2.7 collective-permute-start.11
  97.8 2.4 collective-permute-done.11
  102.8 3.5 %collective-permute-done.13 = f32[2]{0:T(128)S(1)} collective-permute-done((f32[2]{0:T(128)S(1)}, f32[2]{0:T(128)S(1)}, u32[]{:S(2)}, u32[]{:S(2)}) %collective-permute-start.13) | collective-permute-done | bytes 40 | tf_op jit(solution)/shard_map/ppermute | solution.py:115
  106.3 1.8 collective-permute-start.14
  108.2 2.6 collective-permute-done.14
  110.8 5.0 %collective-permute-start.15 = (f32[2]{0:T(128)S(1)}, f32[2]{0:T(128)S(1)}, u32[]{:S(2)}, u32[]{:S(2)}) collective-permute-start(f32[2]{0:T(128)S(1)} %add.99), channel_id=1, source_target_pairs={{0,32},{4,36},{8,40},{12,44},{16,48},{20,52},{24,56},{28,60},{32,0... | collective-permute-start | bytes 32 | tf_op jit(solution)/shard_map/ppermute | solution.py:115
  115.8 2.5 collective-permute-done.15
  118.2 3.5 %collective-permute-done.16 = f32[2]{0:T(128)S(1)} collective-permute-done((f32[2]{0:T(128)S(1)}, f32[2]{0:T(128)S(1)}, u32[]{:S(2)}, u32[]{:S(2)}) %collective-permute-start.16) | collective-permute-done | bytes 40 | tf_op jit(solution)/shard_map/ppermute | solution.py:115
  122.4 4.4 %collective-permute-done.17 = f32[2]{0:T(128)S(1)} collective-permute-done((f32[2]{0:T(128)S(1)}, f32[2]{0:T(128)S(1)}, u32[]{:S(2)}, u32[]{:S(2)}) %collective-permute-start.17) | collective-permute-done | bytes 40 | tf_op jit(solution)/shard_map/ppermute | solution.py:115
  131.4 2.0 collective-permute-done.18
  134.6 4.1 %collective-permute-start.19 = (f32[]{:T(128)}, f32[]{:T(128)}, u32[]{:S(2)}, u32[]{:S(2)}) collective-permute-start(f32[]{:T(128)} %add.103), channel_id=1, source_target_pairs={{0,2},{1,3},{2,0},{3,1},{4,6},{5,7},{6,4},{7,5},{8,10},{9,11},{10,... | collective-permute-start | bytes 20 | tf_op jit(solution)/shard_map/ppermute | solution.py:115
  142.3 2.3 collective-permute-start.21
  146.6 3.2 %collective-permute-start.22 = (f32[]{:T(128)}, f32[]{:T(128)}, u32[]{:S(2)}, u32[]{:S(2)}) collective-permute-start(f32[]{:T(128)} %add.106), channel_id=1, source_target_pairs={{0,16},{4,20},{8,24},{12,28},{16,0},{20,4},{24,8},{28,12},{32,48},... | collective-permute-start | bytes 20 | tf_op jit(solution)/shard_map/ppermute | solution.py:115
  151.8 6.4 %collective-permute-start.23 = (f32[]{:T(128)}, f32[]{:T(128)}, u32[]{:S(2)}, u32[]{:S(2)}) collective-permute-start(f32[]{:T(128)} %add.107), channel_id=1, source_target_pairs={{0,32},{4,36},{8,40},{12,44},{16,48},{20,52},{24,56},{28,60},{32,0... | collective-permute-start | bytes 20 | tf_op jit(solution)/shard_map/ppermute | solution.py:115
  161.4 2.3 collective-permute-done.24
  164.3 2.0 collective-permute-start.25
  166.3 3.2 %collective-permute-done.25 = f32[]{:T(128)} collective-permute-done((f32[]{:T(128)}, f32[]{:T(128)}, u32[]{:S(2)}, u32[]{:S(2)}) %collective-permute-start.25) | collective-permute-done | bytes 36 | tf_op jit(solution)/shard_map/ppermute | solution.py:115
  173.9 2.9 %collective-permute-start.27 = (bf16[64,3072]{1,0:T(8,128)(2,1)S(1)}, bf16[64,3072]{1,0:T(8,128)(2,1)S(1)}, u32[]{:S(2)}, u32[]{:S(2)}) collective-permute-start(bf16[64,3072]{1,0:T(8,128)(2,1)S(1)} %get-tuple-element.16), channel_id=1, source_target_pairs={{2,0},{3,1},{0,2},{1,3},{6,4},{7,5},{4,6},{5,7},{10,8},{11,9},{8,1... | collective-permute-start | bytes 1179656 | tf_op jit(solution)/shard_map/ppermute | solution.py:125
  177.4 6.3 %collective-permute-done.28 = bf16[64,3072]{1,0:T(8,128)(2,1)S(1)} collective-permute-done((bf16[64,3072]{1,0:T(8,128)(2,1)S(1)}, bf16[64,3072]{1,0:T(8,128)(2,1)S(1)}, u32[]{:S(2)}, u32[]{:S(2)}) %collective-permute-start.28) | collective-permute-done | bytes 393248 | tf_op jit(solution)/shard_map/ppermute | solution.py:125
  183.7 4.2 %collective-permute-done.27 = bf16[64,3072]{1,0:T(8,128)(2,1)S(1)} collective-permute-done((bf16[64,3072]{1,0:T(8,128)(2,1)S(1)}, bf16[64,3072]{1,0:T(8,128)(2,1)S(1)}, u32[]{:S(2)}, u32[]{:S(2)}) %collective-permute-start.27) | collective-permute-done | bytes 393248 | tf_op jit(solution)/shard_map/ppermute | solution.py:125
  188.9 1.9 collective-permute-start.29
  190.8 5.8 %collective-permute-start.30 = (bf16[64,1408]{1,0:T(8,128)(2,1)S(1)}, bf16[64,1408]{1,0:T(8,128)(2,1)S(1)}, u32[]{:S(2)}, u32[]{:S(2)}) collective-permute-start(bf16[64,1408]{1,0:T(8,128)(2,1)S(1)} %get-tuple-element.30), channel_id=1, source_target_pairs={{4,0},{8,4},{12,8},{16,12},{20,16},{24,20},{28,24},{32,28},{36,32}... | collective-permute-start | bytes 540680 | tf_op jit(solution)/shard_map/ppermute | solution.py:105
  200.7 8.9 %shard_map.88 = f32[64,3072]{1,0:T(8,128)} custom-call(s32[24]{0:T(128)} %clamp_bitcast_fusion.begin_ref, bf16[46,64,128]{2,1,0:T(8,128)(2,1)} %bitcast_bitcast_fusion.win_ref, bf16[24,128,1536]{2,1,0:T(8,128)(2,1)} %shard_map.86.tile_ref, f32[64,3072]{1,0:T(8,128)} %get-tuple-element.17.p_ref, f32[64,1]{1,0:T(8,128)} %copy.25.noise_ref), custom_call_target="tpu_custom_call" | custom-call | tf_op jit(solution)/shard_map/pallas_call | solution.py:81
  209.6 2.1 multiply_reduce_fusion
  213.3 2.4 copy.28
  216.8 14.4 %scatter_custom_fusion = f32[256,3072]{0,1:T(8,128)S(1)} fusion(s32[3072]{0:T(1024)S(1)} %get-tuple-element.21, f32[3072,256]{1,0:T(8,128)} %copy.28, f32[]{:T(128)} %constant.10.clone.1), kind=kCustom, calls=%fused_computation.19 | custom fusion | bytes 3146240 | tf_op jit(solution)/shard_map/scatter | solution.py:179
  232.6 3.8 %collective-permute-start.32 = (f32[]{:T(128)}, f32[]{:T(128)}, u32[]{:S(2)}, u32[]{:S(2)}) collective-permute-start(f32[]{:T(128)} %add.112), channel_id=1, source_target_pairs={{0,2},{1,3},{2,0},{3,1},{4,6},{5,7},{6,4},{7,5},{8,10},{9,11},{10,... | collective-permute-start | bytes 20 | tf_op jit(solution)/shard_map/ppermute | solution.py:115
  241.6 2.2 collective-permute-done.34
  244.4 3.3 %collective-permute-start.35 = (f32[]{:T(128)}, f32[]{:T(128)}, u32[]{:S(2)}, u32[]{:S(2)}) collective-permute-start(f32[]{:T(128)} %add.115), channel_id=1, source_target_pairs={{0,16},{4,20},{8,24},{12,28},{16,0},{20,4},{24,8},{28,12},{32,48},... | collective-permute-start | bytes 20 | tf_op jit(solution)/shard_map/ppermute | solution.py:115
  249.6 5.5 %collective-permute-start.36 = (f32[]{:T(128)}, f32[]{:T(128)}, u32[]{:S(2)}, u32[]{:S(2)}) collective-permute-start(f32[]{:T(128)} %add.116), channel_id=1, source_target_pairs={{0,32},{4,36},{8,40},{12,44},{16,48},{20,52},{24,56},{28,60},{32,0... | collective-permute-start | bytes 20 | tf_op jit(solution)/shard_map/ppermute | solution.py:115
  255.1 2.0 collective-permute-done.36
  259.1 2.2 collective-permute-done.37
  262.0 2.4 collective-permute-start.38
  264.4 2.7 collective-permute-done.38
  267.8 2.6 fusion
  270.4 2.9 %copy.30 = f32[64,3072]{1,0:T(8,128)} copy(f32[64,3072]{0,1:T(8,128)} %get-tuple-element.22) | data formatting | bytes 1572864
  (101 shorter events, 58.0 us)
Async XLA Ops:
  0.6 6.7 %copy-start.8 = (f32[6,3072]{1,0:T(8,128)S(1)}, f32[6,3072]{1,0:T(8,128)}, u32[]{:S(2)}) copy-start(f32[6,3072]{1,0:T(8,128)} %param.8) | copy-start | bytes 221188
  0.6 38.0 %collective-permute-start.6 = (f32[64,256]{1,0:T(8,128)}, f32[64,256]{1,0:T(8,128)S(1)}, u32[]{:S(2)}, u32[]{:S(2)}) collective-permute-start(f32[64,256]{1,0:T(8,128)} %param.9), channel_id=1, source_target_pairs={{2,0},{3,1},{0,2},{1,3},{6,4},{7,5},{4,6},{5,7},{10,8},{11,9},{8,1... | collective-permute-start | bytes 196616 | tf_op jit(solution)/shard_map/ppermute | solution.py:125
  3.9 60.6 %collective-permute-start.5 = (f32[64,256]{1,0:T(8,128)}, f32[64,256]{1,0:T(8,128)S(1)}, u32[]{:S(2)}, u32[]{:S(2)}) collective-permute-start(f32[64,256]{1,0:T(8,128)} %param.9), channel_id=1, source_target_pairs={{1,0},{2,1},{3,2},{0,3},{5,4},{6,5},{7,6},{4,7},{9,8},{10,9},{11,1... | collective-permute-start | bytes 196616 | tf_op jit(solution)/shard_map/ppermute | solution.py:125
  21.7 11.2 %collective-permute-start = (f32[6,1408]{1,0:T(8,128)S(1)}, f32[6,1408]{1,0:T(8,128)S(1)}, u32[]{:S(2)}, u32[]{:S(2)}) collective-permute-start(f32[6,1408]{1,0:T(8,128)S(1)} %get-tuple-element.26), channel_id=1, source_target_pairs={{0,4},{4,8},{8,12},{12,16},{16,20},{20,24},{24,28},{28,32},{32,36}... | collective-permute-start | bytes 101384 | tf_op jit(solution)/shard_map/ppermute | solution.py:102
  23.6 9.3 %collective-permute-start.1 = (f32[6,1408]{1,0:T(8,128)S(1)}, f32[6,1408]{1,0:T(8,128)S(1)}, u32[]{:S(2)}, u32[]{:S(2)}) collective-permute-start(f32[6,1408]{1,0:T(8,128)S(1)} %get-tuple-element.27), channel_id=1, source_target_pairs={{4,0},{8,4},{12,8},{16,12},{20,16},{24,20},{28,24},{32,28},{36,32}... | collective-permute-start | bytes 101384 | tf_op jit(solution)/shard_map/ppermute | solution.py:105
  33.0 31.9 %collective-permute-start.4 = (bf16[64,3072]{1,0:T(8,128)(2,1)S(1)}, bf16[64,3072]{1,0:T(8,128)(2,1)S(1)}, u32[]{:S(2)}, u32[]{:S(2)}) collective-permute-start(bf16[64,3072]{1,0:T(8,128)(2,1)S(1)} %convert_element_type.18), channel_id=1, source_target_pairs={{3,0},{0,1},{1,2},{2,3},{7,4},{4,5},{5,6},{6,7},{11,8},{8,9},{9,10... | collective-permute-start | bytes 1179656 | tf_op jit(solution)/shard_map/ppermute | solution.py:125
  34.0 30.9 %collective-permute-start.3 = (bf16[64,3072]{1,0:T(8,128)(2,1)S(1)}, bf16[64,3072]{1,0:T(8,128)(2,1)S(1)}, u32[]{:S(2)}, u32[]{:S(2)}) collective-permute-start(bf16[64,3072]{1,0:T(8,128)(2,1)S(1)} %convert_element_type.18), channel_id=1, source_target_pairs={{2,0},{3,1},{0,2},{1,3},{6,4},{7,5},{4,6},{5,7},{10,8},{11,9},{8,1... | collective-permute-start | bytes 1179656 | tf_op jit(solution)/shard_map/ppermute | solution.py:125
  34.9 30.1 %collective-permute-start.2 = (bf16[64,3072]{1,0:T(8,128)(2,1)S(1)}, bf16[64,3072]{1,0:T(8,128)(2,1)S(1)}, u32[]{:S(2)}, u32[]{:S(2)}) collective-permute-start(bf16[64,3072]{1,0:T(8,128)(2,1)S(1)} %convert_element_type.18), channel_id=1, source_target_pairs={{1,0},{2,1},{3,2},{0,3},{5,4},{6,5},{7,6},{4,7},{9,8},{10,9},{11,1... | collective-permute-start | bytes 1179656 | tf_op jit(solution)/shard_map/ppermute | solution.py:125
  38.7 25.9 %collective-permute-start.7 = (f32[64,256]{1,0:T(8,128)S(1)}, f32[64,256]{1,0:T(8,128)S(1)}, u32[]{:S(2)}, u32[]{:S(2)}) collective-permute-start(f32[64,256]{1,0:T(8,128)S(1)} %copy-done.10), channel_id=1, source_target_pairs={{3,0},{0,1},{1,2},{2,3},{7,4},{4,5},{5,6},{6,7},{11,8},{8,9},{9,10... | collective-permute-start | bytes 196616 | tf_op jit(solution)/shard_map/ppermute | solution.py:125
  65.1 8.7 %copy-start.9 = (f32[64]{0:T(128)S(1)}, f32[64]{0:T(128)}, u32[]{:S(2)}) copy-start(f32[64]{0:T(128)} %param.10) | copy-start | bytes 772
  66.0 8.9 %collective-permute-start.8 = (bf16[64,1408]{1,0:T(8,128)(2,1)S(1)}, bf16[64,1408]{1,0:T(8,128)(2,1)S(1)}, u32[]{:S(2)}, u32[]{:S(2)}) collective-permute-start(bf16[64,1408]{1,0:T(8,128)(2,1)S(1)} %get-tuple-element.31), channel_id=1, source_target_pairs={{0,4},{4,8},{8,12},{12,16},{16,20},{20,24},{24,28},{28,32},{32,36}... | collective-permute-start | bytes 540680 | tf_op jit(solution)/shard_map/ppermute | solution.py:102
  68.0 8.8 %collective-permute-start.9 = (bf16[64,1408]{1,0:T(8,128)(2,1)S(1)}, bf16[64,1408]{1,0:T(8,128)(2,1)S(1)}, u32[]{:S(2)}, u32[]{:S(2)}) collective-permute-start(bf16[64,1408]{1,0:T(8,128)(2,1)S(1)} %get-tuple-element.32), channel_id=1, source_target_pairs={{4,0},{8,4},{12,8},{16,12},{20,16},{24,20},{28,24},{32,28},{36,32}... | collective-permute-start | bytes 540680 | tf_op jit(solution)/shard_map/ppermute | solution.py:105
  77.8 9.0 %copy-start.1 = (f32[64,3072]{1,0:T(8,128)S(1)}, f32[64,3072]{1,0:T(8,128)}, u32[]{:S(2)}) copy-start(f32[64,3072]{1,0:T(8,128)} %copy-done) | copy-start | bytes 2359300
  86.8 42.0 %copy-start.5 = (f32[64,3072]{1,0:T(8,128)S(1)}, f32[64,3072]{1,0:T(8,128)}, u32[]{:S(2)}) copy-start(f32[64,3072]{1,0:T(8,128)} %shard_map.87) | copy-start | bytes 2359300
  90.1 3.6 %collective-permute-start.10 = (f32[2]{0:T(128)S(1)}, f32[2]{0:T(128)S(1)}, u32[]{:S(2)}, u32[]{:S(2)}) collective-permute-start(f32[2]{0:T(128)S(1)} %pad_maximum_fusion.3), channel_id=1, source_target_pairs={{0,1},{1,0},{2,3},{3,2},{4,5},{5,4},{6,7},{7,6},{8,9},{9,8},{10,11... | collective-permute-start | bytes 32 | tf_op jit(solution)/shard_map/ppermute | solution.py:115
  95.1 5.1 %collective-permute-start.11 = (f32[2]{0:T(128)S(1)}, f32[2]{0:T(128)S(1)}, u32[]{:S(2)}, u32[]{:S(2)}) collective-permute-start(f32[2]{0:T(128)S(1)} %fusion.29), channel_id=1, source_target_pairs={{0,2},{1,3},{2,0},{3,1},{4,6},{5,7},{6,4},{7,5},{8,10},{9,11},{10,... | collective-permute-start | bytes 32 | tf_op jit(solution)/shard_map/ppermute | solution.py:115
  101.5 1.3 collective-permute-start.12
  102.8 3.5 %collective-permute-start.13 = (f32[2]{0:T(128)S(1)}, f32[2]{0:T(128)S(1)}, u32[]{:S(2)}, u32[]{:S(2)}) collective-permute-start(f32[2]{0:T(128)S(1)} %add.97), channel_id=1, source_target_pairs={{0,8},{4,12},{8,0},{12,4},{16,24},{20,28},{24,16},{28,20},{32,40},... | collective-permute-start | bytes 32 | tf_op jit(solution)/shard_map/ppermute | solution.py:115
  106.3 4.4 %collective-permute-start.14 = (f32[2]{0:T(128)S(1)}, f32[2]{0:T(128)S(1)}, u32[]{:S(2)}, u32[]{:S(2)}) collective-permute-start(f32[2]{0:T(128)S(1)} %add.98), channel_id=1, source_target_pairs={{0,16},{4,20},{8,24},{12,28},{16,0},{20,4},{24,8},{28,12},{32,48},... | collective-permute-start | bytes 32 | tf_op jit(solution)/shard_map/ppermute | solution.py:115
  110.8 7.4 %collective-permute-start.15 = (f32[2]{0:T(128)S(1)}, f32[2]{0:T(128)S(1)}, u32[]{:S(2)}, u32[]{:S(2)}) collective-permute-start(f32[2]{0:T(128)S(1)} %add.99), channel_id=1, source_target_pairs={{0,32},{4,36},{8,40},{12,44},{16,48},{20,52},{24,56},{28,60},{32,0... | collective-permute-start | bytes 32 | tf_op jit(solution)/shard_map/ppermute | solution.py:115
  118.2 3.5 %collective-permute-start.16 = (f32[2]{0:T(128)S(1)}, f32[2]{0:T(128)S(1)}, u32[]{:S(2)}, u32[]{:S(2)}) collective-permute-start(f32[2]{0:T(128)S(1)} %add.100), channel_id=1, source_target_pairs={{0,64},{4,68},{8,72},{12,76},{16,80},{20,84},{24,88},{28,92},{32,9... | collective-permute-start | bytes 32 | tf_op jit(solution)/shard_map/ppermute | solution.py:115
  121.8 5.0 %collective-permute-start.17 = (f32[2]{0:T(128)S(1)}, f32[2]{0:T(128)S(1)}, u32[]{:S(2)}, u32[]{:S(2)}) collective-permute-start(f32[2]{0:T(128)S(1)} %add.101), channel_id=1, source_target_pairs={{0,128},{4,132},{8,136},{12,140},{16,144},{20,148},{24,152},{28,15... | collective-permute-start | bytes 32 | tf_op jit(solution)/shard_map/ppermute | solution.py:115
  129.6 42.5 %copy-start.6 = (f32[64,3072]{1,0:T(8,128)}, f32[64,3072]{1,0:T(8,128)S(1)}, u32[]{:S(2)}) copy-start(f32[64,3072]{1,0:T(8,128)S(1)} %get-tuple-element.19) | copy-start | bytes 2359300
  129.6 3.8 %collective-permute-start.18 = (f32[]{:T(128)}, f32[]{:T(128)}, u32[]{:S(2)}, u32[]{:S(2)}) collective-permute-start(f32[]{:T(128)} %get-tuple-element.18), channel_id=1, source_target_pairs={{0,1},{1,0},{2,3},{3,2},{4,5},{5,4},{6,7},{7,6},{8,9},{9,8},{10,11... | collective-permute-start | bytes 20 | tf_op jit(solution)/shard_map/ppermute | solution.py:115
  134.6 5.2 %collective-permute-start.19 = (f32[]{:T(128)}, f32[]{:T(128)}, u32[]{:S(2)}, u32[]{:S(2)}) collective-permute-start(f32[]{:T(128)} %add.103), channel_id=1, source_target_pairs={{0,2},{1,3},{2,0},{3,1},{4,6},{5,7},{6,4},{7,5},{8,10},{9,11},{10,... | collective-permute-start | bytes 20 | tf_op jit(solution)/shard_map/ppermute | solution.py:115
  140.4 1.3 collective-permute-start.20
  142.3 3.7 %collective-permute-start.21 = (f32[]{:T(128)}, f32[]{:T(128)}, u32[]{:S(2)}, u32[]{:S(2)}) collective-permute-start(f32[]{:T(128)} %add.105), channel_id=1, source_target_pairs={{0,8},{4,12},{8,0},{12,4},{16,24},{20,28},{24,16},{28,20},{32,40},... | collective-permute-start | bytes 20 | tf_op jit(solution)/shard_map/ppermute | solution.py:115
  146.6 4.6 %collective-permute-start.22 = (f32[]{:T(128)}, f32[]{:T(128)}, u32[]{:S(2)}, u32[]{:S(2)}) collective-permute-start(f32[]{:T(128)} %add.106), channel_id=1, source_target_pairs={{0,16},{4,20},{8,24},{12,28},{16,0},{20,4},{24,8},{28,12},{32,48},... | collective-permute-start | bytes 20 | tf_op jit(solution)/shard_map/ppermute | solution.py:115
  151.8 7.6 %collective-permute-start.23 = (f32[]{:T(128)}, f32[]{:T(128)}, u32[]{:S(2)}, u32[]{:S(2)}) collective-permute-start(f32[]{:T(128)} %add.107), channel_id=1, source_target_pairs={{0,32},{4,36},{8,40},{12,44},{16,48},{20,52},{24,56},{28,60},{32,0... | collective-permute-start | bytes 20 | tf_op jit(solution)/shard_map/ppermute | solution.py:115
  160.0 3.7 %collective-permute-start.24 = (f32[]{:T(128)}, f32[]{:T(128)}, u32[]{:S(2)}, u32[]{:S(2)}) collective-permute-start(f32[]{:T(128)} %add.108), channel_id=1, source_target_pairs={{0,64},{4,68},{8,72},{12,76},{16,80},{20,84},{24,88},{28,92},{32,9... | collective-permute-start | bytes 20 | tf_op jit(solution)/shard_map/ppermute | solution.py:115
  164.3 5.2 %collective-permute-start.25 = (f32[]{:T(128)}, f32[]{:T(128)}, u32[]{:S(2)}, u32[]{:S(2)}) collective-permute-start(f32[]{:T(128)} %add.109), channel_id=1, source_target_pairs={{0,128},{4,132},{8,136},{12,140},{16,144},{20,148},{24,152},{28,15... | collective-permute-start | bytes 20 | tf_op jit(solution)/shard_map/ppermute | solution.py:115
  172.1 11.6 %collective-permute-start.28 = (bf16[64,3072]{1,0:T(8,128)(2,1)S(1)}, bf16[64,3072]{1,0:T(8,128)(2,1)S(1)}, u32[]{:S(2)}, u32[]{:S(2)}) collective-permute-start(bf16[64,3072]{1,0:T(8,128)(2,1)S(1)} %get-tuple-element.16), channel_id=1, source_target_pairs={{3,0},{0,1},{1,2},{2,3},{7,4},{4,5},{5,6},{6,7},{11,8},{8,9},{9,10... | collective-permute-start | bytes 1179656 | tf_op jit(solution)/shard_map/ppermute | solution.py:125
  173.9 14.0 %collective-permute-start.27 = (bf16[64,3072]{1,0:T(8,128)(2,1)S(1)}, bf16[64,3072]{1,0:T(8,128)(2,1)S(1)}, u32[]{:S(2)}, u32[]{:S(2)}) collective-permute-start(bf16[64,3072]{1,0:T(8,128)(2,1)S(1)} %get-tuple-element.16), channel_id=1, source_target_pairs={{2,0},{3,1},{0,2},{1,3},{6,4},{7,5},{4,6},{5,7},{10,8},{11,9},{8,1... | collective-permute-start | bytes 1179656 | tf_op jit(solution)/shard_map/ppermute | solution.py:125
  176.8 11.1 %collective-permute-start.26 = (bf16[64,3072]{1,0:T(8,128)(2,1)S(1)}, bf16[64,3072]{1,0:T(8,128)(2,1)S(1)}, u32[]{:S(2)}, u32[]{:S(2)}) collective-permute-start(bf16[64,3072]{1,0:T(8,128)(2,1)S(1)} %get-tuple-element.16), channel_id=1, source_target_pairs={{1,0},{2,1},{3,2},{0,3},{5,4},{6,5},{7,6},{4,7},{9,8},{10,9},{11,1... | collective-permute-start | bytes 1179656 | tf_op jit(solution)/shard_map/ppermute | solution.py:125
  188.9 8.9 %collective-permute-start.29 = (bf16[64,1408]{1,0:T(8,128)(2,1)S(1)}, bf16[64,1408]{1,0:T(8,128)(2,1)S(1)}, u32[]{:S(2)}, u32[]{:S(2)}) collective-permute-start(bf16[64,1408]{1,0:T(8,128)(2,1)S(1)} %get-tuple-element.29), channel_id=1, source_target_pairs={{0,4},{4,8},{8,12},{12,16},{16,20},{20,24},{24,28},{28,32},{32,36}... | collective-permute-start | bytes 540680 | tf_op jit(solution)/shard_map/ppermute | solution.py:102
  190.8 8.8 %collective-permute-start.30 = (bf16[64,1408]{1,0:T(8,128)(2,1)S(1)}, bf16[64,1408]{1,0:T(8,128)(2,1)S(1)}, u32[]{:S(2)}, u32[]{:S(2)}) collective-permute-start(bf16[64,1408]{1,0:T(8,128)(2,1)S(1)} %get-tuple-element.30), channel_id=1, source_target_pairs={{4,0},{8,4},{12,8},{16,12},{20,16},{24,20},{28,24},{32,28},{36,32}... | collective-permute-start | bytes 540680 | tf_op jit(solution)/shard_map/ppermute | solution.py:105
  200.7 8.9 %copy-start.2 = (f32[64,3072]{1,0:T(8,128)S(1)}, f32[64,3072]{1,0:T(8,128)}, u32[]{:S(2)}) copy-start(f32[64,3072]{1,0:T(8,128)} %get-tuple-element.17.p_ref) | copy-start | bytes 2359300
  209.6 2.1 copy-start.3
  209.6 2.1 copy-start.4
  215.7 15.6 %collective-permute-start.31 = (f32[]{:T(128)}, f32[]{:T(128)}, u32[]{:S(2)}, u32[]{:S(2)}) collective-permute-start(f32[]{:T(128)} %multiply_reduce_fusion), channel_id=1, source_target_pairs={{0,1},{1,0},{2,3},{3,2},{4,5},{5,4},{6,7},{7,6},{8,9},{9,8},{10,11... | collective-permute-start | bytes 20 | tf_op jit(solution)/shard_map/ppermute | solution.py:115
  232.6 5.1 %collective-permute-start.32 = (f32[]{:T(128)}, f32[]{:T(128)}, u32[]{:S(2)}, u32[]{:S(2)}) collective-permute-start(f32[]{:T(128)} %add.112), channel_id=1, source_target_pairs={{0,2},{1,3},{2,0},{3,1},{4,6},{5,7},{6,4},{7,5},{8,10},{9,11},{10,... | collective-permute-start | bytes 20 | tf_op jit(solution)/shard_map/ppermute | solution.py:115
  238.3 1.2 collective-permute-start.33
  240.2 3.6 %collective-permute-start.34 = (f32[]{:T(128)}, f32[]{:T(128)}, u32[]{:S(2)}, u32[]{:S(2)}) collective-permute-start(f32[]{:T(128)} %add.114), channel_id=1, source_target_pairs={{0,8},{4,12},{8,0},{12,4},{16,24},{20,28},{24,16},{28,20},{32,40},... | collective-permute-start | bytes 20 | tf_op jit(solution)/shard_map/ppermute | solution.py:115
  244.4 4.5 %collective-permute-start.35 = (f32[]{:T(128)}, f32[]{:T(128)}, u32[]{:S(2)}, u32[]{:S(2)}) collective-permute-start(f32[]{:T(128)} %add.115), channel_id=1, source_target_pairs={{0,16},{4,20},{8,24},{12,28},{16,0},{20,4},{24,8},{28,12},{32,48},... | collective-permute-start | bytes 20 | tf_op jit(solution)/shard_map/ppermute | solution.py:115
  249.6 7.5 %collective-permute-start.36 = (f32[]{:T(128)}, f32[]{:T(128)}, u32[]{:S(2)}, u32[]{:S(2)}) collective-permute-start(f32[]{:T(128)} %add.116), channel_id=1, source_target_pairs={{0,32},{4,36},{8,40},{12,44},{16,48},{20,52},{24,56},{28,60},{32,0... | collective-permute-start | bytes 20 | tf_op jit(solution)/shard_map/ppermute | solution.py:115
  257.8 3.6 %collective-permute-start.37 = (f32[]{:T(128)}, f32[]{:T(128)}, u32[]{:S(2)}, u32[]{:S(2)}) collective-permute-start(f32[]{:T(128)} %add.117), channel_id=1, source_target_pairs={{0,64},{4,68},{8,72},{12,76},{16,80},{20,84},{24,88},{28,92},{32,9... | collective-permute-start | bytes 20 | tf_op jit(solution)/shard_map/ppermute | solution.py:115
  262.0 5.1 %collective-permute-start.38 = (f32[]{:T(128)}, f32[]{:T(128)}, u32[]{:S(2)}, u32[]{:S(2)}) collective-permute-start(f32[]{:T(128)} %add.118), channel_id=1, source_target_pairs={{0,128},{4,132},{8,136},{12,140},{16,144},{20,148},{24,152},{28,15... | collective-permute-start | bytes 20 | tf_op jit(solution)/shard_map/ppermute | solution.py:115
  270.4 2.9 %copy-start.7 = (f32[64,3072]{0,1:T(8,128)S(1)}, f32[64,3072]{0,1:T(8,128)}, u32[]{:S(2)}) copy-start(f32[64,3072]{0,1:T(8,128)} %get-tuple-element.23) | copy-start | bytes 2359300
  (2 other events, 3.2 us)

commit v13 on v12

--- a/solution.py
+++ b/solution.py
@@ -41,7 +41,7 @@
                 out_ref[k, :, cols] = jnp.zeros((runs, runs), out_ref.dtype)
 
 
-def build_tiles(begin, count, own_t, win_c, slots, per_step=2):
+def build_tiles(begin, count, own_t, win_c, slots, per_step=3):
     blocks, runs, dpad = own_t.shape
     kern = functools.partial(tile_kernel, slots=slots, runs=runs, per_step=per_step)
     return pl.pallas_call(
@@ -172,7 +172,7 @@
         mixed_b = mixed.astype(jnp.bfloat16)
         widened = extended(mixed_b, "samp", 1, reach_runs)
         win_v = widened.reshape(chan_local, window_blocks, block_runs).transpose(1, 0, 2)
-        mapped = apply_operator(begin, win_v, tiles, direction, noise_col, 4)
+        mapped = apply_operator(begin, win_v, tiles, direction, noise_col, 6)
         curvature = jnp.sum(direction * mapped)
         if iteration + 1 == ITERS:
             stacked = jnp.concatenate([iterate, remainder, direction, mapped], axis=0)

time: 276 us -> 276 us (level)
  waiting for transfers between devices: 62.5 us -> 76.4 us
  starting transfers between devices: 92.1 us -> 78.2 us
    ppermute x24, starting transfers between devices: 54.2 us -> 40.1 us  [global_sum(): value = value + lax.ppermute(value, axis, pairs)]
    ppermute x24, waiting for transfers between devices: 46.7 us -> 60.8 us  [global_sum(): value = value + lax.ppermute(value, axis, pairs)]
  transfers between devices with their start and end apart: 39 -> 39, of which waited for: 29 -> 29; matrix products, arithmetic and copies ran while one was open for 13% -> 13% of each run, Pallas kernels for 9% -> 10%
where the time goes in v13:
time: 276 us; the launch traced here: 275 us
  starting transfers between devices  78.2 us (28%)
  waiting for transfers between devices  76.4 us (28%)
  Pallas kernels  43.4 us (16%)
  local copies, waits for them, and re-layouts  37.6 us (14%)
  other arithmetic  22.8 us (8%)
  between operations  14.2 us (5%)
    ppermute x24, waiting for transfers between devices, global_sum(): value = value + lax.ppermute(value, axis, pairs)  60.8 us
    ppermute x24, starting transfers between devices, global_sum(): value = value + lax.ppermute(value, axis, pairs)  40.1 us
    pallas_call x1, Pallas kernels, build_tiles(): pl.pallas_call(kern, grid_spec=pltpu.PrefetchScalarGridSpec(num_scalar_pr...  27.2 us
    ppermute x3, starting transfers between devices, extended(): lax.ppermute(lax.slice_in_dim(block, 0, width, axis=dim), axis, backward)  18.3 us
    pallas_call x2, Pallas kernels, apply_operator(): pl.pallas_call(kern, grid_spec=pltpu.PrefetchScalarGridSpec(num_scalar_pr...  16.3 us
    scatter x1, local copies, waits for them, and re-layouts, per_device(): unsorted = jnp.zeros_like(stacked).at[:, local_perm].set(stacked)  14.4 us
    ppermute x9, starting transfers between devices, gather_chan(): parts.append(lax.ppermute(rounded, 'chan', pairs))  14 us
    ppermute x9, waiting for transfers between devices, gather_chan(): parts.append(lax.ppermute(rounded, 'chan', pairs))  10.5 us
  transfers between devices with their start and end apart: 39, of which 29 were waited for; matrix products, arithmetic and copies ran while one was open for 13% of the time, Pallas kernels for 10%

profile of v13, /device:TPU:2, one launch (start us, length us, event | category | flops | bytes accessed | tf_op | source)
XLA Modules:
  0.0 275.0 jit_solution(2576696934495969087)
XLA Ops:
  0.6 3.3 %collective-permute-start.6 = (f32[64,256]{1,0:T(8,128)}, f32[64,256]{1,0:T(8,128)S(1)}, u32[]{:S(2)}, u32[]{:S(2)}) collective-permute-start(f32[64,256]{1,0:T(8,128)} %param.9), channel_id=1, source_target_pairs={{2,0},{3,1},{0,2},{1,3},{6,4},{7,5},{4,6},{5,7},{10,8},{11,9},{8,1... | collective-permute-start | bytes 196616 | tf_op jit(solution)/shard_map/ppermute | solution.py:125
  9.0 1.9 pad_maximum_fusion
  10.9 8.1 %gather_fusion = f32[3072,70]{1,0:T(8,128)S(1)} fusion(f32[70,3072]{0,1:T(8,128)S(1)} %pad_maximum_fusion, s32[3072]{0:T(1024)S(1)} %broadcast_clamp_fusion), kind=kCustom, calls=%fused_computation | custom fusion | bytes 1732608 | tf_op jit(solution)/shard_map/jit(_take)/gather | solution.py:139
  21.7 1.9 collective-permute-start
  23.6 6.6 %collective-permute-start.1 = (f32[6,1408]{1,0:T(8,128)S(1)}, f32[6,1408]{1,0:T(8,128)S(1)}, u32[]{:S(2)}, u32[]{:S(2)}) collective-permute-start(f32[6,1408]{1,0:T(8,128)S(1)} %get-tuple-element.27), channel_id=1, source_target_pairs={{4,0},{8,4},{12,8},{16,12},{20,16},{24,20},{28,24},{32,28},{36,32}... | collective-permute-start | bytes 101384 | tf_op jit(solution)/shard_map/ppermute | solution.py:105
  34.9 2.5 collective-permute-start.2
  39.4 27.2 %shard_map.86.tile_ref = bf16[24,128,1536]{2,1,0:T(8,128)(2,1)} custom-call(s32[24]{0:T(128)} %clamp_bitcast_fusion.begin_ref, s32[24]{0:T(128)} %count_ref.1, f32[24,128,8]{2,1,0:T(8,128)} %pad_bitcast_fusion.own_ref, f32[46,8,128]{2,1,0:T(8,128)} %pad_bitcast_fusion.1.win_ref), custom_call_target="tpu_custom_call" | custom-call | tf_op jit(solution)/shard_map/pallas_call | solution.py:47
  68.0 1.9 collective-permute-start.8
  70.0 5.8 %collective-permute-start.9 = (bf16[64,1408]{1,0:T(8,128)(2,1)S(1)}, bf16[64,1408]{1,0:T(8,128)(2,1)S(1)}, u32[]{:S(2)}, u32[]{:S(2)}) collective-permute-start(bf16[64,1408]{1,0:T(8,128)(2,1)S(1)} %get-tuple-element.32), channel_id=1, source_target_pairs={{4,0},{8,4},{12,8},{16,12},{20,16},{24,20},{28,24},{32,28},{36,32}... | collective-permute-start | bytes 540680 | tf_op jit(solution)/shard_map/ppermute | solution.py:105
  79.8 8.1 %shard_map.87 = f32[64,3072]{1,0:T(8,128)} custom-call(s32[24]{0:T(128)} %clamp_bitcast_fusion.begin_ref, bf16[46,64,128]{2,1,0:T(8,128)(2,1)} %bitcast_bitcast_fusion.1.win_ref, bf16[24,128,1536]{2,1,0:T(8,128)(2,1)} %shard_map.86.tile_ref, f32[64,3072]{1,0:T(8,128)} %copy-done, f32[64,1]{1,0:T(8,128)} %copy.25.noise_ref), custom_call_target="tpu_custom_call" | custom-call | tf_op jit(solution)/shard_map/pallas_call | solution.py:81
  88.0 2.0 multiply_reduce_fusion.2
  91.3 2.0 collective-permute-start.10
  96.4 2.7 collective-permute-start.11
  99.1 2.4 collective-permute-done.11
  104.0 3.5 %collective-permute-done.13 = f32[2]{0:T(128)S(1)} collective-permute-done((f32[2]{0:T(128)S(1)}, f32[2]{0:T(128)S(1)}, u32[]{:S(2)}, u32[]{:S(2)}) %collective-permute-start.13) | collective-permute-done | bytes 40 | tf_op jit(solution)/shard_map/ppermute | solution.py:115
  107.5 4.4 %collective-permute-done.14 = f32[2]{0:T(128)S(1)} collective-permute-done((f32[2]{0:T(128)S(1)}, f32[2]{0:T(128)S(1)}, u32[]{:S(2)}, u32[]{:S(2)}) %collective-permute-start.14) | collective-permute-done | bytes 40 | tf_op jit(solution)/shard_map/ppermute | solution.py:115
  112.9 6.5 %collective-permute-done.15 = f32[2]{0:T(128)S(1)} collective-permute-done((f32[2]{0:T(128)S(1)}, f32[2]{0:T(128)S(1)}, u32[]{:S(2)}, u32[]{:S(2)}) %collective-permute-start.15) | collective-permute-done | bytes 40 | tf_op jit(solution)/shard_map/ppermute | solution.py:115
  119.4 3.5 %collective-permute-done.16 = f32[2]{0:T(128)S(1)} collective-permute-done((f32[2]{0:T(128)S(1)}, f32[2]{0:T(128)S(1)}, u32[]{:S(2)}, u32[]{:S(2)}) %collective-permute-start.16) | collective-permute-done | bytes 40 | tf_op jit(solution)/shard_map/ppermute | solution.py:115
  124.0 4.0 %collective-permute-done.17 = f32[2]{0:T(128)S(1)} collective-permute-done((f32[2]{0:T(128)S(1)}, f32[2]{0:T(128)S(1)}, u32[]{:S(2)}, u32[]{:S(2)}) %collective-permute-start.17) | collective-permute-done | bytes 40 | tf_op jit(solution)/shard_map/ppermute | solution.py:115
  132.5 2.0 collective-permute-done.18
  135.7 4.1 %collective-permute-start.19 = (f32[]{:T(128)}, f32[]{:T(128)}, u32[]{:S(2)}, u32[]{:S(2)}) collective-permute-start(f32[]{:T(128)} %add.103), channel_id=1, source_target_pairs={{0,2},{1,3},{2,0},{3,1},{4,6},{5,7},{6,4},{7,5},{8,10},{9,11},{10,... | collective-permute-start | bytes 20 | tf_op jit(solution)/shard_map/ppermute | solution.py:115
  144.8 2.3 collective-permute-done.21
  149.1 3.2 %collective-permute-done.22 = f32[]{:T(128)} collective-permute-done((f32[]{:T(128)}, f32[]{:T(128)}, u32[]{:S(2)}, u32[]{:S(2)}) %collective-permute-start.22) | collective-permute-done | bytes 36 | tf_op jit(solution)/shard_map/ppermute | solution.py:115
  152.9 3.6 %collective-permute-start.23 = (f32[]{:T(128)}, f32[]{:T(128)}, u32[]{:S(2)}, u32[]{:S(2)}) collective-permute-start(f32[]{:T(128)} %add.107), channel_id=1, source_target_pairs={{0,32},{4,36},{8,40},{12,44},{16,48},{20,52},{24,56},{28,60},{32,0... | collective-permute-start | bytes 20 | tf_op jit(solution)/shard_map/ppermute | solution.py:115
  156.6 4.0 %collective-permute-done.23 = f32[]{:T(128)} collective-permute-done((f32[]{:T(128)}, f32[]{:T(128)}, u32[]{:S(2)}, u32[]{:S(2)}) %collective-permute-start.23) | collective-permute-done | bytes 36 | tf_op jit(solution)/shard_map/ppermute | solution.py:115
  162.7 2.2 collective-permute-done.24
  165.4 2.5 collective-permute-start.25
  167.9 2.8 %collective-permute-done.25 = f32[]{:T(128)} collective-permute-done((f32[]{:T(128)}, f32[]{:T(128)}, u32[]{:S(2)}, u32[]{:S(2)}) %collective-permute-start.25) | collective-permute-done | bytes 36 | tf_op jit(solution)/shard_map/ppermute | solution.py:115
  173.3 1.8 collective-permute-start.28
  175.0 2.9 %collective-permute-start.27 = (bf16[64,3072]{1,0:T(8,128)(2,1)S(1)}, bf16[64,3072]{1,0:T(8,128)(2,1)S(1)}, u32[]{:S(2)}, u32[]{:S(2)}) collective-permute-start(bf16[64,3072]{1,0:T(8,128)(2,1)S(1)} %get-tuple-element.16), channel_id=1, source_target_pairs={{2,0},{3,1},{0,2},{1,3},{6,4},{7,5},{4,6},{5,7},{10,8},{11,9},{8,1... | collective-permute-start | bytes 1179656 | tf_op jit(solution)/shard_map/ppermute | solution.py:125
  178.6 6.3 %collective-permute-done.28 = bf16[64,3072]{1,0:T(8,128)(2,1)S(1)} collective-permute-done((bf16[64,3072]{1,0:T(8,128)(2,1)S(1)}, bf16[64,3072]{1,0:T(8,128)(2,1)S(1)}, u32[]{:S(2)}, u32[]{:S(2)}) %collective-permute-start.28) | collective-permute-done | bytes 393248 | tf_op jit(solution)/shard_map/ppermute | solution.py:125
  184.8 4.2 %collective-permute-done.27 = bf16[64,3072]{1,0:T(8,128)(2,1)S(1)} collective-permute-done((bf16[64,3072]{1,0:T(8,128)(2,1)S(1)}, bf16[64,3072]{1,0:T(8,128)(2,1)S(1)}, u32[]{:S(2)}, u32[]{:S(2)}) %collective-permute-start.27) | collective-permute-done | bytes 393248 | tf_op jit(solution)/shard_map/ppermute | solution.py:125
  190.0 1.9 collective-permute-start.29
  192.0 6.0 %collective-permute-start.30 = (bf16[64,1408]{1,0:T(8,128)(2,1)S(1)}, bf16[64,1408]{1,0:T(8,128)(2,1)S(1)}, u32[]{:S(2)}, u32[]{:S(2)}) collective-permute-start(bf16[64,1408]{1,0:T(8,128)(2,1)S(1)} %get-tuple-element.30), channel_id=1, source_target_pairs={{4,0},{8,4},{12,8},{16,12},{20,16},{24,20},{28,24},{32,28},{36,32}... | collective-permute-start | bytes 540680 | tf_op jit(solution)/shard_map/ppermute | solution.py:105
  201.8 8.1 %shard_map.88 = f32[64,3072]{1,0:T(8,128)} custom-call(s32[24]{0:T(128)} %clamp_bitcast_fusion.begin_ref, bf16[46,64,128]{2,1,0:T(8,128)(2,1)} %bitcast_bitcast_fusion.win_ref, bf16[24,128,1536]{2,1,0:T(8,128)(2,1)} %shard_map.86.tile_ref, f32[64,3072]{1,0:T(8,128)} %get-tuple-element.17.p_ref, f32[64,1]{1,0:T(8,128)} %copy.25.noise_ref), custom_call_target="tpu_custom_call" | custom-call | tf_op jit(solution)/shard_map/pallas_call | solution.py:81
  210.0 2.1 multiply_reduce_fusion
  213.7 2.4 copy.28
  217.2 14.4 %scatter_custom_fusion = f32[256,3072]{0,1:T(8,128)S(1)} fusion(s32[3072]{0:T(1024)S(1)} %get-tuple-element.21, f32[3072,256]{1,0:T(8,128)} %copy.28, f32[]{:T(128)} %constant.10.clone.1), kind=kCustom, calls=%fused_computation.19 | custom fusion | bytes 3146240 | tf_op jit(solution)/shard_map/scatter | solution.py:179
  232.9 3.8 %collective-permute-start.32 = (f32[]{:T(128)}, f32[]{:T(128)}, u32[]{:S(2)}, u32[]{:S(2)}) collective-permute-start(f32[]{:T(128)} %add.112), channel_id=1, source_target_pairs={{0,2},{1,3},{2,0},{3,1},{4,6},{5,7},{6,4},{7,5},{8,10},{9,11},{10,... | collective-permute-start | bytes 20 | tf_op jit(solution)/shard_map/ppermute | solution.py:115
  241.9 2.2 collective-permute-done.34
  246.2 3.1 %collective-permute-done.35 = f32[]{:T(128)} collective-permute-done((f32[]{:T(128)}, f32[]{:T(128)}, u32[]{:S(2)}, u32[]{:S(2)}) %collective-permute-start.35) | collective-permute-done | bytes 36 | tf_op jit(solution)/shard_map/ppermute | solution.py:115
  250.0 3.3 %collective-permute-start.36 = (f32[]{:T(128)}, f32[]{:T(128)}, u32[]{:S(2)}, u32[]{:S(2)}) collective-permute-start(f32[]{:T(128)} %add.116), channel_id=1, source_target_pairs={{0,32},{4,36},{8,40},{12,44},{16,48},{20,52},{24,56},{28,60},{32,0... | collective-permute-start | bytes 20 | tf_op jit(solution)/shard_map/ppermute | solution.py:115
  253.3 4.2 %collective-permute-done.36 = f32[]{:T(128)} collective-permute-done((f32[]{:T(128)}, f32[]{:T(128)}, u32[]{:S(2)}, u32[]{:S(2)}) %collective-permute-start.36) | collective-permute-done | bytes 36 | tf_op jit(solution)/shard_map/ppermute | solution.py:115
  259.5 2.2 collective-permute-done.37
  262.4 2.8 %collective-permute-start.38 = (f32[]{:T(128)}, f32[]{:T(128)}, u32[]{:S(2)}, u32[]{:S(2)}) collective-permute-start(f32[]{:T(128)} %add.118), channel_id=1, source_target_pairs={{0,128},{4,132},{8,136},{12,140},{16,144},{20,148},{24,152},{28,15... | collective-permute-start | bytes 20 | tf_op jit(solution)/shard_map/ppermute | solution.py:115
  265.1 2.3 collective-permute-done.38
  268.2 2.6 fusion
  270.8 2.9 %copy.30 = f32[64,3072]{1,0:T(8,128)} copy(f32[64,3072]{0,1:T(8,128)} %get-tuple-element.22) | data formatting | bytes 1572864
  (101 shorter events, 56.3 us)
Async XLA Ops:
  0.6 6.7 %copy-start.8 = (f32[6,3072]{1,0:T(8,128)S(1)}, f32[6,3072]{1,0:T(8,128)}, u32[]{:S(2)}) copy-start(f32[6,3072]{1,0:T(8,128)} %param.8) | copy-start | bytes 221188
  0.6 38.0 %collective-permute-start.6 = (f32[64,256]{1,0:T(8,128)}, f32[64,256]{1,0:T(8,128)S(1)}, u32[]{:S(2)}, u32[]{:S(2)}) collective-permute-start(f32[64,256]{1,0:T(8,128)} %param.9), channel_id=1, source_target_pairs={{2,0},{3,1},{0,2},{1,3},{6,4},{7,5},{4,6},{5,7},{10,8},{11,9},{8,1... | collective-permute-start | bytes 196616 | tf_op jit(solution)/shard_map/ppermute | solution.py:125
  3.9 62.6 %collective-permute-start.5 = (f32[64,256]{1,0:T(8,128)}, f32[64,256]{1,0:T(8,128)S(1)}, u32[]{:S(2)}, u32[]{:S(2)}) collective-permute-start(f32[64,256]{1,0:T(8,128)} %param.9), channel_id=1, source_target_pairs={{1,0},{2,1},{3,2},{0,3},{5,4},{6,5},{7,6},{4,7},{9,8},{10,9},{11,1... | collective-permute-start | bytes 196616 | tf_op jit(solution)/shard_map/ppermute | solution.py:125
  21.7 11.2 %collective-permute-start = (f32[6,1408]{1,0:T(8,128)S(1)}, f32[6,1408]{1,0:T(8,128)S(1)}, u32[]{:S(2)}, u32[]{:S(2)}) collective-permute-start(f32[6,1408]{1,0:T(8,128)S(1)} %get-tuple-element.26), channel_id=1, source_target_pairs={{0,4},{4,8},{8,12},{12,16},{16,20},{20,24},{24,28},{28,32},{32,36}... | collective-permute-start | bytes 101384 | tf_op jit(solution)/shard_map/ppermute | solution.py:102
  23.6 9.3 %collective-permute-start.1 = (f32[6,1408]{1,0:T(8,128)S(1)}, f32[6,1408]{1,0:T(8,128)S(1)}, u32[]{:S(2)}, u32[]{:S(2)}) collective-permute-start(f32[6,1408]{1,0:T(8,128)S(1)} %get-tuple-element.27), channel_id=1, source_target_pairs={{4,0},{8,4},{12,8},{16,12},{20,16},{24,20},{28,24},{32,28},{36,32}... | collective-permute-start | bytes 101384 | tf_op jit(solution)/shard_map/ppermute | solution.py:105
  33.0 33.9 %collective-permute-start.4 = (bf16[64,3072]{1,0:T(8,128)(2,1)S(1)}, bf16[64,3072]{1,0:T(8,128)(2,1)S(1)}, u32[]{:S(2)}, u32[]{:S(2)}) collective-permute-start(bf16[64,3072]{1,0:T(8,128)(2,1)S(1)} %convert_element_type.18), channel_id=1, source_target_pairs={{3,0},{0,1},{1,2},{2,3},{7,4},{4,5},{5,6},{6,7},{11,8},{8,9},{9,10... | collective-permute-start | bytes 1179656 | tf_op jit(solution)/shard_map/ppermute | solution.py:125
  34.0 32.9 %collective-permute-start.3 = (bf16[64,3072]{1,0:T(8,128)(2,1)S(1)}, bf16[64,3072]{1,0:T(8,128)(2,1)S(1)}, u32[]{:S(2)}, u32[]{:S(2)}) collective-permute-start(bf16[64,3072]{1,0:T(8,128)(2,1)S(1)} %convert_element_type.18), channel_id=1, source_target_pairs={{2,0},{3,1},{0,2},{1,3},{6,4},{7,5},{4,6},{5,7},{10,8},{11,9},{8,1... | collective-permute-start | bytes 1179656 | tf_op jit(solution)/shard_map/ppermute | solution.py:125
  34.9 32.1 %collective-permute-start.2 = (bf16[64,3072]{1,0:T(8,128)(2,1)S(1)}, bf16[64,3072]{1,0:T(8,128)(2,1)S(1)}, u32[]{:S(2)}, u32[]{:S(2)}) collective-permute-start(bf16[64,3072]{1,0:T(8,128)(2,1)S(1)} %convert_element_type.18), channel_id=1, source_target_pairs={{1,0},{2,1},{3,2},{0,3},{5,4},{6,5},{7,6},{4,7},{9,8},{10,9},{11,1... | collective-permute-start | bytes 1179656 | tf_op jit(solution)/shard_map/ppermute | solution.py:125
  38.7 27.9 %collective-permute-start.7 = (f32[64,256]{1,0:T(8,128)S(1)}, f32[64,256]{1,0:T(8,128)S(1)}, u32[]{:S(2)}, u32[]{:S(2)}) collective-permute-start(f32[64,256]{1,0:T(8,128)S(1)} %copy-done.10), channel_id=1, source_target_pairs={{3,0},{0,1},{1,2},{2,3},{7,4},{4,5},{5,6},{6,7},{11,8},{8,9},{9,10... | collective-permute-start | bytes 196616 | tf_op jit(solution)/shard_map/ppermute | solution.py:125
  67.1 8.7 %copy-start.9 = (f32[64]{0:T(128)S(1)}, f32[64]{0:T(128)}, u32[]{:S(2)}) copy-start(f32[64]{0:T(128)} %param.10) | copy-start | bytes 772
  68.0 8.9 %collective-permute-start.8 = (bf16[64,1408]{1,0:T(8,128)(2,1)S(1)}, bf16[64,1408]{1,0:T(8,128)(2,1)S(1)}, u32[]{:S(2)}, u32[]{:S(2)}) collective-permute-start(bf16[64,1408]{1,0:T(8,128)(2,1)S(1)} %get-tuple-element.31), channel_id=1, source_target_pairs={{0,4},{4,8},{8,12},{12,16},{16,20},{20,24},{24,28},{28,32},{32,36}... | collective-permute-start | bytes 540680 | tf_op jit(solution)/shard_map/ppermute | solution.py:102
  70.0 8.8 %collective-permute-start.9 = (bf16[64,1408]{1,0:T(8,128)(2,1)S(1)}, bf16[64,1408]{1,0:T(8,128)(2,1)S(1)}, u32[]{:S(2)}, u32[]{:S(2)}) collective-permute-start(bf16[64,1408]{1,0:T(8,128)(2,1)S(1)} %get-tuple-element.32), channel_id=1, source_target_pairs={{4,0},{8,4},{12,8},{16,12},{20,16},{24,20},{28,24},{32,28},{36,32}... | collective-permute-start | bytes 540680 | tf_op jit(solution)/shard_map/ppermute | solution.py:105
  79.8 8.1 %copy-start.1 = (f32[64,3072]{1,0:T(8,128)S(1)}, f32[64,3072]{1,0:T(8,128)}, u32[]{:S(2)}) copy-start(f32[64,3072]{1,0:T(8,128)} %copy-done) | copy-start | bytes 2359300
  87.9 42.0 %copy-start.5 = (f32[64,3072]{1,0:T(8,128)S(1)}, f32[64,3072]{1,0:T(8,128)}, u32[]{:S(2)}) copy-start(f32[64,3072]{1,0:T(8,128)} %shard_map.87) | copy-start | bytes 2359300
  91.3 3.7 %collective-permute-start.10 = (f32[2]{0:T(128)S(1)}, f32[2]{0:T(128)S(1)}, u32[]{:S(2)}, u32[]{:S(2)}) collective-permute-start(f32[2]{0:T(128)S(1)} %pad_maximum_fusion.3), channel_id=1, source_target_pairs={{0,1},{1,0},{2,3},{3,2},{4,5},{5,4},{6,7},{7,6},{8,9},{9,8},{10,11... | collective-permute-start | bytes 32 | tf_op jit(solution)/shard_map/ppermute | solution.py:115
  96.4 5.1 %collective-permute-start.11 = (f32[2]{0:T(128)S(1)}, f32[2]{0:T(128)S(1)}, u32[]{:S(2)}, u32[]{:S(2)}) collective-permute-start(f32[2]{0:T(128)S(1)} %fusion.29), channel_id=1, source_target_pairs={{0,2},{1,3},{2,0},{3,1},{4,6},{5,7},{6,4},{7,5},{8,10},{9,11},{10,... | collective-permute-start | bytes 32 | tf_op jit(solution)/shard_map/ppermute | solution.py:115
  102.8 1.1 collective-permute-start.12
  104.0 3.5 %collective-permute-start.13 = (f32[2]{0:T(128)S(1)}, f32[2]{0:T(128)S(1)}, u32[]{:S(2)}, u32[]{:S(2)}) collective-permute-start(f32[2]{0:T(128)S(1)} %add.97), channel_id=1, source_target_pairs={{0,8},{4,12},{8,0},{12,4},{16,24},{20,28},{24,16},{28,20},{32,40},... | collective-permute-start | bytes 32 | tf_op jit(solution)/shard_map/ppermute | solution.py:115
  107.5 4.4 %collective-permute-start.14 = (f32[2]{0:T(128)S(1)}, f32[2]{0:T(128)S(1)}, u32[]{:S(2)}, u32[]{:S(2)}) collective-permute-start(f32[2]{0:T(128)S(1)} %add.98), channel_id=1, source_target_pairs={{0,16},{4,20},{8,24},{12,28},{16,0},{20,4},{24,8},{28,12},{32,48},... | collective-permute-start | bytes 32 | tf_op jit(solution)/shard_map/ppermute | solution.py:115
  112.0 7.4 %collective-permute-start.15 = (f32[2]{0:T(128)S(1)}, f32[2]{0:T(128)S(1)}, u32[]{:S(2)}, u32[]{:S(2)}) collective-permute-start(f32[2]{0:T(128)S(1)} %add.99), channel_id=1, source_target_pairs={{0,32},{4,36},{8,40},{12,44},{16,48},{20,52},{24,56},{28,60},{32,0... | collective-permute-start | bytes 32 | tf_op jit(solution)/shard_map/ppermute | solution.py:115
  119.4 3.5 %collective-permute-start.16 = (f32[2]{0:T(128)S(1)}, f32[2]{0:T(128)S(1)}, u32[]{:S(2)}, u32[]{:S(2)}) collective-permute-start(f32[2]{0:T(128)S(1)} %add.100), channel_id=1, source_target_pairs={{0,64},{4,68},{8,72},{12,76},{16,80},{20,84},{24,88},{28,92},{32,9... | collective-permute-start | bytes 32 | tf_op jit(solution)/shard_map/ppermute | solution.py:115
  123.0 5.0 %collective-permute-start.17 = (f32[2]{0:T(128)S(1)}, f32[2]{0:T(128)S(1)}, u32[]{:S(2)}, u32[]{:S(2)}) collective-permute-start(f32[2]{0:T(128)S(1)} %add.101), channel_id=1, source_target_pairs={{0,128},{4,132},{8,136},{12,140},{16,144},{20,148},{24,152},{28,15... | collective-permute-start | bytes 32 | tf_op jit(solution)/shard_map/ppermute | solution.py:115
  130.7 42.5 %copy-start.6 = (f32[64,3072]{1,0:T(8,128)}, f32[64,3072]{1,0:T(8,128)S(1)}, u32[]{:S(2)}) copy-start(f32[64,3072]{1,0:T(8,128)S(1)} %get-tuple-element.19) | copy-start | bytes 2359300
  130.7 3.8 %collective-permute-start.18 = (f32[]{:T(128)}, f32[]{:T(128)}, u32[]{:S(2)}, u32[]{:S(2)}) collective-permute-start(f32[]{:T(128)} %get-tuple-element.18), channel_id=1, source_target_pairs={{0,1},{1,0},{2,3},{3,2},{4,5},{5,4},{6,7},{7,6},{8,9},{9,8},{10,11... | collective-permute-start | bytes 20 | tf_op jit(solution)/shard_map/ppermute | solution.py:115
  135.7 5.2 %collective-permute-start.19 = (f32[]{:T(128)}, f32[]{:T(128)}, u32[]{:S(2)}, u32[]{:S(2)}) collective-permute-start(f32[]{:T(128)} %add.103), channel_id=1, source_target_pairs={{0,2},{1,3},{2,0},{3,1},{4,6},{5,7},{6,4},{7,5},{8,10},{9,11},{10,... | collective-permute-start | bytes 20 | tf_op jit(solution)/shard_map/ppermute | solution.py:115
  141.5 1.3 collective-permute-start.20
  143.4 3.7 %collective-permute-start.21 = (f32[]{:T(128)}, f32[]{:T(128)}, u32[]{:S(2)}, u32[]{:S(2)}) collective-permute-start(f32[]{:T(128)} %add.105), channel_id=1, source_target_pairs={{0,8},{4,12},{8,0},{12,4},{16,24},{20,28},{24,16},{28,20},{32,40},... | collective-permute-start | bytes 20 | tf_op jit(solution)/shard_map/ppermute | solution.py:115
  147.7 4.6 %collective-permute-start.22 = (f32[]{:T(128)}, f32[]{:T(128)}, u32[]{:S(2)}, u32[]{:S(2)}) collective-permute-start(f32[]{:T(128)} %add.106), channel_id=1, source_target_pairs={{0,16},{4,20},{8,24},{12,28},{16,0},{20,4},{24,8},{28,12},{32,48},... | collective-permute-start | bytes 20 | tf_op jit(solution)/shard_map/ppermute | solution.py:115
  152.9 7.6 %collective-permute-start.23 = (f32[]{:T(128)}, f32[]{:T(128)}, u32[]{:S(2)}, u32[]{:S(2)}) collective-permute-start(f32[]{:T(128)} %add.107), channel_id=1, source_target_pairs={{0,32},{4,36},{8,40},{12,44},{16,48},{20,52},{24,56},{28,60},{32,0... | collective-permute-start | bytes 20 | tf_op jit(solution)/shard_map/ppermute | solution.py:115
  161.1 3.7 %collective-permute-start.24 = (f32[]{:T(128)}, f32[]{:T(128)}, u32[]{:S(2)}, u32[]{:S(2)}) collective-permute-start(f32[]{:T(128)} %add.108), channel_id=1, source_target_pairs={{0,64},{4,68},{8,72},{12,76},{16,80},{20,84},{24,88},{28,92},{32,9... | collective-permute-start | bytes 20 | tf_op jit(solution)/shard_map/ppermute | solution.py:115
  165.4 5.2 %collective-permute-start.25 = (f32[]{:T(128)}, f32[]{:T(128)}, u32[]{:S(2)}, u32[]{:S(2)}) collective-permute-start(f32[]{:T(128)} %add.109), channel_id=1, source_target_pairs={{0,128},{4,132},{8,136},{12,140},{16,144},{20,148},{24,152},{28,15... | collective-permute-start | bytes 20 | tf_op jit(solution)/shard_map/ppermute | solution.py:115
  173.3 11.6 %collective-permute-start.28 = (bf16[64,3072]{1,0:T(8,128)(2,1)S(1)}, bf16[64,3072]{1,0:T(8,128)(2,1)S(1)}, u32[]{:S(2)}, u32[]{:S(2)}) collective-permute-start(bf16[64,3072]{1,0:T(8,128)(2,1)S(1)} %get-tuple-element.16), channel_id=1, source_target_pairs={{3,0},{0,1},{1,2},{2,3},{7,4},{4,5},{5,6},{6,7},{11,8},{8,9},{9,10... | collective-permute-start | bytes 1179656 | tf_op jit(solution)/shard_map/ppermute | solution.py:125
  175.0 14.0 %collective-permute-start.27 = (bf16[64,3072]{1,0:T(8,128)(2,1)S(1)}, bf16[64,3072]{1,0:T(8,128)(2,1)S(1)}, u32[]{:S(2)}, u32[]{:S(2)}) collective-permute-start(bf16[64,3072]{1,0:T(8,128)(2,1)S(1)} %get-tuple-element.16), channel_id=1, source_target_pairs={{2,0},{3,1},{0,2},{1,3},{6,4},{7,5},{4,6},{5,7},{10,8},{11,9},{8,1... | collective-permute-start | bytes 1179656 | tf_op jit(solution)/shard_map/ppermute | solution.py:125
  177.9 11.1 %collective-permute-start.26 = (bf16[64,3072]{1,0:T(8,128)(2,1)S(1)}, bf16[64,3072]{1,0:T(8,128)(2,1)S(1)}, u32[]{:S(2)}, u32[]{:S(2)}) collective-permute-start(bf16[64,3072]{1,0:T(8,128)(2,1)S(1)} %get-tuple-element.16), channel_id=1, source_target_pairs={{1,0},{2,1},{3,2},{0,3},{5,4},{6,5},{7,6},{4,7},{9,8},{10,9},{11,1... | collective-permute-start | bytes 1179656 | tf_op jit(solution)/shard_map/ppermute | solution.py:125
  190.0 8.9 %collective-permute-start.29 = (bf16[64,1408]{1,0:T(8,128)(2,1)S(1)}, bf16[64,1408]{1,0:T(8,128)(2,1)S(1)}, u32[]{:S(2)}, u32[]{:S(2)}) collective-permute-start(bf16[64,1408]{1,0:T(8,128)(2,1)S(1)} %get-tuple-element.29), channel_id=1, source_target_pairs={{0,4},{4,8},{8,12},{12,16},{16,20},{20,24},{24,28},{28,32},{32,36}... | collective-permute-start | bytes 540680 | tf_op jit(solution)/shard_map/ppermute | solution.py:102
  192.0 8.8 %collective-permute-start.30 = (bf16[64,1408]{1,0:T(8,128)(2,1)S(1)}, bf16[64,1408]{1,0:T(8,128)(2,1)S(1)}, u32[]{:S(2)}, u32[]{:S(2)}) collective-permute-start(bf16[64,1408]{1,0:T(8,128)(2,1)S(1)} %get-tuple-element.30), channel_id=1, source_target_pairs={{4,0},{8,4},{12,8},{16,12},{20,16},{24,20},{28,24},{32,28},{36,32}... | collective-permute-start | bytes 540680 | tf_op jit(solution)/shard_map/ppermute | solution.py:105
  201.8 8.2 %copy-start.2 = (f32[64,3072]{1,0:T(8,128)S(1)}, f32[64,3072]{1,0:T(8,128)}, u32[]{:S(2)}) copy-start(f32[64,3072]{1,0:T(8,128)} %get-tuple-element.17.p_ref) | copy-start | bytes 2359300
  210.0 2.1 copy-start.3
  210.0 2.1 copy-start.4
  216.1 15.6 %collective-permute-start.31 = (f32[]{:T(128)}, f32[]{:T(128)}, u32[]{:S(2)}, u32[]{:S(2)}) collective-permute-start(f32[]{:T(128)} %multiply_reduce_fusion), channel_id=1, source_target_pairs={{0,1},{1,0},{2,3},{3,2},{4,5},{5,4},{6,7},{7,6},{8,9},{9,8},{10,11... | collective-permute-start | bytes 20 | tf_op jit(solution)/shard_map/ppermute | solution.py:115
  232.9 5.1 %collective-permute-start.32 = (f32[]{:T(128)}, f32[]{:T(128)}, u32[]{:S(2)}, u32[]{:S(2)}) collective-permute-start(f32[]{:T(128)} %add.112), channel_id=1, source_target_pairs={{0,2},{1,3},{2,0},{3,1},{4,6},{5,7},{6,4},{7,5},{8,10},{9,11},{10,... | collective-permute-start | bytes 20 | tf_op jit(solution)/shard_map/ppermute | solution.py:115
  238.7 1.2 collective-permute-start.33
  240.5 3.6 %collective-permute-start.34 = (f32[]{:T(128)}, f32[]{:T(128)}, u32[]{:S(2)}, u32[]{:S(2)}) collective-permute-start(f32[]{:T(128)} %add.114), channel_id=1, source_target_pairs={{0,8},{4,12},{8,0},{12,4},{16,24},{20,28},{24,16},{28,20},{32,40},... | collective-permute-start | bytes 20 | tf_op jit(solution)/shard_map/ppermute | solution.py:115
  244.8 4.5 %collective-permute-start.35 = (f32[]{:T(128)}, f32[]{:T(128)}, u32[]{:S(2)}, u32[]{:S(2)}) collective-permute-start(f32[]{:T(128)} %add.115), channel_id=1, source_target_pairs={{0,16},{4,20},{8,24},{12,28},{16,0},{20,4},{24,8},{28,12},{32,48},... | collective-permute-start | bytes 20 | tf_op jit(solution)/shard_map/ppermute | solution.py:115
  250.0 7.5 %collective-permute-start.36 = (f32[]{:T(128)}, f32[]{:T(128)}, u32[]{:S(2)}, u32[]{:S(2)}) collective-permute-start(f32[]{:T(128)} %add.116), channel_id=1, source_target_pairs={{0,32},{4,36},{8,40},{12,44},{16,48},{20,52},{24,56},{28,60},{32,0... | collective-permute-start | bytes 20 | tf_op jit(solution)/shard_map/ppermute | solution.py:115
  258.1 3.6 %collective-permute-start.37 = (f32[]{:T(128)}, f32[]{:T(128)}, u32[]{:S(2)}, u32[]{:S(2)}) collective-permute-start(f32[]{:T(128)} %add.117), channel_id=1, source_target_pairs={{0,64},{4,68},{8,72},{12,76},{16,80},{20,84},{24,88},{28,92},{32,9... | collective-permute-start | bytes 20 | tf_op jit(solution)/shard_map/ppermute | solution.py:115
  262.4 5.1 %collective-permute-start.38 = (f32[]{:T(128)}, f32[]{:T(128)}, u32[]{:S(2)}, u32[]{:S(2)}) collective-permute-start(f32[]{:T(128)} %add.118), channel_id=1, source_target_pairs={{0,128},{4,132},{8,136},{12,140},{16,144},{20,148},{24,152},{28,15... | collective-permute-start | bytes 20 | tf_op jit(solution)/shard_map/ppermute | solution.py:115
  270.8 2.9 %copy-start.7 = (f32[64,3072]{0,1:T(8,128)S(1)}, f32[64,3072]{0,1:T(8,128)}, u32[]{:S(2)}) copy-start(f32[64,3072]{0,1:T(8,128)} %get-tuple-element.23) | copy-start | bytes 2359300
  (2 other events, 3.2 us)

commit v14 on v12

--- a/solution.py
+++ b/solution.py
@@ -59,9 +59,10 @@
     )(begin, count, own_t, win_c)
 
 
-def apply_kernel(begin_ref, win_ref, tile_ref, p_ref, noise_ref, out_ref, *, per_step, slots, runs):
+def apply_kernel(begin_ref, win_ref, tile_ref, p_ref, noise_ref, out_ref, sum_ref, *, per_step, slots, runs):
     g = pl.program_id(0)
     noise = noise_ref[...]
+    partial = jnp.zeros((1, runs), jnp.float32)
     for k in range(per_step):
         start = begin_ref[g * per_step + k]
         vals = win_ref[pl.ds(start, slots)]
@@ -70,7 +71,11 @@
             cat, tile_ref[k], (((1,), (1,)), ((), ())), preferred_element_type=jnp.float32
         )
         cols = slice(k * runs, (k + 1) * runs)
-        out_ref[:, cols] = AMPLITUDE * acc + noise * p_ref[:, cols]
+        p_blk = p_ref[:, cols]
+        val = AMPLITUDE * acc + noise * p_blk
+        out_ref[:, cols] = val
+        partial = partial + jnp.sum(p_blk * val, axis=0, keepdims=True)
+    sum_ref[...] = jnp.broadcast_to(partial, sum_ref.shape)
 
 
 def apply_operator(begin, win_v, tiles, direction, noise_col, per_step):
@@ -89,9 +94,15 @@
                 pl.BlockSpec((chans, per_step * runs), lambda g, *_: (0, g)),
                 pl.BlockSpec((chans, 1), lambda g, *_: (0, 0)),
             ],
-            out_specs=pl.BlockSpec((chans, per_step * runs), lambda g, *_: (0, g)),
+            out_specs=[
+                pl.BlockSpec((chans, per_step * runs), lambda g, *_: (0, g)),
+                pl.BlockSpec((1, 8, runs), lambda g, *_: (g, 0, 0)),
+            ],
         ),
-        out_shape=jax.ShapeDtypeStruct((chans, total), jnp.float32),
+        out_shape=[
+            jax.ShapeDtypeStruct((chans, total), jnp.float32),
+            jax.ShapeDtypeStruct((blocks // per_step, 8, runs), jnp.float32),
+        ],
     )(begin, win_v, tiles, direction, noise_col)
 
 
@@ -172,8 +183,8 @@
         mixed_b = mixed.astype(jnp.bfloat16)
         widened = extended(mixed_b, "samp", 1, reach_runs)
         win_v = widened.reshape(chan_local, window_blocks, block_runs).transpose(1, 0, 2)
-        mapped = apply_operator(begin, win_v, tiles, direction, noise_col, 4)
-        curvature = jnp.sum(direction * mapped)
+        mapped, partials = apply_operator(begin, win_v, tiles, direction, noise_col, 4)
+        curvature = jnp.sum(partials[:, 0, :])
         if iteration + 1 == ITERS:
             stacked = jnp.concatenate([iterate, remainder, direction, mapped], axis=0)
             unsorted = jnp.zeros_like(stacked).at[:, local_perm].set(stacked)

time: 276 us -> 274 us (level)
  waiting for transfers between devices: 62.5 us -> 78.5 us
  starting transfers between devices: 92.1 us -> 76.2 us
    ppermute x24, waiting for transfers between devices: 46.7 us -> 62.7 us  [global_sum(): value = value + lax.ppermute(value, axis, pairs)]
    ppermute x24, starting transfers between devices: 54.2 us -> 38.3 us  [global_sum(): value = value + lax.ppermute(value, axis, pairs)]
    unnamed x26 -> x18, local copies, waits for them, and re-layouts: 7.51 us -> 7.5 us
  transfers between devices with their start and end apart: 39 -> 39, of which waited for: 29 -> 29; matrix products, arithmetic and copies ran while one was open for 13% -> 13% of each run, Pallas kernels for 9% -> 10%
where the time goes in v14:
time: 274 us
  waiting for transfers between devices  78.5 us (29%)
  starting transfers between devices  76.2 us (28%)
  Pallas kernels  45.2 us (16%)
  local copies, waits for them, and re-layouts  36.7 us (13%)
  other arithmetic  21.4 us (8%)
  between operations  13.7 us (5%)
    ppermute x24, waiting for transfers between devices, global_sum(): value = value + lax.ppermute(value, axis, pairs)  62.7 us
    ppermute x24, starting transfers between devices, global_sum(): value = value + lax.ppermute(value, axis, pairs)  38.3 us
    pallas_call x1, Pallas kernels, build_tiles(): pl.pallas_call(kern, grid_spec=pltpu.PrefetchScalarGridSpec(num_scalar_pr...  27.4 us
    ppermute x3, starting transfers between devices, extended(): lax.ppermute(lax.slice_in_dim(block, 0, width, axis=dim), axis, backward)  18.1 us
    pallas_call x2, Pallas kernels, apply_operator(): pl.pallas_call(kern, grid_spec=pltpu.PrefetchScalarGridSpec(num_scalar_pr...  17.8 us
    scatter x1, local copies, waits for them, and re-layouts, per_device(): unsorted = jnp.zeros_like(stacked).at[:, local_perm].set(stacked)  14.4 us
    ppermute x9, starting transfers between devices, gather_chan(): parts.append(lax.ppermute(rounded, 'chan', pairs))  14 us
    ppermute x9, waiting for transfers between devices, gather_chan(): parts.append(lax.ppermute(rounded, 'chan', pairs))  10.5 us
  transfers between devices with their start and end apart: 39, of which 29 were waited for; matrix products, arithmetic and copies ran while one was open for 13% of the time, Pallas kernels for 10%

profile of v14, /device:TPU:2, one launch (start us, length us, event | category | flops | bytes accessed | tf_op | source)
XLA Modules:
  0.0 273.9 jit_solution(14658184033049987154)
XLA Ops:
  0.6 3.3 %collective-permute-start.6 = (f32[64,256]{1,0:T(8,128)}, f32[64,256]{1,0:T(8,128)S(1)}, u32[]{:S(2)}, u32[]{:S(2)}) collective-permute-start(f32[64,256]{1,0:T(8,128)} %param.9), channel_id=1, source_target_pairs={{2,0},{3,1},{0,2},{1,3},{6,4},{7,5},{4,6},{5,7},{10,8},{11,9},{8,1... | collective-permute-start | bytes 196616 | tf_op jit(solution)/shard_map/ppermute | solution.py:136
  9.0 1.9 pad_maximum_fusion
  10.9 8.1 %gather_fusion = f32[3072,70]{1,0:T(8,128)S(1)} fusion(f32[70,3072]{0,1:T(8,128)S(1)} %pad_maximum_fusion, s32[3072]{0:T(1024)S(1)} %broadcast_clamp_fusion), kind=kCustom, calls=%fused_computation | custom fusion | bytes 1732608 | tf_op jit(solution)/shard_map/jit(_take)/gather | solution.py:150
  19.6 1.9 collective-permute-start
  21.5 6.6 %collective-permute-start.1 = (f32[6,1408]{1,0:T(8,128)S(1)}, f32[6,1408]{1,0:T(8,128)S(1)}, u32[]{:S(2)}, u32[]{:S(2)}) collective-permute-start(f32[6,1408]{1,0:T(8,128)S(1)} %get-tuple-element.35), channel_id=1, source_target_pairs={{4,0},{8,4},{12,8},{16,12},{20,16},{24,20},{28,24},{32,28},{36,32}... | collective-permute-start | bytes 101384 | tf_op jit(solution)/shard_map/ppermute | solution.py:116
  32.8 2.5 collective-permute-start.2
  37.2 27.4 %shard_map.86.tile_ref = bf16[24,128,1536]{2,1,0:T(8,128)(2,1)} custom-call(s32[24]{0:T(128)} %clamp_bitcast_fusion.begin_ref, s32[24]{0:T(128)} %count_ref.1, f32[24,128,8]{2,1,0:T(8,128)} %pad_bitcast_fusion.own_ref, f32[46,8,128]{2,1,0:T(8,128)} %pad_bitcast_fusion.1.win_ref), custom_call_target="tpu_custom_call" | custom-call | tf_op jit(solution)/shard_map/pallas_call | solution.py:47
  66.2 1.9 collective-permute-start.8
  68.1 5.8 %collective-permute-start.9 = (bf16[64,1408]{1,0:T(8,128)(2,1)S(1)}, bf16[64,1408]{1,0:T(8,128)(2,1)S(1)}, u32[]{:S(2)}, u32[]{:S(2)}) collective-permute-start(bf16[64,1408]{1,0:T(8,128)(2,1)S(1)} %get-tuple-element.40), channel_id=1, source_target_pairs={{4,0},{8,4},{12,8},{16,12},{20,16},{24,20},{28,24},{32,28},{36,32}... | collective-permute-start | bytes 540680 | tf_op jit(solution)/shard_map/ppermute | solution.py:116
  77.9 9.0 %shard_map.87 = (f32[64,3072]{1,0:T(8,128)}, f32[6,8,128]{2,1,0:T(8,128)}) custom-call(s32[24]{0:T(128)} %clamp_bitcast_fusion.begin_ref, bf16[46,64,128]{2,1,0:T(8,128)(2,1)} %bitcast_bitcast_fusion.1.win_ref, bf16[24,128,1536]{2,1,0:T(8,128)(2,1)} %shard_map.86.tile_ref, f32[64,3072]{1,0:T(8,128)} %copy-done, f32[64,1]{1,0:T(8,128)} %copy.25.noise_ref), custom_call_target="tpu_custom_call" | custom-call | tf_op jit(solution)/shard_map/pallas_call | solution.py:86
  89.5 1.8 collective-permute-start.10
  94.2 2.7 collective-permute-start.11
  96.9 2.4 collective-permute-done.11
  101.8 3.5 %collective-permute-done.13 = f32[2]{0:T(128)S(1)} collective-permute-done((f32[2]{0:T(128)S(1)}, f32[2]{0:T(128)S(1)}, u32[]{:S(2)}, u32[]{:S(2)}) %collective-permute-start.13) | collective-permute-done | bytes 40 | tf_op jit(solution)/shard_map/ppermute | solution.py:126
  105.4 4.4 %collective-permute-done.14 = f32[2]{0:T(128)S(1)} collective-permute-done((f32[2]{0:T(128)S(1)}, f32[2]{0:T(128)S(1)}, u32[]{:S(2)}, u32[]{:S(2)}) %collective-permute-start.14) | collective-permute-done | bytes 40 | tf_op jit(solution)/shard_map/ppermute | solution.py:126
  111.4 5.8 %collective-permute-done.15 = f32[2]{0:T(128)S(1)} collective-permute-done((f32[2]{0:T(128)S(1)}, f32[2]{0:T(128)S(1)}, u32[]{:S(2)}, u32[]{:S(2)}) %collective-permute-start.15) | collective-permute-done | bytes 40 | tf_op jit(solution)/shard_map/ppermute | solution.py:126
  117.3 3.5 %collective-permute-done.16 = f32[2]{0:T(128)S(1)} collective-permute-done((f32[2]{0:T(128)S(1)}, f32[2]{0:T(128)S(1)}, u32[]{:S(2)}, u32[]{:S(2)}) %collective-permute-start.16) | collective-permute-done | bytes 40 | tf_op jit(solution)/shard_map/ppermute | solution.py:126
  121.0 4.9 %collective-permute-done.17 = f32[2]{0:T(128)S(1)} collective-permute-done((f32[2]{0:T(128)S(1)}, f32[2]{0:T(128)S(1)}, u32[]{:S(2)}, u32[]{:S(2)}) %collective-permute-start.17) | collective-permute-done | bytes 40 | tf_op jit(solution)/shard_map/ppermute | solution.py:126
  127.6 1.9 multiply_reduce_fusion
  129.6 1.8 collective-permute-start.18
  131.4 2.0 collective-permute-done.18
  134.5 4.1 %collective-permute-start.19 = (f32[]{:T(128)}, f32[]{:T(128)}, u32[]{:S(2)}, u32[]{:S(2)}) collective-permute-start(f32[]{:T(128)} %add.103), channel_id=1, source_target_pairs={{0,2},{1,3},{2,0},{3,1},{4,6},{5,7},{6,4},{7,5},{8,10},{9,11},{10,... | collective-permute-start | bytes 20 | tf_op jit(solution)/shard_map/ppermute | solution.py:126
  143.6 2.3 collective-permute-done.21
  147.9 3.2 %collective-permute-done.22 = f32[]{:T(128)} collective-permute-done((f32[]{:T(128)}, f32[]{:T(128)}, u32[]{:S(2)}, u32[]{:S(2)}) %collective-permute-start.22) | collective-permute-done | bytes 36 | tf_op jit(solution)/shard_map/ppermute | solution.py:126
  151.7 3.9 %collective-permute-start.23 = (f32[]{:T(128)}, f32[]{:T(128)}, u32[]{:S(2)}, u32[]{:S(2)}) collective-permute-start(f32[]{:T(128)} %add.107), channel_id=1, source_target_pairs={{0,32},{4,36},{8,40},{12,44},{16,48},{20,52},{24,56},{28,60},{32,0... | collective-permute-start | bytes 20 | tf_op jit(solution)/shard_map/ppermute | solution.py:126
  155.7 3.7 %collective-permute-done.23 = f32[]{:T(128)} collective-permute-done((f32[]{:T(128)}, f32[]{:T(128)}, u32[]{:S(2)}, u32[]{:S(2)}) %collective-permute-start.23) | collective-permute-done | bytes 36 | tf_op jit(solution)/shard_map/ppermute | solution.py:126
  161.3 2.3 collective-permute-done.24
  165.8 3.7 %collective-permute-done.25 = f32[]{:T(128)} collective-permute-done((f32[]{:T(128)}, f32[]{:T(128)}, u32[]{:S(2)}, u32[]{:S(2)}) %collective-permute-start.25) | collective-permute-done | bytes 36 | tf_op jit(solution)/shard_map/ppermute | solution.py:126
  172.0 1.8 collective-permute-start.28
  173.8 2.9 %collective-permute-start.27 = (bf16[64,3072]{1,0:T(8,128)(2,1)S(1)}, bf16[64,3072]{1,0:T(8,128)(2,1)S(1)}, u32[]{:S(2)}, u32[]{:S(2)}) collective-permute-start(bf16[64,3072]{1,0:T(8,128)(2,1)S(1)} %get-tuple-element.24), channel_id=1, source_target_pairs={{2,0},{3,1},{0,2},{1,3},{6,4},{7,5},{4,6},{5,7},{10,8},{11,9},{8,1... | collective-permute-start | bytes 1179656 | tf_op jit(solution)/shard_map/ppermute | solution.py:136
  177.3 6.3 %collective-permute-done.28 = bf16[64,3072]{1,0:T(8,128)(2,1)S(1)} collective-permute-done((bf16[64,3072]{1,0:T(8,128)(2,1)S(1)}, bf16[64,3072]{1,0:T(8,128)(2,1)S(1)}, u32[]{:S(2)}, u32[]{:S(2)}) %collective-permute-start.28) | collective-permute-done | bytes 393248 | tf_op jit(solution)/shard_map/ppermute | solution.py:136
  183.6 4.2 %collective-permute-done.27 = bf16[64,3072]{1,0:T(8,128)(2,1)S(1)} collective-permute-done((bf16[64,3072]{1,0:T(8,128)(2,1)S(1)}, bf16[64,3072]{1,0:T(8,128)(2,1)S(1)}, u32[]{:S(2)}, u32[]{:S(2)}) %collective-permute-start.27) | collective-permute-done | bytes 393248 | tf_op jit(solution)/shard_map/ppermute | solution.py:136
  188.8 1.9 collective-permute-start.29
  190.7 5.8 %collective-permute-start.30 = (bf16[64,1408]{1,0:T(8,128)(2,1)S(1)}, bf16[64,1408]{1,0:T(8,128)(2,1)S(1)}, u32[]{:S(2)}, u32[]{:S(2)}) collective-permute-start(bf16[64,1408]{1,0:T(8,128)(2,1)S(1)} %get-tuple-element.38), channel_id=1, source_target_pairs={{4,0},{8,4},{12,8},{16,12},{20,16},{24,20},{28,24},{32,28},{36,32}... | collective-permute-start | bytes 540680 | tf_op jit(solution)/shard_map/ppermute | solution.py:116
  200.5 8.8 %shard_map.88 = (f32[64,3072]{1,0:T(8,128)}, f32[6,8,128]{2,1,0:T(8,128)}) custom-call(s32[24]{0:T(128)} %clamp_bitcast_fusion.begin_ref, bf16[46,64,128]{2,1,0:T(8,128)(2,1)} %bitcast_bitcast_fusion.win_ref, bf16[24,128,1536]{2,1,0:T(8,128)(2,1)} %shard_map.86.tile_ref, f32[64,3072]{1,0:T(8,128)} %get-tuple-element.25.p_ref, f32[64,1]{1,0:T(8,128)} %copy.25.noise_ref), custom_call_target="tpu_custom_call" | custom-call | tf_op jit(solution)/shard_map/pallas_call | solution.py:86
  210.8 2.1 maximum_bitcast_fusion
  212.9 2.3 copy.28
  216.4 14.4 %scatter_custom_fusion = f32[256,3072]{0,1:T(8,128)S(1)} fusion(s32[3072]{0:T(1024)S(1)} %get-tuple-element.29, f32[3072,256]{1,0:T(8,128)} %copy.28, f32[]{:T(128)} %constant.10.clone.1), kind=kCustom, calls=%fused_computation.19 | custom fusion | bytes 3146240 | tf_op jit(solution)/shard_map/scatter | solution.py:190
  232.1 3.8 %collective-permute-start.32 = (f32[]{:T(128)}, f32[]{:T(128)}, u32[]{:S(2)}, u32[]{:S(2)}) collective-permute-start(f32[]{:T(128)} %add.112), channel_id=1, source_target_pairs={{0,2},{1,3},{2,0},{3,1},{4,6},{5,7},{6,4},{7,5},{8,10},{9,11},{10,... | collective-permute-start | bytes 20 | tf_op jit(solution)/shard_map/ppermute | solution.py:126
  241.1 2.2 collective-permute-done.34
  245.3 3.1 %collective-permute-done.35 = f32[]{:T(128)} collective-permute-done((f32[]{:T(128)}, f32[]{:T(128)}, u32[]{:S(2)}, u32[]{:S(2)}) %collective-permute-start.35) | collective-permute-done | bytes 36 | tf_op jit(solution)/shard_map/ppermute | solution.py:126
  249.0 3.3 %collective-permute-start.36 = (f32[]{:T(128)}, f32[]{:T(128)}, u32[]{:S(2)}, u32[]{:S(2)}) collective-permute-start(f32[]{:T(128)} %add.116), channel_id=1, source_target_pairs={{0,32},{4,36},{8,40},{12,44},{16,48},{20,52},{24,56},{28,60},{32,0... | collective-permute-start | bytes 20 | tf_op jit(solution)/shard_map/ppermute | solution.py:126
  252.3 4.2 %collective-permute-done.36 = f32[]{:T(128)} collective-permute-done((f32[]{:T(128)}, f32[]{:T(128)}, u32[]{:S(2)}, u32[]{:S(2)}) %collective-permute-start.36) | collective-permute-done | bytes 36 | tf_op jit(solution)/shard_map/ppermute | solution.py:126
  258.5 2.2 collective-permute-done.37
  261.4 1.9 collective-permute-start.38
  263.2 3.2 %collective-permute-done.38 = f32[]{:T(128)} collective-permute-done((f32[]{:T(128)}, f32[]{:T(128)}, u32[]{:S(2)}, u32[]{:S(2)}) %collective-permute-start.38) | collective-permute-done | bytes 36 | tf_op jit(solution)/shard_map/ppermute | solution.py:126
  267.1 2.6 fusion
  269.7 2.9 %copy.30 = f32[64,3072]{1,0:T(8,128)} copy(f32[64,3072]{0,1:T(8,128)} %get-tuple-element.30) | data formatting | bytes 1572864
  (93 shorter events, 53.9 us)
Async XLA Ops:
  0.6 6.7 %copy-start.4 = (f32[6,3072]{1,0:T(8,128)S(1)}, f32[6,3072]{1,0:T(8,128)}, u32[]{:S(2)}) copy-start(f32[6,3072]{1,0:T(8,128)} %param.8) | copy-start | bytes 221188
  0.6 35.9 %collective-permute-start.6 = (f32[64,256]{1,0:T(8,128)}, f32[64,256]{1,0:T(8,128)S(1)}, u32[]{:S(2)}, u32[]{:S(2)}) collective-permute-start(f32[64,256]{1,0:T(8,128)} %param.9), channel_id=1, source_target_pairs={{2,0},{3,1},{0,2},{1,3},{6,4},{7,5},{4,6},{5,7},{10,8},{11,9},{8,1... | collective-permute-start | bytes 196616 | tf_op jit(solution)/shard_map/ppermute | solution.py:136
  3.9 60.7 %collective-permute-start.5 = (f32[64,256]{1,0:T(8,128)}, f32[64,256]{1,0:T(8,128)S(1)}, u32[]{:S(2)}, u32[]{:S(2)}) collective-permute-start(f32[64,256]{1,0:T(8,128)} %param.9), channel_id=1, source_target_pairs={{1,0},{2,1},{3,2},{0,3},{5,4},{6,5},{7,6},{4,7},{9,8},{10,9},{11,1... | collective-permute-start | bytes 196616 | tf_op jit(solution)/shard_map/ppermute | solution.py:136
  19.6 11.2 %collective-permute-start = (f32[6,1408]{1,0:T(8,128)S(1)}, f32[6,1408]{1,0:T(8,128)S(1)}, u32[]{:S(2)}, u32[]{:S(2)}) collective-permute-start(f32[6,1408]{1,0:T(8,128)S(1)} %get-tuple-element.34), channel_id=1, source_target_pairs={{0,4},{4,8},{8,12},{12,16},{16,20},{20,24},{24,28},{28,32},{32,36}... | collective-permute-start | bytes 101384 | tf_op jit(solution)/shard_map/ppermute | solution.py:113
  21.5 9.2 %collective-permute-start.1 = (f32[6,1408]{1,0:T(8,128)S(1)}, f32[6,1408]{1,0:T(8,128)S(1)}, u32[]{:S(2)}, u32[]{:S(2)}) collective-permute-start(f32[6,1408]{1,0:T(8,128)S(1)} %get-tuple-element.35), channel_id=1, source_target_pairs={{4,0},{8,4},{12,8},{16,12},{20,16},{24,20},{28,24},{32,28},{36,32}... | collective-permute-start | bytes 101384 | tf_op jit(solution)/shard_map/ppermute | solution.py:116
  29.0 1.9 copy-start
  30.9 34.2 %collective-permute-start.4 = (bf16[64,3072]{1,0:T(8,128)(2,1)S(1)}, bf16[64,3072]{1,0:T(8,128)(2,1)S(1)}, u32[]{:S(2)}, u32[]{:S(2)}) collective-permute-start(bf16[64,3072]{1,0:T(8,128)(2,1)S(1)} %convert_element_type.18), channel_id=1, source_target_pairs={{3,0},{0,1},{1,2},{2,3},{7,4},{4,5},{5,6},{6,7},{11,8},{8,9},{9,10... | collective-permute-start | bytes 1179656 | tf_op jit(solution)/shard_map/ppermute | solution.py:136
  31.9 33.1 %collective-permute-start.3 = (bf16[64,3072]{1,0:T(8,128)(2,1)S(1)}, bf16[64,3072]{1,0:T(8,128)(2,1)S(1)}, u32[]{:S(2)}, u32[]{:S(2)}) collective-permute-start(bf16[64,3072]{1,0:T(8,128)(2,1)S(1)} %convert_element_type.18), channel_id=1, source_target_pairs={{2,0},{3,1},{0,2},{1,3},{6,4},{7,5},{4,6},{5,7},{10,8},{11,9},{8,1... | collective-permute-start | bytes 1179656 | tf_op jit(solution)/shard_map/ppermute | solution.py:136
  32.8 32.3 %collective-permute-start.2 = (bf16[64,3072]{1,0:T(8,128)(2,1)S(1)}, bf16[64,3072]{1,0:T(8,128)(2,1)S(1)}, u32[]{:S(2)}, u32[]{:S(2)}) collective-permute-start(bf16[64,3072]{1,0:T(8,128)(2,1)S(1)} %convert_element_type.18), channel_id=1, source_target_pairs={{1,0},{2,1},{3,2},{0,3},{5,4},{6,5},{7,6},{4,7},{9,8},{10,9},{11,1... | collective-permute-start | bytes 1179656 | tf_op jit(solution)/shard_map/ppermute | solution.py:136
  35.3 1.3 copy-start.6
  36.6 28.1 %collective-permute-start.7 = (f32[64,256]{1,0:T(8,128)S(1)}, f32[64,256]{1,0:T(8,128)S(1)}, u32[]{:S(2)}, u32[]{:S(2)}) collective-permute-start(f32[64,256]{1,0:T(8,128)S(1)} %copy-done.6), channel_id=1, source_target_pairs={{3,0},{0,1},{1,2},{2,3},{7,4},{4,5},{5,6},{6,7},{11,8},{8,9},{9,10... | collective-permute-start | bytes 196616 | tf_op jit(solution)/shard_map/ppermute | solution.py:136
  65.2 8.7 %copy-start.5 = (f32[64]{0:T(128)S(1)}, f32[64]{0:T(128)}, u32[]{:S(2)}) copy-start(f32[64]{0:T(128)} %param.10) | copy-start | bytes 772
  66.2 8.9 %collective-permute-start.8 = (bf16[64,1408]{1,0:T(8,128)(2,1)S(1)}, bf16[64,1408]{1,0:T(8,128)(2,1)S(1)}, u32[]{:S(2)}, u32[]{:S(2)}) collective-permute-start(bf16[64,1408]{1,0:T(8,128)(2,1)S(1)} %get-tuple-element.39), channel_id=1, source_target_pairs={{0,4},{4,8},{8,12},{12,16},{16,20},{20,24},{24,28},{28,32},{32,36}... | collective-permute-start | bytes 540680 | tf_op jit(solution)/shard_map/ppermute | solution.py:113
  68.1 8.8 %collective-permute-start.9 = (bf16[64,1408]{1,0:T(8,128)(2,1)S(1)}, bf16[64,1408]{1,0:T(8,128)(2,1)S(1)}, u32[]{:S(2)}, u32[]{:S(2)}) collective-permute-start(bf16[64,1408]{1,0:T(8,128)(2,1)S(1)} %get-tuple-element.40), channel_id=1, source_target_pairs={{4,0},{8,4},{12,8},{16,12},{20,16},{24,20},{28,24},{32,28},{36,32}... | collective-permute-start | bytes 540680 | tf_op jit(solution)/shard_map/ppermute | solution.py:116
  77.9 49.7 %copy-start.1 = (f32[64,3072]{1,0:T(8,128)S(1)}, f32[64,3072]{1,0:T(8,128)}, u32[]{:S(2)}) copy-start(f32[64,3072]{1,0:T(8,128)} %copy-done) | copy-start | bytes 2359300
  89.5 3.6 %collective-permute-start.10 = (f32[2]{0:T(128)S(1)}, f32[2]{0:T(128)S(1)}, u32[]{:S(2)}, u32[]{:S(2)}) collective-permute-start(f32[2]{0:T(128)S(1)} %pad_maximum_fusion.3), channel_id=1, source_target_pairs={{0,1},{1,0},{2,3},{3,2},{4,5},{5,4},{6,7},{7,6},{8,9},{9,8},{10,11... | collective-permute-start | bytes 32 | tf_op jit(solution)/shard_map/ppermute | solution.py:126
  94.2 5.1 %collective-permute-start.11 = (f32[2]{0:T(128)S(1)}, f32[2]{0:T(128)S(1)}, u32[]{:S(2)}, u32[]{:S(2)}) collective-permute-start(f32[2]{0:T(128)S(1)} %fusion.29), channel_id=1, source_target_pairs={{0,2},{1,3},{2,0},{3,1},{4,6},{5,7},{6,4},{7,5},{8,10},{9,11},{10,... | collective-permute-start | bytes 32 | tf_op jit(solution)/shard_map/ppermute | solution.py:126
  100.5 1.3 collective-permute-start.12
  101.8 3.5 %collective-permute-start.13 = (f32[2]{0:T(128)S(1)}, f32[2]{0:T(128)S(1)}, u32[]{:S(2)}, u32[]{:S(2)}) collective-permute-start(f32[2]{0:T(128)S(1)} %add.97), channel_id=1, source_target_pairs={{0,8},{4,12},{8,0},{12,4},{16,24},{20,28},{24,16},{28,20},{32,40},... | collective-permute-start | bytes 32 | tf_op jit(solution)/shard_map/ppermute | solution.py:126
  105.4 4.4 %collective-permute-start.14 = (f32[2]{0:T(128)S(1)}, f32[2]{0:T(128)S(1)}, u32[]{:S(2)}, u32[]{:S(2)}) collective-permute-start(f32[2]{0:T(128)S(1)} %add.98), channel_id=1, source_target_pairs={{0,16},{4,20},{8,24},{12,28},{16,0},{20,4},{24,8},{28,12},{32,48},... | collective-permute-start | bytes 32 | tf_op jit(solution)/shard_map/ppermute | solution.py:126
  109.8 7.4 %collective-permute-start.15 = (f32[2]{0:T(128)S(1)}, f32[2]{0:T(128)S(1)}, u32[]{:S(2)}, u32[]{:S(2)}) collective-permute-start(f32[2]{0:T(128)S(1)} %add.99), channel_id=1, source_target_pairs={{0,32},{4,36},{8,40},{12,44},{16,48},{20,52},{24,56},{28,60},{32,0... | collective-permute-start | bytes 32 | tf_op jit(solution)/shard_map/ppermute | solution.py:126
  117.3 3.5 %collective-permute-start.16 = (f32[2]{0:T(128)S(1)}, f32[2]{0:T(128)S(1)}, u32[]{:S(2)}, u32[]{:S(2)}) collective-permute-start(f32[2]{0:T(128)S(1)} %add.100), channel_id=1, source_target_pairs={{0,64},{4,68},{8,72},{12,76},{16,80},{20,84},{24,88},{28,92},{32,9... | collective-permute-start | bytes 32 | tf_op jit(solution)/shard_map/ppermute | solution.py:126
  120.8 5.0 %collective-permute-start.17 = (f32[2]{0:T(128)S(1)}, f32[2]{0:T(128)S(1)}, u32[]{:S(2)}, u32[]{:S(2)}) collective-permute-start(f32[2]{0:T(128)S(1)} %add.101), channel_id=1, source_target_pairs={{0,128},{4,132},{8,136},{12,140},{16,144},{20,148},{24,152},{28,15... | collective-permute-start | bytes 32 | tf_op jit(solution)/shard_map/ppermute | solution.py:126
  129.6 42.4 %copy-start.2 = (f32[64,3072]{1,0:T(8,128)}, f32[64,3072]{1,0:T(8,128)S(1)}, u32[]{:S(2)}) copy-start(f32[64,3072]{1,0:T(8,128)S(1)} %get-tuple-element.27) | copy-start | bytes 2359300
  129.6 3.8 %collective-permute-start.18 = (f32[]{:T(128)}, f32[]{:T(128)}, u32[]{:S(2)}, u32[]{:S(2)}) collective-permute-start(f32[]{:T(128)} %get-tuple-element.26), channel_id=1, source_target_pairs={{0,1},{1,0},{2,3},{3,2},{4,5},{5,4},{6,7},{7,6},{8,9},{9,8},{10,11... | collective-permute-start | bytes 20 | tf_op jit(solution)/shard_map/ppermute | solution.py:126
  134.5 5.2 %collective-permute-start.19 = (f32[]{:T(128)}, f32[]{:T(128)}, u32[]{:S(2)}, u32[]{:S(2)}) collective-permute-start(f32[]{:T(128)} %add.103), channel_id=1, source_target_pairs={{0,2},{1,3},{2,0},{3,1},{4,6},{5,7},{6,4},{7,5},{8,10},{9,11},{10,... | collective-permute-start | bytes 20 | tf_op jit(solution)/shard_map/ppermute | solution.py:126
  140.3 1.3 collective-permute-start.20
  142.3 3.7 %collective-permute-start.21 = (f32[]{:T(128)}, f32[]{:T(128)}, u32[]{:S(2)}, u32[]{:S(2)}) collective-permute-start(f32[]{:T(128)} %add.105), channel_id=1, source_target_pairs={{0,8},{4,12},{8,0},{12,4},{16,24},{20,28},{24,16},{28,20},{32,40},... | collective-permute-start | bytes 20 | tf_op jit(solution)/shard_map/ppermute | solution.py:126
  146.5 4.6 %collective-permute-start.22 = (f32[]{:T(128)}, f32[]{:T(128)}, u32[]{:S(2)}, u32[]{:S(2)}) collective-permute-start(f32[]{:T(128)} %add.106), channel_id=1, source_target_pairs={{0,16},{4,20},{8,24},{12,28},{16,0},{20,4},{24,8},{28,12},{32,48},... | collective-permute-start | bytes 20 | tf_op jit(solution)/shard_map/ppermute | solution.py:126
  151.7 7.6 %collective-permute-start.23 = (f32[]{:T(128)}, f32[]{:T(128)}, u32[]{:S(2)}, u32[]{:S(2)}) collective-permute-start(f32[]{:T(128)} %add.107), channel_id=1, source_target_pairs={{0,32},{4,36},{8,40},{12,44},{16,48},{20,52},{24,56},{28,60},{32,0... | collective-permute-start | bytes 20 | tf_op jit(solution)/shard_map/ppermute | solution.py:126
  159.9 3.7 %collective-permute-start.24 = (f32[]{:T(128)}, f32[]{:T(128)}, u32[]{:S(2)}, u32[]{:S(2)}) collective-permute-start(f32[]{:T(128)} %add.108), channel_id=1, source_target_pairs={{0,64},{4,68},{8,72},{12,76},{16,80},{20,84},{24,88},{28,92},{32,9... | collective-permute-start | bytes 20 | tf_op jit(solution)/shard_map/ppermute | solution.py:126
  164.2 5.2 %collective-permute-start.25 = (f32[]{:T(128)}, f32[]{:T(128)}, u32[]{:S(2)}, u32[]{:S(2)}) collective-permute-start(f32[]{:T(128)} %add.109), channel_id=1, source_target_pairs={{0,128},{4,132},{8,136},{12,140},{16,144},{20,148},{24,152},{28,15... | collective-permute-start | bytes 20 | tf_op jit(solution)/shard_map/ppermute | solution.py:126
  172.0 11.6 %collective-permute-start.28 = (bf16[64,3072]{1,0:T(8,128)(2,1)S(1)}, bf16[64,3072]{1,0:T(8,128)(2,1)S(1)}, u32[]{:S(2)}, u32[]{:S(2)}) collective-permute-start(bf16[64,3072]{1,0:T(8,128)(2,1)S(1)} %get-tuple-element.24), channel_id=1, source_target_pairs={{3,0},{0,1},{1,2},{2,3},{7,4},{4,5},{5,6},{6,7},{11,8},{8,9},{9,10... | collective-permute-start | bytes 1179656 | tf_op jit(solution)/shard_map/ppermute | solution.py:136
  173.8 14.0 %collective-permute-start.27 = (bf16[64,3072]{1,0:T(8,128)(2,1)S(1)}, bf16[64,3072]{1,0:T(8,128)(2,1)S(1)}, u32[]{:S(2)}, u32[]{:S(2)}) collective-permute-start(bf16[64,3072]{1,0:T(8,128)(2,1)S(1)} %get-tuple-element.24), channel_id=1, source_target_pairs={{2,0},{3,1},{0,2},{1,3},{6,4},{7,5},{4,6},{5,7},{10,8},{11,9},{8,1... | collective-permute-start | bytes 1179656 | tf_op jit(solution)/shard_map/ppermute | solution.py:136
  176.7 11.1 %collective-permute-start.26 = (bf16[64,3072]{1,0:T(8,128)(2,1)S(1)}, bf16[64,3072]{1,0:T(8,128)(2,1)S(1)}, u32[]{:S(2)}, u32[]{:S(2)}) collective-permute-start(bf16[64,3072]{1,0:T(8,128)(2,1)S(1)} %get-tuple-element.24), channel_id=1, source_target_pairs={{1,0},{2,1},{3,2},{0,3},{5,4},{6,5},{7,6},{4,7},{9,8},{10,9},{11,1... | collective-permute-start | bytes 1179656 | tf_op jit(solution)/shard_map/ppermute | solution.py:136
  188.8 8.9 %collective-permute-start.29 = (bf16[64,1408]{1,0:T(8,128)(2,1)S(1)}, bf16[64,1408]{1,0:T(8,128)(2,1)S(1)}, u32[]{:S(2)}, u32[]{:S(2)}) collective-permute-start(bf16[64,1408]{1,0:T(8,128)(2,1)S(1)} %get-tuple-element.37), channel_id=1, source_target_pairs={{0,4},{4,8},{8,12},{12,16},{16,20},{20,24},{24,28},{28,32},{32,36}... | collective-permute-start | bytes 540680 | tf_op jit(solution)/shard_map/ppermute | solution.py:113
  190.7 8.8 %collective-permute-start.30 = (bf16[64,1408]{1,0:T(8,128)(2,1)S(1)}, bf16[64,1408]{1,0:T(8,128)(2,1)S(1)}, u32[]{:S(2)}, u32[]{:S(2)}) collective-permute-start(bf16[64,1408]{1,0:T(8,128)(2,1)S(1)} %get-tuple-element.38), channel_id=1, source_target_pairs={{4,0},{8,4},{12,8},{16,12},{20,16},{24,20},{28,24},{32,28},{36,32}... | collective-permute-start | bytes 540680 | tf_op jit(solution)/shard_map/ppermute | solution.py:116
  215.2 15.6 %collective-permute-start.31 = (f32[]{:T(128)}, f32[]{:T(128)}, u32[]{:S(2)}, u32[]{:S(2)}) collective-permute-start(f32[]{:T(128)} %slice_reduce_fusion), channel_id=1, source_target_pairs={{0,1},{1,0},{2,3},{3,2},{4,5},{5,4},{6,7},{7,6},{8,9},{9,8},{10,11... | collective-permute-start | bytes 20 | tf_op jit(solution)/shard_map/ppermute | solution.py:126
  232.1 5.1 %collective-permute-start.32 = (f32[]{:T(128)}, f32[]{:T(128)}, u32[]{:S(2)}, u32[]{:S(2)}) collective-permute-start(f32[]{:T(128)} %add.112), channel_id=1, source_target_pairs={{0,2},{1,3},{2,0},{3,1},{4,6},{5,7},{6,4},{7,5},{8,10},{9,11},{10,... | collective-permute-start | bytes 20 | tf_op jit(solution)/shard_map/ppermute | solution.py:126
  237.9 1.2 collective-permute-start.33
  239.7 3.6 %collective-permute-start.34 = (f32[]{:T(128)}, f32[]{:T(128)}, u32[]{:S(2)}, u32[]{:S(2)}) collective-permute-start(f32[]{:T(128)} %add.114), channel_id=1, source_target_pairs={{0,8},{4,12},{8,0},{12,4},{16,24},{20,28},{24,16},{28,20},{32,40},... | collective-permute-start | bytes 20 | tf_op jit(solution)/shard_map/ppermute | solution.py:126
  243.9 4.5 %collective-permute-start.35 = (f32[]{:T(128)}, f32[]{:T(128)}, u32[]{:S(2)}, u32[]{:S(2)}) collective-permute-start(f32[]{:T(128)} %add.115), channel_id=1, source_target_pairs={{0,16},{4,20},{8,24},{12,28},{16,0},{20,4},{24,8},{28,12},{32,48},... | collective-permute-start | bytes 20 | tf_op jit(solution)/shard_map/ppermute | solution.py:126
  249.0 7.5 %collective-permute-start.36 = (f32[]{:T(128)}, f32[]{:T(128)}, u32[]{:S(2)}, u32[]{:S(2)}) collective-permute-start(f32[]{:T(128)} %add.116), channel_id=1, source_target_pairs={{0,32},{4,36},{8,40},{12,44},{16,48},{20,52},{24,56},{28,60},{32,0... | collective-permute-start | bytes 20 | tf_op jit(solution)/shard_map/ppermute | solution.py:126
  257.1 3.6 %collective-permute-start.37 = (f32[]{:T(128)}, f32[]{:T(128)}, u32[]{:S(2)}, u32[]{:S(2)}) collective-permute-start(f32[]{:T(128)} %add.117), channel_id=1, source_target_pairs={{0,64},{4,68},{8,72},{12,76},{16,80},{20,84},{24,88},{28,92},{32,9... | collective-permute-start | bytes 20 | tf_op jit(solution)/shard_map/ppermute | solution.py:126
  261.4 5.1 %collective-permute-start.38 = (f32[]{:T(128)}, f32[]{:T(128)}, u32[]{:S(2)}, u32[]{:S(2)}) collective-permute-start(f32[]{:T(128)} %add.118), channel_id=1, source_target_pairs={{0,128},{4,132},{8,136},{12,140},{16,144},{20,148},{24,152},{28,15... | collective-permute-start | bytes 20 | tf_op jit(solution)/shard_map/ppermute | solution.py:126
  269.7 2.9 %copy-start.3 = (f32[64,3072]{0,1:T(8,128)S(1)}, f32[64,3072]{0,1:T(8,128)}, u32[]{:S(2)}) copy-start(f32[64,3072]{0,1:T(8,128)} %get-tuple-element.31) | copy-start | bytes 2359300

commit v15 on v14

--- a/solution.py
+++ b/solution.py
@@ -117,7 +117,8 @@
     return jnp.concatenate([low, block, high], axis=dim)
 
 
-def global_sum(value):
+def global_sum(value, rider=None):
+    rounds = 0
     for axis in ("chan", "samp"):
         count = lax.axis_size(axis)
         step = 1
@@ -125,7 +126,12 @@
             pairs = [(i, i ^ step) for i in range(count)]
             value = value + lax.ppermute(value, axis, pairs)
             step *= 2
-    return value
+            rounds += 1
+            if rider is not None and rounds == 2:
+                value, rider = lax.optimization_barrier((value, rider))
+    if rider is None:
+        return value
+    return value, rider
 
 
 def gather_chan(rounded):
@@ -186,9 +192,10 @@
         mapped, partials = apply_operator(begin, win_v, tiles, direction, noise_col, 4)
         curvature = jnp.sum(partials[:, 0, :])
         if iteration + 1 == ITERS:
-            stacked = jnp.concatenate([iterate, remainder, direction, mapped], axis=0)
+            stacked = jnp.concatenate([direction, mapped], axis=0)
             unsorted = jnp.zeros_like(stacked).at[:, local_perm].set(stacked)
-            iterate, remainder, direction, mapped = jnp.split(unsorted, 4, axis=0)
+            direction, mapped = jnp.split(unsorted, 2, axis=0)
+            iterate, remainder = jnp.split(early, 2, axis=0)
         if iteration == 0:
             sums = global_sum(jnp.stack([norm_local, curvature]))
             norm_now, curvature = sums[0], sums[1]
@@ -198,7 +205,9 @@
         iterate = iterate + step_size * direction
         remainder = remainder - step_size * mapped
         if iteration + 1 < ITERS:
-            norm_next = global_sum(jnp.sum(remainder * remainder))
+            both = jnp.concatenate([iterate, remainder], axis=0)
+            early = jnp.zeros_like(both).at[:, local_perm].set(both)
+            norm_next, early = global_sum(jnp.sum(remainder * remainder), early)
             direction = remainder + norm_next / norm_now * direction
             norm_now = norm_next
     return (iterate, remainder)

time: 274 us -> 279 us (1.018)
  waiting for transfers between devices: 78.5 us -> 50.7 us
  starting transfers between devices: 76.2 us -> 103 us
  local copies, waits for them, and re-layouts: 36.7 us -> 42.3 us
    ppermute x24, waiting for transfers between devices: 62.7 us -> 35.9 us  [global_sum(): value = value + lax.ppermute(value, axis, pairs)]
    ppermute x24, starting transfers between devices: 38.3 us -> 64.6 us  [global_sum(): value = value + lax.ppermute(value, axis, pairs)]
    scatter x0 -> x1, local copies, waits for them, and re-layouts: none -> 8.83 us  [per_device(): early = jnp.zeros_like(both).at[:, local_perm].set(both)]
    scatter x1, local copies, waits for them, and re-layouts: 14.4 us -> 8.83 us  [per_device(): unsorted = jnp.zeros_like(stacked).at[:, local_perm].set(stacked)]
  transfers between devices with their start and end apart: 39 -> 39, of which waited for: 29 -> 28; matrix products, arithmetic and copies ran while one was open for 13% -> 16% of each run, Pallas kernels for 10% -> 9%
where the time goes in v15:
time: 279 us; the launch traced here: 277 us
  starting transfers between devices  103 us (37%)
  waiting for transfers between devices  50.7 us (18%)
  Pallas kernels  42.7 us (15%)
  local copies, waits for them, and re-layouts  42.3 us (15%)
  other arithmetic  22.2 us (8%)
  between operations  14.5 us (5%)
    ppermute x24, starting transfers between devices, global_sum(): value = value + lax.ppermute(value, axis, pairs)  64.6 us
    ppermute x24, waiting for transfers between devices, global_sum(): value = value + lax.ppermute(value, axis, pairs)  35.9 us
    pallas_call x1, Pallas kernels, build_tiles(): pl.pallas_call(kern, grid_spec=pltpu.PrefetchScalarGridSpec(num_scalar_pr...  24.8 us
    ppermute x3, starting transfers between devices, extended(): lax.ppermute(lax.slice_in_dim(block, 0, width, axis=dim), axis, backward)  18.1 us
    pallas_call x2, Pallas kernels, apply_operator(): pl.pallas_call(kern, grid_spec=pltpu.PrefetchScalarGridSpec(num_scalar_pr...  17.9 us
    ppermute x9, starting transfers between devices, gather_chan(): parts.append(lax.ppermute(rounded, 'chan', pairs))  14.3 us
    ppermute x9, waiting for transfers between devices, gather_chan(): parts.append(lax.ppermute(rounded, 'chan', pairs))  9.51 us
    scatter x1, local copies, waits for them, and re-layouts, per_device(): unsorted = jnp.zeros_like(stacked).at[:, local_perm].set(stacked)  8.83 us
  transfers between devices with their start and end apart: 39, of which 28 were waited for; matrix products, arithmetic and copies ran while one was open for 16% of the time, Pallas kernels for 9%

profile of v15, /device:TPU:2, one launch (start us, length us, event | category | flops | bytes accessed | tf_op | source)
XLA Modules:
  0.0 277.3 jit_solution(16689317324865595055)
XLA Ops:
  0.6 3.3 %collective-permute-start.6 = (f32[64,256]{1,0:T(8,128)}, f32[64,256]{1,0:T(8,128)S(1)}, u32[]{:S(2)}, u32[]{:S(2)}) collective-permute-start(f32[64,256]{1,0:T(8,128)} %param.9), channel_id=1, source_target_pairs={{2,0},{3,1},{0,2},{1,3},{6,4},{7,5},{4,6},{5,7},{10,8},{11,9},{8,1... | collective-permute-start | bytes 196616 | tf_op jit(solution)/shard_map/ppermute | solution.py:142
  9.0 1.9 pad_maximum_fusion
  10.9 8.1 %gather_fusion = f32[3072,70]{1,0:T(8,128)S(1)} fusion(f32[70,3072]{0,1:T(8,128)S(1)} %pad_maximum_fusion, s32[3072]{0:T(1024)S(1)} %broadcast_clamp_fusion), kind=kCustom, calls=%fused_computation | custom fusion | bytes 1732608 | tf_op jit(solution)/shard_map/jit(_take)/gather | solution.py:156
  19.6 1.9 collective-permute-start
  21.6 6.6 %collective-permute-start.1 = (f32[6,1408]{1,0:T(8,128)S(1)}, f32[6,1408]{1,0:T(8,128)S(1)}, u32[]{:S(2)}, u32[]{:S(2)}) collective-permute-start(f32[6,1408]{1,0:T(8,128)S(1)} %get-tuple-element.39), channel_id=1, source_target_pairs={{4,0},{8,4},{12,8},{16,12},{20,16},{24,20},{28,24},{32,28},{36,32}... | collective-permute-start | bytes 101384 | tf_op jit(solution)/shard_map/ppermute | solution.py:116
  32.8 2.5 collective-permute-start.2
  37.3 24.8 %shard_map.86.tile_ref = bf16[24,128,1536]{2,1,0:T(8,128)(2,1)} custom-call(s32[24]{0:T(128)} %clamp_bitcast_fusion.begin_ref, s32[24]{0:T(128)} %count_ref.1, f32[24,128,8]{2,1,0:T(8,128)} %pad_bitcast_fusion.own_ref, f32[46,8,128]{2,1,0:T(8,128)} %pad_bitcast_fusion.1.win_ref), custom_call_target="tpu_custom_call" | custom-call | tf_op jit(solution)/shard_map/pallas_call | solution.py:47
  63.6 1.9 collective-permute-start.8
  65.5 5.8 %collective-permute-start.9 = (bf16[64,1408]{1,0:T(8,128)(2,1)S(1)}, bf16[64,1408]{1,0:T(8,128)(2,1)S(1)}, u32[]{:S(2)}, u32[]{:S(2)}) collective-permute-start(bf16[64,1408]{1,0:T(8,128)(2,1)S(1)} %get-tuple-element.44), channel_id=1, source_target_pairs={{4,0},{8,4},{12,8},{16,12},{20,16},{24,20},{28,24},{32,28},{36,32}... | collective-permute-start | bytes 540680 | tf_op jit(solution)/shard_map/ppermute | solution.py:116
  75.4 9.0 %shard_map.87 = (f32[64,3072]{1,0:T(8,128)}, f32[6,8,128]{2,1,0:T(8,128)}) custom-call(s32[24]{0:T(128)} %clamp_bitcast_fusion.begin_ref, bf16[46,64,128]{2,1,0:T(8,128)(2,1)} %bitcast_bitcast_fusion.1.win_ref, bf16[24,128,1536]{2,1,0:T(8,128)(2,1)} %shard_map.86.tile_ref, f32[64,3072]{1,0:T(8,128)} %copy-done, f32[64,1]{1,0:T(8,128)} %copy.26.noise_ref), custom_call_target="tpu_custom_call" | custom-call | tf_op jit(solution)/shard_map/pallas_call | solution.py:86
  87.1 1.8 collective-permute-start.10
  92.0 2.7 collective-permute-start.11
  94.7 2.4 collective-permute-done.11
  99.7 3.5 %collective-permute-done.13 = f32[2]{0:T(128)S(1)} collective-permute-done((f32[2]{0:T(128)S(1)}, f32[2]{0:T(128)S(1)}, u32[]{:S(2)}, u32[]{:S(2)}) %collective-permute-start.13) | collective-permute-done | bytes 40 | tf_op jit(solution)/shard_map/ppermute | solution.py:127
  103.3 2.2 collective-permute-start.14
  105.5 2.2 collective-permute-done.14
  107.7 5.4 %collective-permute-start.15 = (f32[2]{0:T(128)S(1)}, f32[2]{0:T(128)S(1)}, u32[]{:S(2)}, u32[]{:S(2)}) collective-permute-start(f32[2]{0:T(128)S(1)} %add.99), channel_id=1, source_target_pairs={{0,32},{4,36},{8,40},{12,44},{16,48},{20,52},{24,56},{28,60},{32,0... | collective-permute-start | bytes 32 | tf_op jit(solution)/shard_map/ppermute | solution.py:127
  113.1 2.1 collective-permute-done.15
  115.2 3.5 %collective-permute-done.16 = f32[2]{0:T(128)S(1)} collective-permute-done((f32[2]{0:T(128)S(1)}, f32[2]{0:T(128)S(1)}, u32[]{:S(2)}, u32[]{:S(2)}) %collective-permute-start.16) | collective-permute-done | bytes 40 | tf_op jit(solution)/shard_map/ppermute | solution.py:127
  118.7 3.1 %collective-permute-start.17 = (f32[2]{0:T(128)S(1)}, f32[2]{0:T(128)S(1)}, u32[]{:S(2)}, u32[]{:S(2)}) collective-permute-start(f32[2]{0:T(128)S(1)} %add.101), channel_id=1, source_target_pairs={{0,128},{4,132},{8,136},{12,140},{16,144},{20,148},{24,152},{28,15... | collective-permute-start | bytes 32 | tf_op jit(solution)/shard_map/ppermute | solution.py:127
  121.8 1.9 collective-permute-done.17
  125.7 2.0 multiply_reduce_fusion
  127.6 1.8 collective-permute-start.18
  131.2 8.8 %scatter_custom_fusion = f32[128,3072]{0,1:T(8,128)S(1)} fusion(s32[3072]{0:T(1024)S(1)} %get-tuple-element.33, f32[3072,128]{1,0:T(8,128)} %copy.27, f32[]{:T(128)} %constant.16.clone.1), kind=kCustom, calls=%fused_computation.26 | custom fusion | bytes 1573376 | tf_op jit(solution)/shard_map/scatter | solution.py:209
  141.3 4.3 %collective-permute-start.19 = (f32[]{:T(128)}, f32[]{:T(128)}, u32[]{:S(2)}, u32[]{:S(2)}) collective-permute-start(f32[]{:T(128)} %add.103), channel_id=1, source_target_pairs={{0,2},{1,3},{2,0},{3,1},{4,6},{5,7},{6,4},{7,5},{8,10},{9,11},{10,... | collective-permute-start | bytes 20 | tf_op jit(solution)/shard_map/ppermute | solution.py:127
  149.2 2.7 collective-permute-start.21
  153.5 3.6 %collective-permute-start.22 = (f32[]{:T(128)}, f32[]{:T(128)}, u32[]{:S(2)}, u32[]{:S(2)}) collective-permute-start(f32[]{:T(128)} %add.106), channel_id=1, source_target_pairs={{0,16},{4,20},{8,24},{12,28},{16,0},{20,4},{24,8},{28,12},{32,48},... | collective-permute-start | bytes 20 | tf_op jit(solution)/shard_map/ppermute | solution.py:127
  158.8 6.8 %collective-permute-start.23 = (f32[]{:T(128)}, f32[]{:T(128)}, u32[]{:S(2)}, u32[]{:S(2)}) collective-permute-start(f32[]{:T(128)} %add.107), channel_id=1, source_target_pairs={{0,32},{4,36},{8,40},{12,44},{16,48},{20,52},{24,56},{28,60},{32,0... | collective-permute-start | bytes 20 | tf_op jit(solution)/shard_map/ppermute | solution.py:127
  168.6 2.2 collective-permute-done.24
  171.4 4.5 %collective-permute-start.25 = (f32[]{:T(128)}, f32[]{:T(128)}, u32[]{:S(2)}, u32[]{:S(2)}) collective-permute-start(f32[]{:T(128)} %add.109), channel_id=1, source_target_pairs={{0,128},{4,132},{8,136},{12,140},{16,144},{20,148},{24,152},{28,15... | collective-permute-start | bytes 20 | tf_op jit(solution)/shard_map/ppermute | solution.py:127
  179.2 2.7 collective-permute-start.27
  181.9 2.6 collective-permute-start.26
  184.5 8.9 %collective-permute-done.28 = bf16[64,3072]{1,0:T(8,128)(2,1)S(1)} collective-permute-done((bf16[64,3072]{1,0:T(8,128)(2,1)S(1)}, bf16[64,3072]{1,0:T(8,128)(2,1)S(1)}, u32[]{:S(2)}, u32[]{:S(2)}) %collective-permute-start.28) | collective-permute-done | bytes 393248 | tf_op jit(solution)/shard_map/ppermute | solution.py:142
  195.0 1.9 collective-permute-start.29
  196.9 5.8 %collective-permute-start.30 = (bf16[64,1408]{1,0:T(8,128)(2,1)S(1)}, bf16[64,1408]{1,0:T(8,128)(2,1)S(1)}, u32[]{:S(2)}, u32[]{:S(2)}) collective-permute-start(bf16[64,1408]{1,0:T(8,128)(2,1)S(1)} %get-tuple-element.42), channel_id=1, source_target_pairs={{4,0},{8,4},{12,8},{16,12},{20,16},{24,20},{28,24},{32,28},{36,32}... | collective-permute-start | bytes 540680 | tf_op jit(solution)/shard_map/ppermute | solution.py:116
  206.8 9.0 %shard_map.88 = (f32[64,3072]{1,0:T(8,128)}, f32[6,8,128]{2,1,0:T(8,128)}) custom-call(s32[24]{0:T(128)} %clamp_bitcast_fusion.begin_ref, bf16[46,64,128]{2,1,0:T(8,128)(2,1)} %bitcast_bitcast_fusion.win_ref, bf16[24,128,1536]{2,1,0:T(8,128)(2,1)} %shard_map.86.tile_ref, f32[64,3072]{1,0:T(8,128)} %get-tuple-element.29.p_ref, f32[64,1]{1,0:T(8,128)} %copy.26.noise_ref), custom_call_target="tpu_custom_call" | custom-call | tf_op jit(solution)/shard_map/pallas_call | solution.py:86
  218.8 2.5 maximum_bitcast_fusion.1
  221.3 3.0 %copy.30 = f32[3072,128]{1,0:T(8,128)} copy(f32[3072,128]{0,1:T(8,128)} %maximum_bitcast_fusion.1) | data formatting | bytes 3145728 | tf_op jit(solution)/shard_map/concatenate | solution.py:195
  224.3 8.8 %scatter_custom_fusion.1 = f32[128,3072]{0,1:T(8,128)S(1)} fusion(s32[3072]{0:T(1024)S(1)} %get-tuple-element.33, f32[3072,128]{1,0:T(8,128)} %copy.30, f32[]{:T(128)} %constant.16.clone.1), kind=kCustom, calls=%fused_computation.24 | custom fusion | bytes 1573376 | tf_op jit(solution)/shard_map/scatter | solution.py:196
  234.4 3.8 %collective-permute-start.32 = (f32[]{:T(128)}, f32[]{:T(128)}, u32[]{:S(2)}, u32[]{:S(2)}) collective-permute-start(f32[]{:T(128)} %add.112), channel_id=1, source_target_pairs={{0,2},{1,3},{2,0},{3,1},{4,6},{5,7},{6,4},{7,5},{8,10},{9,11},{10,... | collective-permute-start | bytes 20 | tf_op jit(solution)/shard_map/ppermute | solution.py:127
  243.7 2.3 collective-permute-done.34
  246.7 3.4 %collective-permute-start.35 = (f32[]{:T(128)}, f32[]{:T(128)}, u32[]{:S(2)}, u32[]{:S(2)}) collective-permute-start(f32[]{:T(128)} %add.115), channel_id=1, source_target_pairs={{0,16},{4,20},{8,24},{12,28},{16,0},{20,4},{24,8},{28,12},{32,48},... | collective-permute-start | bytes 20 | tf_op jit(solution)/shard_map/ppermute | solution.py:127
  251.9 5.9 %collective-permute-start.36 = (f32[]{:T(128)}, f32[]{:T(128)}, u32[]{:S(2)}, u32[]{:S(2)}) collective-permute-start(f32[]{:T(128)} %add.116), channel_id=1, source_target_pairs={{0,32},{4,36},{8,40},{12,44},{16,48},{20,52},{24,56},{28,60},{32,0... | collective-permute-start | bytes 20 | tf_op jit(solution)/shard_map/ppermute | solution.py:127
  257.8 1.8 collective-permute-done.36
  261.6 2.3 collective-permute-done.37
  264.6 4.5 %collective-permute-start.38 = (f32[]{:T(128)}, f32[]{:T(128)}, u32[]{:S(2)}, u32[]{:S(2)}) collective-permute-start(f32[]{:T(128)} %add.118), channel_id=1, source_target_pairs={{0,128},{4,132},{8,136},{12,140},{16,144},{20,148},{24,152},{28,15... | collective-permute-start | bytes 20 | tf_op jit(solution)/shard_map/ppermute | solution.py:127
  270.5 2.6 fusion
  273.1 2.9 %copy.32 = f32[64,3072]{1,0:T(8,128)} copy(f32[64,3072]{0,1:T(8,128)} %get-tuple-element.34) | data formatting | bytes 1572864
  (96 shorter events, 55.0 us)
Async XLA Ops:
  0.6 6.7 %copy-start.4 = (f32[6,3072]{1,0:T(8,128)S(1)}, f32[6,3072]{1,0:T(8,128)}, u32[]{:S(2)}) copy-start(f32[6,3072]{1,0:T(8,128)} %param.8) | copy-start | bytes 221188
  0.6 36.0 %collective-permute-start.6 = (f32[64,256]{1,0:T(8,128)}, f32[64,256]{1,0:T(8,128)S(1)}, u32[]{:S(2)}, u32[]{:S(2)}) collective-permute-start(f32[64,256]{1,0:T(8,128)} %param.9), channel_id=1, source_target_pairs={{2,0},{3,1},{0,2},{1,3},{6,4},{7,5},{4,6},{5,7},{10,8},{11,9},{8,1... | collective-permute-start | bytes 196616 | tf_op jit(solution)/shard_map/ppermute | solution.py:142
  3.9 58.2 %collective-permute-start.5 = (f32[64,256]{1,0:T(8,128)}, f32[64,256]{1,0:T(8,128)S(1)}, u32[]{:S(2)}, u32[]{:S(2)}) collective-permute-start(f32[64,256]{1,0:T(8,128)} %param.9), channel_id=1, source_target_pairs={{1,0},{2,1},{3,2},{0,3},{5,4},{6,5},{7,6},{4,7},{9,8},{10,9},{11,1... | collective-permute-start | bytes 196616 | tf_op jit(solution)/shard_map/ppermute | solution.py:142
  19.6 11.2 %collective-permute-start = (f32[6,1408]{1,0:T(8,128)S(1)}, f32[6,1408]{1,0:T(8,128)S(1)}, u32[]{:S(2)}, u32[]{:S(2)}) collective-permute-start(f32[6,1408]{1,0:T(8,128)S(1)} %get-tuple-element.38), channel_id=1, source_target_pairs={{0,4},{4,8},{8,12},{12,16},{16,20},{20,24},{24,28},{28,32},{32,36}... | collective-permute-start | bytes 101384 | tf_op jit(solution)/shard_map/ppermute | solution.py:113
  21.6 9.3 %collective-permute-start.1 = (f32[6,1408]{1,0:T(8,128)S(1)}, f32[6,1408]{1,0:T(8,128)S(1)}, u32[]{:S(2)}, u32[]{:S(2)}) collective-permute-start(f32[6,1408]{1,0:T(8,128)S(1)} %get-tuple-element.39), channel_id=1, source_target_pairs={{4,0},{8,4},{12,8},{16,12},{20,16},{24,20},{28,24},{32,28},{36,32}... | collective-permute-start | bytes 101384 | tf_op jit(solution)/shard_map/ppermute | solution.py:116
  29.1 1.9 copy-start
  31.0 31.5 %collective-permute-start.4 = (bf16[64,3072]{1,0:T(8,128)(2,1)S(1)}, bf16[64,3072]{1,0:T(8,128)(2,1)S(1)}, u32[]{:S(2)}, u32[]{:S(2)}) collective-permute-start(bf16[64,3072]{1,0:T(8,128)(2,1)S(1)} %convert_element_type.18), channel_id=1, source_target_pairs={{3,0},{0,1},{1,2},{2,3},{7,4},{4,5},{5,6},{6,7},{11,8},{8,9},{9,10... | collective-permute-start | bytes 1179656 | tf_op jit(solution)/shard_map/ppermute | solution.py:142
  32.0 30.5 %collective-permute-start.3 = (bf16[64,3072]{1,0:T(8,128)(2,1)S(1)}, bf16[64,3072]{1,0:T(8,128)(2,1)S(1)}, u32[]{:S(2)}, u32[]{:S(2)}) collective-permute-start(bf16[64,3072]{1,0:T(8,128)(2,1)S(1)} %convert_element_type.18), channel_id=1, source_target_pairs={{2,0},{3,1},{0,2},{1,3},{6,4},{7,5},{4,6},{5,7},{10,8},{11,9},{8,1... | collective-permute-start | bytes 1179656 | tf_op jit(solution)/shard_map/ppermute | solution.py:142
  32.8 29.7 %collective-permute-start.2 = (bf16[64,3072]{1,0:T(8,128)(2,1)S(1)}, bf16[64,3072]{1,0:T(8,128)(2,1)S(1)}, u32[]{:S(2)}, u32[]{:S(2)}) collective-permute-start(bf16[64,3072]{1,0:T(8,128)(2,1)S(1)} %convert_element_type.18), channel_id=1, source_target_pairs={{1,0},{2,1},{3,2},{0,3},{5,4},{6,5},{7,6},{4,7},{9,8},{10,9},{11,1... | collective-permute-start | bytes 1179656 | tf_op jit(solution)/shard_map/ppermute | solution.py:142
  35.4 1.3 copy-start.6
  36.6 25.5 %collective-permute-start.7 = (f32[64,256]{1,0:T(8,128)S(1)}, f32[64,256]{1,0:T(8,128)S(1)}, u32[]{:S(2)}, u32[]{:S(2)}) collective-permute-start(f32[64,256]{1,0:T(8,128)S(1)} %copy-done.6), channel_id=1, source_target_pairs={{3,0},{0,1},{1,2},{2,3},{7,4},{4,5},{5,6},{6,7},{11,8},{8,9},{9,10... | collective-permute-start | bytes 196616 | tf_op jit(solution)/shard_map/ppermute | solution.py:142
  62.6 8.7 %copy-start.5 = (f32[64]{0:T(128)S(1)}, f32[64]{0:T(128)}, u32[]{:S(2)}) copy-start(f32[64]{0:T(128)} %param.10) | copy-start | bytes 772
  63.6 8.9 %collective-permute-start.8 = (bf16[64,1408]{1,0:T(8,128)(2,1)S(1)}, bf16[64,1408]{1,0:T(8,128)(2,1)S(1)}, u32[]{:S(2)}, u32[]{:S(2)}) collective-permute-start(bf16[64,1408]{1,0:T(8,128)(2,1)S(1)} %get-tuple-element.43), channel_id=1, source_target_pairs={{0,4},{4,8},{8,12},{12,16},{16,20},{20,24},{24,28},{28,32},{32,36}... | collective-permute-start | bytes 540680 | tf_op jit(solution)/shard_map/ppermute | solution.py:113
  65.5 8.8 %collective-permute-start.9 = (bf16[64,1408]{1,0:T(8,128)(2,1)S(1)}, bf16[64,1408]{1,0:T(8,128)(2,1)S(1)}, u32[]{:S(2)}, u32[]{:S(2)}) collective-permute-start(bf16[64,1408]{1,0:T(8,128)(2,1)S(1)} %get-tuple-element.44), channel_id=1, source_target_pairs={{4,0},{8,4},{12,8},{16,12},{20,16},{24,20},{28,24},{32,28},{36,32}... | collective-permute-start | bytes 540680 | tf_op jit(solution)/shard_map/ppermute | solution.py:116
  75.4 50.3 %copy-start.1 = (f32[64,3072]{1,0:T(8,128)S(1)}, f32[64,3072]{1,0:T(8,128)}, u32[]{:S(2)}) copy-start(f32[64,3072]{1,0:T(8,128)} %copy-done) | copy-start | bytes 2359300
  87.1 3.6 %collective-permute-start.10 = (f32[2]{0:T(128)S(1)}, f32[2]{0:T(128)S(1)}, u32[]{:S(2)}, u32[]{:S(2)}) collective-permute-start(f32[2]{0:T(128)S(1)} %pad_maximum_fusion.3), channel_id=1, source_target_pairs={{0,1},{1,0},{2,3},{3,2},{4,5},{5,4},{6,7},{7,6},{8,9},{9,8},{10,11... | collective-permute-start | bytes 32 | tf_op jit(solution)/shard_map/ppermute | solution.py:127
  92.0 5.1 %collective-permute-start.11 = (f32[2]{0:T(128)S(1)}, f32[2]{0:T(128)S(1)}, u32[]{:S(2)}, u32[]{:S(2)}) collective-permute-start(f32[2]{0:T(128)S(1)} %fusion.31), channel_id=1, source_target_pairs={{0,2},{1,3},{2,0},{3,1},{4,6},{5,7},{6,4},{7,5},{8,10},{9,11},{10,... | collective-permute-start | bytes 32 | tf_op jit(solution)/shard_map/ppermute | solution.py:127
  98.4 1.3 collective-permute-start.12
  99.7 3.5 %collective-permute-start.13 = (f32[2]{0:T(128)S(1)}, f32[2]{0:T(128)S(1)}, u32[]{:S(2)}, u32[]{:S(2)}) collective-permute-start(f32[2]{0:T(128)S(1)} %add.97), channel_id=1, source_target_pairs={{0,8},{4,12},{8,0},{12,4},{16,24},{20,28},{24,16},{28,20},{32,40},... | collective-permute-start | bytes 32 | tf_op jit(solution)/shard_map/ppermute | solution.py:127
  103.3 4.4 %collective-permute-start.14 = (f32[2]{0:T(128)S(1)}, f32[2]{0:T(128)S(1)}, u32[]{:S(2)}, u32[]{:S(2)}) collective-permute-start(f32[2]{0:T(128)S(1)} %add.98), channel_id=1, source_target_pairs={{0,16},{4,20},{8,24},{12,28},{16,0},{20,4},{24,8},{28,12},{32,48},... | collective-permute-start | bytes 32 | tf_op jit(solution)/shard_map/ppermute | solution.py:127
  107.7 7.4 %collective-permute-start.15 = (f32[2]{0:T(128)S(1)}, f32[2]{0:T(128)S(1)}, u32[]{:S(2)}, u32[]{:S(2)}) collective-permute-start(f32[2]{0:T(128)S(1)} %add.99), channel_id=1, source_target_pairs={{0,32},{4,36},{8,40},{12,44},{16,48},{20,52},{24,56},{28,60},{32,0... | collective-permute-start | bytes 32 | tf_op jit(solution)/shard_map/ppermute | solution.py:127
  115.2 3.5 %collective-permute-start.16 = (f32[2]{0:T(128)S(1)}, f32[2]{0:T(128)S(1)}, u32[]{:S(2)}, u32[]{:S(2)}) collective-permute-start(f32[2]{0:T(128)S(1)} %add.100), channel_id=1, source_target_pairs={{0,64},{4,68},{8,72},{12,76},{16,80},{20,84},{24,88},{28,92},{32,9... | collective-permute-start | bytes 32 | tf_op jit(solution)/shard_map/ppermute | solution.py:127
  118.7 5.0 %collective-permute-start.17 = (f32[2]{0:T(128)S(1)}, f32[2]{0:T(128)S(1)}, u32[]{:S(2)}, u32[]{:S(2)}) collective-permute-start(f32[2]{0:T(128)S(1)} %add.101), channel_id=1, source_target_pairs={{0,128},{4,132},{8,136},{12,140},{16,144},{20,148},{24,152},{28,15... | collective-permute-start | bytes 32 | tf_op jit(solution)/shard_map/ppermute | solution.py:127
  127.6 12.4 %collective-permute-start.18 = (f32[]{:T(128)}, f32[]{:T(128)}, u32[]{:S(2)}, u32[]{:S(2)}) collective-permute-start(f32[]{:T(128)} %get-tuple-element.30), channel_id=1, source_target_pairs={{0,1},{1,0},{2,3},{3,2},{4,5},{5,4},{6,7},{7,6},{8,9},{9,8},{10,11... | collective-permute-start | bytes 20 | tf_op jit(solution)/shard_map/ppermute | solution.py:127
  141.3 5.2 %collective-permute-start.19 = (f32[]{:T(128)}, f32[]{:T(128)}, u32[]{:S(2)}, u32[]{:S(2)}) collective-permute-start(f32[]{:T(128)} %add.103), channel_id=1, source_target_pairs={{0,2},{1,3},{2,0},{3,1},{4,6},{5,7},{6,4},{7,5},{8,10},{9,11},{10,... | collective-permute-start | bytes 20 | tf_op jit(solution)/shard_map/ppermute | solution.py:127
  147.2 1.3 collective-permute-start.20
  149.2 3.7 %collective-permute-start.21 = (f32[]{:T(128)}, f32[]{:T(128)}, u32[]{:S(2)}, u32[]{:S(2)}) collective-permute-start(f32[]{:T(128)} %add.105), channel_id=1, source_target_pairs={{0,8},{4,12},{8,0},{12,4},{16,24},{20,28},{24,16},{28,20},{32,40},... | collective-permute-start | bytes 20 | tf_op jit(solution)/shard_map/ppermute | solution.py:127
  153.5 4.6 %collective-permute-start.22 = (f32[]{:T(128)}, f32[]{:T(128)}, u32[]{:S(2)}, u32[]{:S(2)}) collective-permute-start(f32[]{:T(128)} %add.106), channel_id=1, source_target_pairs={{0,16},{4,20},{8,24},{12,28},{16,0},{20,4},{24,8},{28,12},{32,48},... | collective-permute-start | bytes 20 | tf_op jit(solution)/shard_map/ppermute | solution.py:127
  158.8 7.6 %collective-permute-start.23 = (f32[]{:T(128)}, f32[]{:T(128)}, u32[]{:S(2)}, u32[]{:S(2)}) collective-permute-start(f32[]{:T(128)} %add.107), channel_id=1, source_target_pairs={{0,32},{4,36},{8,40},{12,44},{16,48},{20,52},{24,56},{28,60},{32,0... | collective-permute-start | bytes 20 | tf_op jit(solution)/shard_map/ppermute | solution.py:127
  167.1 3.7 %collective-permute-start.24 = (f32[]{:T(128)}, f32[]{:T(128)}, u32[]{:S(2)}, u32[]{:S(2)}) collective-permute-start(f32[]{:T(128)} %add.108), channel_id=1, source_target_pairs={{0,64},{4,68},{8,72},{12,76},{16,80},{20,84},{24,88},{28,92},{32,9... | collective-permute-start | bytes 20 | tf_op jit(solution)/shard_map/ppermute | solution.py:127
  171.4 5.2 %collective-permute-start.25 = (f32[]{:T(128)}, f32[]{:T(128)}, u32[]{:S(2)}, u32[]{:S(2)}) collective-permute-start(f32[]{:T(128)} %add.109), channel_id=1, source_target_pairs={{0,128},{4,132},{8,136},{12,140},{16,144},{20,148},{24,152},{28,15... | collective-permute-start | bytes 20 | tf_op jit(solution)/shard_map/ppermute | solution.py:127
  179.0 14.4 %collective-permute-start.28 = (bf16[64,3072]{1,0:T(8,128)(2,1)S(1)}, bf16[64,3072]{1,0:T(8,128)(2,1)S(1)}, u32[]{:S(2)}, u32[]{:S(2)}) collective-permute-start(bf16[64,3072]{1,0:T(8,128)(2,1)S(1)} %get-tuple-element.28), channel_id=1, source_target_pairs={{3,0},{0,1},{1,2},{2,3},{7,4},{4,5},{5,6},{6,7},{11,8},{8,9},{9,10... | collective-permute-start | bytes 1179656 | tf_op jit(solution)/shard_map/ppermute | solution.py:142
  179.2 14.2 %collective-permute-start.27 = (bf16[64,3072]{1,0:T(8,128)(2,1)S(1)}, bf16[64,3072]{1,0:T(8,128)(2,1)S(1)}, u32[]{:S(2)}, u32[]{:S(2)}) collective-permute-start(bf16[64,3072]{1,0:T(8,128)(2,1)S(1)} %get-tuple-element.28), channel_id=1, source_target_pairs={{2,0},{3,1},{0,2},{1,3},{6,4},{7,5},{4,6},{5,7},{10,8},{11,9},{8,1... | collective-permute-start | bytes 1179656 | tf_op jit(solution)/shard_map/ppermute | solution.py:142
  181.9 12.1 %collective-permute-start.26 = (bf16[64,3072]{1,0:T(8,128)(2,1)S(1)}, bf16[64,3072]{1,0:T(8,128)(2,1)S(1)}, u32[]{:S(2)}, u32[]{:S(2)}) collective-permute-start(bf16[64,3072]{1,0:T(8,128)(2,1)S(1)} %get-tuple-element.28), channel_id=1, source_target_pairs={{1,0},{2,1},{3,2},{0,3},{5,4},{6,5},{7,6},{4,7},{9,8},{10,9},{11,1... | collective-permute-start | bytes 1179656 | tf_op jit(solution)/shard_map/ppermute | solution.py:142
  195.0 8.9 %collective-permute-start.29 = (bf16[64,1408]{1,0:T(8,128)(2,1)S(1)}, bf16[64,1408]{1,0:T(8,128)(2,1)S(1)}, u32[]{:S(2)}, u32[]{:S(2)}) collective-permute-start(bf16[64,1408]{1,0:T(8,128)(2,1)S(1)} %get-tuple-element.41), channel_id=1, source_target_pairs={{0,4},{4,8},{8,12},{12,16},{16,20},{20,24},{24,28},{28,32},{32,36}... | collective-permute-start | bytes 540680 | tf_op jit(solution)/shard_map/ppermute | solution.py:113
  196.9 8.8 %collective-permute-start.30 = (bf16[64,1408]{1,0:T(8,128)(2,1)S(1)}, bf16[64,1408]{1,0:T(8,128)(2,1)S(1)}, u32[]{:S(2)}, u32[]{:S(2)}) collective-permute-start(bf16[64,1408]{1,0:T(8,128)(2,1)S(1)} %get-tuple-element.42), channel_id=1, source_target_pairs={{4,0},{8,4},{12,8},{16,12},{20,16},{24,20},{28,24},{32,28},{36,32}... | collective-permute-start | bytes 540680 | tf_op jit(solution)/shard_map/ppermute | solution.py:116
  206.8 12.1 %copy-start.2 = (f32[64,3072]{1,0:T(8,128)S(1)}, f32[64,3072]{1,0:T(8,128)}, u32[]{:S(2)}) copy-start(f32[64,3072]{1,0:T(8,128)} %get-tuple-element.29.p_ref) | copy-start | bytes 2359300
  217.1 16.0 %collective-permute-start.31 = (f32[]{:T(128)}, f32[]{:T(128)}, u32[]{:S(2)}, u32[]{:S(2)}) collective-permute-start(f32[]{:T(128)} %slice_reduce_fusion), channel_id=1, source_target_pairs={{0,1},{1,0},{2,3},{3,2},{4,5},{5,4},{6,7},{7,6},{8,9},{9,8},{10,11... | collective-permute-start | bytes 20 | tf_op jit(solution)/shard_map/ppermute | solution.py:127
  234.4 5.2 %collective-permute-start.32 = (f32[]{:T(128)}, f32[]{:T(128)}, u32[]{:S(2)}, u32[]{:S(2)}) collective-permute-start(f32[]{:T(128)} %add.112), channel_id=1, source_target_pairs={{0,2},{1,3},{2,0},{3,1},{4,6},{5,7},{6,4},{7,5},{8,10},{9,11},{10,... | collective-permute-start | bytes 20 | tf_op jit(solution)/shard_map/ppermute | solution.py:127
  240.3 1.3 collective-permute-start.33
  242.3 3.7 %collective-permute-start.34 = (f32[]{:T(128)}, f32[]{:T(128)}, u32[]{:S(2)}, u32[]{:S(2)}) collective-permute-start(f32[]{:T(128)} %add.114), channel_id=1, source_target_pairs={{0,8},{4,12},{8,0},{12,4},{16,24},{20,28},{24,16},{28,20},{32,40},... | collective-permute-start | bytes 20 | tf_op jit(solution)/shard_map/ppermute | solution.py:127
  246.7 4.6 %collective-permute-start.35 = (f32[]{:T(128)}, f32[]{:T(128)}, u32[]{:S(2)}, u32[]{:S(2)}) collective-permute-start(f32[]{:T(128)} %add.115), channel_id=1, source_target_pairs={{0,16},{4,20},{8,24},{12,28},{16,0},{20,4},{24,8},{28,12},{32,48},... | collective-permute-start | bytes 20 | tf_op jit(solution)/shard_map/ppermute | solution.py:127
  251.9 7.6 %collective-permute-start.36 = (f32[]{:T(128)}, f32[]{:T(128)}, u32[]{:S(2)}, u32[]{:S(2)}) collective-permute-start(f32[]{:T(128)} %add.116), channel_id=1, source_target_pairs={{0,32},{4,36},{8,40},{12,44},{16,48},{20,52},{24,56},{28,60},{32,0... | collective-permute-start | bytes 20 | tf_op jit(solution)/shard_map/ppermute | solution.py:127
  260.2 3.7 %collective-permute-start.37 = (f32[]{:T(128)}, f32[]{:T(128)}, u32[]{:S(2)}, u32[]{:S(2)}) collective-permute-start(f32[]{:T(128)} %add.117), channel_id=1, source_target_pairs={{0,64},{4,68},{8,72},{12,76},{16,80},{20,84},{24,88},{28,92},{32,9... | collective-permute-start | bytes 20 | tf_op jit(solution)/shard_map/ppermute | solution.py:127
  264.6 5.2 %collective-permute-start.38 = (f32[]{:T(128)}, f32[]{:T(128)}, u32[]{:S(2)}, u32[]{:S(2)}) collective-permute-start(f32[]{:T(128)} %add.118), channel_id=1, source_target_pairs={{0,128},{4,132},{8,136},{12,140},{16,144},{20,148},{24,152},{28,15... | collective-permute-start | bytes 20 | tf_op jit(solution)/shard_map/ppermute | solution.py:127
  273.1 2.9 %copy-start.3 = (f32[64,3072]{0,1:T(8,128)S(1)}, f32[64,3072]{0,1:T(8,128)}, u32[]{:S(2)}) copy-start(f32[64,3072]{0,1:T(8,128)} %get-tuple-element.35) | copy-start | bytes 2359300

commit v16 on v14

--- a/solution.py
+++ b/solution.py
@@ -183,7 +183,7 @@
         mixed_b = mixed.astype(jnp.bfloat16)
         widened = extended(mixed_b, "samp", 1, reach_runs)
         win_v = widened.reshape(chan_local, window_blocks, block_runs).transpose(1, 0, 2)
-        mapped, partials = apply_operator(begin, win_v, tiles, direction, noise_col, 4)
+        mapped, partials = apply_operator(begin, win_v, tiles, direction, noise_col, 8)
         curvature = jnp.sum(partials[:, 0, :])
         if iteration + 1 == ITERS:
             stacked = jnp.concatenate([iterate, remainder, direction, mapped], axis=0)

time: 274 us -> 273 us (level)
  Pallas kernels: 45.2 us -> 41.7 us
  transfers between devices with their start and end apart: 39 -> 39, of which waited for: 29 -> 29; matrix products, arithmetic and copies ran while one was open for 13% -> 13% of each run, Pallas kernels for 10% -> 9%
where the time goes in v16:
time: 273 us; the launch traced here: 272 us
  starting transfers between devices  78.5 us (29%)
  waiting for transfers between devices  76.9 us (28%)
  Pallas kernels  41.7 us (15%)
  local copies, waits for them, and re-layouts  36.7 us (13%)
  other arithmetic  21.4 us (8%)
  between operations  14.2 us (5%)
    ppermute x24, waiting for transfers between devices, global_sum(): value = value + lax.ppermute(value, axis, pairs)  61.1 us
    ppermute x24, starting transfers between devices, global_sum(): value = value + lax.ppermute(value, axis, pairs)  39.8 us
    pallas_call x1, Pallas kernels, build_tiles(): pl.pallas_call(kern, grid_spec=pltpu.PrefetchScalarGridSpec(num_scalar_pr...  25.8 us
    ppermute x3, starting transfers between devices, extended(): lax.ppermute(lax.slice_in_dim(block, 0, width, axis=dim), axis, backward)  19.2 us
    pallas_call x2, Pallas kernels, apply_operator(): pl.pallas_call(kern, grid_spec=pltpu.PrefetchScalarGridSpec(num_scalar_pr...  15.9 us
    scatter x1, local copies, waits for them, and re-layouts, per_device(): unsorted = jnp.zeros_like(stacked).at[:, local_perm].set(stacked)  14.4 us
    ppermute x9, starting transfers between devices, gather_chan(): parts.append(lax.ppermute(rounded, 'chan', pairs))  13.8 us
    ppermute x9, waiting for transfers between devices, gather_chan(): parts.append(lax.ppermute(rounded, 'chan', pairs))  10.5 us
  transfers between devices with their start and end apart: 39, of which 29 were waited for; matrix products, arithmetic and copies ran while one was open for 13% of the time, Pallas kernels for 9%

profile of v16, /device:TPU:2, one launch (start us, length us, event | category | flops | bytes accessed | tf_op | source)
XLA Modules:
  0.0 271.7 jit_solution(15247989025995872431)
XLA Ops:
  0.6 3.3 %collective-permute-start.6 = (f32[64,256]{1,0:T(8,128)}, f32[64,256]{1,0:T(8,128)S(1)}, u32[]{:S(2)}, u32[]{:S(2)}) collective-permute-start(f32[64,256]{1,0:T(8,128)} %param.9), channel_id=1, source_target_pairs={{2,0},{3,1},{0,2},{1,3},{6,4},{7,5},{4,6},{5,7},{10,8},{11,9},{8,1... | collective-permute-start | bytes 196616 | tf_op jit(solution)/shard_map/ppermute | solution.py:136
  9.0 1.9 pad_maximum_fusion
  10.9 8.1 %gather_fusion = f32[3072,70]{1,0:T(8,128)S(1)} fusion(f32[70,3072]{0,1:T(8,128)S(1)} %pad_maximum_fusion, s32[3072]{0:T(1024)S(1)} %broadcast_clamp_fusion), kind=kCustom, calls=%fused_computation | custom fusion | bytes 1732608 | tf_op jit(solution)/shard_map/jit(_take)/gather | solution.py:150
  19.6 1.9 collective-permute-start
  21.5 6.6 %collective-permute-start.1 = (f32[6,1408]{1,0:T(8,128)S(1)}, f32[6,1408]{1,0:T(8,128)S(1)}, u32[]{:S(2)}, u32[]{:S(2)}) collective-permute-start(f32[6,1408]{1,0:T(8,128)S(1)} %get-tuple-element.35), channel_id=1, source_target_pairs={{4,0},{8,4},{12,8},{16,12},{20,16},{24,20},{28,24},{32,28},{36,32}... | collective-permute-start | bytes 101384 | tf_op jit(solution)/shard_map/ppermute | solution.py:116
  32.7 2.5 collective-permute-start.2
  37.2 25.8 %shard_map.86.tile_ref = bf16[24,128,1536]{2,1,0:T(8,128)(2,1)} custom-call(s32[24]{0:T(128)} %clamp_bitcast_fusion.begin_ref, s32[24]{0:T(128)} %count_ref.1, f32[24,128,8]{2,1,0:T(8,128)} %pad_bitcast_fusion.own_ref, f32[46,8,128]{2,1,0:T(8,128)} %pad_bitcast_fusion.1.win_ref), custom_call_target="tpu_custom_call" | custom-call | tf_op jit(solution)/shard_map/pallas_call | solution.py:47
  64.5 1.9 collective-permute-start.8
  66.4 6.8 %collective-permute-start.9 = (bf16[64,1408]{1,0:T(8,128)(2,1)S(1)}, bf16[64,1408]{1,0:T(8,128)(2,1)S(1)}, u32[]{:S(2)}, u32[]{:S(2)}) collective-permute-start(bf16[64,1408]{1,0:T(8,128)(2,1)S(1)} %get-tuple-element.40), channel_id=1, source_target_pairs={{4,0},{8,4},{12,8},{16,12},{20,16},{24,20},{28,24},{32,28},{36,32}... | collective-permute-start | bytes 540680 | tf_op jit(solution)/shard_map/ppermute | solution.py:116
  74.5 1.8 collective-permute-done.9
  77.3 8.0 %shard_map.87 = (f32[64,3072]{1,0:T(8,128)}, f32[3,8,128]{2,1,0:T(8,128)}) custom-call(s32[24]{0:T(128)} %clamp_bitcast_fusion.begin_ref, bf16[46,64,128]{2,1,0:T(8,128)(2,1)} %bitcast_bitcast_fusion.1.win_ref, bf16[24,128,1536]{2,1,0:T(8,128)(2,1)} %shard_map.86.tile_ref, f32[64,3072]{1,0:T(8,128)} %copy-done, f32[64,1]{1,0:T(8,128)} %copy.25.noise_ref), custom_call_target="tpu_custom_call" | custom-call | tf_op jit(solution)/shard_map/pallas_call | solution.py:86
  89.5 2.0 collective-permute-done.10
  92.8 2.4 collective-permute-start.11
  95.2 2.7 collective-permute-done.11
  100.4 3.5 %collective-permute-done.13 = f32[2]{0:T(128)S(1)} collective-permute-done((f32[2]{0:T(128)S(1)}, f32[2]{0:T(128)S(1)}, u32[]{:S(2)}, u32[]{:S(2)}) %collective-permute-start.13) | collective-permute-done | bytes 40 | tf_op jit(solution)/shard_map/ppermute | solution.py:126
  103.9 4.4 %collective-permute-done.14 = f32[2]{0:T(128)S(1)} collective-permute-done((f32[2]{0:T(128)S(1)}, f32[2]{0:T(128)S(1)}, u32[]{:S(2)}, u32[]{:S(2)}) %collective-permute-start.14) | collective-permute-done | bytes 40 | tf_op jit(solution)/shard_map/ppermute | solution.py:126
  109.9 5.9 %collective-permute-done.15 = f32[2]{0:T(128)S(1)} collective-permute-done((f32[2]{0:T(128)S(1)}, f32[2]{0:T(128)S(1)}, u32[]{:S(2)}, u32[]{:S(2)}) %collective-permute-start.15) | collective-permute-done | bytes 40 | tf_op jit(solution)/shard_map/ppermute | solution.py:126
  115.8 3.5 %collective-permute-done.16 = f32[2]{0:T(128)S(1)} collective-permute-done((f32[2]{0:T(128)S(1)}, f32[2]{0:T(128)S(1)}, u32[]{:S(2)}, u32[]{:S(2)}) %collective-permute-start.16) | collective-permute-done | bytes 40 | tf_op jit(solution)/shard_map/ppermute | solution.py:126
  121.1 3.3 %collective-permute-done.17 = f32[2]{0:T(128)S(1)} collective-permute-done((f32[2]{0:T(128)S(1)}, f32[2]{0:T(128)S(1)}, u32[]{:S(2)}, u32[]{:S(2)}) %collective-permute-start.17) | collective-permute-done | bytes 40 | tf_op jit(solution)/shard_map/ppermute | solution.py:126
  126.3 1.9 multiply_reduce_fusion
  129.7 2.3 collective-permute-done.18
  133.3 3.8 %collective-permute-start.19 = (f32[]{:T(128)}, f32[]{:T(128)}, u32[]{:S(2)}, u32[]{:S(2)}) collective-permute-start(f32[]{:T(128)} %add.103), channel_id=1, source_target_pairs={{0,2},{1,3},{2,0},{3,1},{4,6},{5,7},{6,4},{7,5},{8,10},{9,11},{10,... | collective-permute-start | bytes 20 | tf_op jit(solution)/shard_map/ppermute | solution.py:126
  142.5 2.3 collective-permute-done.21
  146.8 3.2 %collective-permute-done.22 = f32[]{:T(128)} collective-permute-done((f32[]{:T(128)}, f32[]{:T(128)}, u32[]{:S(2)}, u32[]{:S(2)}) %collective-permute-start.22) | collective-permute-done | bytes 36 | tf_op jit(solution)/shard_map/ppermute | solution.py:126
  150.7 2.9 %collective-permute-start.23 = (f32[]{:T(128)}, f32[]{:T(128)}, u32[]{:S(2)}, u32[]{:S(2)}) collective-permute-start(f32[]{:T(128)} %add.107), channel_id=1, source_target_pairs={{0,32},{4,36},{8,40},{12,44},{16,48},{20,52},{24,56},{28,60},{32,0... | collective-permute-start | bytes 20 | tf_op jit(solution)/shard_map/ppermute | solution.py:126
  153.6 4.7 %collective-permute-done.23 = f32[]{:T(128)} collective-permute-done((f32[]{:T(128)}, f32[]{:T(128)}, u32[]{:S(2)}, u32[]{:S(2)}) %collective-permute-start.23) | collective-permute-done | bytes 36 | tf_op jit(solution)/shard_map/ppermute | solution.py:126
  160.3 2.3 collective-permute-done.24
  163.3 3.1 %collective-permute-start.25 = (f32[]{:T(128)}, f32[]{:T(128)}, u32[]{:S(2)}, u32[]{:S(2)}) collective-permute-start(f32[]{:T(128)} %add.109), channel_id=1, source_target_pairs={{0,128},{4,132},{8,136},{12,140},{16,144},{20,148},{24,152},{28,15... | collective-permute-start | bytes 20 | tf_op jit(solution)/shard_map/ppermute | solution.py:126
  166.4 2.1 collective-permute-done.25
  172.6 2.9 %collective-permute-start.27 = (bf16[64,3072]{1,0:T(8,128)(2,1)S(1)}, bf16[64,3072]{1,0:T(8,128)(2,1)S(1)}, u32[]{:S(2)}, u32[]{:S(2)}) collective-permute-start(bf16[64,3072]{1,0:T(8,128)(2,1)S(1)} %get-tuple-element.24), channel_id=1, source_target_pairs={{2,0},{3,1},{0,2},{1,3},{6,4},{7,5},{4,6},{5,7},{10,8},{11,9},{8,1... | collective-permute-start | bytes 1179656 | tf_op jit(solution)/shard_map/ppermute | solution.py:136
  176.1 6.3 %collective-permute-done.28 = bf16[64,3072]{1,0:T(8,128)(2,1)S(1)} collective-permute-done((bf16[64,3072]{1,0:T(8,128)(2,1)S(1)}, bf16[64,3072]{1,0:T(8,128)(2,1)S(1)}, u32[]{:S(2)}, u32[]{:S(2)}) %collective-permute-start.28) | collective-permute-done | bytes 393248 | tf_op jit(solution)/shard_map/ppermute | solution.py:136
  182.4 4.2 %collective-permute-done.27 = bf16[64,3072]{1,0:T(8,128)(2,1)S(1)} collective-permute-done((bf16[64,3072]{1,0:T(8,128)(2,1)S(1)}, bf16[64,3072]{1,0:T(8,128)(2,1)S(1)}, u32[]{:S(2)}, u32[]{:S(2)}) %collective-permute-start.27) | collective-permute-done | bytes 393248 | tf_op jit(solution)/shard_map/ppermute | solution.py:136
  187.6 1.9 collective-permute-start.29
  189.5 5.8 %collective-permute-start.30 = (bf16[64,1408]{1,0:T(8,128)(2,1)S(1)}, bf16[64,1408]{1,0:T(8,128)(2,1)S(1)}, u32[]{:S(2)}, u32[]{:S(2)}) collective-permute-start(bf16[64,1408]{1,0:T(8,128)(2,1)S(1)} %get-tuple-element.38), channel_id=1, source_target_pairs={{4,0},{8,4},{12,8},{16,12},{20,16},{24,20},{28,24},{32,28},{36,32}... | collective-permute-start | bytes 540680 | tf_op jit(solution)/shard_map/ppermute | solution.py:116
  196.5 1.8 collective-permute-done.30
  199.4 7.9 %shard_map.88 = (f32[64,3072]{1,0:T(8,128)}, f32[3,8,128]{2,1,0:T(8,128)}) custom-call(s32[24]{0:T(128)} %clamp_bitcast_fusion.begin_ref, bf16[46,64,128]{2,1,0:T(8,128)(2,1)} %bitcast_bitcast_fusion.win_ref, bf16[24,128,1536]{2,1,0:T(8,128)(2,1)} %shard_map.86.tile_ref, f32[64,3072]{1,0:T(8,128)} %get-tuple-element.25.p_ref, f32[64,1]{1,0:T(8,128)} %copy.25.noise_ref), custom_call_target="tpu_custom_call" | custom-call | tf_op jit(solution)/shard_map/pallas_call | solution.py:86
  208.7 2.1 maximum_bitcast_fusion
  210.7 2.3 copy.28
  214.2 14.4 %scatter_custom_fusion = f32[256,3072]{0,1:T(8,128)S(1)} fusion(s32[3072]{0:T(1024)S(1)} %get-tuple-element.29, f32[3072,256]{1,0:T(8,128)} %copy.28, f32[]{:T(128)} %constant.10.clone.1), kind=kCustom, calls=%fused_computation.19 | custom fusion | bytes 3146240 | tf_op jit(solution)/shard_map/scatter | solution.py:190
  230.0 3.8 %collective-permute-start.32 = (f32[]{:T(128)}, f32[]{:T(128)}, u32[]{:S(2)}, u32[]{:S(2)}) collective-permute-start(f32[]{:T(128)} %add.112), channel_id=1, source_target_pairs={{0,2},{1,3},{2,0},{3,1},{4,6},{5,7},{6,4},{7,5},{8,10},{9,11},{10,... | collective-permute-start | bytes 20 | tf_op jit(solution)/shard_map/ppermute | solution.py:126
  238.9 2.2 collective-permute-done.34
  243.1 3.1 %collective-permute-done.35 = f32[]{:T(128)} collective-permute-done((f32[]{:T(128)}, f32[]{:T(128)}, u32[]{:S(2)}, u32[]{:S(2)}) %collective-permute-start.35) | collective-permute-done | bytes 36 | tf_op jit(solution)/shard_map/ppermute | solution.py:126
  246.8 2.5 collective-permute-start.36
  249.3 5.0 %collective-permute-done.36 = f32[]{:T(128)} collective-permute-done((f32[]{:T(128)}, f32[]{:T(128)}, u32[]{:S(2)}, u32[]{:S(2)}) %collective-permute-start.36) | collective-permute-done | bytes 36 | tf_op jit(solution)/shard_map/ppermute | solution.py:126
  256.4 2.2 collective-permute-done.37
  259.2 3.4 %collective-permute-start.38 = (f32[]{:T(128)}, f32[]{:T(128)}, u32[]{:S(2)}, u32[]{:S(2)}) collective-permute-start(f32[]{:T(128)} %add.118), channel_id=1, source_target_pairs={{0,128},{4,132},{8,136},{12,140},{16,144},{20,148},{24,152},{28,15... | collective-permute-start | bytes 20 | tf_op jit(solution)/shard_map/ppermute | solution.py:126
  264.9 2.6 fusion
  267.5 2.9 %copy.30 = f32[64,3072]{1,0:T(8,128)} copy(f32[64,3072]{0,1:T(8,128)} %get-tuple-element.30) | data formatting | bytes 1572864
  (93 shorter events, 55.1 us)
Async XLA Ops:
  0.6 6.7 %copy-start.4 = (f32[6,3072]{1,0:T(8,128)S(1)}, f32[6,3072]{1,0:T(8,128)}, u32[]{:S(2)}) copy-start(f32[6,3072]{1,0:T(8,128)} %param.8) | copy-start | bytes 221188
  0.6 35.8 %collective-permute-start.6 = (f32[64,256]{1,0:T(8,128)}, f32[64,256]{1,0:T(8,128)S(1)}, u32[]{:S(2)}, u32[]{:S(2)}) collective-permute-start(f32[64,256]{1,0:T(8,128)} %param.9), channel_id=1, source_target_pairs={{2,0},{3,1},{0,2},{1,3},{6,4},{7,5},{4,6},{5,7},{10,8},{11,9},{8,1... | collective-permute-start | bytes 196616 | tf_op jit(solution)/shard_map/ppermute | solution.py:136
  3.9 59.0 %collective-permute-start.5 = (f32[64,256]{1,0:T(8,128)}, f32[64,256]{1,0:T(8,128)S(1)}, u32[]{:S(2)}, u32[]{:S(2)}) collective-permute-start(f32[64,256]{1,0:T(8,128)} %param.9), channel_id=1, source_target_pairs={{1,0},{2,1},{3,2},{0,3},{5,4},{6,5},{7,6},{4,7},{9,8},{10,9},{11,1... | collective-permute-start | bytes 196616 | tf_op jit(solution)/shard_map/ppermute | solution.py:136
  19.6 11.1 %collective-permute-start = (f32[6,1408]{1,0:T(8,128)S(1)}, f32[6,1408]{1,0:T(8,128)S(1)}, u32[]{:S(2)}, u32[]{:S(2)}) collective-permute-start(f32[6,1408]{1,0:T(8,128)S(1)} %get-tuple-element.34), channel_id=1, source_target_pairs={{0,4},{4,8},{8,12},{12,16},{16,20},{20,24},{24,28},{28,32},{32,36}... | collective-permute-start | bytes 101384 | tf_op jit(solution)/shard_map/ppermute | solution.py:113
  21.5 9.2 %collective-permute-start.1 = (f32[6,1408]{1,0:T(8,128)S(1)}, f32[6,1408]{1,0:T(8,128)S(1)}, u32[]{:S(2)}, u32[]{:S(2)}) collective-permute-start(f32[6,1408]{1,0:T(8,128)S(1)} %get-tuple-element.35), channel_id=1, source_target_pairs={{4,0},{8,4},{12,8},{16,12},{20,16},{24,20},{28,24},{32,28},{36,32}... | collective-permute-start | bytes 101384 | tf_op jit(solution)/shard_map/ppermute | solution.py:116
  29.0 1.8 copy-start
  30.8 32.5 %collective-permute-start.4 = (bf16[64,3072]{1,0:T(8,128)(2,1)S(1)}, bf16[64,3072]{1,0:T(8,128)(2,1)S(1)}, u32[]{:S(2)}, u32[]{:S(2)}) collective-permute-start(bf16[64,3072]{1,0:T(8,128)(2,1)S(1)} %convert_element_type.18), channel_id=1, source_target_pairs={{3,0},{0,1},{1,2},{2,3},{7,4},{4,5},{5,6},{6,7},{11,8},{8,9},{9,10... | collective-permute-start | bytes 1179656 | tf_op jit(solution)/shard_map/ppermute | solution.py:136
  31.8 31.5 %collective-permute-start.3 = (bf16[64,3072]{1,0:T(8,128)(2,1)S(1)}, bf16[64,3072]{1,0:T(8,128)(2,1)S(1)}, u32[]{:S(2)}, u32[]{:S(2)}) collective-permute-start(bf16[64,3072]{1,0:T(8,128)(2,1)S(1)} %convert_element_type.18), channel_id=1, source_target_pairs={{2,0},{3,1},{0,2},{1,3},{6,4},{7,5},{4,6},{5,7},{10,8},{11,9},{8,1... | collective-permute-start | bytes 1179656 | tf_op jit(solution)/shard_map/ppermute | solution.py:136
  32.7 30.7 %collective-permute-start.2 = (bf16[64,3072]{1,0:T(8,128)(2,1)S(1)}, bf16[64,3072]{1,0:T(8,128)(2,1)S(1)}, u32[]{:S(2)}, u32[]{:S(2)}) collective-permute-start(bf16[64,3072]{1,0:T(8,128)(2,1)S(1)} %convert_element_type.18), channel_id=1, source_target_pairs={{1,0},{2,1},{3,2},{0,3},{5,4},{6,5},{7,6},{4,7},{9,8},{10,9},{11,1... | collective-permute-start | bytes 1179656 | tf_op jit(solution)/shard_map/ppermute | solution.py:136
  35.2 1.3 copy-start.6
  36.5 26.5 %collective-permute-start.7 = (f32[64,256]{1,0:T(8,128)S(1)}, f32[64,256]{1,0:T(8,128)S(1)}, u32[]{:S(2)}, u32[]{:S(2)}) collective-permute-start(f32[64,256]{1,0:T(8,128)S(1)} %copy-done.6), channel_id=1, source_target_pairs={{3,0},{0,1},{1,2},{2,3},{7,4},{4,5},{5,6},{6,7},{11,8},{8,9},{9,10... | collective-permute-start | bytes 196616 | tf_op jit(solution)/shard_map/ppermute | solution.py:136
  63.5 9.8 %copy-start.5 = (f32[64]{0:T(128)S(1)}, f32[64]{0:T(128)}, u32[]{:S(2)}) copy-start(f32[64]{0:T(128)} %param.10) | copy-start | bytes 772
  64.5 10.0 %collective-permute-start.8 = (bf16[64,1408]{1,0:T(8,128)(2,1)S(1)}, bf16[64,1408]{1,0:T(8,128)(2,1)S(1)}, u32[]{:S(2)}, u32[]{:S(2)}) collective-permute-start(bf16[64,1408]{1,0:T(8,128)(2,1)S(1)} %get-tuple-element.39), channel_id=1, source_target_pairs={{0,4},{4,8},{8,12},{12,16},{16,20},{20,24},{24,28},{28,32},{32,36}... | collective-permute-start | bytes 540680 | tf_op jit(solution)/shard_map/ppermute | solution.py:113
  66.4 9.8 %collective-permute-start.9 = (bf16[64,1408]{1,0:T(8,128)(2,1)S(1)}, bf16[64,1408]{1,0:T(8,128)(2,1)S(1)}, u32[]{:S(2)}, u32[]{:S(2)}) collective-permute-start(bf16[64,1408]{1,0:T(8,128)(2,1)S(1)} %get-tuple-element.40), channel_id=1, source_target_pairs={{4,0},{8,4},{12,8},{16,12},{20,16},{24,20},{28,24},{32,28},{36,32}... | collective-permute-start | bytes 540680 | tf_op jit(solution)/shard_map/ppermute | solution.py:116
  77.3 48.9 %copy-start.1 = (f32[64,3072]{1,0:T(8,128)S(1)}, f32[64,3072]{1,0:T(8,128)}, u32[]{:S(2)}) copy-start(f32[64,3072]{1,0:T(8,128)} %copy-done) | copy-start | bytes 2359300
  87.9 3.6 %collective-permute-start.10 = (f32[2]{0:T(128)S(1)}, f32[2]{0:T(128)S(1)}, u32[]{:S(2)}, u32[]{:S(2)}) collective-permute-start(f32[2]{0:T(128)S(1)} %pad_maximum_fusion.3), channel_id=1, source_target_pairs={{0,1},{1,0},{2,3},{3,2},{4,5},{5,4},{6,7},{7,6},{8,9},{9,8},{10,11... | collective-permute-start | bytes 32 | tf_op jit(solution)/shard_map/ppermute | solution.py:126
  92.8 5.1 %collective-permute-start.11 = (f32[2]{0:T(128)S(1)}, f32[2]{0:T(128)S(1)}, u32[]{:S(2)}, u32[]{:S(2)}) collective-permute-start(f32[2]{0:T(128)S(1)} %fusion.29), channel_id=1, source_target_pairs={{0,2},{1,3},{2,0},{3,1},{4,6},{5,7},{6,4},{7,5},{8,10},{9,11},{10,... | collective-permute-start | bytes 32 | tf_op jit(solution)/shard_map/ppermute | solution.py:126
  99.1 1.3 collective-permute-start.12
  100.4 3.5 %collective-permute-start.13 = (f32[2]{0:T(128)S(1)}, f32[2]{0:T(128)S(1)}, u32[]{:S(2)}, u32[]{:S(2)}) collective-permute-start(f32[2]{0:T(128)S(1)} %add.97), channel_id=1, source_target_pairs={{0,8},{4,12},{8,0},{12,4},{16,24},{20,28},{24,16},{28,20},{32,40},... | collective-permute-start | bytes 32 | tf_op jit(solution)/shard_map/ppermute | solution.py:126
  103.9 4.4 %collective-permute-start.14 = (f32[2]{0:T(128)S(1)}, f32[2]{0:T(128)S(1)}, u32[]{:S(2)}, u32[]{:S(2)}) collective-permute-start(f32[2]{0:T(128)S(1)} %add.98), channel_id=1, source_target_pairs={{0,16},{4,20},{8,24},{12,28},{16,0},{20,4},{24,8},{28,12},{32,48},... | collective-permute-start | bytes 32 | tf_op jit(solution)/shard_map/ppermute | solution.py:126
  108.4 7.4 %collective-permute-start.15 = (f32[2]{0:T(128)S(1)}, f32[2]{0:T(128)S(1)}, u32[]{:S(2)}, u32[]{:S(2)}) collective-permute-start(f32[2]{0:T(128)S(1)} %add.99), channel_id=1, source_target_pairs={{0,32},{4,36},{8,40},{12,44},{16,48},{20,52},{24,56},{28,60},{32,0... | collective-permute-start | bytes 32 | tf_op jit(solution)/shard_map/ppermute | solution.py:126
  115.8 3.5 %collective-permute-start.16 = (f32[2]{0:T(128)S(1)}, f32[2]{0:T(128)S(1)}, u32[]{:S(2)}, u32[]{:S(2)}) collective-permute-start(f32[2]{0:T(128)S(1)} %add.100), channel_id=1, source_target_pairs={{0,64},{4,68},{8,72},{12,76},{16,80},{20,84},{24,88},{28,92},{32,9... | collective-permute-start | bytes 32 | tf_op jit(solution)/shard_map/ppermute | solution.py:126
  119.4 5.0 %collective-permute-start.17 = (f32[2]{0:T(128)S(1)}, f32[2]{0:T(128)S(1)}, u32[]{:S(2)}, u32[]{:S(2)}) collective-permute-start(f32[2]{0:T(128)S(1)} %add.101), channel_id=1, source_target_pairs={{0,128},{4,132},{8,136},{12,140},{16,144},{20,148},{24,152},{28,15... | collective-permute-start | bytes 32 | tf_op jit(solution)/shard_map/ppermute | solution.py:126
  128.2 42.9 %copy-start.2 = (f32[64,3072]{1,0:T(8,128)}, f32[64,3072]{1,0:T(8,128)S(1)}, u32[]{:S(2)}) copy-start(f32[64,3072]{1,0:T(8,128)S(1)} %get-tuple-element.27) | copy-start | bytes 2359300
  128.2 3.8 %collective-permute-start.18 = (f32[]{:T(128)}, f32[]{:T(128)}, u32[]{:S(2)}, u32[]{:S(2)}) collective-permute-start(f32[]{:T(128)} %get-tuple-element.26), channel_id=1, source_target_pairs={{0,1},{1,0},{2,3},{3,2},{4,5},{5,4},{6,7},{7,6},{8,9},{9,8},{10,11... | collective-permute-start | bytes 20 | tf_op jit(solution)/shard_map/ppermute | solution.py:126
  133.3 5.2 %collective-permute-start.19 = (f32[]{:T(128)}, f32[]{:T(128)}, u32[]{:S(2)}, u32[]{:S(2)}) collective-permute-start(f32[]{:T(128)} %add.103), channel_id=1, source_target_pairs={{0,2},{1,3},{2,0},{3,1},{4,6},{5,7},{6,4},{7,5},{8,10},{9,11},{10,... | collective-permute-start | bytes 20 | tf_op jit(solution)/shard_map/ppermute | solution.py:126
  139.1 1.3 collective-permute-start.20
  141.1 3.7 %collective-permute-start.21 = (f32[]{:T(128)}, f32[]{:T(128)}, u32[]{:S(2)}, u32[]{:S(2)}) collective-permute-start(f32[]{:T(128)} %add.105), channel_id=1, source_target_pairs={{0,8},{4,12},{8,0},{12,4},{16,24},{20,28},{24,16},{28,20},{32,40},... | collective-permute-start | bytes 20 | tf_op jit(solution)/shard_map/ppermute | solution.py:126
  145.4 4.6 %collective-permute-start.22 = (f32[]{:T(128)}, f32[]{:T(128)}, u32[]{:S(2)}, u32[]{:S(2)}) collective-permute-start(f32[]{:T(128)} %add.106), channel_id=1, source_target_pairs={{0,16},{4,20},{8,24},{12,28},{16,0},{20,4},{24,8},{28,12},{32,48},... | collective-permute-start | bytes 20 | tf_op jit(solution)/shard_map/ppermute | solution.py:126
  150.7 7.6 %collective-permute-start.23 = (f32[]{:T(128)}, f32[]{:T(128)}, u32[]{:S(2)}, u32[]{:S(2)}) collective-permute-start(f32[]{:T(128)} %add.107), channel_id=1, source_target_pairs={{0,32},{4,36},{8,40},{12,44},{16,48},{20,52},{24,56},{28,60},{32,0... | collective-permute-start | bytes 20 | tf_op jit(solution)/shard_map/ppermute | solution.py:126
  159.0 3.7 %collective-permute-start.24 = (f32[]{:T(128)}, f32[]{:T(128)}, u32[]{:S(2)}, u32[]{:S(2)}) collective-permute-start(f32[]{:T(128)} %add.108), channel_id=1, source_target_pairs={{0,64},{4,68},{8,72},{12,76},{16,80},{20,84},{24,88},{28,92},{32,9... | collective-permute-start | bytes 20 | tf_op jit(solution)/shard_map/ppermute | solution.py:126
  163.3 5.2 %collective-permute-start.25 = (f32[]{:T(128)}, f32[]{:T(128)}, u32[]{:S(2)}, u32[]{:S(2)}) collective-permute-start(f32[]{:T(128)} %add.109), channel_id=1, source_target_pairs={{0,128},{4,132},{8,136},{12,140},{16,144},{20,148},{24,152},{28,15... | collective-permute-start | bytes 20 | tf_op jit(solution)/shard_map/ppermute | solution.py:126
  171.1 11.3 %collective-permute-start.28 = (bf16[64,3072]{1,0:T(8,128)(2,1)S(1)}, bf16[64,3072]{1,0:T(8,128)(2,1)S(1)}, u32[]{:S(2)}, u32[]{:S(2)}) collective-permute-start(bf16[64,3072]{1,0:T(8,128)(2,1)S(1)} %get-tuple-element.24), channel_id=1, source_target_pairs={{3,0},{0,1},{1,2},{2,3},{7,4},{4,5},{5,6},{6,7},{11,8},{8,9},{9,10... | collective-permute-start | bytes 1179656 | tf_op jit(solution)/shard_map/ppermute | solution.py:136
  172.6 14.0 %collective-permute-start.27 = (bf16[64,3072]{1,0:T(8,128)(2,1)S(1)}, bf16[64,3072]{1,0:T(8,128)(2,1)S(1)}, u32[]{:S(2)}, u32[]{:S(2)}) collective-permute-start(bf16[64,3072]{1,0:T(8,128)(2,1)S(1)} %get-tuple-element.24), channel_id=1, source_target_pairs={{2,0},{3,1},{0,2},{1,3},{6,4},{7,5},{4,6},{5,7},{10,8},{11,9},{8,1... | collective-permute-start | bytes 1179656 | tf_op jit(solution)/shard_map/ppermute | solution.py:136
  175.5 11.1 %collective-permute-start.26 = (bf16[64,3072]{1,0:T(8,128)(2,1)S(1)}, bf16[64,3072]{1,0:T(8,128)(2,1)S(1)}, u32[]{:S(2)}, u32[]{:S(2)}) collective-permute-start(bf16[64,3072]{1,0:T(8,128)(2,1)S(1)} %get-tuple-element.24), channel_id=1, source_target_pairs={{1,0},{2,1},{3,2},{0,3},{5,4},{6,5},{7,6},{4,7},{9,8},{10,9},{11,1... | collective-permute-start | bytes 1179656 | tf_op jit(solution)/shard_map/ppermute | solution.py:136
  187.6 8.9 %collective-permute-start.29 = (bf16[64,1408]{1,0:T(8,128)(2,1)S(1)}, bf16[64,1408]{1,0:T(8,128)(2,1)S(1)}, u32[]{:S(2)}, u32[]{:S(2)}) collective-permute-start(bf16[64,1408]{1,0:T(8,128)(2,1)S(1)} %get-tuple-element.37), channel_id=1, source_target_pairs={{0,4},{4,8},{8,12},{12,16},{16,20},{20,24},{24,28},{28,32},{32,36}... | collective-permute-start | bytes 540680 | tf_op jit(solution)/shard_map/ppermute | solution.py:113
  189.5 8.8 %collective-permute-start.30 = (bf16[64,1408]{1,0:T(8,128)(2,1)S(1)}, bf16[64,1408]{1,0:T(8,128)(2,1)S(1)}, u32[]{:S(2)}, u32[]{:S(2)}) collective-permute-start(bf16[64,1408]{1,0:T(8,128)(2,1)S(1)} %get-tuple-element.38), channel_id=1, source_target_pairs={{4,0},{8,4},{12,8},{16,12},{20,16},{24,20},{28,24},{32,28},{36,32}... | collective-permute-start | bytes 540680 | tf_op jit(solution)/shard_map/ppermute | solution.py:116
  213.1 15.6 %collective-permute-start.31 = (f32[]{:T(128)}, f32[]{:T(128)}, u32[]{:S(2)}, u32[]{:S(2)}) collective-permute-start(f32[]{:T(128)} %slice_reduce_fusion), channel_id=1, source_target_pairs={{0,1},{1,0},{2,3},{3,2},{4,5},{5,4},{6,7},{7,6},{8,9},{9,8},{10,11... | collective-permute-start | bytes 20 | tf_op jit(solution)/shard_map/ppermute | solution.py:126
  230.0 5.1 %collective-permute-start.32 = (f32[]{:T(128)}, f32[]{:T(128)}, u32[]{:S(2)}, u32[]{:S(2)}) collective-permute-start(f32[]{:T(128)} %add.112), channel_id=1, source_target_pairs={{0,2},{1,3},{2,0},{3,1},{4,6},{5,7},{6,4},{7,5},{8,10},{9,11},{10,... | collective-permute-start | bytes 20 | tf_op jit(solution)/shard_map/ppermute | solution.py:126
  235.7 1.2 collective-permute-start.33
  237.5 3.6 %collective-permute-start.34 = (f32[]{:T(128)}, f32[]{:T(128)}, u32[]{:S(2)}, u32[]{:S(2)}) collective-permute-start(f32[]{:T(128)} %add.114), channel_id=1, source_target_pairs={{0,8},{4,12},{8,0},{12,4},{16,24},{20,28},{24,16},{28,20},{32,40},... | collective-permute-start | bytes 20 | tf_op jit(solution)/shard_map/ppermute | solution.py:126
  241.7 4.5 %collective-permute-start.35 = (f32[]{:T(128)}, f32[]{:T(128)}, u32[]{:S(2)}, u32[]{:S(2)}) collective-permute-start(f32[]{:T(128)} %add.115), channel_id=1, source_target_pairs={{0,16},{4,20},{8,24},{12,28},{16,0},{20,4},{24,8},{28,12},{32,48},... | collective-permute-start | bytes 20 | tf_op jit(solution)/shard_map/ppermute | solution.py:126
  246.8 7.5 %collective-permute-start.36 = (f32[]{:T(128)}, f32[]{:T(128)}, u32[]{:S(2)}, u32[]{:S(2)}) collective-permute-start(f32[]{:T(128)} %add.116), channel_id=1, source_target_pairs={{0,32},{4,36},{8,40},{12,44},{16,48},{20,52},{24,56},{28,60},{32,0... | collective-permute-start | bytes 20 | tf_op jit(solution)/shard_map/ppermute | solution.py:126
  255.0 3.6 %collective-permute-start.37 = (f32[]{:T(128)}, f32[]{:T(128)}, u32[]{:S(2)}, u32[]{:S(2)}) collective-permute-start(f32[]{:T(128)} %add.117), channel_id=1, source_target_pairs={{0,64},{4,68},{8,72},{12,76},{16,80},{20,84},{24,88},{28,92},{32,9... | collective-permute-start | bytes 20 | tf_op jit(solution)/shard_map/ppermute | solution.py:126
  259.2 5.1 %collective-permute-start.38 = (f32[]{:T(128)}, f32[]{:T(128)}, u32[]{:S(2)}, u32[]{:S(2)}) collective-permute-start(f32[]{:T(128)} %add.118), channel_id=1, source_target_pairs={{0,128},{4,132},{8,136},{12,140},{16,144},{20,148},{24,152},{28,15... | collective-permute-start | bytes 20 | tf_op jit(solution)/shard_map/ppermute | solution.py:126
  267.5 2.9 %copy-start.3 = (f32[64,3072]{0,1:T(8,128)S(1)}, f32[64,3072]{0,1:T(8,128)}, u32[]{:S(2)}) copy-start(f32[64,3072]{0,1:T(8,128)} %get-tuple-element.31) | copy-start | bytes 2359300
